TPU v7x, 32 devices: a whole 2x2x4 slice. The times are simulated.
32 devices in a mesh: groups: 2 (over y), inner: 16 (over z, x, core).
Axes of the slice: x: 2, y: 2, z: 4, core: 2. Of those that a mesh axis runs over, the one named last changes fastest.
Arguments:
- ticks: bfloat16 [262144, 128], P(('groups', 'inner')), parts along dimension 0, may hold values from -6 to 6
- conv_weight: bfloat16 [2048, 768], replicated, may hold values from -0.125 to 0.125
- norm_gain: float32 [768], replicated, may hold values from 0.25 to 1.75
- qkv_weight: bfloat16 [768, 2304], replicated, may hold values from -0.21875 to 0.21875
- head_gain: float32 [768], replicated, may hold values from 0.25 to 1.75
- out_weight: bfloat16 [768, 768], replicated, may hold values from -0.21875 to 0.21875
- state_in: float32 [24, 64, 64], P('groups'), parts along dimension 0, may hold values from -768 to 768
Outputs:
- layer_out: bfloat16 [32768, 768], P(('groups', 'inner')), parts along dimension 0
There are 2 independent parts, one for each index of `groups`. A program takes and returns all parts, laid end to end along the dimension named above; an argument that names none is the same for every part. Nothing has to cross between parts.
All inputs are finite; a program needn't handle non-finite values.
Results may differ from a plain program's by a relative error of at most 0.008.
Values may be sent and summed in bfloat16 or wider, within the bound.
No kernel may reach another device: no remote copies, remote signals or barrier semaphores. Data moves between devices by JAX's collectives and lax.ppermute only.
A program may use at most 192 MiB of HBM per device.

v0:
```python
import jax
import jax.numpy as jnp
from jax import lax
from jax.sharding import PartitionSpec as P

STRIDE = 8
BLK = 512


def from_behind(value, axis, steps):
    count = lax.axis_size(axis)
    initial, last = (max(0, -steps), min(count, count - steps))
    return lax.ppermute(value, axis, [(source, source + steps) for source in range(initial, last)])


def shards(ticks, conv_weight, norm_gain, qkv_weight, head_gain, out_weight, state_in):
    row_width = STRIDE * ticks.shape[1]
    token_count = ticks.shape[0] // STRIDE
    tick_rows = ticks.reshape(token_count, row_width)
    weight_prev = conv_weight[:row_width]
    current = jnp.dot(tick_rows, conv_weight[row_width:], preferred_element_type=jnp.float32)
    last_row = from_behind(tick_rows[token_count - 1 :], "inner", 1)
    earlier_rows = jnp.concatenate([last_row, tick_rows[:-1]], 0)
    embedded_f = current + jnp.dot(earlier_rows, weight_prev, preferred_element_type=jnp.float32)
    embedded = embedded_f.astype(jnp.bfloat16)
    embed_f = embedded.astype(jnp.float32)
    normed = (
        embed_f * lax.rsqrt(jnp.mean(embed_f * embed_f, -1, keepdims=True) + 1e-05) * norm_gain
    ).astype(jnp.bfloat16)
    qkv = jnp.dot(normed, qkv_weight, preferred_element_type=jnp.float32).astype(jnp.bfloat16)
    model_width = embedded.shape[1]
    head_count = state_in.shape[0]
    head_size = state_in.shape[1]
    block_count = token_count // BLK
    queries = qkv[:, :model_width].reshape(block_count, BLK, head_count, head_size)
    keys_all = qkv[:, model_width : 2 * model_width].reshape(
        block_count, BLK, head_count, head_size
    )
    values_all = qkv[:, 2 * model_width :].reshape(block_count, BLK, head_count, head_size)
    block_states = jnp.einsum(
        "bthi,bthj->bhij", keys_all, values_all, preferred_element_type=jnp.float32
    )
    local_state = jnp.sum(block_states, 0)
    every_state = lax.all_gather(local_state[None], "inner", axis=0, tiled=True)
    lower_dev = (jnp.arange(every_state.shape[0]) < lax.axis_index("inner")).astype(jnp.float32)
    prefix = jnp.einsum("n,nhij->hij", lower_dev, every_state, precision=lax.Precision.HIGHEST)
    carried = state_in + prefix
    within = jnp.cumsum(block_states, 0) - block_states
    state_before = carried[None] + within
    lower = jnp.arange(BLK)[:, None] >= jnp.arange(BLK)[None, :]
    scores = jnp.einsum("bthd,bshd->bhts", queries, keys_all, preferred_element_type=jnp.float32)
    scores = jnp.where(lower[None, None], scores, 0.0).astype(jnp.bfloat16)
    inside_term = jnp.einsum(
        "bhts,bshd->bthd", scores, values_all, preferred_element_type=jnp.float32
    )
    carried_term = jnp.einsum(
        "bthi,bhij->bthj",
        queries.astype(jnp.float32),
        state_before,
        precision=lax.Precision.HIGHEST,
    )
    combined = (inside_term + carried_term).reshape(token_count, head_count, head_size)
    attended = (
        combined
        * lax.rsqrt(jnp.mean(combined * combined, -1, keepdims=True) + 1e-06)
        * head_gain.reshape(head_count, head_size)
    )
    attended = attended.reshape(token_count, model_width).astype(jnp.bfloat16)
    return (embed_f + jnp.dot(attended, out_weight, preferred_element_type=jnp.float32)).astype(
        jnp.bfloat16
    )


def solution(mesh):
    in_specs = (P(("groups", "inner"), None), P(), P(), P(), P(), P(), P("groups", None, None))
    out_specs = P(("groups", "inner"), None)
    return jax.shard_map(shards, mesh=mesh, in_specs=in_specs, out_specs=out_specs, check_vma=False)
```

profile of v0, /device:TPU:0, one launch (start us, length us, event | category | flops | bytes accessed | tf_op | source)
XLA Modules:
  0.0 145.3 jit_solution(13970756868127508273)
XLA Ops:
  6.5 0.0 copy-start
  6.5 0.0 all-gather.3.cloned.1.call-start
  6.5 0.8 slice_bitcast_fusion
  7.4 2.5 %collective-permute-start = (bf16[1,1024]{1,0:T(2,128)(2,1)S(1)}, bf16[1,1024]{1,0:T(2,128)(2,1)S(1)}, u32[]{:S(2)}, u32[]{:S(2)}) collective-permute-start(bf16[1,1024]{1,0:T(2,128)(2,1)S(1)} %bitcast.53), channel_id=1, source_target_pairs={{0,1},{1,2},{2,3},{3,4},{4,5},{5,6},{6,7},{7,8},{8,9},{9,10},{10,1... | collective-permute-start | bytes 6152 | tf_op jit(solution)/shard_map/ppermute | solution.py:13
  9.9 4.2 %reshape.62 = bf16[1024,1024]{1,0:T(8,128)(2,1)} reshape(bf16[8192,128]{1,0:T(8,128)(2,1)} %param.7) | data formatting | bytes 4194304 | tf_op jit(solution)/shard_map/reshape | solution.py:19
  14.0 0.0 copy-start.2
  14.0 5.7 %fusion.21 = f32[1024,768]{0,1:T(8,128)} fusion(bf16[1024,1024]{1,0:T(8,128)(2,1)} %reshape.62, bf16[2048,768]{1,0:T(8,128)(2,1)} %param.8), kind=kOutput, calls=%fused_computation.28 | convolution fusion | flops 1610612736 | bytes 6815744 | tf_op jit(solution)/shard_map/dot_general | solution.py:21
  19.7 0.0 copy-done.2
  19.7 1.5 %slice.30 = bf16[8184,128]{1,0:T(8,128)(2,1)} slice(bf16[8192,128]{1,0:T(8,128)(2,1)S(1)} %copy-done.2), slice={[0:8184], [0:128]} | slice | bytes 4190208 | tf_op jit(solution)/shard_map/slice | solution.py:23
  21.2 4.2 %slice.31 = bf16[1023,1024]{1,0:T(8,128)(2,1)} reshape(bf16[8184,128]{1,0:T(8,128)(2,1)} %slice.30) | data formatting | bytes 4190208 | tf_op jit(solution)/shard_map/slice | solution.py:23
  25.3 0.0 copy-start.11
  25.3 0.0 collective-permute-done
  25.3 5.0 %fusion.7 = (f32[1024]{0:T(1024)S(1)}, bf16[1024,768]{0,1:T(8,128)(2,1)S(1)}) fusion(f32[1024,768]{0,1:T(8,128)} %fusion.21, bf16[2048,768]{1,0:T(8,128)(2,1)} %param.8, bf16[1023,1024]{1,0:T(8,128)(2,1)} %slice.31, bf16[1,1024]{1,0:T(2,128)(2,1)S(1)} %collective-permute-done), kind=kOutput, calls=%fused_computation.11 | convolution fusion | flops 1618738176 | bytes 8394752 | tf_op jit(solution)/shard_map/dot_general | solution.py:24
  30.3 0.0 copy-start.12
  30.3 0.0 copy-done
  30.4 0.0 copy-done.11
  30.4 4.4 %convolution_convert_fusion = bf16[1024,2304]{1,0:T(8,128)(2,1)S(1)} fusion(bf16[768,2304]{1,0:T(8,128)(2,1)S(1)} %copy-done, bf16[1024,768]{0,1:T(8,128)(2,1)S(1)} %get-tuple-element.9, f32[768]{0:T(1024)S(1)} %copy-done.11, f32[1024]{0:T(1024)S(1)} %add_rsqrt_fusion.1), kind=kOutput, calls=%fused_computation.7 | convolution fusion | flops 3629383680 | bytes 9837568 | tf_op jit(solution)/shard_map/dot_general | solution.py:30
  34.7 0.0 copy-done.12
  34.8 1.5 %fusion.43 = (bf16[1024,768]{1,0:T(8,128)(2,1)S(1)}, bf16[1024,768]{1,0:T(8,128)(2,1)S(1)}, bf16[1024,768]{1,0:T(8,128)(2,1)}) fusion(bf16[1024,2304]{1,0:T(8,128)(2,1)S(1)} %convolution_convert_fusion), kind=kLoop, calls=%fused_computation.51 | loop fusion | bytes 9437184 | tf_op jit(solution)/shard_map/slice | solution.py:35
  36.2 2.6 %copy.39 = bf16[1024,768]{0,1:T(8,128)(2,1)} copy(bf16[1024,768]{1,0:T(8,128)(2,1)} %get-tuple-element.7) | data formatting | bytes 3145728 | tf_op jit(solution)/shard_map/slice | solution.py:39
  38.8 3.9 %reshape.63 = bf16[2,512,12,64]{1,0,3,2:T(2,128)(2,1)} reshape(bf16[1024,768]{0,1:T(8,128)(2,1)} %copy.39) | data formatting | bytes 3145728 | tf_op jit(solution)/shard_map/reshape | solution.py:39
  42.7 1.7 %copy.41 = bf16[1024,768]{0,1:T(8,128)(2,1)} copy(bf16[1024,768]{1,0:T(8,128)(2,1)S(1)} %get-tuple-element.6) | data formatting | bytes 3145728 | tf_op jit(solution)/shard_map/slice | solution.py:36
  44.4 0.0 copy-start.7
  44.4 4.0 %reshape.65 = bf16[2,512,12,64]{1,0,3,2:T(2,128)(2,1)} reshape(bf16[1024,768]{0,1:T(8,128)(2,1)} %copy.41) | data formatting | bytes 3145728 | tf_op jit(solution)/shard_map/reshape | solution.py:36
  48.3 0.0 copy-done.7
  48.3 3.7 %fusion.44 = (f32[12,64,64]{2,1,0:T(8,128)}, f32[2,12,64,64]{3,2,1,0:T(8,128)}) fusion(bf16[2,512,12,64]{1,0,3,2:T(2,128)(2,1)S(1)} %copy-done.7, bf16[2,512,12,64]{1,0,3,2:T(2,128)(2,1)} %reshape.65), kind=kOutput, calls=%fused_computation.52 | convolution fusion | flops 100712448 | bytes 3735552 | tf_op jit(solution)/shard_map/bthi,bthj->bhij/dot_general | solution.py:40
  52.0 0.0 all-gather.3.cloned.1.call-update
  52.0 0.1 iota_compare_fusion
  52.1 0.8 copy.40
  52.9 1.2 reshape.64
  54.1 0.0 copy-start.3
  54.1 10.5 %fusion = f32[2,12,64,512]{3,2,1,0:T(8,128)} fusion(pred[512,512]{1,0:T(8,128)(4,1)S(1)} %iota_compare_fusion, bf16[2,512,12,64]{1,0,3,2:T(2,128)(2,1)} %reshape.63, bf16[2,512,12,64]{1,0,3,2:T(2,128)(2,1)} %reshape.65, bf16[2,512,12,64]{1,0,3,2:T(2,128)(2,1)S(1)} %reshape.64), kind=kOutput, calls=%fused_computation.1 | convolution fusion | flops 1623195648 | bytes 8126464 | tf_op jit(solution)/shard_map/bhts,bshd->bthd/dot_general | solution.py:53
  64.6 0.0 copy-done.3
  64.6 52.0 %all-gather.3.cloned.1.call-done = f32[192,64,64]{2,1,0:T(8,128)} async-done(((f32[12,64,64]{2,1,0:T(8,128)}), f32[192,64,64]{2,1,0:T(8,128)}) %all-gather.3.cloned.1.call-update) | async-done | bytes 3145744 | tf_op jit(solution)/shard_map/all_gather | solution.py:44
  116.6 0.0 copy-start.8
  116.6 0.0 copy-start.6
  116.6 0.0 copy-start.5
  116.6 8.4 %fusion.5 = f32[1,12,64,64]{3,0,2,1:T(1,128)S(1)} fusion(f32[16,12,64,64]{3,2,1,0:T(8,128)} %bitcast.48, s32[]{:T(128)S(6)} %axis_index.12), kind=kOutput, calls=%fused_computation.5 | convolution fusion | flops 9437200 | bytes 3342340 | tf_op jit(solution)/shard_map/n,nhij->hij/dot_general | solution.py:46
  125.0 0.0 copy-start.4
  125.0 0.0 copy-done.8
  125.1 0.0 copy-done.6
  125.1 0.5 fusion.27
  125.6 0.0 copy-done.5
  125.6 0.8 copy-done.4
  126.4 1.7 %multiply_reduce_fusion = (f32[2,512,12]{1,2,0:T(8,128)S(1)}, f32[2,512,12,64]{1,3,2,0:T(8,128)S(1)}) fusion(f32[2,12,64,512]{3,2,1,0:T(8,128)S(1)} %copy-done.5, f32[2,12,64,64]{3,2,1,0:T(8,128)S(1)} %fusion.27, bf16[2,512,12,64]{1,0,3,2:T(2,128)(2,1)S(1)} %copy-done.4), kind=kOutput, calls=%fused_computation.18 | convolution fusion | flops 606326784 | bytes 8306688 | tf_op jit(solution)/shard_map/bthi,bhij->bthj/dot_general | solution.py:56
  128.2 2.4 %copy.49 = f32[2,512,12,64]{1,0,3,2:T(2,128)S(1)} copy(f32[2,512,12,64]{1,3,2,0:T(8,128)S(1)} %get-tuple-element.13) | data formatting | bytes 6291456 | tf_op jit(solution)/shard_map/add | solution.py:62
  130.6 0.0 copy-start.9
  130.6 0.7 copy.59
  131.5 0.0 copy-done.9
  131.5 0.0 copy-start.10
  131.5 0.0 copy-start.13
  131.5 0.4 fusion.12
  131.9 0.9 copy-done.10
  132.8 0.5 copy-done.13
  133.3 0.0 copy-start.1
  133.3 2.6 %fusion.10 = bf16[1024,768]{0,1:T(8,128)(2,1)} fusion(bf16[1024,768]{0,1:T(8,128)(2,1)S(1)} %copy-done.13, bf16[1024,768]{0,1:T(8,128)(2,1)S(1)} %fusion.12, bf16[768,768]{1,0:T(8,128)(2,1)S(1)} %copy-done.10), kind=kOutput, calls=%fused_computation.14 | convolution fusion | flops 1210318848 | bytes 5898240 | tf_op jit(solution)/shard_map/dot_general | solution.py:69
  135.9 2.6 %copy.52 = bf16[1024,768]{1,0:T(8,128)(2,1)} copy(bf16[1024,768]{0,1:T(8,128)(2,1)} %fusion.10) | data formatting | bytes 3145728 | tf_op jit(solution)/shard_map/convert_element_type | solution.py:69
  138.5 0.0 copy-done.1
  (7 shorter events, 0.2 us)
Async XLA Ops:
  6.5 23.8 %copy-start = (bf16[768,2304]{1,0:T(8,128)(2,1)S(1)}, bf16[768,2304]{1,0:T(8,128)(2,1)}, u32[]{:S(2)}) copy-start(bf16[768,2304]{1,0:T(8,128)(2,1)} %param.10) | copy-start | bytes 10616836
  6.5 110.0 %all-gather.3.cloned.1.call-start = ((), (), s32[]{:S(2)}) async-start(), calls=%async_computation | async-start | bytes 6684672 | tf_op jit(solution)/shard_map/all_gather | solution.py:44
  7.4 18.0 %collective-permute-start = (bf16[1,1024]{1,0:T(2,128)(2,1)S(1)}, bf16[1,1024]{1,0:T(2,128)(2,1)S(1)}, u32[]{:S(2)}, u32[]{:S(2)}) collective-permute-start(bf16[1,1024]{1,0:T(2,128)(2,1)S(1)} %bitcast.53), channel_id=1, source_target_pairs={{0,1},{1,2},{2,3},{3,4},{4,5},{5,6},{6,7},{7,8},{8,9},{9,10},{10,1... | collective-permute-start | bytes 6152 | tf_op jit(solution)/shard_map/ppermute | solution.py:13
  14.0 5.7 %copy-start.2 = (bf16[8192,128]{1,0:T(8,128)(2,1)S(1)}, bf16[8192,128]{1,0:T(8,128)(2,1)}, u32[]{:S(2)}) copy-start(bf16[8192,128]{1,0:T(8,128)(2,1)} %param.7) | copy-start | bytes 6291460
  25.3 5.0 %copy-start.11 = (f32[768]{0:T(1024)S(1)}, f32[768]{0:T(1024)}, u32[]{:S(2)}) copy-start(f32[768]{0:T(1024)} %param.9) | copy-start | bytes 9220
  30.3 4.4 %copy-start.12 = (bf16[1024,768]{0,1:T(8,128)(2,1)}, bf16[1024,768]{0,1:T(8,128)(2,1)S(1)}, u32[]{:S(2)}) copy-start(bf16[1024,768]{0,1:T(8,128)(2,1)S(1)} %get-tuple-element.9) | copy-start | bytes 4718596
  44.4 4.0 %copy-start.7 = (bf16[2,512,12,64]{1,0,3,2:T(2,128)(2,1)S(1)}, bf16[2,512,12,64]{1,0,3,2:T(2,128)(2,1)}, u32[]{:S(2)}) copy-start(bf16[2,512,12,64]{1,0,3,2:T(2,128)(2,1)} %reshape.63) | copy-start | bytes 4718596
  54.1 10.5 %copy-start.3 = (bf16[2,512,12,64]{1,0,3,2:T(2,128)(2,1)}, bf16[2,512,12,64]{1,0,3,2:T(2,128)(2,1)S(1)}, u32[]{:S(2)}) copy-start(bf16[2,512,12,64]{1,0,3,2:T(2,128)(2,1)S(1)} %reshape.64) | copy-start | bytes 4718596
  116.6 8.5 %copy-start.8 = (f32[12,64,64]{2,1,0:T(8,128)S(1)}, f32[12,64,64]{2,1,0:T(8,128)}, u32[]{:S(2)}) copy-start(f32[12,64,64]{2,1,0:T(8,128)} %param.13) | copy-start | bytes 589828
  116.6 8.5 %copy-start.6 = (f32[2,12,64,64]{3,2,1,0:T(8,128)S(1)}, f32[2,12,64,64]{3,2,1,0:T(8,128)}, u32[]{:S(2)}) copy-start(f32[2,12,64,64]{3,2,1,0:T(8,128)} %get-tuple-element.11) | copy-start | bytes 1179652
  116.6 9.0 %copy-start.5 = (f32[2,12,64,512]{3,2,1,0:T(8,128)S(1)}, f32[2,12,64,512]{3,2,1,0:T(8,128)}, u32[]{:S(2)}) copy-start(f32[2,12,64,512]{3,2,1,0:T(8,128)} %fusion) | copy-start | bytes 9437188
  125.0 1.4 copy-start.4
  130.6 0.9 copy-start.9
  131.5 1.3 copy-start.10
  131.5 1.8 %copy-start.13 = (bf16[1024,768]{0,1:T(8,128)(2,1)S(1)}, bf16[1024,768]{0,1:T(8,128)(2,1)}, u32[]{:S(2)}) copy-start(bf16[1024,768]{0,1:T(8,128)(2,1)} %copy-done.12) | copy-start | bytes 4718596
  133.3 5.2 %copy-start.1 = (bf16[768,2304]{1,0:T(8,128)(2,1)S(1)}, bf16[768,2304]{1,0:T(8,128)(2,1)}, u32[]{:S(2)}) copy-start(bf16[768,2304]{1,0:T(8,128)(2,1)} %param.10) | copy-start | bytes 10616836
Sparse Core Ops, SparseCore 0:
  52.1 64.4 all-gather.2
where the time goes:
time: 146 us; the launch traced here: 145 us
  waiting for transfers between devices  52 us (36%)
  matrix products  42 us (29%)
  local copies, waits for them, and re-layouts  34.2 us (23%)
  between operations  13.6 us (9%)
  starting transfers between devices  2.48 us (2%)
    all_gather x1, waiting for transfers between devices, shards(): every_state = lax.all_gather(local_state[None], 'inner', axis=0, tiled=True)  52 us
    dot_general x1, matrix products, shards(): jnp.einsum('bhts,bshd->bthd', scores, values_all, preferred_element_type=...  10.5 us
    dot_general x1, matrix products, shards(): jnp.einsum('n,nhij->hij', lower_dev, every_state, precision=lax.Precision...  8.42 us
    dot_general x1, matrix products, shards(): jnp.dot(tick_rows, conv_weight[row_width:], preferred_element_type=jnp.fl...  5.66 us
    slice x2, local copies, waits for them, and re-layouts, shards(): earlier_rows = jnp.concatenate([last_row, tick_rows[:-1]], 0)  5.64 us
    dot_general x1, matrix products, shards(): jnp.dot(earlier_rows, weight_prev, preferred_element_type=jnp.float32)  4.97 us
    dot_general x1, matrix products, shards(): jnp.dot(normed, qkv_weight, preferred_element_type=jnp.float32)  4.36 us
    reshape x1, local copies, waits for them, and re-layouts, shards(): tick_rows = ticks.reshape(token_count, row_width)  4.17 us
  transfers between devices with their start and end apart: 2, of which 1 were waited for; matrix products, arithmetic and copies ran while one was open for 19% of the time, Pallas kernels for 0%

commit v1 on v0

--- a/solution.py
+++ b/solution.py
@@ -11,6 +11,16 @@
     count = lax.axis_size(axis)
     initial, last = (max(0, -steps), min(count, count - steps))
     return lax.ppermute(value, axis, [(source, source + steps) for source in range(initial, last)])
+
+
+def exclusive_scan(value, axis):
+    count = lax.axis_size(axis)
+    total = value
+    steps = 1
+    while steps < count:
+        total = total + from_behind(total, axis, steps)
+        steps *= 2
+    return total - value
 
 
 def shards(ticks, conv_weight, norm_gain, qkv_weight, head_gain, out_weight, state_in):
@@ -41,9 +51,7 @@
         "bthi,bthj->bhij", keys_all, values_all, preferred_element_type=jnp.float32
     )
     local_state = jnp.sum(block_states, 0)
-    every_state = lax.all_gather(local_state[None], "inner", axis=0, tiled=True)
-    lower_dev = (jnp.arange(every_state.shape[0]) < lax.axis_index("inner")).astype(jnp.float32)
-    prefix = jnp.einsum("n,nhij->hij", lower_dev, every_state, precision=lax.Precision.HIGHEST)
+    prefix = exclusive_scan(local_state, "inner")
     carried = state_in + prefix
     within = jnp.cumsum(block_states, 0) - block_states
     state_before = carried[None] + within

time: 146 us -> 119 us (0.82)
  the two profiles are of different devices: /device:TPU:0 before, /device:TPU:30 now
where the time goes in v1:
time: 119 us; the launch traced here: 117 us
  local copies, waits for them, and re-layouts  39.4 us (33%)
  matrix products  33.7 us (28%)
  waiting for transfers between devices  28.5 us (24%)
  starting transfers between devices  8.11 us (7%)
  other arithmetic  7.15 us (6%)
    ppermute x5, waiting for transfers between devices, from_behind(): lax.ppermute(value, axis, [(source, source + steps) for source in range(i...  28.5 us
    dot_general x1, matrix products, shards(): jnp.einsum('bhts,bshd->bthd', scores, values_all, preferred_element_type=...  10.7 us
    ppermute x5, starting transfers between devices, from_behind(): lax.ppermute(value, axis, [(source, source + steps) for source in range(i...  8.11 us
    dot_general x1, matrix products, shards(): jnp.dot(tick_rows, conv_weight[row_width:], preferred_element_type=jnp.fl...  5.67 us
    slice x2, local copies, waits for them, and re-layouts, shards(): earlier_rows = jnp.concatenate([last_row, tick_rows[:-1]], 0)  5.65 us
    dot_general x1, matrix products, shards(): jnp.dot(earlier_rows, weight_prev, preferred_element_type=jnp.float32)  4.97 us
    slice x2, local copies, waits for them, and re-layouts, shards(): qkv[:, :model_width].reshape(block_count, BLK, head_count, head_size)  4.81 us
    dot_general x1, matrix products, shards(): jnp.dot(normed, qkv_weight, preferred_element_type=jnp.float32)  4.36 us
  transfers between devices with their start and end apart: 5, of which 3 were waited for; matrix products, arithmetic and copies ran while one was open for 29% of the time, Pallas kernels for 0%

profile of v1, /device:TPU:30, one launch (start us, length us, event | category | flops | bytes accessed | tf_op | source)
XLA Modules:
  0.0 117.1 jit_solution(16157298808978232891)
XLA Ops:
  0.0 0.0 copy-start
  0.0 0.8 slice_bitcast_fusion
  0.8 2.0 %collective-permute-start = (bf16[1,1024]{1,0:T(2,128)(2,1)S(1)}, bf16[1,1024]{1,0:T(2,128)(2,1)S(1)}, u32[]{:S(2)}, u32[]{:S(2)}) collective-permute-start(bf16[1,1024]{1,0:T(2,128)(2,1)S(1)} %bitcast.42), channel_id=1, source_target_pairs={{0,1},{1,2},{2,3},{3,4},{4,5},{5,6},{6,7},{7,8},{8,9},{9,10},{10,1... | collective-permute-start | bytes 6152 | tf_op jit(solution)/shard_map/ppermute | solution.py:13
  2.9 4.2 %reshape.62 = bf16[1024,1024]{1,0:T(8,128)(2,1)} reshape(bf16[8192,128]{1,0:T(8,128)(2,1)} %param.7) | data formatting | bytes 4194304 | tf_op jit(solution)/shard_map/reshape | solution.py:29
  7.1 0.0 copy-start.1
  7.1 5.7 %fusion.19 = f32[1024,768]{0,1:T(8,128)} fusion(bf16[1024,1024]{1,0:T(8,128)(2,1)} %reshape.62, bf16[2048,768]{1,0:T(8,128)(2,1)} %param.8), kind=kOutput, calls=%fused_computation.26 | convolution fusion | flops 1610612736 | bytes 6815744 | tf_op jit(solution)/shard_map/dot_general | solution.py:31
  12.7 0.0 copy-done.1
  12.7 1.5 %slice.30 = bf16[8184,128]{1,0:T(8,128)(2,1)} slice(bf16[8192,128]{1,0:T(8,128)(2,1)S(1)} %copy-done.1), slice={[0:8184], [0:128]} | slice | bytes 4190208 | tf_op jit(solution)/shard_map/slice | solution.py:33
  14.2 4.2 %slice.31 = bf16[1023,1024]{1,0:T(8,128)(2,1)} reshape(bf16[8184,128]{1,0:T(8,128)(2,1)} %slice.30) | data formatting | bytes 4190208 | tf_op jit(solution)/shard_map/slice | solution.py:33
  18.4 0.0 copy-start.8
  18.4 0.0 collective-permute-done
  18.4 5.0 %fusion.5 = (f32[1024]{0:T(1024)S(1)}, bf16[1024,768]{0,1:T(8,128)(2,1)S(1)}) fusion(f32[1024,768]{0,1:T(8,128)} %fusion.19, bf16[2048,768]{1,0:T(8,128)(2,1)} %param.8, bf16[1023,1024]{1,0:T(8,128)(2,1)} %slice.31, bf16[1,1024]{1,0:T(2,128)(2,1)S(1)} %collective-permute-done), kind=kOutput, calls=%fused_computation.9 | convolution fusion | flops 1618738176 | bytes 8394752 | tf_op jit(solution)/shard_map/dot_general | solution.py:34
  23.4 0.0 copy-start.9
  23.4 0.0 copy-done
  23.4 0.0 copy-done.8
  23.4 4.4 %convolution_convert_fusion = bf16[1024,2304]{1,0:T(8,128)(2,1)S(1)} fusion(bf16[768,2304]{1,0:T(8,128)(2,1)S(1)} %copy-done, bf16[1024,768]{0,1:T(8,128)(2,1)S(1)} %get-tuple-element.9, f32[768]{0:T(1024)S(1)} %copy-done.8, f32[1024]{0:T(1024)S(1)} %add_rsqrt_fusion.1), kind=kOutput, calls=%fused_computation.5 | convolution fusion | flops 3629383680 | bytes 9837568 | tf_op jit(solution)/shard_map/dot_general | solution.py:40
  27.8 0.0 copy-done.9
  27.8 2.2 %fusion.38 = (bf16[1024,768]{1,0:T(8,128)(2,1)}, bf16[1024,768]{1,0:T(8,128)(2,1)}, bf16[1024,768]{1,0:T(8,128)(2,1)}) fusion(bf16[1024,2304]{1,0:T(8,128)(2,1)S(1)} %convolution_convert_fusion), kind=kLoop, calls=%fused_computation.47 | loop fusion | bytes 9437184 | tf_op jit(solution)/shard_map/slice | solution.py:45
  30.0 2.6 %copy.39 = bf16[1024,768]{0,1:T(8,128)(2,1)} copy(bf16[1024,768]{1,0:T(8,128)(2,1)} %get-tuple-element.7) | data formatting | bytes 3145728 | tf_op jit(solution)/shard_map/slice | solution.py:49
  32.6 3.9 %reshape.63 = bf16[2,512,12,64]{1,0,3,2:T(2,128)(2,1)} reshape(bf16[1024,768]{0,1:T(8,128)(2,1)} %copy.39) | data formatting | bytes 3145728 | tf_op jit(solution)/shard_map/reshape | solution.py:49
  36.5 2.6 %copy.41 = bf16[1024,768]{0,1:T(8,128)(2,1)} copy(bf16[1024,768]{1,0:T(8,128)(2,1)} %get-tuple-element.6) | data formatting | bytes 3145728 | tf_op jit(solution)/shard_map/slice | solution.py:46
  39.0 3.8 %reshape.65 = bf16[2,512,12,64]{1,0,3,2:T(2,128)(2,1)} reshape(bf16[1024,768]{0,1:T(8,128)(2,1)} %copy.41) | data formatting | bytes 3145728 | tf_op jit(solution)/shard_map/reshape | solution.py:46
  42.9 3.4 %fusion.39 = (f32[12,64,64]{2,1,0:T(8,128)S(1)}, f32[2,12,64,64]{3,2,1,0:T(8,128)}) fusion(bf16[2,512,12,64]{1,0,3,2:T(2,128)(2,1)} %reshape.63, bf16[2,512,12,64]{1,0,3,2:T(2,128)(2,1)} %reshape.65), kind=kOutput, calls=%fused_computation.48 | convolution fusion | flops 100712448 | bytes 3735552 | tf_op jit(solution)/shard_map/bthi,bthj->bhij/dot_general | solution.py:50
  46.3 0.0 copy-start.5
  46.3 1.9 %collective-permute-start.1 = (f32[12,64,64]{2,1,0:T(8,128)S(1)}, f32[12,64,64]{2,1,0:T(8,128)S(1)}, u32[]{:S(2)}, u32[]{:S(2)}) collective-permute-start(f32[12,64,64]{2,1,0:T(8,128)S(1)} %get-tuple-element.10), channel_id=1, source_target_pairs={{0,1},{1,2},{2,3},{3,4},{4,5},{5,6},{6,7},{7,8},{8,9},{9,10},{10,1... | collective-permute-start | bytes 589832 | tf_op jit(solution)/shard_map/ppermute | solution.py:13
  48.3 7.2 %collective-permute-done.1 = f32[12,64,64]{2,1,0:T(8,128)S(1)} collective-permute-done((f32[12,64,64]{2,1,0:T(8,128)S(1)}, f32[12,64,64]{2,1,0:T(8,128)S(1)}, u32[]{:S(2)}, u32[]{:S(2)}) %collective-permute-start.1) | collective-permute-done | bytes 196640 | tf_op jit(solution)/shard_map/ppermute | solution.py:13
  55.4 0.0 copy-done.5
  55.4 0.8 add.61
  56.2 1.3 %collective-permute-start.2 = (f32[12,64,64]{2,1,0:T(8,128)}, f32[12,64,64]{2,1,0:T(8,128)}, u32[]{:S(2)}, u32[]{:S(2)}) collective-permute-start(f32[12,64,64]{2,1,0:T(8,128)} %add.61), channel_id=1, source_target_pairs={{0,2},{1,3},{2,4},{3,5},{4,6},{5,7},{6,8},{7,9},{8,10},{9,11},{10,... | collective-permute-start | bytes 589832 | tf_op jit(solution)/shard_map/ppermute | solution.py:13
  57.5 0.8 iota_compare_fusion
  58.3 2.6 %copy.40 = bf16[1024,768]{0,1:T(8,128)(2,1)} copy(bf16[1024,768]{1,0:T(8,128)(2,1)} %get-tuple-element.5) | data formatting | bytes 3145728 | tf_op jit(solution)/shard_map/slice | solution.py:45
  60.9 3.8 %reshape.64 = bf16[2,512,12,64]{1,0,3,2:T(2,128)(2,1)} reshape(bf16[1024,768]{0,1:T(8,128)(2,1)} %copy.40) | data formatting | bytes 3145728 | tf_op jit(solution)/shard_map/reshape | solution.py:45
  64.7 2.7 %collective-permute-done.2 = f32[12,64,64]{2,1,0:T(8,128)} collective-permute-done((f32[12,64,64]{2,1,0:T(8,128)}, f32[12,64,64]{2,1,0:T(8,128)}, u32[]{:S(2)}, u32[]{:S(2)}) %collective-permute-start.2) | collective-permute-done | bytes 196640 | tf_op jit(solution)/shard_map/ppermute | solution.py:13
  67.4 1.9 %add.62 = f32[12,64,64]{2,1,0:T(8,128)} add(f32[12,64,64]{2,1,0:T(8,128)} %add.61, f32[12,64,64]{2,1,0:T(8,128)} %collective-permute-done.2) | non-fusion elementwise | flops 49152 | bytes 589824 | tf_op jit(solution)/shard_map/add | solution.py:21
  69.3 1.5 %collective-permute-start.3 = (f32[12,64,64]{2,1,0:T(8,128)}, f32[12,64,64]{2,1,0:T(8,128)}, u32[]{:S(2)}, u32[]{:S(2)}) collective-permute-start(f32[12,64,64]{2,1,0:T(8,128)} %add.62), channel_id=1, source_target_pairs={{0,4},{1,5},{2,6},{3,7},{4,8},{5,9},{6,10},{7,11},{8,12},{9,13},{1... | collective-permute-start | bytes 589832 | tf_op jit(solution)/shard_map/ppermute | solution.py:13
  70.7 10.7 %fusion = f32[2,12,64,512]{3,2,1,0:T(8,128)} fusion(pred[512,512]{1,0:T(8,128)(4,1)} %iota_compare_fusion, bf16[2,512,12,64]{1,0,3,2:T(2,128)(2,1)} %reshape.63, bf16[2,512,12,64]{1,0,3,2:T(2,128)(2,1)} %reshape.65, bf16[2,512,12,64]{1,0,3,2:T(2,128)(2,1)} %reshape.64), kind=kOutput, calls=%fused_computation.1 | convolution fusion | flops 1623195648 | bytes 8126464 | tf_op jit(solution)/shard_map/bhts,bshd->bthd/dot_general | solution.py:61
  81.4 0.0 copy-start.4
  81.4 0.0 collective-permute-done.3
  81.4 0.0 copy-start.3
  81.4 1.3 %add.63 = f32[12,64,64]{2,1,0:T(8,128)S(1)} add(f32[12,64,64]{2,1,0:T(8,128)} %add.62, f32[12,64,64]{2,1,0:T(8,128)} %collective-permute-done.3) | non-fusion elementwise | flops 49152 | bytes 589824 | tf_op jit(solution)/shard_map/add | solution.py:21
  82.8 1.4 %collective-permute-start.4 = (f32[12,64,64]{2,1,0:T(8,128)S(1)}, f32[12,64,64]{2,1,0:T(8,128)S(1)}, u32[]{:S(2)}, u32[]{:S(2)}) collective-permute-start(f32[12,64,64]{2,1,0:T(8,128)S(1)} %add.63), channel_id=1, source_target_pairs={{0,8},{1,9},{2,10},{3,11},{4,12},{5,13},{6,14},{7,15},{16,24},{17,... | collective-permute-start | bytes 589832 | tf_op jit(solution)/shard_map/ppermute | solution.py:13
  84.2 0.0 copy-done.4
  84.2 0.0 copy-start.2
  84.2 0.7 reduce-window_subtract_fusion
  85.0 18.7 %collective-permute-done.4 = f32[12,64,64]{2,1,0:T(8,128)S(1)} collective-permute-done((f32[12,64,64]{2,1,0:T(8,128)S(1)}, f32[12,64,64]{2,1,0:T(8,128)S(1)}, u32[]{:S(2)}, u32[]{:S(2)}) %collective-permute-start.4) | collective-permute-done | bytes 196640 | tf_op jit(solution)/shard_map/ppermute | solution.py:13
  103.6 1.2 %subtract_add_fusion = f32[12,64,64]{2,1,0:T(8,128)S(1)} fusion(f32[12,64,64]{2,1,0:T(8,128)} %param.13, f32[12,64,64]{2,1,0:T(8,128)} %copy-done.5, f32[12,64,64]{2,1,0:T(8,128)S(1)} %add.63, f32[12,64,64]{2,1,0:T(8,128)S(1)} %collective-permute-done.4), kind=kLoop, calls=%fused_computation.39 | loop fusion | flops 147456 | bytes 983040 | tf_op jit(solution)/shard_map/add | solution.py:55
  104.8 0.0 copy-done.3
  104.9 0.0 copy-done.2
  104.9 1.9 %multiply_reduce_fusion = (f32[2,512,12]{1,2,0:T(8,128)S(1)}, f32[2,512,12,64]{1,3,2,0:T(8,128)S(1)}) fusion(f32[2,12,64,512]{3,2,1,0:T(8,128)S(1)} %copy-done.3, bf16[2,512,12,64]{1,0,3,2:T(2,128)(2,1)S(1)} %copy-done.2, f32[2,12,64,64]{3,2,1,0:T(8,128)S(1)} %reduce-window_subtract_fusion, f32[12,64,64]{2,1,0:T(8,128)S(1)} %subtract_add_fusion), kind=kOutput, calls=%fused_computation.16 | convolution fusion | flops 606425088 | bytes 8503296 | tf_op jit(solution)/shard_map/bthi,bhij->bthj/dot_general | solution.py:64
  106.8 2.4 %copy.49 = f32[2,512,12,64]{1,0,3,2:T(2,128)S(1)} copy(f32[2,512,12,64]{1,3,2,0:T(8,128)S(1)} %get-tuple-element.13) | data formatting | bytes 6291456 | tf_op jit(solution)/shard_map/add | solution.py:70
  109.2 0.0 copy-start.6
  109.2 0.7 copy.56
  110.1 0.0 copy-done.6
  110.1 0.0 copy-start.7
  110.1 0.0 copy-start.10
  110.1 0.4 fusion.10
  110.5 0.9 copy-done.7
  111.4 0.5 copy-done.10
  111.9 2.7 %fusion.8 = bf16[1024,768]{0,1:T(8,128)(2,1)} fusion(bf16[1024,768]{0,1:T(8,128)(2,1)S(1)} %copy-done.10, bf16[1024,768]{0,1:T(8,128)(2,1)S(1)} %fusion.10, bf16[768,768]{1,0:T(8,128)(2,1)S(1)} %copy-done.7), kind=kOutput, calls=%fused_computation.12 | convolution fusion | flops 1210318848 | bytes 5898240 | tf_op jit(solution)/shard_map/dot_general | solution.py:77
  114.5 2.6 %copy.52 = bf16[1024,768]{1,0:T(8,128)(2,1)} copy(bf16[1024,768]{0,1:T(8,128)(2,1)} %fusion.8) | data formatting | bytes 3145728 | tf_op jit(solution)/shard_map/convert_element_type | solution.py:77
  (6 shorter events, 0.1 us)
Async XLA Ops:
  0.0 23.4 %copy-start = (bf16[768,2304]{1,0:T(8,128)(2,1)S(1)}, bf16[768,2304]{1,0:T(8,128)(2,1)}, u32[]{:S(2)}) copy-start(bf16[768,2304]{1,0:T(8,128)(2,1)} %param.10) | copy-start | bytes 10616836
  0.8 17.5 %collective-permute-start = (bf16[1,1024]{1,0:T(2,128)(2,1)S(1)}, bf16[1,1024]{1,0:T(2,128)(2,1)S(1)}, u32[]{:S(2)}, u32[]{:S(2)}) collective-permute-start(bf16[1,1024]{1,0:T(2,128)(2,1)S(1)} %bitcast.42), channel_id=1, source_target_pairs={{0,1},{1,2},{2,3},{3,4},{4,5},{5,6},{6,7},{7,8},{8,9},{9,10},{10,1... | collective-permute-start | bytes 6152 | tf_op jit(solution)/shard_map/ppermute | solution.py:13
  7.1 5.7 %copy-start.1 = (bf16[8192,128]{1,0:T(8,128)(2,1)S(1)}, bf16[8192,128]{1,0:T(8,128)(2,1)}, u32[]{:S(2)}) copy-start(bf16[8192,128]{1,0:T(8,128)(2,1)} %param.7) | copy-start | bytes 6291460
  18.4 5.0 %copy-start.8 = (f32[768]{0:T(1024)S(1)}, f32[768]{0:T(1024)}, u32[]{:S(2)}) copy-start(f32[768]{0:T(1024)} %param.9) | copy-start | bytes 9220
  23.4 4.4 %copy-start.9 = (bf16[1024,768]{0,1:T(8,128)(2,1)}, bf16[1024,768]{0,1:T(8,128)(2,1)S(1)}, u32[]{:S(2)}) copy-start(bf16[1024,768]{0,1:T(8,128)(2,1)S(1)} %get-tuple-element.9) | copy-start | bytes 4718596
  46.3 9.1 %copy-start.5 = (f32[12,64,64]{2,1,0:T(8,128)}, f32[12,64,64]{2,1,0:T(8,128)S(1)}, u32[]{:S(2)}) copy-start(f32[12,64,64]{2,1,0:T(8,128)S(1)} %get-tuple-element.10) | copy-start | bytes 589828
  46.3 9.1 %collective-permute-start.1 = (f32[12,64,64]{2,1,0:T(8,128)S(1)}, f32[12,64,64]{2,1,0:T(8,128)S(1)}, u32[]{:S(2)}, u32[]{:S(2)}) collective-permute-start(f32[12,64,64]{2,1,0:T(8,128)S(1)} %get-tuple-element.10), channel_id=1, source_target_pairs={{0,1},{1,2},{2,3},{3,4},{4,5},{5,6},{6,7},{7,8},{8,9},{9,10},{10,1... | collective-permute-start | bytes 589832 | tf_op jit(solution)/shard_map/ppermute | solution.py:13
  56.2 11.1 %collective-permute-start.2 = (f32[12,64,64]{2,1,0:T(8,128)}, f32[12,64,64]{2,1,0:T(8,128)}, u32[]{:S(2)}, u32[]{:S(2)}) collective-permute-start(f32[12,64,64]{2,1,0:T(8,128)} %add.61), channel_id=1, source_target_pairs={{0,2},{1,3},{2,4},{3,5},{4,6},{5,7},{6,8},{7,9},{8,10},{9,11},{10,... | collective-permute-start | bytes 589832 | tf_op jit(solution)/shard_map/ppermute | solution.py:13
  69.3 12.1 %collective-permute-start.3 = (f32[12,64,64]{2,1,0:T(8,128)}, f32[12,64,64]{2,1,0:T(8,128)}, u32[]{:S(2)}, u32[]{:S(2)}) collective-permute-start(f32[12,64,64]{2,1,0:T(8,128)} %add.62), channel_id=1, source_target_pairs={{0,4},{1,5},{2,6},{3,7},{4,8},{5,9},{6,10},{7,11},{8,12},{9,13},{1... | collective-permute-start | bytes 589832 | tf_op jit(solution)/shard_map/ppermute | solution.py:13
  81.4 2.8 %copy-start.4 = (f32[2,12,64,64]{3,2,1,0:T(8,128)S(1)}, f32[2,12,64,64]{3,2,1,0:T(8,128)}, u32[]{:S(2)}) copy-start(f32[2,12,64,64]{3,2,1,0:T(8,128)} %get-tuple-element.11) | copy-start | bytes 1179652
  81.4 23.4 %copy-start.3 = (f32[2,12,64,512]{3,2,1,0:T(8,128)S(1)}, f32[2,12,64,512]{3,2,1,0:T(8,128)}, u32[]{:S(2)}) copy-start(f32[2,12,64,512]{3,2,1,0:T(8,128)} %fusion) | copy-start | bytes 9437188
  82.8 20.9 %collective-permute-start.4 = (f32[12,64,64]{2,1,0:T(8,128)S(1)}, f32[12,64,64]{2,1,0:T(8,128)S(1)}, u32[]{:S(2)}, u32[]{:S(2)}) collective-permute-start(f32[12,64,64]{2,1,0:T(8,128)S(1)} %add.63), channel_id=1, source_target_pairs={{0,8},{1,9},{2,10},{3,11},{4,12},{5,13},{6,14},{7,15},{16,24},{17,... | collective-permute-start | bytes 589832 | tf_op jit(solution)/shard_map/ppermute | solution.py:13
  84.2 20.7 %copy-start.2 = (bf16[2,512,12,64]{1,0,3,2:T(2,128)(2,1)S(1)}, bf16[2,512,12,64]{1,0,3,2:T(2,128)(2,1)}, u32[]{:S(2)}) copy-start(bf16[2,512,12,64]{1,0,3,2:T(2,128)(2,1)} %reshape.64) | copy-start | bytes 4718596
  109.2 0.9 copy-start.6
  110.1 1.3 %copy-start.7 = (bf16[768,768]{1,0:T(8,128)(2,1)S(1)}, bf16[768,768]{1,0:T(8,128)(2,1)}, u32[]{:S(2)}) copy-start(bf16[768,768]{1,0:T(8,128)(2,1)} %param.12) | copy-start | bytes 3538948
  110.1 1.8 %copy-start.10 = (bf16[1024,768]{0,1:T(8,128)(2,1)S(1)}, bf16[1024,768]{0,1:T(8,128)(2,1)}, u32[]{:S(2)}) copy-start(bf16[1024,768]{0,1:T(8,128)(2,1)} %copy-done.9) | copy-start | bytes 4718596

commit v2 on v1

v2 whole, which is shorter than its diff:
```python
import functools

import jax
import jax.numpy as jnp
from jax import lax
from jax.experimental import pallas as pl
from jax.experimental.pallas import tpu as pltpu
from jax.sharding import PartitionSpec as P

STRIDE = 8
BLK = 512
PAIR = 128


def from_behind(value, axis, steps):
    count = lax.axis_size(axis)
    initial, last = (max(0, -steps), min(count, count - steps))
    return lax.ppermute(value, axis, [(source, source + steps) for source in range(initial, last)])


def exclusive_scan(value, axis):
    count = lax.axis_size(axis)
    total = value
    steps = 1
    while steps < count:
        total = total + from_behind(total, axis, steps)
        steps *= 2
    return total - value


def embed_kernel(ticks_ref, prev_ref, conv_ref, gain_ref, qkv_w_ref,
                 emb_ref, q_ref, inside_ref, state_ref, wide_ref):
    b = pl.program_id(0)
    block_ticks = ticks_ref.shape[0]
    tokens = block_ticks // STRIDE
    model_width = emb_ref.shape[1]

    @pl.when(b == 0)
    def _():
        wide_ref[0:STRIDE, :] = prev_ref[STRIDE : 2 * STRIDE, :].astype(jnp.float32)

    @pl.when(b > 0)
    def _():
        wide_ref[0:STRIDE, :] = wide_ref[block_ticks : block_ticks + STRIDE, :]

    wide_ref[STRIDE:, :] = ticks_ref[...].astype(jnp.float32)
    pieces = [wide_ref[pl.ds(j, tokens, stride=STRIDE), :] for j in range(2 * STRIDE)]
    lhs = jnp.concatenate(pieces, axis=1).astype(jnp.bfloat16)
    emb = jnp.dot(lhs, conv_ref[...], preferred_element_type=jnp.float32).astype(jnp.bfloat16)
    emb_ref[...] = emb
    embed_f = emb.astype(jnp.float32)
    mean_sq = jnp.mean(embed_f * embed_f, axis=-1, keepdims=True)
    normed = (embed_f * lax.rsqrt(mean_sq + 1e-05) * gain_ref[...]).astype(jnp.bfloat16)

    def project(part):
        weight = qkv_w_ref[:, part * model_width : (part + 1) * model_width]
        return jnp.dot(normed, weight, preferred_element_type=jnp.float32).astype(jnp.bfloat16)

    queries, keys, values = project(0), project(1), project(2)
    q_ref[...] = queries
    lane = lax.broadcasted_iota(jnp.int32, (1, PAIR), 1)
    first = lane < PAIR // 2
    causal = (lax.broadcasted_iota(jnp.int32, (tokens, tokens), 0)
              >= lax.broadcasted_iota(jnp.int32, (tokens, tokens), 1))
    zero = jnp.zeros((), jnp.bfloat16)
    for pair in range(model_width // PAIR):
        cols = slice(pair * PAIR, (pair + 1) * PAIR)
        q_pair, k_pair, v_pair = queries[:, cols], keys[:, cols], values[:, cols]
        inside = None
        for use in (first, ~first):
            q_one = jnp.where(use, q_pair, zero)
            scores = lax.dot_general(q_one, k_pair, (((1,), (1,)), ((), ())),
                                     preferred_element_type=jnp.float32)
            scores = jnp.where(causal, scores, 0.0).astype(jnp.bfloat16)
            term = jnp.dot(scores, jnp.where(use, v_pair, zero), preferred_element_type=jnp.float32)
            inside = term if inside is None else inside + term
        inside_ref[:, cols] = inside
        kv = lax.dot_general(k_pair, v_pair, (((0,), (0,)), ((), ())),
                             preferred_element_type=jnp.float32)
        half = PAIR // 2
        state_ref[0, pair] = jnp.where(first, kv[:half], kv[half:])


def out_kernel(q_ref, state_ref, inside_ref, emb_ref, hgain_ref, out_w_ref, out_ref, att_ref):
    model_width = out_ref.shape[1]
    lane = lax.broadcasted_iota(jnp.int32, (1, PAIR), 1)
    first = lane < PAIR // 2
    head_size = PAIR // 2
    for pair in range(model_width // PAIR):
        cols = slice(pair * PAIR, (pair + 1) * PAIR)
        packed = state_ref[0, pair]
        diag = jnp.concatenate([jnp.where(first, packed, 0.0), jnp.where(first, 0.0, packed)], axis=0)
        high = diag.astype(jnp.bfloat16)
        low = (diag - high.astype(jnp.float32)).astype(jnp.bfloat16)
        q_pair = q_ref[:, cols]
        carried = (jnp.dot(q_pair, high, preferred_element_type=jnp.float32)
                   + jnp.dot(q_pair, low, preferred_element_type=jnp.float32))
        combined = inside_ref[:, cols] + carried
        square = combined * combined
        sum_first = jnp.sum(jnp.where(first, square, 0.0), axis=-1, keepdims=True)
        sum_second = jnp.sum(jnp.where(first, 0.0, square), axis=-1, keepdims=True)
        scale = jnp.where(first, lax.rsqrt(sum_first / head_size + 1e-06),
                          lax.rsqrt(sum_second / head_size + 1e-06))
        att_ref[:, cols] = (combined * scale * hgain_ref[:, cols]).astype(jnp.bfloat16)
    out = emb_ref[...].astype(jnp.float32) + jnp.dot(att_ref[...], out_w_ref[...],
                                                     preferred_element_type=jnp.float32)
    out_ref[...] = out.astype(jnp.bfloat16)


def full(shape):
    return pl.BlockSpec(shape, lambda b: (0,) * len(shape))


def shards(ticks, conv_weight, norm_gain, qkv_weight, head_gain, out_weight, state_in):
    tick_count, feat = ticks.shape
    token_count = tick_count // STRIDE
    model_width = conv_weight.shape[1]
    head_count, head_size = state_in.shape[0], state_in.shape[1]
    pairs = model_width // PAIR
    blocks = token_count // BLK
    block_ticks = BLK * STRIDE

    prev = from_behind(ticks[tick_count - 2 * STRIDE :], "inner", 1)
    rows_spec = pl.BlockSpec((BLK, model_width), lambda b: (b, 0))
    state_spec = pl.BlockSpec((1, pairs, head_size, PAIR), lambda b: (b, 0, 0, 0))
    emb, queries, inside, states = pl.pallas_call(
        embed_kernel,
        grid=(blocks,),
        in_specs=[
            pl.BlockSpec((block_ticks, feat), lambda b: (b, 0)),
            full((2 * STRIDE, feat)),
            full(conv_weight.shape),
            full((1, model_width)),
            full(qkv_weight.shape),
        ],
        out_specs=[rows_spec, rows_spec, rows_spec, state_spec],
        out_shape=[
            jax.ShapeDtypeStruct((token_count, model_width), jnp.bfloat16),
            jax.ShapeDtypeStruct((token_count, model_width), jnp.bfloat16),
            jax.ShapeDtypeStruct((token_count, model_width), jnp.float32),
            jax.ShapeDtypeStruct((blocks, pairs, head_size, PAIR), jnp.float32),
        ],
        scratch_shapes=[pltpu.VMEM((block_ticks + STRIDE, feat), jnp.float32)],
        compiler_params=pltpu.CompilerParams(dimension_semantics=("arbitrary",)),
    )(ticks, prev, conv_weight, norm_gain.reshape(1, model_width), qkv_weight)

    local = states[0]
    for block in range(1, blocks):
        local = local + states[block]
    prefix = exclusive_scan(local, "inner")
    packed_in = state_in.reshape(pairs, 2, head_size, head_size).transpose(0, 2, 1, 3)
    carried = packed_in.reshape(pairs, head_size, PAIR) + prefix
    before = [carried]
    for block in range(1, blocks):
        before.append(before[-1] + states[block - 1])
    before = jnp.stack(before)

    return pl.pallas_call(
        out_kernel,
        grid=(blocks,),
        in_specs=[
            rows_spec,
            state_spec,
            rows_spec,
            rows_spec,
            full((1, model_width)),
            full(out_weight.shape),
        ],
        out_specs=rows_spec,
        out_shape=jax.ShapeDtypeStruct((token_count, model_width), jnp.bfloat16),
        scratch_shapes=[pltpu.VMEM((BLK, model_width), jnp.bfloat16)],
        compiler_params=pltpu.CompilerParams(dimension_semantics=("arbitrary",)),
    )(queries, before, inside, emb, head_gain.reshape(1, model_width), out_weight)


def solution(mesh):
    in_specs = (P(("groups", "inner"), None), P(), P(), P(), P(), P(), P("groups", None, None))
    out_specs = P(("groups", "inner"), None)
    return jax.shard_map(shards, mesh=mesh, in_specs=in_specs, out_specs=out_specs, check_vma=False)
```

time: 119 us -> 73.4 us (0.62)
  the two profiles are of different devices: /device:TPU:30 before, /device:TPU:24 now
where the time goes in v2:
time: 73.4 us; the launch traced here: 73.1 us
  waiting for transfers between devices  29.4 us (40%)
  Pallas kernels  28.5 us (39%)
  starting transfers between devices  8.33 us (11%)
  local copies, waits for them, and re-layouts  3.71 us (5%)
  other arithmetic  3.08 us (4%)
    ppermute x5, waiting for transfers between devices, from_behind(): lax.ppermute(value, axis, [(source, source + steps) for source in range(i...  29.4 us
    pallas_call x1, Pallas kernels, shards(): pl.pallas_call(embed_kernel, grid=(blocks,), in_specs=[pl.BlockSpec((bloc...  21.6 us
    ppermute x5, starting transfers between devices, from_behind(): lax.ppermute(value, axis, [(source, source + steps) for source in range(i...  8.33 us
    pallas_call x1, Pallas kernels, shards(): pl.pallas_call(out_kernel, grid=(blocks,), in_specs=[rows_spec, state_spe...  6.88 us
  transfers between devices with their start and end apart: 5, of which 5 were waited for; matrix products, arithmetic and copies ran while one was open for 3% of the time, Pallas kernels for 0%

profile of v2, /device:TPU:24, one launch (start us, length us, event | category | flops | bytes accessed | tf_op | source)
XLA Modules:
  0.0 73.1 jit_solution(386166525573482414)
XLA Ops:
  0.0 0.7 slice.10
  0.7 1.9 %collective-permute-start = (bf16[16,128]{1,0:T(8,128)(2,1)S(1)}, bf16[16,128]{1,0:T(8,128)(2,1)S(1)}, u32[]{:S(2)}, u32[]{:S(2)}) collective-permute-start(bf16[16,128]{1,0:T(8,128)(2,1)S(1)} %slice.10), channel_id=1, source_target_pairs={{0,1},{1,2},{2,3},{3,4},{4,5},{5,6},{6,7},{7,8},{8,9},{9,10},{10,1... | collective-permute-start | bytes 12296 | tf_op jit(solution)/shard_map/ppermute | solution.py:18
  2.6 1.3 %reshape.12.gain_ref = f32[1,768]{1,0:T(1,128)} reshape(f32[768]{0:T(1024)} %param.9) | data formatting | bytes 6144 | tf_op jit(solution)/shard_map/reshape | solution.py:145
  3.9 2.6 %collective-permute-done.prev_ref = bf16[16,128]{1,0:T(8,128)(2,1)S(1)} collective-permute-done((bf16[16,128]{1,0:T(8,128)(2,1)S(1)}, bf16[16,128]{1,0:T(8,128)(2,1)S(1)}, u32[]{:S(2)}, u32[]{:S(2)}) %collective-permute-start) | collective-permute-done | bytes 4128 | tf_op jit(solution)/shard_map/ppermute | solution.py:18
  6.5 0.0 copy-start.2
  6.5 0.6 copy-done.2
  7.1 21.6 %shard_map.73 = (bf16[1024,768]{1,0:T(8,128)(2,1)}, bf16[1024,768]{1,0:T(8,128)(2,1)}, f32[1024,768]{1,0:T(8,128)}, f32[2,6,64,128]{3,2,1,0:T(8,128)}) custom-call(bf16[8192,128]{1,0:T(8,128)(2,1)} %ticks_ref.1, bf16[16,128]{1,0:T(8,128)(2,1)} %copy-done.2, bf16[2048,768]{1,0:T(8,128)(2,1)} %conv_ref.1, f32[1,768]{1,0:T(1,128)} %reshape.12.gain_ref, ...), custom_call_target="tpu_custom_call" | custom-call | tf_op jit(solution)/shard_map/pallas_call | solution.py:126
  28.7 0.0 copy-start.3
  28.7 0.0 copy-start.1
  28.7 0.0 copy-start
  28.7 1.1 %bitcast_add_fusion = f32[6,64,128]{2,1,0:T(8,128)S(1)} fusion(f32[2,6,64,128]{3,2,1,0:T(8,128)} %get-tuple-element.10), kind=kLoop, calls=%fused_computation.2 | loop fusion | flops 49152 | bytes 589824 | tf_op jit(solution)/shard_map/add | solution.py:149
  29.8 1.9 %collective-permute-start.1 = (f32[6,64,128]{2,1,0:T(8,128)S(1)}, f32[6,64,128]{2,1,0:T(8,128)S(1)}, u32[]{:S(2)}, u32[]{:S(2)}) collective-permute-start(f32[6,64,128]{2,1,0:T(8,128)S(1)} %bitcast_add_fusion), channel_id=1, source_target_pairs={{0,1},{1,2},{2,3},{3,4},{4,5},{5,6},{6,7},{7,8},{8,9},{9,10},{10,1... | collective-permute-start | bytes 589832 | tf_op jit(solution)/shard_map/ppermute | solution.py:18
  31.8 6.0 %collective-permute-done.1 = f32[6,64,128]{2,1,0:T(8,128)S(1)} collective-permute-done((f32[6,64,128]{2,1,0:T(8,128)S(1)}, f32[6,64,128]{2,1,0:T(8,128)S(1)}, u32[]{:S(2)}, u32[]{:S(2)}) %collective-permute-start.1) | collective-permute-done | bytes 196640 | tf_op jit(solution)/shard_map/ppermute | solution.py:18
  37.7 1.1 %fusion.1 = f32[6,64,128]{2,1,0:T(8,128)S(1)} fusion(f32[6,64,128]{2,1,0:T(8,128)S(1)} %collective-permute-done.1, f32[2,6,64,128]{3,2,1,0:T(8,128)} %get-tuple-element.10), kind=kLoop, calls=%fused_computation.6 | loop fusion | flops 98304 | bytes 786432 | tf_op jit(solution)/shard_map/add | solution.py:26
  38.8 1.9 %collective-permute-start.2 = (f32[6,64,128]{2,1,0:T(8,128)S(1)}, f32[6,64,128]{2,1,0:T(8,128)S(1)}, u32[]{:S(2)}, u32[]{:S(2)}) collective-permute-start(f32[6,64,128]{2,1,0:T(8,128)S(1)} %fusion.1), channel_id=1, source_target_pairs={{0,2},{1,3},{2,4},{3,5},{4,6},{5,7},{6,8},{7,9},{8,10},{9,11},{10,... | collective-permute-start | bytes 589832 | tf_op jit(solution)/shard_map/ppermute | solution.py:18
  40.7 6.5 %collective-permute-done.2 = f32[6,64,128]{2,1,0:T(8,128)S(1)} collective-permute-done((f32[6,64,128]{2,1,0:T(8,128)S(1)}, f32[6,64,128]{2,1,0:T(8,128)S(1)}, u32[]{:S(2)}, u32[]{:S(2)}) %collective-permute-start.2) | collective-permute-done | bytes 196640 | tf_op jit(solution)/shard_map/ppermute | solution.py:18
  47.3 1.3 %collective-permute-start.3 = (f32[6,64,128]{2,1,0:T(8,128)S(1)}, f32[6,64,128]{2,1,0:T(8,128)S(1)}, u32[]{:S(2)}, u32[]{:S(2)}) collective-permute-start(f32[6,64,128]{2,1,0:T(8,128)S(1)} %add.23), channel_id=1, source_target_pairs={{0,4},{1,5},{2,6},{3,7},{4,8},{5,9},{6,10},{7,11},{8,12},{9,13},{1... | collective-permute-start | bytes 589832 | tf_op jit(solution)/shard_map/ppermute | solution.py:18
  48.6 6.3 %collective-permute-done.3 = f32[6,64,128]{2,1,0:T(8,128)S(1)} collective-permute-done((f32[6,64,128]{2,1,0:T(8,128)S(1)}, f32[6,64,128]{2,1,0:T(8,128)S(1)}, u32[]{:S(2)}, u32[]{:S(2)}) %collective-permute-start.3) | collective-permute-done | bytes 196640 | tf_op jit(solution)/shard_map/ppermute | solution.py:18
  54.9 1.3 %collective-permute-start.4 = (f32[6,64,128]{2,1,0:T(8,128)S(1)}, f32[6,64,128]{2,1,0:T(8,128)S(1)}, u32[]{:S(2)}, u32[]{:S(2)}) collective-permute-start(f32[6,64,128]{2,1,0:T(8,128)S(1)} %add.24), channel_id=1, source_target_pairs={{0,8},{1,9},{2,10},{3,11},{4,12},{5,13},{6,14},{7,15},{16,24},{17,... | collective-permute-start | bytes 589832 | tf_op jit(solution)/shard_map/ppermute | solution.py:18
  56.2 0.0 copy-done.3
  56.2 0.6 reshape.15.hgain_ref
  56.8 0.0 copy-done.1
  56.8 0.3 copy.10
  57.1 0.2 reshape.14
  57.3 8.0 %collective-permute-done.4 = f32[6,64,128]{2,1,0:T(8,128)S(1)} collective-permute-done((f32[6,64,128]{2,1,0:T(8,128)S(1)}, f32[6,64,128]{2,1,0:T(8,128)S(1)}, u32[]{:S(2)}, u32[]{:S(2)}) %collective-permute-start.4) | collective-permute-done | bytes 196640 | tf_op jit(solution)/shard_map/ppermute | solution.py:18
  65.3 0.0 copy-done
  65.3 0.1 fusion
  65.4 0.8 %pad_maximum_fusion.state_ref = f32[2,6,64,128]{3,2,1,0:T(8,128)} fusion(f32[1,6,64,128]{3,2,1,0:T(8,128)S(1)} %get-tuple-element.13, f32[1,6,64,128]{3,2,1,0:T(8,128)S(1)} %bitcast.23), kind=kLoop, calls=%fused_computation | loop fusion | flops 98304 | bytes 786432 | tf_op jit(solution)/shard_map/stack | solution.py:156
  66.2 6.9 %shard_map.74 = bf16[1024,768]{1,0:T(8,128)(2,1)} custom-call(bf16[1024,768]{1,0:T(8,128)(2,1)} %get-tuple-element.9.q_ref, f32[2,6,64,128]{3,2,1,0:T(8,128)} %pad_maximum_fusion.state_ref, f32[1024,768]{1,0:T(8,128)} %get-tuple-element.11.inside_ref, bf16[1024,768]{1,0:T(8,128)(2,1)} %get-tuple-element.12.emb_ref, f32[1,768]{1,0:T(1,128)} %reshape.15.hgain_ref, ...), custom_call_target="tpu_custom_call" | custom-call | tf_op jit(solution)/shard_map/pallas_call | solution.py:158
  (2 shorter events, 0.0 us)
Async XLA Ops:
  0.7 5.8 %collective-permute-start = (bf16[16,128]{1,0:T(8,128)(2,1)S(1)}, bf16[16,128]{1,0:T(8,128)(2,1)S(1)}, u32[]{:S(2)}, u32[]{:S(2)}) collective-permute-start(bf16[16,128]{1,0:T(8,128)(2,1)S(1)} %slice.10), channel_id=1, source_target_pairs={{0,1},{1,2},{2,3},{3,4},{4,5},{5,6},{6,7},{7,8},{8,9},{9,10},{10,1... | collective-permute-start | bytes 12296 | tf_op jit(solution)/shard_map/ppermute | solution.py:18
  6.5 0.6 copy-start.2
  28.7 27.5 %copy-start.3 = (f32[768]{0:T(1024)S(1)}, f32[768]{0:T(1024)}, u32[]{:S(2)}) copy-start(f32[768]{0:T(1024)} %param.11) | copy-start | bytes 9220
  28.7 28.1 %copy-start.1 = (f32[12,64,64]{2,1,0:T(8,128)S(1)}, f32[12,64,64]{2,1,0:T(8,128)}, u32[]{:S(2)}) copy-start(f32[12,64,64]{2,1,0:T(8,128)} %param.13) | copy-start | bytes 589828
  28.7 36.6 %copy-start = (f32[2,6,64,128]{3,2,1,0:T(8,128)S(1)}, f32[2,6,64,128]{3,2,1,0:T(8,128)}, u32[]{:S(2)}) copy-start(f32[2,6,64,128]{3,2,1,0:T(8,128)} %get-tuple-element.10) | copy-start | bytes 1179652
  29.8 7.9 %collective-permute-start.1 = (f32[6,64,128]{2,1,0:T(8,128)S(1)}, f32[6,64,128]{2,1,0:T(8,128)S(1)}, u32[]{:S(2)}, u32[]{:S(2)}) collective-permute-start(f32[6,64,128]{2,1,0:T(8,128)S(1)} %bitcast_add_fusion), channel_id=1, source_target_pairs={{0,1},{1,2},{2,3},{3,4},{4,5},{5,6},{6,7},{7,8},{8,9},{9,10},{10,1... | collective-permute-start | bytes 589832 | tf_op jit(solution)/shard_map/ppermute | solution.py:18
  38.8 8.5 %collective-permute-start.2 = (f32[6,64,128]{2,1,0:T(8,128)S(1)}, f32[6,64,128]{2,1,0:T(8,128)S(1)}, u32[]{:S(2)}, u32[]{:S(2)}) collective-permute-start(f32[6,64,128]{2,1,0:T(8,128)S(1)} %fusion.1), channel_id=1, source_target_pairs={{0,2},{1,3},{2,4},{3,5},{4,6},{5,7},{6,8},{7,9},{8,10},{9,11},{10,... | collective-permute-start | bytes 589832 | tf_op jit(solution)/shard_map/ppermute | solution.py:18
  47.3 7.6 %collective-permute-start.3 = (f32[6,64,128]{2,1,0:T(8,128)S(1)}, f32[6,64,128]{2,1,0:T(8,128)S(1)}, u32[]{:S(2)}, u32[]{:S(2)}) collective-permute-start(f32[6,64,128]{2,1,0:T(8,128)S(1)} %add.23), channel_id=1, source_target_pairs={{0,4},{1,5},{2,6},{3,7},{4,8},{5,9},{6,10},{7,11},{8,12},{9,13},{1... | collective-permute-start | bytes 589832 | tf_op jit(solution)/shard_map/ppermute | solution.py:18
  54.9 10.5 %collective-permute-start.4 = (f32[6,64,128]{2,1,0:T(8,128)S(1)}, f32[6,64,128]{2,1,0:T(8,128)S(1)}, u32[]{:S(2)}, u32[]{:S(2)}) collective-permute-start(f32[6,64,128]{2,1,0:T(8,128)S(1)} %add.24), channel_id=1, source_target_pairs={{0,8},{1,9},{2,10},{3,11},{4,12},{5,13},{6,14},{7,15},{16,24},{17,... | collective-permute-start | bytes 589832 | tf_op jit(solution)/shard_map/ppermute | solution.py:18

commit v3 on v2

v3 whole, which is shorter than its diff:
```python
import jax
import jax.numpy as jnp
from jax import lax
from jax.experimental import pallas as pl
from jax.experimental.pallas import tpu as pltpu
from jax.sharding import PartitionSpec as P

STRIDE = 8
BLK = 512
PAIR = 128


def from_behind(value, axis, steps):
    count = lax.axis_size(axis)
    initial, last = (max(0, -steps), min(count, count - steps))
    return lax.ppermute(value, axis, [(source, source + steps) for source in range(initial, last)])


def exclusive_scan(value, axis):
    count = lax.axis_size(axis)
    total = value
    steps = 1
    while steps < count:
        total = total + from_behind(total, axis, steps)
        steps *= 2
    return total - value


def conv_kernel(ticks_ref, prev_ref, conv_ref, gain_ref, emb_ref, normed_ref, wide_ref):
    b = pl.program_id(0)
    block_ticks = ticks_ref.shape[0]
    tokens = block_ticks // STRIDE

    @pl.when(b == 0)
    def _():
        wide_ref[0:STRIDE, :] = prev_ref[STRIDE : 2 * STRIDE, :].astype(jnp.float32)

    @pl.when(b > 0)
    def _():
        wide_ref[0:STRIDE, :] = wide_ref[block_ticks : block_ticks + STRIDE, :]

    wide_ref[STRIDE:, :] = ticks_ref[...].astype(jnp.float32)
    pieces = [wide_ref[pl.ds(j, tokens, stride=STRIDE), :] for j in range(2 * STRIDE)]
    lhs = jnp.concatenate(pieces, axis=1).astype(jnp.bfloat16)
    emb = jnp.dot(lhs, conv_ref[...], preferred_element_type=jnp.float32).astype(jnp.bfloat16)
    emb_ref[...] = emb
    embed_f = emb.astype(jnp.float32)
    mean_sq = jnp.mean(embed_f * embed_f, axis=-1, keepdims=True)
    normed_ref[...] = (embed_f * lax.rsqrt(mean_sq + 1e-05) * gain_ref[...]).astype(jnp.bfloat16)


def attend_kernel(normed_ref, wq_ref, wk_ref, wv_ref, q_ref, inside_ref, state_ref):
    normed = normed_ref[...]
    tokens = normed.shape[0]

    def project(weight_ref):
        return jnp.dot(normed, weight_ref[...], preferred_element_type=jnp.float32).astype(jnp.bfloat16)

    queries, keys, values = project(wq_ref), project(wk_ref), project(wv_ref)
    q_ref[...] = queries
    lane = lax.broadcasted_iota(jnp.int32, (1, PAIR), 1)
    first = lane < PAIR // 2
    causal = (lax.broadcasted_iota(jnp.int32, (tokens, tokens), 0)
              >= lax.broadcasted_iota(jnp.int32, (tokens, tokens), 1))
    zero = jnp.zeros((), jnp.bfloat16)
    for pair in range(queries.shape[1] // PAIR):
        cols = slice(pair * PAIR, (pair + 1) * PAIR)
        q_pair, k_pair, v_pair = queries[:, cols], keys[:, cols], values[:, cols]
        kv = lax.dot_general(k_pair, v_pair, (((0,), (0,)), ((), ())),
                             preferred_element_type=jnp.float32)
        half = PAIR // 2
        state_ref[0, pair] = jnp.where(first, kv[:half], kv[half:])
        inside = None
        for use in (first, ~first):
            q_one = jnp.where(use, q_pair, zero)
            scores = lax.dot_general(q_one, k_pair, (((1,), (1,)), ((), ())),
                                     preferred_element_type=jnp.float32)
            scores = jnp.where(causal, scores, 0.0).astype(jnp.bfloat16)
            term = jnp.dot(scores, jnp.where(use, v_pair, zero), preferred_element_type=jnp.float32)
            inside = term if inside is None else inside + term
        inside_ref[:, cols] = inside


def head_norm_kernel(q_ref, state_ref, inside_ref, hgain_ref, att_ref):
    lane = lax.broadcasted_iota(jnp.int32, (1, PAIR), 1)
    first = lane < PAIR // 2
    head_size = PAIR // 2
    for pair in range(att_ref.shape[1] // PAIR):
        cols = slice(pair * PAIR, (pair + 1) * PAIR)
        packed = state_ref[0, pair]
        diag = jnp.concatenate([jnp.where(first, packed, 0.0), jnp.where(first, 0.0, packed)], axis=0)
        high = diag.astype(jnp.bfloat16)
        low = (diag - high.astype(jnp.float32)).astype(jnp.bfloat16)
        q_pair = q_ref[:, cols]
        carried = (jnp.dot(q_pair, high, preferred_element_type=jnp.float32)
                   + jnp.dot(q_pair, low, preferred_element_type=jnp.float32))
        combined = inside_ref[:, cols] + carried
        square = combined * combined
        sum_first = jnp.sum(jnp.where(first, square, 0.0), axis=-1, keepdims=True)
        sum_second = jnp.sum(jnp.where(first, 0.0, square), axis=-1, keepdims=True)
        scale = jnp.where(first, lax.rsqrt(sum_first / head_size + 1e-06),
                          lax.rsqrt(sum_second / head_size + 1e-06))
        att_ref[:, cols] = (combined * scale * hgain_ref[...][:, cols]).astype(jnp.bfloat16)


def project_kernel(*refs):
    emb_ref, w_ref = refs[0], refs[1]
    att_refs, out_ref = refs[2:-1], refs[-1]
    width = att_refs[0].shape[1]
    total = emb_ref[...].astype(jnp.float32)
    for chunk, att_ref in enumerate(att_refs):
        total = total + jnp.dot(att_ref[...], w_ref[chunk * width : (chunk + 1) * width, :],
                                preferred_element_type=jnp.float32)
    out_ref[...] = total.astype(jnp.bfloat16)


def full(shape):
    return pl.BlockSpec(shape, lambda b: (0,) * len(shape))


def rows(width):
    return pl.BlockSpec((BLK, width), lambda b: (b, 0))


def cost(flops, nbytes):
    return pl.CostEstimate(flops=int(flops), transcendentals=0, bytes_accessed=int(nbytes))


CHUNKS = 3


def shards(ticks, conv_weight, norm_gain, qkv_weight, head_gain, out_weight, state_in):
    tick_count, feat = ticks.shape
    token_count = tick_count // STRIDE
    model_width = conv_weight.shape[1]
    head_size = state_in.shape[1]
    pairs = model_width // PAIR
    blocks = token_count // BLK
    block_ticks = BLK * STRIDE
    width = model_width // CHUNKS
    chunk_pairs = width // PAIR
    params = pltpu.CompilerParams(dimension_semantics=("arbitrary",))
    bf16, f32 = jnp.bfloat16, jnp.float32

    prev = from_behind(ticks[tick_count - 2 * STRIDE :], "inner", 1)
    emb, normed = pl.pallas_call(
        conv_kernel,
        grid=(blocks,),
        in_specs=[
            pl.BlockSpec((block_ticks, feat), lambda b: (b, 0)),
            full((2 * STRIDE, feat)),
            full(conv_weight.shape),
            full((1, model_width)),
        ],
        out_specs=[rows(model_width), rows(model_width)],
        out_shape=[jax.ShapeDtypeStruct((token_count, model_width), bf16)] * 2,
        scratch_shapes=[pltpu.VMEM((block_ticks + STRIDE, feat), f32)],
        compiler_params=params,
        cost_estimate=cost(2 * token_count * conv_weight.size, 2 * (ticks.size + conv_weight.size) + 4 * emb_bytes(token_count, model_width)),
    )(ticks, prev, conv_weight, norm_gain.reshape(1, model_width))

    packed_in = state_in.reshape(pairs, 2, head_size, head_size).transpose(0, 2, 1, 3)
    packed_in = packed_in.reshape(pairs, head_size, PAIR)
    state_spec = pl.BlockSpec((1, chunk_pairs, head_size, PAIR), lambda b: (b, 0, 0, 0))
    atts = []
    for chunk in range(CHUNKS):
        def weight_spec(part, chunk=chunk):
            return pl.BlockSpec((model_width, width), lambda b: (0, part * CHUNKS + chunk))

        queries, inside, states = pl.pallas_call(
            attend_kernel,
            grid=(blocks,),
            in_specs=[rows(model_width), weight_spec(0), weight_spec(1), weight_spec(2)],
            out_specs=[rows(width), rows(width), state_spec],
            out_shape=[
                jax.ShapeDtypeStruct((token_count, width), bf16),
                jax.ShapeDtypeStruct((token_count, width), f32),
                jax.ShapeDtypeStruct((blocks, chunk_pairs, head_size, PAIR), f32),
            ],
            compiler_params=params,
            cost_estimate=cost(2 * token_count * model_width * 3 * width + 4 * token_count * BLK * width * 2,
                               2 * token_count * model_width + 6 * model_width * width + 6 * token_count * width),
        )(normed, qkv_weight, qkv_weight, qkv_weight)
        local = states[0]
        for block in range(1, blocks):
            local = local + states[block]
        prefix = exclusive_scan(local, "inner")
        carried = packed_in[chunk * chunk_pairs : (chunk + 1) * chunk_pairs] + prefix
        before = [carried]
        for block in range(1, blocks):
            before.append(before[-1] + states[block - 1])
        before = jnp.stack(before)
        atts.append(pl.pallas_call(
            head_norm_kernel,
            grid=(blocks,),
            in_specs=[rows(width), state_spec, rows(width), pl.BlockSpec((1, width), lambda b, chunk=chunk: (0, chunk))],
            out_specs=rows(width),
            out_shape=jax.ShapeDtypeStruct((token_count, width), bf16),
            compiler_params=params,
            cost_estimate=cost(4 * token_count * width * PAIR, 8 * token_count * width),
        )(queries, before, inside, head_gain.reshape(1, model_width)))

    return pl.pallas_call(
        project_kernel,
        grid=(blocks,),
        in_specs=[rows(model_width), full(out_weight.shape)] + [rows(width)] * CHUNKS,
        out_specs=rows(model_width),
        out_shape=jax.ShapeDtypeStruct((token_count, model_width), bf16),
        compiler_params=params,
        cost_estimate=cost(2 * token_count * out_weight.size, 2 * out_weight.size + 6 * token_count * model_width),
    )(emb, out_weight, *atts)


def emb_bytes(tokens, width):
    return tokens * width


def solution(mesh):
    in_specs = (P(("groups", "inner"), None), P(), P(), P(), P(), P(), P("groups", None, None))
    out_specs = P(("groups", "inner"), None)
    return jax.shard_map(shards, mesh=mesh, in_specs=in_specs, out_specs=out_specs, check_vma=False)
```

time: 73.4 us -> 91 us (1.24)
  the two profiles are of different devices: /device:TPU:24 before, /device:TPU:25 now
where the time goes in v3:
time: 91 us; the launch traced here: 90.3 us
  Pallas kernels  45.4 us (50%)
  starting transfers between devices  24.8 us (27%)
  waiting for transfers between devices  12 us (13%)
  other arithmetic  3.94 us (4%)
  local copies, waits for them, and re-layouts  3.88 us (4%)
    ppermute x13, starting transfers between devices, from_behind(): lax.ppermute(value, axis, [(source, source + steps) for source in range(i...  24.8 us
    pallas_call x3, Pallas kernels, shards(): pl.pallas_call(attend_kernel, grid=(blocks,), in_specs=[rows(model_width)...  24 us
    ppermute x13, waiting for transfers between devices, from_behind(): lax.ppermute(value, axis, [(source, source + steps) for source in range(i...  12 us
    pallas_call x3, Pallas kernels, shards(): pl.pallas_call(head_norm_kernel, grid=(blocks,), in_specs=[rows(width), s...  9.18 us
    pallas_call x1, Pallas kernels, shards(): pl.pallas_call(conv_kernel, grid=(blocks,), in_specs=[pl.BlockSpec((block...  7.88 us
    pallas_call x1, Pallas kernels, shards(): pl.pallas_call(project_kernel, grid=(blocks,), in_specs=[rows(model_width...  4.33 us
    another operation x6, other arithmetic, shards(): before = jnp.stack(before)  2.07 us
  transfers between devices with their start and end apart: 13, of which 8 were waited for; matrix products, arithmetic and copies ran while one was open for 6% of the time, Pallas kernels for 0%

profile of v3, /device:TPU:25, one launch (start us, length us, event | category | flops | bytes accessed | tf_op | source)
XLA Modules:
  0.0 90.3 jit_solution(17064481902273992758)
XLA Ops:
  0.0 0.7 slice.42
  0.7 3.7 %collective-permute-start = (bf16[16,128]{1,0:T(8,128)(2,1)S(1)}, bf16[16,128]{1,0:T(8,128)(2,1)S(1)}, u32[]{:S(2)}, u32[]{:S(2)}) collective-permute-start(bf16[16,128]{1,0:T(8,128)(2,1)S(1)} %slice.42), channel_id=1, source_target_pairs={{0,1},{1,2},{2,3},{3,4},{4,5},{5,6},{6,7},{7,8},{8,9},{9,10},{10,1... | collective-permute-start | bytes 12296 | tf_op jit(solution)/shard_map/ppermute | solution.py:16
  4.4 1.3 %reshape.15.gain_ref = f32[1,768]{1,0:T(1,128)} reshape(f32[768]{0:T(1024)} %param.9) | data formatting | bytes 6144 | tf_op jit(solution)/shard_map/reshape | solution.py:160
  5.6 0.0 collective-permute-done.prev_ref
  5.6 0.0 copy-start.5
  5.6 0.6 copy-done.5
  6.2 7.9 %shard_map.73 = (bf16[1024,768]{1,0:T(8,128)(2,1)}, bf16[1024,768]{1,0:T(8,128)(2,1)}) custom-call(bf16[8192,128]{1,0:T(8,128)(2,1)} %ticks_ref.1, bf16[16,128]{1,0:T(8,128)(2,1)} %copy-done.5, bf16[2048,768]{1,0:T(8,128)(2,1)} %conv_ref.1, f32[1,768]{1,0:T(1,128)} %reshape.15.gain_ref), custom_call_target="tpu_custom_call" | custom-call | flops 3221225472 | bytes 8388608 | tf_op jit(solution)/shard_map/pallas_call | solution.py:146
  14.1 8.0 %shard_map.78 = (bf16[1024,256]{1,0:T(8,128)(2,1)}, f32[1024,256]{1,0:T(8,128)}, f32[2,2,64,128]{3,2,1,0:T(8,128)}) custom-call(bf16[1024,768]{1,0:T(8,128)(2,1)} %get-tuple-element.17.normed_ref, bf16[768,2304]{1,0:T(8,128)(2,1)} %wv_ref.5, bf16[768,2304]{1,0:T(8,128)(2,1)} %wv_ref.5, bf16[768,2304]{1,0:T(8,128)(2,1)} %wv_ref.5), custom_call_target="tpu_custom_call" | custom-call | flops 2281701376 | bytes 4325376 | tf_op jit(solution)/shard_map/pallas_call | solution.py:170
  22.1 8.0 %shard_map.76 = (bf16[1024,256]{1,0:T(8,128)(2,1)}, f32[1024,256]{1,0:T(8,128)}, f32[2,2,64,128]{3,2,1,0:T(8,128)}) custom-call(bf16[1024,768]{1,0:T(8,128)(2,1)} %get-tuple-element.17.normed_ref, bf16[768,2304]{1,0:T(8,128)(2,1)} %wv_ref.5, bf16[768,2304]{1,0:T(8,128)(2,1)} %wv_ref.5, bf16[768,2304]{1,0:T(8,128)(2,1)} %wv_ref.5), custom_call_target="tpu_custom_call" | custom-call | flops 2281701376 | bytes 4325376 | tf_op jit(solution)/shard_map/pallas_call | solution.py:170
  30.1 0.0 copy-start.2
  30.1 0.0 copy-start.1
  30.1 8.0 %shard_map.74 = (bf16[1024,256]{1,0:T(8,128)(2,1)}, f32[1024,256]{1,0:T(8,128)}, f32[2,2,64,128]{3,2,1,0:T(8,128)}) custom-call(bf16[1024,768]{1,0:T(8,128)(2,1)} %get-tuple-element.17.normed_ref, bf16[768,2304]{1,0:T(8,128)(2,1)} %wv_ref.5, bf16[768,2304]{1,0:T(8,128)(2,1)} %wv_ref.5, bf16[768,2304]{1,0:T(8,128)(2,1)} %wv_ref.5), custom_call_target="tpu_custom_call" | custom-call | flops 2281701376 | bytes 4325376 | tf_op jit(solution)/shard_map/pallas_call | solution.py:170
  38.1 0.0 copy-start.3
  38.1 0.0 copy-done.2
  38.1 3.8 %collective-permute-start.9 = (f32[2,64,128]{2,1,0:T(8,128)S(1)}, f32[2,64,128]{2,1,0:T(8,128)S(1)}, u32[]{:S(2)}, u32[]{:S(2)}) collective-permute-start(f32[2,64,128]{2,1,0:T(8,128)S(1)} %bitcast_add_fusion), channel_id=1, source_target_pairs={{0,1},{1,2},{2,3},{3,4},{4,5},{5,6},{6,7},{7,8},{8,9},{9,10},{10,1... | collective-permute-start | bytes 196616 | tf_op jit(solution)/shard_map/ppermute | solution.py:16
  41.9 0.0 copy-done.1
  41.9 1.9 %collective-permute-start.5 = (f32[2,64,128]{2,1,0:T(8,128)S(1)}, f32[2,64,128]{2,1,0:T(8,128)S(1)}, u32[]{:S(2)}, u32[]{:S(2)}) collective-permute-start(f32[2,64,128]{2,1,0:T(8,128)S(1)} %bitcast_add_fusion.2), channel_id=1, source_target_pairs={{0,1},{1,2},{2,3},{3,4},{4,5},{5,6},{6,7},{7,8},{8,9},{9,10},{10,1... | collective-permute-start | bytes 196616 | tf_op jit(solution)/shard_map/ppermute | solution.py:16
  43.9 0.9 bitcast_add_fusion.4
  44.7 0.0 copy-start.4
  44.7 1.9 %collective-permute-start.1 = (f32[2,64,128]{2,1,0:T(8,128)S(1)}, f32[2,64,128]{2,1,0:T(8,128)S(1)}, u32[]{:S(2)}, u32[]{:S(2)}) collective-permute-start(f32[2,64,128]{2,1,0:T(8,128)S(1)} %bitcast_add_fusion.4), channel_id=1, source_target_pairs={{0,1},{1,2},{2,3},{3,4},{4,5},{5,6},{6,7},{7,8},{8,9},{9,10},{10,1... | collective-permute-start | bytes 196616 | tf_op jit(solution)/shard_map/ppermute | solution.py:16
  46.7 0.0 collective-permute-done.9
  46.7 1.9 %collective-permute-start.10 = (f32[2,64,128]{2,1,0:T(8,128)S(1)}, f32[2,64,128]{2,1,0:T(8,128)S(1)}, u32[]{:S(2)}, u32[]{:S(2)}) collective-permute-start(f32[2,64,128]{2,1,0:T(8,128)S(1)} %fusion.4), channel_id=1, source_target_pairs={{0,2},{1,3},{2,4},{3,5},{4,6},{5,7},{6,8},{7,9},{8,10},{9,11},{10,... | collective-permute-start | bytes 196616 | tf_op jit(solution)/shard_map/ppermute | solution.py:16
  48.6 0.0 collective-permute-done.5
  48.7 1.9 %collective-permute-start.6 = (f32[2,64,128]{2,1,0:T(8,128)S(1)}, f32[2,64,128]{2,1,0:T(8,128)S(1)}, u32[]{:S(2)}, u32[]{:S(2)}) collective-permute-start(f32[2,64,128]{2,1,0:T(8,128)S(1)} %fusion.5), channel_id=1, source_target_pairs={{0,2},{1,3},{2,4},{3,5},{4,6},{5,7},{6,8},{7,9},{8,10},{9,11},{10,... | collective-permute-start | bytes 196616 | tf_op jit(solution)/shard_map/ppermute | solution.py:16
  50.6 0.0 collective-permute-done.1
  50.6 0.9 fusion.6
  51.5 1.9 %collective-permute-start.2 = (f32[2,64,128]{2,1,0:T(8,128)S(1)}, f32[2,64,128]{2,1,0:T(8,128)S(1)}, u32[]{:S(2)}, u32[]{:S(2)}) collective-permute-start(f32[2,64,128]{2,1,0:T(8,128)S(1)} %fusion.6), channel_id=1, source_target_pairs={{0,2},{1,3},{2,4},{3,5},{4,6},{5,7},{6,8},{7,9},{8,10},{9,11},{10,... | collective-permute-start | bytes 196616 | tf_op jit(solution)/shard_map/ppermute | solution.py:16
  53.4 0.1 collective-permute-done.10
  53.5 1.3 %collective-permute-start.11 = (f32[2,64,128]{2,1,0:T(8,128)S(1)}, f32[2,64,128]{2,1,0:T(8,128)S(1)}, u32[]{:S(2)}, u32[]{:S(2)}) collective-permute-start(f32[2,64,128]{2,1,0:T(8,128)S(1)} %add.79), channel_id=1, source_target_pairs={{0,4},{1,5},{2,6},{3,7},{4,8},{5,9},{6,10},{7,11},{8,12},{9,13},{1... | collective-permute-start | bytes 196616 | tf_op jit(solution)/shard_map/ppermute | solution.py:16
  54.8 0.0 copy-done.3
  54.8 0.3 copy.10
  55.1 0.3 collective-permute-done.6
  55.5 1.3 %collective-permute-start.7 = (f32[2,64,128]{2,1,0:T(8,128)S(1)}, f32[2,64,128]{2,1,0:T(8,128)S(1)}, u32[]{:S(2)}, u32[]{:S(2)}) collective-permute-start(f32[2,64,128]{2,1,0:T(8,128)S(1)} %add.72), channel_id=1, source_target_pairs={{0,4},{1,5},{2,6},{3,7},{4,8},{5,9},{6,10},{7,11},{8,12},{9,13},{1... | collective-permute-start | bytes 196616 | tf_op jit(solution)/shard_map/ppermute | solution.py:16
  56.8 1.0 %collective-permute-done.2 = f32[2,64,128]{2,1,0:T(8,128)S(1)} collective-permute-done((f32[2,64,128]{2,1,0:T(8,128)S(1)}, f32[2,64,128]{2,1,0:T(8,128)S(1)}, u32[]{:S(2)}, u32[]{:S(2)}) %collective-permute-start.2) | collective-permute-done | bytes 65568 | tf_op jit(solution)/shard_map/ppermute | solution.py:16
  57.8 1.3 %collective-permute-start.3 = (f32[2,64,128]{2,1,0:T(8,128)S(1)}, f32[2,64,128]{2,1,0:T(8,128)S(1)}, u32[]{:S(2)}, u32[]{:S(2)}) collective-permute-start(f32[2,64,128]{2,1,0:T(8,128)S(1)} %add.65), channel_id=1, source_target_pairs={{0,4},{1,5},{2,6},{3,7},{4,8},{5,9},{6,10},{7,11},{8,12},{9,13},{1... | collective-permute-start | bytes 196616 | tf_op jit(solution)/shard_map/ppermute | solution.py:16
  59.1 0.9 %collective-permute-done.11 = f32[2,64,128]{2,1,0:T(8,128)S(1)} collective-permute-done((f32[2,64,128]{2,1,0:T(8,128)S(1)}, f32[2,64,128]{2,1,0:T(8,128)S(1)}, u32[]{:S(2)}, u32[]{:S(2)}) %collective-permute-start.11) | collective-permute-done | bytes 65568 | tf_op jit(solution)/shard_map/ppermute | solution.py:16
  60.0 1.3 %collective-permute-start.12 = (f32[2,64,128]{2,1,0:T(8,128)S(1)}, f32[2,64,128]{2,1,0:T(8,128)S(1)}, u32[]{:S(2)}, u32[]{:S(2)}) collective-permute-start(f32[2,64,128]{2,1,0:T(8,128)S(1)} %add.80), channel_id=1, source_target_pairs={{0,8},{1,9},{2,10},{3,11},{4,12},{5,13},{6,14},{7,15},{16,24},{17,... | collective-permute-start | bytes 196616 | tf_op jit(solution)/shard_map/ppermute | solution.py:16
  61.3 0.0 copy-start
  61.4 0.0 copy-done.4
  61.4 0.6 reshape.17.hgain_ref
  62.0 0.1 slice.52
  62.1 0.1 slice.48
  62.2 0.1 slice.44
  62.4 0.0 collective-permute-done.7
  62.4 1.3 %collective-permute-start.8 = (f32[2,64,128]{2,1,0:T(8,128)S(1)}, f32[2,64,128]{2,1,0:T(8,128)S(1)}, u32[]{:S(2)}, u32[]{:S(2)}) collective-permute-start(f32[2,64,128]{2,1,0:T(8,128)S(1)} %add.73), channel_id=1, source_target_pairs={{0,8},{1,9},{2,10},{3,11},{4,12},{5,13},{6,14},{7,15},{16,24},{17,... | collective-permute-start | bytes 196616 | tf_op jit(solution)/shard_map/ppermute | solution.py:16
  63.7 0.6 collective-permute-done.3
  64.3 1.3 %collective-permute-start.4 = (f32[2,64,128]{2,1,0:T(8,128)S(1)}, f32[2,64,128]{2,1,0:T(8,128)S(1)}, u32[]{:S(2)}, u32[]{:S(2)}) collective-permute-start(f32[2,64,128]{2,1,0:T(8,128)S(1)} %add.66), channel_id=1, source_target_pairs={{0,8},{1,9},{2,10},{3,11},{4,12},{5,13},{6,14},{7,15},{16,24},{17,... | collective-permute-start | bytes 196616 | tf_op jit(solution)/shard_map/ppermute | solution.py:16
  65.6 3.0 %collective-permute-done.12 = f32[2,64,128]{2,1,0:T(8,128)S(1)} collective-permute-done((f32[2,64,128]{2,1,0:T(8,128)S(1)}, f32[2,64,128]{2,1,0:T(8,128)S(1)}, u32[]{:S(2)}, u32[]{:S(2)}) %collective-permute-start.12) | collective-permute-done | bytes 65568 | tf_op jit(solution)/shard_map/ppermute | solution.py:16
  68.6 0.7 pad_maximum_fusion.2.state_ref
  69.2 4.8 %collective-permute-done.8 = f32[2,64,128]{2,1,0:T(8,128)S(1)} collective-permute-done((f32[2,64,128]{2,1,0:T(8,128)S(1)}, f32[2,64,128]{2,1,0:T(8,128)S(1)}, u32[]{:S(2)}, u32[]{:S(2)}) %collective-permute-start.8) | collective-permute-done | bytes 65568 | tf_op jit(solution)/shard_map/ppermute | solution.py:16
  74.0 0.7 pad_maximum_fusion.1.state_ref
  74.7 1.4 %collective-permute-done.4 = f32[2,64,128]{2,1,0:T(8,128)S(1)} collective-permute-done((f32[2,64,128]{2,1,0:T(8,128)S(1)}, f32[2,64,128]{2,1,0:T(8,128)S(1)}, u32[]{:S(2)}, u32[]{:S(2)}) %collective-permute-start.4) | collective-permute-done | bytes 65568 | tf_op jit(solution)/shard_map/ppermute | solution.py:16
  76.1 0.0 copy-done
  76.1 0.7 pad_maximum_fusion.state_ref
  76.8 3.1 %shard_map.79.refs_4_ = bf16[1024,256]{1,0:T(8,128)(2,1)} custom-call(bf16[1024,256]{1,0:T(8,128)(2,1)} %get-tuple-element.24.q_ref, f32[2,2,64,128]{3,2,1,0:T(8,128)} %pad_maximum_fusion.2.state_ref, f32[1024,256]{1,0:T(8,128)} %get-tuple-element.26.inside_ref, f32[1,768]{1,0:T(1,128)} %reshape.17.hgain_ref), custom_call_target="tpu_custom_call" | custom-call | flops 134217728 | bytes 2097152 | tf_op jit(solution)/shard_map/pallas_call | solution.py:193
  79.8 3.1 %shard_map.77.refs_3_ = bf16[1024,256]{1,0:T(8,128)(2,1)} custom-call(bf16[1024,256]{1,0:T(8,128)(2,1)} %get-tuple-element.21.q_ref, f32[2,2,64,128]{3,2,1,0:T(8,128)} %pad_maximum_fusion.1.state_ref, f32[1024,256]{1,0:T(8,128)} %get-tuple-element.23.inside_ref, f32[1,768]{1,0:T(1,128)} %reshape.17.hgain_ref), custom_call_target="tpu_custom_call" | custom-call | flops 134217728 | bytes 2097152 | tf_op jit(solution)/shard_map/pallas_call | solution.py:193
  82.9 3.1 %shard_map.75.refs_2_ = bf16[1024,256]{1,0:T(8,128)(2,1)} custom-call(bf16[1024,256]{1,0:T(8,128)(2,1)} %get-tuple-element.18.q_ref, f32[2,2,64,128]{3,2,1,0:T(8,128)} %pad_maximum_fusion.state_ref, f32[1024,256]{1,0:T(8,128)} %get-tuple-element.20.inside_ref, f32[1,768]{1,0:T(1,128)} %reshape.17.hgain_ref), custom_call_target="tpu_custom_call" | custom-call | flops 134217728 | bytes 2097152 | tf_op jit(solution)/shard_map/pallas_call | solution.py:193
  86.0 4.3 %shard_map.80 = bf16[1024,768]{1,0:T(8,128)(2,1)} custom-call(bf16[1024,768]{1,0:T(8,128)(2,1)} %get-tuple-element.16.refs_0_, bf16[768,768]{1,0:T(8,128)(2,1)} %refs_1_.1, bf16[1024,256]{1,0:T(8,128)(2,1)} %shard_map.75.refs_2_, bf16[1024,256]{1,0:T(8,128)(2,1)} %shard_map.77.refs_3_, bf16[1024,256]{1,0:T(8,128)(2,1)} %shard_map.79.refs_4_), custom_call_target="tpu_custom_call" | custom-call | flops 1207959552 | bytes 5898240 | tf_op jit(solution)/shard_map/pallas_call | solution.py:203
  (14 shorter events, 0.2 us)
Async XLA Ops:
  0.7 5.0 %collective-permute-start = (bf16[16,128]{1,0:T(8,128)(2,1)S(1)}, bf16[16,128]{1,0:T(8,128)(2,1)S(1)}, u32[]{:S(2)}, u32[]{:S(2)}) collective-permute-start(bf16[16,128]{1,0:T(8,128)(2,1)S(1)} %slice.42), channel_id=1, source_target_pairs={{0,1},{1,2},{2,3},{3,4},{4,5},{5,6},{6,7},{7,8},{8,9},{9,10},{10,1... | collective-permute-start | bytes 12296 | tf_op jit(solution)/shard_map/ppermute | solution.py:16
  5.6 0.6 copy-start.5
  30.1 8.0 %copy-start.2 = (f32[2,2,64,128]{3,2,1,0:T(8,128)S(1)}, f32[2,2,64,128]{3,2,1,0:T(8,128)}, u32[]{:S(2)}) copy-start(f32[2,2,64,128]{3,2,1,0:T(8,128)} %get-tuple-element.25) | copy-start | bytes 393220
  30.1 11.8 %copy-start.1 = (f32[2,2,64,128]{3,2,1,0:T(8,128)S(1)}, f32[2,2,64,128]{3,2,1,0:T(8,128)}, u32[]{:S(2)}) copy-start(f32[2,2,64,128]{3,2,1,0:T(8,128)} %get-tuple-element.22) | copy-start | bytes 393220
  38.1 16.7 %copy-start.3 = (f32[12,64,64]{2,1,0:T(8,128)S(1)}, f32[12,64,64]{2,1,0:T(8,128)}, u32[]{:S(2)}) copy-start(f32[12,64,64]{2,1,0:T(8,128)} %param.13) | copy-start | bytes 589828
  38.1 8.6 %collective-permute-start.9 = (f32[2,64,128]{2,1,0:T(8,128)S(1)}, f32[2,64,128]{2,1,0:T(8,128)S(1)}, u32[]{:S(2)}, u32[]{:S(2)}) collective-permute-start(f32[2,64,128]{2,1,0:T(8,128)S(1)} %bitcast_add_fusion), channel_id=1, source_target_pairs={{0,1},{1,2},{2,3},{3,4},{4,5},{5,6},{6,7},{7,8},{8,9},{9,10},{10,1... | collective-permute-start | bytes 196616 | tf_op jit(solution)/shard_map/ppermute | solution.py:16
  41.9 6.7 %collective-permute-start.5 = (f32[2,64,128]{2,1,0:T(8,128)S(1)}, f32[2,64,128]{2,1,0:T(8,128)S(1)}, u32[]{:S(2)}, u32[]{:S(2)}) collective-permute-start(f32[2,64,128]{2,1,0:T(8,128)S(1)} %bitcast_add_fusion.2), channel_id=1, source_target_pairs={{0,1},{1,2},{2,3},{3,4},{4,5},{5,6},{6,7},{7,8},{8,9},{9,10},{10,1... | collective-permute-start | bytes 196616 | tf_op jit(solution)/shard_map/ppermute | solution.py:16
  44.7 16.6 %copy-start.4 = (f32[768]{0:T(1024)S(1)}, f32[768]{0:T(1024)}, u32[]{:S(2)}) copy-start(f32[768]{0:T(1024)} %param.11) | copy-start | bytes 9220
  44.7 5.9 %collective-permute-start.1 = (f32[2,64,128]{2,1,0:T(8,128)S(1)}, f32[2,64,128]{2,1,0:T(8,128)S(1)}, u32[]{:S(2)}, u32[]{:S(2)}) collective-permute-start(f32[2,64,128]{2,1,0:T(8,128)S(1)} %bitcast_add_fusion.4), channel_id=1, source_target_pairs={{0,1},{1,2},{2,3},{3,4},{4,5},{5,6},{6,7},{7,8},{8,9},{9,10},{10,1... | collective-permute-start | bytes 196616 | tf_op jit(solution)/shard_map/ppermute | solution.py:16
  46.7 6.8 %collective-permute-start.10 = (f32[2,64,128]{2,1,0:T(8,128)S(1)}, f32[2,64,128]{2,1,0:T(8,128)S(1)}, u32[]{:S(2)}, u32[]{:S(2)}) collective-permute-start(f32[2,64,128]{2,1,0:T(8,128)S(1)} %fusion.4), channel_id=1, source_target_pairs={{0,2},{1,3},{2,4},{3,5},{4,6},{5,7},{6,8},{7,9},{8,10},{9,11},{10,... | collective-permute-start | bytes 196616 | tf_op jit(solution)/shard_map/ppermute | solution.py:16
  48.7 6.8 %collective-permute-start.6 = (f32[2,64,128]{2,1,0:T(8,128)S(1)}, f32[2,64,128]{2,1,0:T(8,128)S(1)}, u32[]{:S(2)}, u32[]{:S(2)}) collective-permute-start(f32[2,64,128]{2,1,0:T(8,128)S(1)} %fusion.5), channel_id=1, source_target_pairs={{0,2},{1,3},{2,4},{3,5},{4,6},{5,7},{6,8},{7,9},{8,10},{9,11},{10,... | collective-permute-start | bytes 196616 | tf_op jit(solution)/shard_map/ppermute | solution.py:16
  51.5 6.3 %collective-permute-start.2 = (f32[2,64,128]{2,1,0:T(8,128)S(1)}, f32[2,64,128]{2,1,0:T(8,128)S(1)}, u32[]{:S(2)}, u32[]{:S(2)}) collective-permute-start(f32[2,64,128]{2,1,0:T(8,128)S(1)} %fusion.6), channel_id=1, source_target_pairs={{0,2},{1,3},{2,4},{3,5},{4,6},{5,7},{6,8},{7,9},{8,10},{9,11},{10,... | collective-permute-start | bytes 196616 | tf_op jit(solution)/shard_map/ppermute | solution.py:16
  53.5 6.5 %collective-permute-start.11 = (f32[2,64,128]{2,1,0:T(8,128)S(1)}, f32[2,64,128]{2,1,0:T(8,128)S(1)}, u32[]{:S(2)}, u32[]{:S(2)}) collective-permute-start(f32[2,64,128]{2,1,0:T(8,128)S(1)} %add.79), channel_id=1, source_target_pairs={{0,4},{1,5},{2,6},{3,7},{4,8},{5,9},{6,10},{7,11},{8,12},{9,13},{1... | collective-permute-start | bytes 196616 | tf_op jit(solution)/shard_map/ppermute | solution.py:16
  55.5 6.9 %collective-permute-start.7 = (f32[2,64,128]{2,1,0:T(8,128)S(1)}, f32[2,64,128]{2,1,0:T(8,128)S(1)}, u32[]{:S(2)}, u32[]{:S(2)}) collective-permute-start(f32[2,64,128]{2,1,0:T(8,128)S(1)} %add.72), channel_id=1, source_target_pairs={{0,4},{1,5},{2,6},{3,7},{4,8},{5,9},{6,10},{7,11},{8,12},{9,13},{1... | collective-permute-start | bytes 196616 | tf_op jit(solution)/shard_map/ppermute | solution.py:16
  57.8 6.5 %collective-permute-start.3 = (f32[2,64,128]{2,1,0:T(8,128)S(1)}, f32[2,64,128]{2,1,0:T(8,128)S(1)}, u32[]{:S(2)}, u32[]{:S(2)}) collective-permute-start(f32[2,64,128]{2,1,0:T(8,128)S(1)} %add.65), channel_id=1, source_target_pairs={{0,4},{1,5},{2,6},{3,7},{4,8},{5,9},{6,10},{7,11},{8,12},{9,13},{1... | collective-permute-start | bytes 196616 | tf_op jit(solution)/shard_map/ppermute | solution.py:16
  60.0 8.5 %collective-permute-start.12 = (f32[2,64,128]{2,1,0:T(8,128)S(1)}, f32[2,64,128]{2,1,0:T(8,128)S(1)}, u32[]{:S(2)}, u32[]{:S(2)}) collective-permute-start(f32[2,64,128]{2,1,0:T(8,128)S(1)} %add.80), channel_id=1, source_target_pairs={{0,8},{1,9},{2,10},{3,11},{4,12},{5,13},{6,14},{7,15},{16,24},{17,... | collective-permute-start | bytes 196616 | tf_op jit(solution)/shard_map/ppermute | solution.py:16
  61.3 14.8 %copy-start = (f32[2,2,64,128]{3,2,1,0:T(8,128)S(1)}, f32[2,2,64,128]{3,2,1,0:T(8,128)}, u32[]{:S(2)}) copy-start(f32[2,2,64,128]{3,2,1,0:T(8,128)} %get-tuple-element.19) | copy-start | bytes 393220
  62.4 11.6 %collective-permute-start.8 = (f32[2,64,128]{2,1,0:T(8,128)S(1)}, f32[2,64,128]{2,1,0:T(8,128)S(1)}, u32[]{:S(2)}, u32[]{:S(2)}) collective-permute-start(f32[2,64,128]{2,1,0:T(8,128)S(1)} %add.73), channel_id=1, source_target_pairs={{0,8},{1,9},{2,10},{3,11},{4,12},{5,13},{6,14},{7,15},{16,24},{17,... | collective-permute-start | bytes 196616 | tf_op jit(solution)/shard_map/ppermute | solution.py:16
  64.3 11.8 %collective-permute-start.4 = (f32[2,64,128]{2,1,0:T(8,128)S(1)}, f32[2,64,128]{2,1,0:T(8,128)S(1)}, u32[]{:S(2)}, u32[]{:S(2)}) collective-permute-start(f32[2,64,128]{2,1,0:T(8,128)S(1)} %add.66), channel_id=1, source_target_pairs={{0,8},{1,9},{2,10},{3,11},{4,12},{5,13},{6,14},{7,15},{16,24},{17,... | collective-permute-start | bytes 196616 | tf_op jit(solution)/shard_map/ppermute | solution.py:16

commit v4 on v2

--- a/solution.py
+++ b/solution.py
@@ -10,6 +10,7 @@
 STRIDE = 8
 BLK = 512
 PAIR = 128
+SUB = 128
 
 
 def from_behind(value, axis, steps):
@@ -29,7 +30,7 @@
 
 
 def embed_kernel(ticks_ref, prev_ref, conv_ref, gain_ref, qkv_w_ref,
-                 emb_ref, q_ref, inside_ref, state_ref, wide_ref):
+                 emb_ref, q_ref, inside_ref, state_ref, wide_ref, run_ref):
     b = pl.program_id(0)
     block_ticks = ticks_ref.shape[0]
     tokens = block_ticks // STRIDE
@@ -58,27 +59,47 @@
 
     queries, keys, values = project(0), project(1), project(2)
     q_ref[...] = queries
+
+    @pl.when(b == 0)
+    def _():
+        run_ref[...] = jnp.zeros_like(run_ref)
+
     lane = lax.broadcasted_iota(jnp.int32, (1, PAIR), 1)
     first = lane < PAIR // 2
-    causal = (lax.broadcasted_iota(jnp.int32, (tokens, tokens), 0)
-              >= lax.broadcasted_iota(jnp.int32, (tokens, tokens), 1))
+    half = PAIR // 2
+    causal = (lax.broadcasted_iota(jnp.int32, (2 * SUB, SUB), 0) % SUB
+              >= lax.broadcasted_iota(jnp.int32, (2 * SUB, SUB), 1))
+    same_head = ((lax.broadcasted_iota(jnp.int32, (PAIR, PAIR), 0) < half)
+                 == (lax.broadcasted_iota(jnp.int32, (PAIR, PAIR), 1) < half))
     zero = jnp.zeros((), jnp.bfloat16)
     for pair in range(model_width // PAIR):
         cols = slice(pair * PAIR, (pair + 1) * PAIR)
-        q_pair, k_pair, v_pair = queries[:, cols], keys[:, cols], values[:, cols]
-        inside = None
-        for use in (first, ~first):
-            q_one = jnp.where(use, q_pair, zero)
-            scores = lax.dot_general(q_one, k_pair, (((1,), (1,)), ((), ())),
+        running = run_ref[pair]
+        for sub in range(tokens // SUB):
+            span = slice(sub * SUB, (sub + 1) * SUB)
+            q_sub, k_sub, v_sub = queries[span, cols], keys[span, cols], values[span, cols]
+            stacked_q = jnp.concatenate([jnp.where(first, q_sub, zero), jnp.where(first, zero, q_sub)], axis=0)
+            scores = lax.dot_general(stacked_q, k_sub, (((1,), (1,)), ((), ())),
                                      preferred_element_type=jnp.float32)
             scores = jnp.where(causal, scores, 0.0).astype(jnp.bfloat16)
-            term = jnp.dot(scores, jnp.where(use, v_pair, zero), preferred_element_type=jnp.float32)
-            inside = term if inside is None else inside + term
-        inside_ref[:, cols] = inside
-        kv = lax.dot_general(k_pair, v_pair, (((0,), (0,)), ((), ())),
-                             preferred_element_type=jnp.float32)
-        half = PAIR // 2
-        state_ref[0, pair] = jnp.where(first, kv[:half], kv[half:])
+            side = jnp.concatenate([scores[:SUB], scores[SUB:]], axis=1)
+            stacked_v = jnp.concatenate([jnp.where(first, v_sub, zero), jnp.where(first, zero, v_sub)], axis=0)
+            intra = jnp.dot(side, stacked_v, preferred_element_type=jnp.float32)
+            high = running.astype(jnp.bfloat16)
+            low = (running - high.astype(jnp.float32)).astype(jnp.bfloat16)
+            inter = (jnp.dot(q_sub, high, preferred_element_type=jnp.float32)
+                     + jnp.dot(q_sub, low, preferred_element_type=jnp.float32))
+            inside_ref[span, cols] = intra + inter
+            kv = lax.dot_general(k_sub, v_sub, (((0,), (0,)), ((), ())),
+                                 preferred_element_type=jnp.float32)
+            running = running + jnp.where(same_head, kv, 0.0)
+        run_ref[pair] = running
+
+    @pl.when(b == pl.num_programs(0) - 1)
+    def _():
+        for pair in range(model_width // PAIR):
+            total = run_ref[pair]
+            state_ref[pair] = jnp.where(first, total[:half], total[half:])
 
 
 def out_kernel(q_ref, state_ref, inside_ref, emb_ref, hgain_ref, out_w_ref, out_ref, att_ref):
@@ -88,7 +109,7 @@
     head_size = PAIR // 2
     for pair in range(model_width // PAIR):
         cols = slice(pair * PAIR, (pair + 1) * PAIR)
-        packed = state_ref[0, pair]
+        packed = state_ref[pair]
         diag = jnp.concatenate([jnp.where(first, packed, 0.0), jnp.where(first, 0.0, packed)], axis=0)
         high = diag.astype(jnp.bfloat16)
         low = (diag - high.astype(jnp.float32)).astype(jnp.bfloat16)
@@ -122,7 +143,7 @@
 
     prev = from_behind(ticks[tick_count - 2 * STRIDE :], "inner", 1)
     rows_spec = pl.BlockSpec((BLK, model_width), lambda b: (b, 0))
-    state_spec = pl.BlockSpec((1, pairs, head_size, PAIR), lambda b: (b, 0, 0, 0))
+    state_spec = full((pairs, head_size, PAIR))
     emb, queries, inside, states = pl.pallas_call(
         embed_kernel,
         grid=(blocks,),
@@ -138,22 +159,16 @@
             jax.ShapeDtypeStruct((token_count, model_width), jnp.bfloat16),
             jax.ShapeDtypeStruct((token_count, model_width), jnp.bfloat16),
             jax.ShapeDtypeStruct((token_count, model_width), jnp.float32),
-            jax.ShapeDtypeStruct((blocks, pairs, head_size, PAIR), jnp.float32),
+            jax.ShapeDtypeStruct((pairs, head_size, PAIR), jnp.float32),
         ],
-        scratch_shapes=[pltpu.VMEM((block_ticks + STRIDE, feat), jnp.float32)],
+        scratch_shapes=[pltpu.VMEM((block_ticks + STRIDE, feat), jnp.float32),
+                        pltpu.VMEM((pairs, PAIR, PAIR), jnp.float32)],
         compiler_params=pltpu.CompilerParams(dimension_semantics=("arbitrary",)),
     )(ticks, prev, conv_weight, norm_gain.reshape(1, model_width), qkv_weight)
 
-    local = states[0]
-    for block in range(1, blocks):
-        local = local + states[block]
-    prefix = exclusive_scan(local, "inner")
+    prefix = exclusive_scan(states, "inner")
     packed_in = state_in.reshape(pairs, 2, head_size, head_size).transpose(0, 2, 1, 3)
     carried = packed_in.reshape(pairs, head_size, PAIR) + prefix
-    before = [carried]
-    for block in range(1, blocks):
-        before.append(before[-1] + states[block - 1])
-    before = jnp.stack(before)
 
     return pl.pallas_call(
         out_kernel,
@@ -170,7 +185,7 @@
         out_shape=jax.ShapeDtypeStruct((token_count, model_width), jnp.bfloat16),
         scratch_shapes=[pltpu.VMEM((BLK, model_width), jnp.bfloat16)],
         compiler_params=pltpu.CompilerParams(dimension_semantics=("arbitrary",)),
-    )(queries, before, inside, emb, head_gain.reshape(1, model_width), out_weight)
+    )(queries, carried, inside, emb, head_gain.reshape(1, model_width), out_weight)
 
 
 def solution(mesh):

time: 73.4 us -> 75 us (1.022)
  Pallas kernels: 28.5 us -> 31.1 us
  other arithmetic: 3.08 us -> 1.71 us
    pallas_call x1, Pallas kernels: 21.6 us -> 23.9 us  [shards(): pl.pallas_call(embed_kernel, grid=(blocks,), in_specs=[pl.BlockSpec((bloc...]
    another operation x2 -> x0, other arithmetic: 0.85 us -> none  [shards(): before = jnp.stack(before)]
where the time goes in v4:
time: 75 us; the launch traced here: 74.7 us
  Pallas kernels  31.1 us (41%)
  waiting for transfers between devices  29.6 us (39%)
  starting transfers between devices  8.46 us (11%)
  local copies, waits for them, and re-layouts  3.71 us (5%)
  other arithmetic  1.71 us (2%)
    ppermute x5, waiting for transfers between devices, from_behind(): lax.ppermute(value, axis, [(source, source + steps) for source in range(i...  29.6 us
    pallas_call x1, Pallas kernels, shards(): pl.pallas_call(embed_kernel, grid=(blocks,), in_specs=[pl.BlockSpec((bloc...  23.9 us
    ppermute x5, starting transfers between devices, from_behind(): lax.ppermute(value, axis, [(source, source + steps) for source in range(i...  8.46 us
    pallas_call x1, Pallas kernels, shards(): pl.pallas_call(out_kernel, grid=(blocks,), in_specs=[rows_spec, state_spe...  7.18 us
  transfers between devices with their start and end apart: 5, of which 5 were waited for; matrix products, arithmetic and copies ran while one was open for 3% of the time, Pallas kernels for 0%

profile of v4, /device:TPU:24, one launch (start us, length us, event | category | flops | bytes accessed | tf_op | source)
XLA Modules:
  0.0 74.7 jit_solution(3680687512717726276)
XLA Ops:
  0.0 0.7 slice.3
  0.7 1.9 %collective-permute-start = (bf16[16,128]{1,0:T(8,128)(2,1)S(1)}, bf16[16,128]{1,0:T(8,128)(2,1)S(1)}, u32[]{:S(2)}, u32[]{:S(2)}) collective-permute-start(bf16[16,128]{1,0:T(8,128)(2,1)S(1)} %slice.3), channel_id=1, source_target_pairs={{0,1},{1,2},{2,3},{3,4},{4,5},{5,6},{6,7},{7,8},{8,9},{9,10},{10,1... | collective-permute-start | bytes 12296 | tf_op jit(solution)/shard_map/ppermute | solution.py:19
  2.6 1.3 %reshape.12.gain_ref = f32[1,768]{1,0:T(1,128)} reshape(f32[768]{0:T(1024)} %param.9) | data formatting | bytes 6144 | tf_op jit(solution)/shard_map/reshape | solution.py:167
  3.9 0.0 copy-start.3
  3.9 0.0 copy-start.1
  3.9 2.6 %collective-permute-done.prev_ref = bf16[16,128]{1,0:T(8,128)(2,1)S(1)} collective-permute-done((bf16[16,128]{1,0:T(8,128)(2,1)S(1)}, bf16[16,128]{1,0:T(8,128)(2,1)S(1)}, u32[]{:S(2)}, u32[]{:S(2)}) %collective-permute-start) | collective-permute-done | bytes 4128 | tf_op jit(solution)/shard_map/ppermute | solution.py:19
  6.5 0.0 copy-start.2
  6.5 0.6 copy-done.2
  7.1 23.9 %shard_map.73 = (bf16[1024,768]{1,0:T(8,128)(2,1)}, bf16[1024,768]{1,0:T(8,128)(2,1)}, f32[1024,768]{1,0:T(8,128)}, f32[6,64,128]{2,1,0:T(8,128)}) custom-call(bf16[8192,128]{1,0:T(8,128)(2,1)} %ticks_ref.1, bf16[16,128]{1,0:T(8,128)(2,1)} %copy-done.2, bf16[2048,768]{1,0:T(8,128)(2,1)} %conv_ref.1, f32[1,768]{1,0:T(1,128)} %reshape.12.gain_ref, ...), custom_call_target="tpu_custom_call" | custom-call | tf_op jit(solution)/shard_map/pallas_call | solution.py:147
  31.0 0.0 copy-start
  31.0 2.1 %collective-permute-start.1 = (f32[6,64,128]{2,1,0:T(8,128)}, f32[6,64,128]{2,1,0:T(8,128)S(1)}, u32[]{:S(2)}, u32[]{:S(2)}) collective-permute-start(f32[6,64,128]{2,1,0:T(8,128)} %get-tuple-element.10), channel_id=1, source_target_pairs={{0,1},{1,2},{2,3},{3,4},{4,5},{5,6},{6,7},{7,8},{8,9},{9,10},{10,1... | collective-permute-start | bytes 589832 | tf_op jit(solution)/shard_map/ppermute | solution.py:19
  33.1 6.2 %collective-permute-done.1 = f32[6,64,128]{2,1,0:T(8,128)S(1)} collective-permute-done((f32[6,64,128]{2,1,0:T(8,128)}, f32[6,64,128]{2,1,0:T(8,128)S(1)}, u32[]{:S(2)}, u32[]{:S(2)}) %collective-permute-start.1) | collective-permute-done | bytes 196640 | tf_op jit(solution)/shard_map/ppermute | solution.py:19
  39.3 1.0 %add.15 = f32[6,64,128]{2,1,0:T(8,128)S(1)} add(f32[6,64,128]{2,1,0:T(8,128)} %get-tuple-element.10, f32[6,64,128]{2,1,0:T(8,128)S(1)} %collective-permute-done.1) | non-fusion elementwise | flops 49152 | bytes 589824 | tf_op jit(solution)/shard_map/add | solution.py:27
  40.2 1.9 %collective-permute-start.2 = (f32[6,64,128]{2,1,0:T(8,128)S(1)}, f32[6,64,128]{2,1,0:T(8,128)S(1)}, u32[]{:S(2)}, u32[]{:S(2)}) collective-permute-start(f32[6,64,128]{2,1,0:T(8,128)S(1)} %add.15), channel_id=1, source_target_pairs={{0,2},{1,3},{2,4},{3,5},{4,6},{5,7},{6,8},{7,9},{8,10},{9,11},{10,... | collective-permute-start | bytes 589832 | tf_op jit(solution)/shard_map/ppermute | solution.py:19
  42.2 6.5 %collective-permute-done.2 = f32[6,64,128]{2,1,0:T(8,128)S(1)} collective-permute-done((f32[6,64,128]{2,1,0:T(8,128)S(1)}, f32[6,64,128]{2,1,0:T(8,128)S(1)}, u32[]{:S(2)}, u32[]{:S(2)}) %collective-permute-start.2) | collective-permute-done | bytes 196640 | tf_op jit(solution)/shard_map/ppermute | solution.py:19
  48.7 1.3 %collective-permute-start.3 = (f32[6,64,128]{2,1,0:T(8,128)S(1)}, f32[6,64,128]{2,1,0:T(8,128)S(1)}, u32[]{:S(2)}, u32[]{:S(2)}) collective-permute-start(f32[6,64,128]{2,1,0:T(8,128)S(1)} %add.16), channel_id=1, source_target_pairs={{0,4},{1,5},{2,6},{3,7},{4,8},{5,9},{6,10},{7,11},{8,12},{9,13},{1... | collective-permute-start | bytes 589832 | tf_op jit(solution)/shard_map/ppermute | solution.py:19
  50.0 6.3 %collective-permute-done.3 = f32[6,64,128]{2,1,0:T(8,128)S(1)} collective-permute-done((f32[6,64,128]{2,1,0:T(8,128)S(1)}, f32[6,64,128]{2,1,0:T(8,128)S(1)}, u32[]{:S(2)}, u32[]{:S(2)}) %collective-permute-start.3) | collective-permute-done | bytes 196640 | tf_op jit(solution)/shard_map/ppermute | solution.py:19
  56.3 1.3 %collective-permute-start.4 = (f32[6,64,128]{2,1,0:T(8,128)S(1)}, f32[6,64,128]{2,1,0:T(8,128)S(1)}, u32[]{:S(2)}, u32[]{:S(2)}) collective-permute-start(f32[6,64,128]{2,1,0:T(8,128)S(1)} %add.17), channel_id=1, source_target_pairs={{0,8},{1,9},{2,10},{3,11},{4,12},{5,13},{6,14},{7,15},{16,24},{17,... | collective-permute-start | bytes 589832 | tf_op jit(solution)/shard_map/ppermute | solution.py:19
  57.6 0.0 copy-done.3
  57.6 0.6 reshape.15.hgain_ref
  58.2 0.0 copy-done.1
  58.2 0.3 copy.10
  58.5 0.2 reshape.14
  58.8 8.0 %collective-permute-done.4 = f32[6,64,128]{2,1,0:T(8,128)S(1)} collective-permute-done((f32[6,64,128]{2,1,0:T(8,128)S(1)}, f32[6,64,128]{2,1,0:T(8,128)S(1)}, u32[]{:S(2)}, u32[]{:S(2)}) %collective-permute-start.4) | collective-permute-done | bytes 196640 | tf_op jit(solution)/shard_map/ppermute | solution.py:19
  66.8 0.0 copy-done
  66.8 0.7 subtract_add_fusion.state_ref
  67.5 7.2 %shard_map.74 = bf16[1024,768]{1,0:T(8,128)(2,1)} custom-call(bf16[1024,768]{1,0:T(8,128)(2,1)} %get-tuple-element.9.q_ref, f32[6,64,128]{2,1,0:T(8,128)} %subtract_add_fusion.state_ref, f32[1024,768]{1,0:T(8,128)} %get-tuple-element.11.inside_ref, bf16[1024,768]{1,0:T(8,128)(2,1)} %get-tuple-element.12.emb_ref, f32[1,768]{1,0:T(1,128)} %reshape.15.hgain_ref, ...), custom_call_target="tpu_custom_call" | custom-call | tf_op jit(solution)/shard_map/pallas_call | solution.py:173
  (2 shorter events, 0.1 us)
Async XLA Ops:
  0.7 5.8 %collective-permute-start = (bf16[16,128]{1,0:T(8,128)(2,1)S(1)}, bf16[16,128]{1,0:T(8,128)(2,1)S(1)}, u32[]{:S(2)}, u32[]{:S(2)}) collective-permute-start(bf16[16,128]{1,0:T(8,128)(2,1)S(1)} %slice.3), channel_id=1, source_target_pairs={{0,1},{1,2},{2,3},{3,4},{4,5},{5,6},{6,7},{7,8},{8,9},{9,10},{10,1... | collective-permute-start | bytes 12296 | tf_op jit(solution)/shard_map/ppermute | solution.py:19
  3.9 53.7 %copy-start.3 = (f32[768]{0:T(1024)S(1)}, f32[768]{0:T(1024)}, u32[]{:S(2)}) copy-start(f32[768]{0:T(1024)} %param.11) | copy-start | bytes 9220
  3.9 54.3 %copy-start.1 = (f32[12,64,64]{2,1,0:T(8,128)S(1)}, f32[12,64,64]{2,1,0:T(8,128)}, u32[]{:S(2)}) copy-start(f32[12,64,64]{2,1,0:T(8,128)} %param.13) | copy-start | bytes 589828
  6.5 0.6 copy-start.2
  31.0 35.7 %copy-start = (f32[6,64,128]{2,1,0:T(8,128)S(1)}, f32[6,64,128]{2,1,0:T(8,128)}, u32[]{:S(2)}) copy-start(f32[6,64,128]{2,1,0:T(8,128)} %get-tuple-element.10) | copy-start | bytes 589828
  31.0 8.2 %collective-permute-start.1 = (f32[6,64,128]{2,1,0:T(8,128)}, f32[6,64,128]{2,1,0:T(8,128)S(1)}, u32[]{:S(2)}, u32[]{:S(2)}) collective-permute-start(f32[6,64,128]{2,1,0:T(8,128)} %get-tuple-element.10), channel_id=1, source_target_pairs={{0,1},{1,2},{2,3},{3,4},{4,5},{5,6},{6,7},{7,8},{8,9},{9,10},{10,1... | collective-permute-start | bytes 589832 | tf_op jit(solution)/shard_map/ppermute | solution.py:19
  40.2 8.5 %collective-permute-start.2 = (f32[6,64,128]{2,1,0:T(8,128)S(1)}, f32[6,64,128]{2,1,0:T(8,128)S(1)}, u32[]{:S(2)}, u32[]{:S(2)}) collective-permute-start(f32[6,64,128]{2,1,0:T(8,128)S(1)} %add.15), channel_id=1, source_target_pairs={{0,2},{1,3},{2,4},{3,5},{4,6},{5,7},{6,8},{7,9},{8,10},{9,11},{10,... | collective-permute-start | bytes 589832 | tf_op jit(solution)/shard_map/ppermute | solution.py:19
  48.7 7.6 %collective-permute-start.3 = (f32[6,64,128]{2,1,0:T(8,128)S(1)}, f32[6,64,128]{2,1,0:T(8,128)S(1)}, u32[]{:S(2)}, u32[]{:S(2)}) collective-permute-start(f32[6,64,128]{2,1,0:T(8,128)S(1)} %add.16), channel_id=1, source_target_pairs={{0,4},{1,5},{2,6},{3,7},{4,8},{5,9},{6,10},{7,11},{8,12},{9,13},{1... | collective-permute-start | bytes 589832 | tf_op jit(solution)/shard_map/ppermute | solution.py:19
  56.3 10.5 %collective-permute-start.4 = (f32[6,64,128]{2,1,0:T(8,128)S(1)}, f32[6,64,128]{2,1,0:T(8,128)S(1)}, u32[]{:S(2)}, u32[]{:S(2)}) collective-permute-start(f32[6,64,128]{2,1,0:T(8,128)S(1)} %add.17), channel_id=1, source_target_pairs={{0,8},{1,9},{2,10},{3,11},{4,12},{5,13},{6,14},{7,15},{16,24},{17,... | collective-permute-start | bytes 589832 | tf_op jit(solution)/shard_map/ppermute | solution.py:19

commit v5 on v2

--- a/solution.py
+++ b/solution.py
@@ -29,7 +29,7 @@
 
 
 def embed_kernel(ticks_ref, prev_ref, conv_ref, gain_ref, qkv_w_ref,
-                 emb_ref, q_ref, inside_ref, state_ref, wide_ref):
+                 emb_ref, q_ref, inside_ref, total_ref, first_ref, wide_ref):
     b = pl.program_id(0)
     block_ticks = ticks_ref.shape[0]
     tokens = block_ticks // STRIDE
@@ -78,17 +78,29 @@
         kv = lax.dot_general(k_pair, v_pair, (((0,), (0,)), ((), ())),
                              preferred_element_type=jnp.float32)
         half = PAIR // 2
-        state_ref[0, pair] = jnp.where(first, kv[:half], kv[half:])
+        packed = jnp.where(first, kv[:half], kv[half:])
+
+        @pl.when(b == 0)
+        def _():
+            first_ref[pair] = packed
+            total_ref[pair] = packed
+
+        @pl.when(b > 0)
+        def _():
+            total_ref[pair] = total_ref[pair] + packed
 
 
-def out_kernel(q_ref, state_ref, inside_ref, emb_ref, hgain_ref, out_w_ref, out_ref, att_ref):
+def out_kernel(q_ref, carried_ref, first_ref, inside_ref, emb_ref, hgain_ref, out_w_ref, out_ref, att_ref):
+    b = pl.program_id(0)
     model_width = out_ref.shape[1]
     lane = lax.broadcasted_iota(jnp.int32, (1, PAIR), 1)
     first = lane < PAIR // 2
     head_size = PAIR // 2
+    same_head = ((lax.broadcasted_iota(jnp.int32, (PAIR, PAIR), 0) < head_size)
+                 == (lax.broadcasted_iota(jnp.int32, (PAIR, PAIR), 1) < head_size)).astype(jnp.bfloat16)
     for pair in range(model_width // PAIR):
         cols = slice(pair * PAIR, (pair + 1) * PAIR)
-        packed = state_ref[0, pair]
+        packed = carried_ref[pair] + jnp.where(b > 0, first_ref[pair], 0.0)
         diag = jnp.concatenate([jnp.where(first, packed, 0.0), jnp.where(first, 0.0, packed)], axis=0)
         high = diag.astype(jnp.bfloat16)
         low = (diag - high.astype(jnp.float32)).astype(jnp.bfloat16)
@@ -97,10 +109,11 @@
                    + jnp.dot(q_pair, low, preferred_element_type=jnp.float32))
         combined = inside_ref[:, cols] + carried
         square = combined * combined
-        sum_first = jnp.sum(jnp.where(first, square, 0.0), axis=-1, keepdims=True)
-        sum_second = jnp.sum(jnp.where(first, 0.0, square), axis=-1, keepdims=True)
-        scale = jnp.where(first, lax.rsqrt(sum_first / head_size + 1e-06),
-                          lax.rsqrt(sum_second / head_size + 1e-06))
+        square_high = square.astype(jnp.bfloat16)
+        square_low = (square - square_high.astype(jnp.float32)).astype(jnp.bfloat16)
+        head_sum = (jnp.dot(square_high, same_head, preferred_element_type=jnp.float32)
+                    + jnp.dot(square_low, same_head, preferred_element_type=jnp.float32))
+        scale = lax.rsqrt(head_sum / head_size + 1e-06)
         att_ref[:, cols] = (combined * scale * hgain_ref[:, cols]).astype(jnp.bfloat16)
     out = emb_ref[...].astype(jnp.float32) + jnp.dot(att_ref[...], out_w_ref[...],
                                                      preferred_element_type=jnp.float32)
@@ -122,8 +135,8 @@
 
     prev = from_behind(ticks[tick_count - 2 * STRIDE :], "inner", 1)
     rows_spec = pl.BlockSpec((BLK, model_width), lambda b: (b, 0))
-    state_spec = pl.BlockSpec((1, pairs, head_size, PAIR), lambda b: (b, 0, 0, 0))
-    emb, queries, inside, states = pl.pallas_call(
+    state_spec = full((pairs, head_size, PAIR))
+    emb, queries, inside, total, first_state = pl.pallas_call(
         embed_kernel,
         grid=(blocks,),
         in_specs=[
@@ -133,33 +146,28 @@
             full((1, model_width)),
             full(qkv_weight.shape),
         ],
-        out_specs=[rows_spec, rows_spec, rows_spec, state_spec],
+        out_specs=[rows_spec, rows_spec, rows_spec, state_spec, state_spec],
         out_shape=[
             jax.ShapeDtypeStruct((token_count, model_width), jnp.bfloat16),
             jax.ShapeDtypeStruct((token_count, model_width), jnp.bfloat16),
             jax.ShapeDtypeStruct((token_count, model_width), jnp.float32),
-            jax.ShapeDtypeStruct((blocks, pairs, head_size, PAIR), jnp.float32),
+            jax.ShapeDtypeStruct((pairs, head_size, PAIR), jnp.float32),
+            jax.ShapeDtypeStruct((pairs, head_size, PAIR), jnp.float32),
         ],
         scratch_shapes=[pltpu.VMEM((block_ticks + STRIDE, feat), jnp.float32)],
         compiler_params=pltpu.CompilerParams(dimension_semantics=("arbitrary",)),
     )(ticks, prev, conv_weight, norm_gain.reshape(1, model_width), qkv_weight)
 
-    local = states[0]
-    for block in range(1, blocks):
-        local = local + states[block]
-    prefix = exclusive_scan(local, "inner")
+    prefix = exclusive_scan(total, "inner")
     packed_in = state_in.reshape(pairs, 2, head_size, head_size).transpose(0, 2, 1, 3)
     carried = packed_in.reshape(pairs, head_size, PAIR) + prefix
-    before = [carried]
-    for block in range(1, blocks):
-        before.append(before[-1] + states[block - 1])
-    before = jnp.stack(before)
 
     return pl.pallas_call(
         out_kernel,
         grid=(blocks,),
         in_specs=[
             rows_spec,
+            state_spec,
             state_spec,
             rows_spec,
             rows_spec,
@@ -170,7 +178,7 @@
         out_shape=jax.ShapeDtypeStruct((token_count, model_width), jnp.bfloat16),
         scratch_shapes=[pltpu.VMEM((BLK, model_width), jnp.bfloat16)],
         compiler_params=pltpu.CompilerParams(dimension_semantics=("arbitrary",)),
-    )(queries, before, inside, emb, head_gain.reshape(1, model_width), out_weight)
+    )(queries, carried, first_state, inside, emb, head_gain.reshape(1, model_width), out_weight)
 
 
 def solution(mesh):

time: 73.4 us -> 78.8 us (1.074)
  Pallas kernels: 28.5 us -> 34.9 us
  other arithmetic: 3.08 us -> 1.73 us
    pallas_call x1, Pallas kernels: 21.6 us -> 27.7 us  [shards(): pl.pallas_call(embed_kernel, grid=(blocks,), in_specs=[pl.BlockSpec((bloc...]
    another operation x2 -> x0, other arithmetic: 0.85 us -> none  [shards(): before = jnp.stack(before)]
where the time goes in v5:
time: 78.8 us; the launch traced here: 78.5 us
  Pallas kernels  34.9 us (44%)
  waiting for transfers between devices  29.6 us (38%)
  starting transfers between devices  8.46 us (11%)
  local copies, waits for them, and re-layouts  3.69 us (5%)
  other arithmetic  1.73 us (2%)
    ppermute x5, waiting for transfers between devices, from_behind(): lax.ppermute(value, axis, [(source, source + steps) for source in range(i...  29.6 us
    pallas_call x1, Pallas kernels, shards(): pl.pallas_call(embed_kernel, grid=(blocks,), in_specs=[pl.BlockSpec((bloc...  27.7 us
    ppermute x5, starting transfers between devices, from_behind(): lax.ppermute(value, axis, [(source, source + steps) for source in range(i...  8.46 us
    pallas_call x1, Pallas kernels, shards(): pl.pallas_call(out_kernel, grid=(blocks,), in_specs=[rows_spec, state_spe...  7.16 us
  transfers between devices with their start and end apart: 5, of which 5 were waited for; matrix products, arithmetic and copies ran while one was open for 3% of the time, Pallas kernels for 0%

profile of v5, /device:TPU:24, one launch (start us, length us, event | category | flops | bytes accessed | tf_op | source)
XLA Modules:
  0.0 78.5 jit_solution(16217787884084065004)
XLA Ops:
  0.0 0.7 slice.3
  0.7 1.9 %collective-permute-start = (bf16[16,128]{1,0:T(8,128)(2,1)S(1)}, bf16[16,128]{1,0:T(8,128)(2,1)S(1)}, u32[]{:S(2)}, u32[]{:S(2)}) collective-permute-start(bf16[16,128]{1,0:T(8,128)(2,1)S(1)} %slice.3), channel_id=1, source_target_pairs={{0,1},{1,2},{2,3},{3,4},{4,5},{5,6},{6,7},{7,8},{8,9},{9,10},{10,1... | collective-permute-start | bytes 12296 | tf_op jit(solution)/shard_map/ppermute | solution.py:18
  2.6 1.3 %reshape.12.gain_ref = f32[1,768]{1,0:T(1,128)} reshape(f32[768]{0:T(1024)} %param.9) | data formatting | bytes 6144 | tf_op jit(solution)/shard_map/reshape | solution.py:159
  3.9 0.0 copy-start.3
  3.9 0.0 copy-start.1
  3.9 2.6 %collective-permute-done.prev_ref = bf16[16,128]{1,0:T(8,128)(2,1)S(1)} collective-permute-done((bf16[16,128]{1,0:T(8,128)(2,1)S(1)}, bf16[16,128]{1,0:T(8,128)(2,1)S(1)}, u32[]{:S(2)}, u32[]{:S(2)}) %collective-permute-start) | collective-permute-done | bytes 4128 | tf_op jit(solution)/shard_map/ppermute | solution.py:18
  6.5 0.0 copy-start.2
  6.5 0.6 copy-done.2
  7.1 27.7 %shard_map.73 = (bf16[1024,768]{1,0:T(8,128)(2,1)}, bf16[1024,768]{1,0:T(8,128)(2,1)}, f32[1024,768]{1,0:T(8,128)}, f32[6,64,128]{2,1,0:T(8,128)}, f32[6,64,128]{2,1,0:T(8,128)}) custom-call(bf16[8192,128]{1,0:T(8,128)(2,1)} %ticks_ref.1, bf16[16,128]{1,0:T(8,128)(2,1)} %copy-done.2, bf16[2048,768]{1,0:T(8,128)(2,1)} %conv_ref.1, ...), custom_call_target="tpu_custom_call" | custom-call | tf_op jit(solution)/shard_map/pallas_call | solution.py:139
  34.8 0.0 copy-start
  34.8 2.1 %collective-permute-start.1 = (f32[6,64,128]{2,1,0:T(8,128)}, f32[6,64,128]{2,1,0:T(8,128)S(1)}, u32[]{:S(2)}, u32[]{:S(2)}) collective-permute-start(f32[6,64,128]{2,1,0:T(8,128)} %get-tuple-element.11), channel_id=1, source_target_pairs={{0,1},{1,2},{2,3},{3,4},{4,5},{5,6},{6,7},{7,8},{8,9},{9,10},{10,1... | collective-permute-start | bytes 589832 | tf_op jit(solution)/shard_map/ppermute | solution.py:18
  36.9 6.2 %collective-permute-done.1 = f32[6,64,128]{2,1,0:T(8,128)S(1)} collective-permute-done((f32[6,64,128]{2,1,0:T(8,128)}, f32[6,64,128]{2,1,0:T(8,128)S(1)}, u32[]{:S(2)}, u32[]{:S(2)}) %collective-permute-start.1) | collective-permute-done | bytes 196640 | tf_op jit(solution)/shard_map/ppermute | solution.py:18
  43.1 1.0 %add.15 = f32[6,64,128]{2,1,0:T(8,128)S(1)} add(f32[6,64,128]{2,1,0:T(8,128)} %get-tuple-element.11, f32[6,64,128]{2,1,0:T(8,128)S(1)} %collective-permute-done.1) | non-fusion elementwise | flops 49152 | bytes 589824 | tf_op jit(solution)/shard_map/add | solution.py:26
  44.0 1.9 %collective-permute-start.2 = (f32[6,64,128]{2,1,0:T(8,128)S(1)}, f32[6,64,128]{2,1,0:T(8,128)S(1)}, u32[]{:S(2)}, u32[]{:S(2)}) collective-permute-start(f32[6,64,128]{2,1,0:T(8,128)S(1)} %add.15), channel_id=1, source_target_pairs={{0,2},{1,3},{2,4},{3,5},{4,6},{5,7},{6,8},{7,9},{8,10},{9,11},{10,... | collective-permute-start | bytes 589832 | tf_op jit(solution)/shard_map/ppermute | solution.py:18
  45.9 6.5 %collective-permute-done.2 = f32[6,64,128]{2,1,0:T(8,128)S(1)} collective-permute-done((f32[6,64,128]{2,1,0:T(8,128)S(1)}, f32[6,64,128]{2,1,0:T(8,128)S(1)}, u32[]{:S(2)}, u32[]{:S(2)}) %collective-permute-start.2) | collective-permute-done | bytes 196640 | tf_op jit(solution)/shard_map/ppermute | solution.py:18
  52.5 1.3 %collective-permute-start.3 = (f32[6,64,128]{2,1,0:T(8,128)S(1)}, f32[6,64,128]{2,1,0:T(8,128)S(1)}, u32[]{:S(2)}, u32[]{:S(2)}) collective-permute-start(f32[6,64,128]{2,1,0:T(8,128)S(1)} %add.16), channel_id=1, source_target_pairs={{0,4},{1,5},{2,6},{3,7},{4,8},{5,9},{6,10},{7,11},{8,12},{9,13},{1... | collective-permute-start | bytes 589832 | tf_op jit(solution)/shard_map/ppermute | solution.py:18
  53.8 6.3 %collective-permute-done.3 = f32[6,64,128]{2,1,0:T(8,128)S(1)} collective-permute-done((f32[6,64,128]{2,1,0:T(8,128)S(1)}, f32[6,64,128]{2,1,0:T(8,128)S(1)}, u32[]{:S(2)}, u32[]{:S(2)}) %collective-permute-start.3) | collective-permute-done | bytes 196640 | tf_op jit(solution)/shard_map/ppermute | solution.py:18
  60.1 1.3 %collective-permute-start.4 = (f32[6,64,128]{2,1,0:T(8,128)S(1)}, f32[6,64,128]{2,1,0:T(8,128)S(1)}, u32[]{:S(2)}, u32[]{:S(2)}) collective-permute-start(f32[6,64,128]{2,1,0:T(8,128)S(1)} %add.17), channel_id=1, source_target_pairs={{0,8},{1,9},{2,10},{3,11},{4,12},{5,13},{6,14},{7,15},{16,24},{17,... | collective-permute-start | bytes 589832 | tf_op jit(solution)/shard_map/ppermute | solution.py:18
  61.4 0.0 copy-done.3
  61.4 0.6 reshape.15.hgain_ref
  62.0 0.0 copy-done.1
  62.0 0.3 copy.10
  62.3 0.2 reshape.14
  62.5 8.0 %collective-permute-done.4 = f32[6,64,128]{2,1,0:T(8,128)S(1)} collective-permute-done((f32[6,64,128]{2,1,0:T(8,128)S(1)}, f32[6,64,128]{2,1,0:T(8,128)S(1)}, u32[]{:S(2)}, u32[]{:S(2)}) %collective-permute-start.4) | collective-permute-done | bytes 196640 | tf_op jit(solution)/shard_map/ppermute | solution.py:18
  70.6 0.0 copy-done
  70.6 0.7 subtract_add_fusion.carried_ref
  71.3 7.2 %shard_map.74 = bf16[1024,768]{1,0:T(8,128)(2,1)} custom-call(bf16[1024,768]{1,0:T(8,128)(2,1)} %get-tuple-element.10.q_ref, f32[6,64,128]{2,1,0:T(8,128)} %subtract_add_fusion.carried_ref, f32[6,64,128]{2,1,0:T(8,128)} %get-tuple-element.12.first_ref, f32[1024,768]{1,0:T(8,128)} %get-tuple-element.13.inside_ref, ...), custom_call_target="tpu_custom_call" | custom-call | tf_op jit(solution)/shard_map/pallas_call | solution.py:165
  (2 shorter events, 0.1 us)
Async XLA Ops:
  0.7 5.8 %collective-permute-start = (bf16[16,128]{1,0:T(8,128)(2,1)S(1)}, bf16[16,128]{1,0:T(8,128)(2,1)S(1)}, u32[]{:S(2)}, u32[]{:S(2)}) collective-permute-start(bf16[16,128]{1,0:T(8,128)(2,1)S(1)} %slice.3), channel_id=1, source_target_pairs={{0,1},{1,2},{2,3},{3,4},{4,5},{5,6},{6,7},{7,8},{8,9},{9,10},{10,1... | collective-permute-start | bytes 12296 | tf_op jit(solution)/shard_map/ppermute | solution.py:18
  3.9 57.5 %copy-start.3 = (f32[768]{0:T(1024)S(1)}, f32[768]{0:T(1024)}, u32[]{:S(2)}) copy-start(f32[768]{0:T(1024)} %param.11) | copy-start | bytes 9220
  3.9 58.1 %copy-start.1 = (f32[12,64,64]{2,1,0:T(8,128)S(1)}, f32[12,64,64]{2,1,0:T(8,128)}, u32[]{:S(2)}) copy-start(f32[12,64,64]{2,1,0:T(8,128)} %param.13) | copy-start | bytes 589828
  6.5 0.6 copy-start.2
  34.8 35.8 %copy-start = (f32[6,64,128]{2,1,0:T(8,128)S(1)}, f32[6,64,128]{2,1,0:T(8,128)}, u32[]{:S(2)}) copy-start(f32[6,64,128]{2,1,0:T(8,128)} %get-tuple-element.11) | copy-start | bytes 589828
  34.8 8.2 %collective-permute-start.1 = (f32[6,64,128]{2,1,0:T(8,128)}, f32[6,64,128]{2,1,0:T(8,128)S(1)}, u32[]{:S(2)}, u32[]{:S(2)}) collective-permute-start(f32[6,64,128]{2,1,0:T(8,128)} %get-tuple-element.11), channel_id=1, source_target_pairs={{0,1},{1,2},{2,3},{3,4},{4,5},{5,6},{6,7},{7,8},{8,9},{9,10},{10,1... | collective-permute-start | bytes 589832 | tf_op jit(solution)/shard_map/ppermute | solution.py:18
  44.0 8.5 %collective-permute-start.2 = (f32[6,64,128]{2,1,0:T(8,128)S(1)}, f32[6,64,128]{2,1,0:T(8,128)S(1)}, u32[]{:S(2)}, u32[]{:S(2)}) collective-permute-start(f32[6,64,128]{2,1,0:T(8,128)S(1)} %add.15), channel_id=1, source_target_pairs={{0,2},{1,3},{2,4},{3,5},{4,6},{5,7},{6,8},{7,9},{8,10},{9,11},{10,... | collective-permute-start | bytes 589832 | tf_op jit(solution)/shard_map/ppermute | solution.py:18
  52.5 7.6 %collective-permute-start.3 = (f32[6,64,128]{2,1,0:T(8,128)S(1)}, f32[6,64,128]{2,1,0:T(8,128)S(1)}, u32[]{:S(2)}, u32[]{:S(2)}) collective-permute-start(f32[6,64,128]{2,1,0:T(8,128)S(1)} %add.16), channel_id=1, source_target_pairs={{0,4},{1,5},{2,6},{3,7},{4,8},{5,9},{6,10},{7,11},{8,12},{9,13},{1... | collective-permute-start | bytes 589832 | tf_op jit(solution)/shard_map/ppermute | solution.py:18
  60.1 10.5 %collective-permute-start.4 = (f32[6,64,128]{2,1,0:T(8,128)S(1)}, f32[6,64,128]{2,1,0:T(8,128)S(1)}, u32[]{:S(2)}, u32[]{:S(2)}) collective-permute-start(f32[6,64,128]{2,1,0:T(8,128)S(1)} %add.17), channel_id=1, source_target_pairs={{0,8},{1,9},{2,10},{3,11},{4,12},{5,13},{6,14},{7,15},{16,24},{17,... | collective-permute-start | bytes 589832 | tf_op jit(solution)/shard_map/ppermute | solution.py:18

commit v6 on v2

--- a/solution.py
+++ b/solution.py
@@ -29,7 +29,7 @@
 
 
 def embed_kernel(ticks_ref, prev_ref, conv_ref, gain_ref, qkv_w_ref,
-                 emb_ref, q_ref, inside_ref, state_ref, wide_ref):
+                 emb_ref, q_ref, k_ref, v_ref, state_ref, wide_ref):
     b = pl.program_id(0)
     block_ticks = ticks_ref.shape[0]
     tokens = block_ticks // STRIDE
@@ -58,12 +58,28 @@
 
     queries, keys, values = project(0), project(1), project(2)
     q_ref[...] = queries
+    k_ref[...] = keys
+    v_ref[...] = values
+    lane = lax.broadcasted_iota(jnp.int32, (1, PAIR), 1)
+    first = lane < PAIR // 2
+    for pair in range(model_width // PAIR):
+        cols = slice(pair * PAIR, (pair + 1) * PAIR)
+        kv = lax.dot_general(keys[:, cols], values[:, cols], (((0,), (0,)), ((), ())),
+                             preferred_element_type=jnp.float32)
+        half = PAIR // 2
+        state_ref[0, pair] = jnp.where(first, kv[:half], kv[half:])
+
+
+def inside_kernel(q_ref, k_ref, v_ref, earlier_ref, inside_ref):
+    del earlier_ref
+    queries, keys, values = q_ref[...], k_ref[...], v_ref[...]
+    tokens = queries.shape[0]
     lane = lax.broadcasted_iota(jnp.int32, (1, PAIR), 1)
     first = lane < PAIR // 2
     causal = (lax.broadcasted_iota(jnp.int32, (tokens, tokens), 0)
               >= lax.broadcasted_iota(jnp.int32, (tokens, tokens), 1))
     zero = jnp.zeros((), jnp.bfloat16)
-    for pair in range(model_width // PAIR):
+    for pair in range(queries.shape[1] // PAIR):
         cols = slice(pair * PAIR, (pair + 1) * PAIR)
         q_pair, k_pair, v_pair = queries[:, cols], keys[:, cols], values[:, cols]
         inside = None
@@ -75,10 +91,6 @@
             term = jnp.dot(scores, jnp.where(use, v_pair, zero), preferred_element_type=jnp.float32)
             inside = term if inside is None else inside + term
         inside_ref[:, cols] = inside
-        kv = lax.dot_general(k_pair, v_pair, (((0,), (0,)), ((), ())),
-                             preferred_element_type=jnp.float32)
-        half = PAIR // 2
-        state_ref[0, pair] = jnp.where(first, kv[:half], kv[half:])
 
 
 def out_kernel(q_ref, state_ref, inside_ref, emb_ref, hgain_ref, out_w_ref, out_ref, att_ref):
@@ -123,7 +135,7 @@
     prev = from_behind(ticks[tick_count - 2 * STRIDE :], "inner", 1)
     rows_spec = pl.BlockSpec((BLK, model_width), lambda b: (b, 0))
     state_spec = pl.BlockSpec((1, pairs, head_size, PAIR), lambda b: (b, 0, 0, 0))
-    emb, queries, inside, states = pl.pallas_call(
+    emb, queries, keys, values, states = pl.pallas_call(
         embed_kernel,
         grid=(blocks,),
         in_specs=[
@@ -133,21 +145,47 @@
             full((1, model_width)),
             full(qkv_weight.shape),
         ],
-        out_specs=[rows_spec, rows_spec, rows_spec, state_spec],
-        out_shape=[
-            jax.ShapeDtypeStruct((token_count, model_width), jnp.bfloat16),
-            jax.ShapeDtypeStruct((token_count, model_width), jnp.bfloat16),
-            jax.ShapeDtypeStruct((token_count, model_width), jnp.float32),
+        out_specs=[rows_spec, rows_spec, rows_spec, rows_spec, state_spec],
+        out_shape=[jax.ShapeDtypeStruct((token_count, model_width), jnp.bfloat16)] * 4 + [
             jax.ShapeDtypeStruct((blocks, pairs, head_size, PAIR), jnp.float32),
         ],
         scratch_shapes=[pltpu.VMEM((block_ticks + STRIDE, feat), jnp.float32)],
         compiler_params=pltpu.CompilerParams(dimension_semantics=("arbitrary",)),
     )(ticks, prev, conv_weight, norm_gain.reshape(1, model_width), qkv_weight)
 
+    def inside_block(block, earlier, q, k, v):
+        spec = pl.BlockSpec((BLK, model_width), lambda i, block=block: (block, 0))
+        return pl.pallas_call(
+            inside_kernel,
+            grid=(1,),
+            in_specs=[spec, spec, spec, pl.BlockSpec(memory_space=pl.ANY)],
+            out_specs=spec,
+            out_shape=jax.ShapeDtypeStruct((token_count, model_width), jnp.float32),
+            input_output_aliases={3: 0},
+            cost_estimate=pl.CostEstimate(flops=8 * BLK * BLK * model_width, transcendentals=0,
+                                          bytes_accessed=6 * BLK * model_width + 4 * BLK * model_width),
+        )(q, k, v, earlier)
+
     local = states[0]
     for block in range(1, blocks):
         local = local + states[block]
-    prefix = exclusive_scan(local, "inner")
+    count = lax.axis_size("inner")
+    inside = jnp.zeros((token_count, model_width), jnp.float32)
+    total, steps, block = local, 1, 0
+    while steps < count:
+        if block < blocks:
+            total, q_in, k_in, v_in = lax.optimization_barrier((total, queries, keys, values))
+        received = from_behind(total, "inner", steps)
+        if block < blocks:
+            inside = inside_block(block, inside, q_in, k_in, v_in)
+            received, inside = lax.optimization_barrier((received, inside))
+            block += 1
+        total = total + received
+        steps *= 2
+    while block < blocks:
+        inside = inside_block(block, inside, queries, keys, values)
+        block += 1
+    prefix = total - local
     packed_in = state_in.reshape(pairs, 2, head_size, head_size).transpose(0, 2, 1, 3)
     carried = packed_in.reshape(pairs, head_size, PAIR) + prefix
     before = [carried]

time: 73.4 us -> 73.5 us (level)
  the two profiles are of different devices: /device:TPU:24 before, /device:TPU:30 now
where the time goes in v6:
time: 73.5 us; the launch traced here: 73 us
  Pallas kernels  34.9 us (47%)
  waiting for transfers between devices  22.7 us (31%)
  starting transfers between devices  7.84 us (11%)
  local copies, waits for them, and re-layouts  5.54 us (8%)
  other arithmetic  1.98 us (3%)
    ppermute x5, waiting for transfers between devices, from_behind(): lax.ppermute(value, axis, [(source, source + steps) for source in range(i...  22.7 us
    pallas_call x1, Pallas kernels, shards(): pl.pallas_call(embed_kernel, grid=(blocks,), in_specs=[pl.BlockSpec((bloc...  14.9 us
    pallas_call x2, Pallas kernels, inside_block(): pl.pallas_call(inside_kernel, grid=(1,), in_specs=[spec, spec, spec, pl.B...  13.2 us
    ppermute x5, starting transfers between devices, from_behind(): lax.ppermute(value, axis, [(source, source + steps) for source in range(i...  7.84 us
    pallas_call x1, Pallas kernels, shards(): pl.pallas_call(out_kernel, grid=(blocks,), in_specs=[rows_spec, state_spe...  6.88 us
    broadcast_in_dim x1, local copies, waits for them, and re-layouts, shards(): inside = jnp.zeros((token_count, model_width), jnp.float32)  1.84 us
  transfers between devices with their start and end apart: 5, of which 4 were waited for; matrix products, arithmetic and copies ran while one was open for 6% of the time, Pallas kernels for 18%

profile of v6, /device:TPU:30, one launch (start us, length us, event | category | flops | bytes accessed | tf_op | source)
XLA Modules:
  0.0 73.0 jit_solution(12036121687447121487)
XLA Ops:
  0.0 0.7 slice.10
  0.7 1.9 %collective-permute-start = (bf16[16,128]{1,0:T(8,128)(2,1)S(1)}, bf16[16,128]{1,0:T(8,128)(2,1)S(1)}, u32[]{:S(2)}, u32[]{:S(2)}) collective-permute-start(bf16[16,128]{1,0:T(8,128)(2,1)S(1)} %slice.10), channel_id=1, source_target_pairs={{0,1},{1,2},{2,3},{3,4},{4,5},{5,6},{6,7},{7,8},{8,9},{9,10},{10,1... | collective-permute-start | bytes 12296 | tf_op jit(solution)/shard_map/ppermute | solution.py:18
  2.6 1.3 %reshape.12.gain_ref = f32[1,768]{1,0:T(1,128)} reshape(f32[768]{0:T(1024)} %param.9) | data formatting | bytes 6144 | tf_op jit(solution)/shard_map/reshape | solution.py:154
  3.9 1.7 %collective-permute-done.prev_ref = bf16[16,128]{1,0:T(8,128)(2,1)S(1)} collective-permute-done((bf16[16,128]{1,0:T(8,128)(2,1)S(1)}, bf16[16,128]{1,0:T(8,128)(2,1)S(1)}, u32[]{:S(2)}, u32[]{:S(2)}) %collective-permute-start) | collective-permute-done | bytes 4128 | tf_op jit(solution)/shard_map/ppermute | solution.py:18
  5.6 0.0 copy-start.2
  5.6 0.6 copy-done.2
  6.2 14.9 %shard_map.73 = (bf16[1024,768]{1,0:T(8,128)(2,1)}, bf16[1024,768]{1,0:T(8,128)(2,1)}, bf16[1024,768]{1,0:T(8,128)(2,1)}, bf16[1024,768]{1,0:T(8,128)(2,1)}, f32[2,6,64,128]{3,2,1,0:T(8,128)}) custom-call(bf16[8192,128]{1,0:T(8,128)(2,1)} %ticks_ref.1, bf16[16,128]{1,0:T(8,128)(2,1)} %copy-done.2, bf16[2048,768]{1,0:T(8,128)(2,1)} %conv_ref.1, ...), custom_call_target="tpu_custom_call" | custom-call | tf_op jit(solution)/shard_map/pallas_call | solution.py:138
  21.1 1.0 %bitcast_add_fusion = f32[6,64,128]{2,1,0:T(8,128)S(1)} fusion(f32[2,6,64,128]{3,2,1,0:T(8,128)} %get-tuple-element.23), kind=kLoop, calls=%fused_computation.2 | loop fusion | flops 49152 | bytes 589824 | tf_op jit(solution)/shard_map/add | solution.py:171
  22.1 1.9 %collective-permute-start.1 = (f32[6,64,128]{2,1,0:T(8,128)S(1)}, f32[6,64,128]{2,1,0:T(8,128)S(1)}, u32[]{:S(2)}, u32[]{:S(2)}) collective-permute-start(f32[6,64,128]{2,1,0:T(8,128)S(1)} %bitcast_add_fusion), channel_id=1, source_target_pairs={{0,1},{1,2},{2,3},{3,4},{4,5},{5,6},{6,7},{7,8},{8,9},{9,10},{10,1... | collective-permute-start | bytes 589832 | tf_op jit(solution)/shard_map/ppermute | solution.py:18
  24.1 1.8 %broadcast_in_dim.3.earlier_ref = f32[1024,768]{1,0:T(8,128)} broadcast(f32[]{:T(128)} %constant.0.clone.1), dimensions={} | broadcast | bytes 3145732 | tf_op jit(solution)/shard_map/broadcast_in_dim | solution.py:173
  25.9 6.6 %shard_map.74.earlier_ref = f32[1024,768]{1,0:T(8,128)} custom-call(bf16[1024,768]{1,0:T(8,128)(2,1)} %get-tuple-element.32.q_ref, bf16[1024,768]{1,0:T(8,128)(2,1)} %get-tuple-element.33.k_ref, bf16[1024,768]{1,0:T(8,128)(2,1)} %get-tuple-element.34.v_ref, f32[1024,768]{1,0:T(8,128)} %broadcast_in_dim.3.earlier_ref), custom_call_target="tpu_custom_call", output_to_operand_aliasing={{}: (3, {})} | custom-call | flops 1610612736 | bytes 3932160 | tf_op jit(solution)/shard_map/pallas_call | solution.py:158
  32.5 0.0 collective-permute-done.1
  32.5 0.0 copy-start.1
  32.5 1.4 %collective-permute-start.2 = (f32[6,64,128]{2,1,0:T(8,128)S(1)}, f32[6,64,128]{2,1,0:T(8,128)S(1)}, u32[]{:S(2)}, u32[]{:S(2)}) collective-permute-start(f32[6,64,128]{2,1,0:T(8,128)S(1)} %add.22), channel_id=1, source_target_pairs={{0,2},{1,3},{2,4},{3,5},{4,6},{5,7},{6,8},{7,9},{8,10},{9,11},{10,... | collective-permute-start | bytes 589832 | tf_op jit(solution)/shard_map/ppermute | solution.py:18
  34.0 6.6 %shard_map.75.inside_ref = f32[1024,768]{1,0:T(8,128)} custom-call(bf16[1024,768]{1,0:T(8,128)(2,1)} %get-tuple-element.32.q_ref, bf16[1024,768]{1,0:T(8,128)(2,1)} %get-tuple-element.33.k_ref, bf16[1024,768]{1,0:T(8,128)(2,1)} %get-tuple-element.34.v_ref, f32[1024,768]{1,0:T(8,128)} %shard_map.74.earlier_ref), custom_call_target="tpu_custom_call", output_to_operand_aliasing={{}: (3, {})} | custom-call | flops 1610612736 | bytes 3932160 | tf_op jit(solution)/shard_map/pallas_call | solution.py:158
  40.5 0.0 copy-start.3
  40.5 0.0 copy-start
  40.6 1.2 %collective-permute-done.2 = f32[6,64,128]{2,1,0:T(8,128)S(1)} collective-permute-done((f32[6,64,128]{2,1,0:T(8,128)S(1)}, f32[6,64,128]{2,1,0:T(8,128)S(1)}, u32[]{:S(2)}, u32[]{:S(2)}) %collective-permute-start.2) | collective-permute-done | bytes 196640 | tf_op jit(solution)/shard_map/ppermute | solution.py:18
  41.8 1.3 %collective-permute-start.3 = (f32[6,64,128]{2,1,0:T(8,128)S(1)}, f32[6,64,128]{2,1,0:T(8,128)S(1)}, u32[]{:S(2)}, u32[]{:S(2)}) collective-permute-start(f32[6,64,128]{2,1,0:T(8,128)S(1)} %add.23), channel_id=1, source_target_pairs={{0,4},{1,5},{2,6},{3,7},{4,8},{5,9},{6,10},{7,11},{8,12},{9,13},{1... | collective-permute-start | bytes 589832 | tf_op jit(solution)/shard_map/ppermute | solution.py:18
  43.1 8.5 %collective-permute-done.3 = f32[6,64,128]{2,1,0:T(8,128)S(1)} collective-permute-done((f32[6,64,128]{2,1,0:T(8,128)S(1)}, f32[6,64,128]{2,1,0:T(8,128)S(1)}, u32[]{:S(2)}, u32[]{:S(2)}) %collective-permute-start.3) | collective-permute-done | bytes 196640 | tf_op jit(solution)/shard_map/ppermute | solution.py:18
  51.6 1.3 %collective-permute-start.4 = (f32[6,64,128]{2,1,0:T(8,128)S(1)}, f32[6,64,128]{2,1,0:T(8,128)S(1)}, u32[]{:S(2)}, u32[]{:S(2)}) collective-permute-start(f32[6,64,128]{2,1,0:T(8,128)S(1)} %add.24), channel_id=1, source_target_pairs={{0,8},{1,9},{2,10},{3,11},{4,12},{5,13},{6,14},{7,15},{16,24},{17,... | collective-permute-start | bytes 589832 | tf_op jit(solution)/shard_map/ppermute | solution.py:18
  52.9 0.0 copy-done.1
  53.0 0.3 copy.12
  53.3 0.2 reshape.14
  53.5 0.0 copy-done.3
  53.5 0.6 reshape.15.hgain_ref
  54.1 11.2 %collective-permute-done.4 = f32[6,64,128]{2,1,0:T(8,128)S(1)} collective-permute-done((f32[6,64,128]{2,1,0:T(8,128)S(1)}, f32[6,64,128]{2,1,0:T(8,128)S(1)}, u32[]{:S(2)}, u32[]{:S(2)}) %collective-permute-start.4) | collective-permute-done | bytes 196640 | tf_op jit(solution)/shard_map/ppermute | solution.py:18
  65.3 0.0 copy-done
  65.3 0.1 fusion
  65.4 0.8 %pad_maximum_fusion.state_ref = f32[2,6,64,128]{3,2,1,0:T(8,128)} fusion(f32[1,6,64,128]{3,2,1,0:T(8,128)S(1)} %get-tuple-element.39, f32[1,6,64,128]{3,2,1,0:T(8,128)S(1)} %bitcast.19), kind=kLoop, calls=%fused_computation | loop fusion | flops 98304 | bytes 786432 | tf_op jit(solution)/shard_map/stack | solution.py:194
  66.2 6.9 %shard_map.76 = bf16[1024,768]{1,0:T(8,128)(2,1)} custom-call(bf16[1024,768]{1,0:T(8,128)(2,1)} %get-tuple-element.32.q_ref, f32[2,6,64,128]{3,2,1,0:T(8,128)} %pad_maximum_fusion.state_ref, f32[1024,768]{1,0:T(8,128)} %shard_map.75.inside_ref, bf16[1024,768]{1,0:T(8,128)(2,1)} %get-tuple-element.38.emb_ref, f32[1,768]{1,0:T(1,128)} %reshape.15.hgain_ref, ...), custom_call_target="tpu_custom_call" | custom-call | tf_op jit(solution)/shard_map/pallas_call | solution.py:196
  (3 shorter events, 0.1 us)
Async XLA Ops:
  0.7 4.9 %collective-permute-start = (bf16[16,128]{1,0:T(8,128)(2,1)S(1)}, bf16[16,128]{1,0:T(8,128)(2,1)S(1)}, u32[]{:S(2)}, u32[]{:S(2)}) collective-permute-start(bf16[16,128]{1,0:T(8,128)(2,1)S(1)} %slice.10), channel_id=1, source_target_pairs={{0,1},{1,2},{2,3},{3,4},{4,5},{5,6},{6,7},{7,8},{8,9},{9,10},{10,1... | collective-permute-start | bytes 12296 | tf_op jit(solution)/shard_map/ppermute | solution.py:18
  5.6 0.6 copy-start.2
  22.1 10.3 %collective-permute-start.1 = (f32[6,64,128]{2,1,0:T(8,128)S(1)}, f32[6,64,128]{2,1,0:T(8,128)S(1)}, u32[]{:S(2)}, u32[]{:S(2)}) collective-permute-start(f32[6,64,128]{2,1,0:T(8,128)S(1)} %bitcast_add_fusion), channel_id=1, source_target_pairs={{0,1},{1,2},{2,3},{3,4},{4,5},{5,6},{6,7},{7,8},{8,9},{9,10},{10,1... | collective-permute-start | bytes 589832 | tf_op jit(solution)/shard_map/ppermute | solution.py:18
  32.5 20.4 %copy-start.1 = (f32[12,64,64]{2,1,0:T(8,128)S(1)}, f32[12,64,64]{2,1,0:T(8,128)}, u32[]{:S(2)}) copy-start(f32[12,64,64]{2,1,0:T(8,128)} %param.13) | copy-start | bytes 589828
  32.5 9.2 %collective-permute-start.2 = (f32[6,64,128]{2,1,0:T(8,128)S(1)}, f32[6,64,128]{2,1,0:T(8,128)S(1)}, u32[]{:S(2)}, u32[]{:S(2)}) collective-permute-start(f32[6,64,128]{2,1,0:T(8,128)S(1)} %add.22), channel_id=1, source_target_pairs={{0,2},{1,3},{2,4},{3,5},{4,6},{5,7},{6,8},{7,9},{8,10},{9,11},{10,... | collective-permute-start | bytes 589832 | tf_op jit(solution)/shard_map/ppermute | solution.py:18
  40.5 13.0 %copy-start.3 = (f32[768]{0:T(1024)S(1)}, f32[768]{0:T(1024)}, u32[]{:S(2)}) copy-start(f32[768]{0:T(1024)} %param.11) | copy-start | bytes 9220
  40.5 24.7 %copy-start = (f32[2,6,64,128]{3,2,1,0:T(8,128)S(1)}, f32[2,6,64,128]{3,2,1,0:T(8,128)}, u32[]{:S(2)}) copy-start(f32[2,6,64,128]{3,2,1,0:T(8,128)} %get-tuple-element.23) | copy-start | bytes 1179652
  41.8 9.8 %collective-permute-start.3 = (f32[6,64,128]{2,1,0:T(8,128)S(1)}, f32[6,64,128]{2,1,0:T(8,128)S(1)}, u32[]{:S(2)}, u32[]{:S(2)}) collective-permute-start(f32[6,64,128]{2,1,0:T(8,128)S(1)} %add.23), channel_id=1, source_target_pairs={{0,4},{1,5},{2,6},{3,7},{4,8},{5,9},{6,10},{7,11},{8,12},{9,13},{1... | collective-permute-start | bytes 589832 | tf_op jit(solution)/shard_map/ppermute | solution.py:18
  51.6 13.7 %collective-permute-start.4 = (f32[6,64,128]{2,1,0:T(8,128)S(1)}, f32[6,64,128]{2,1,0:T(8,128)S(1)}, u32[]{:S(2)}, u32[]{:S(2)}) collective-permute-start(f32[6,64,128]{2,1,0:T(8,128)S(1)} %add.24), channel_id=1, source_target_pairs={{0,8},{1,9},{2,10},{3,11},{4,12},{5,13},{6,14},{7,15},{16,24},{17,... | collective-permute-start | bytes 589832 | tf_op jit(solution)/shard_map/ppermute | solution.py:18

commit v7 on v6

--- a/solution.py
+++ b/solution.py
@@ -72,6 +72,10 @@
 
 def inside_kernel(q_ref, k_ref, v_ref, earlier_ref, inside_ref):
     del earlier_ref
+    first_inside_kernel(q_ref, k_ref, v_ref, inside_ref)
+
+
+def first_inside_kernel(q_ref, k_ref, v_ref, inside_ref):
     queries, keys, values = q_ref[...], k_ref[...], v_ref[...]
     tokens = queries.shape[0]
     lane = lax.broadcasted_iota(jnp.int32, (1, PAIR), 1)
@@ -154,23 +158,31 @@
     )(ticks, prev, conv_weight, norm_gain.reshape(1, model_width), qkv_weight)
 
     def inside_block(block, earlier, q, k, v):
-        spec = pl.BlockSpec((BLK, model_width), lambda i, block=block: (block, 0))
+        spec = pl.BlockSpec((BLK, PAIR), lambda p, block=block: (block, p))
+        in_specs, operands, aliases = [spec, spec, spec], [q, k, v], {}
+        kernel = inside_kernel
+        if earlier is not None:
+            in_specs.append(pl.BlockSpec(memory_space=pl.ANY))
+            operands.append(earlier)
+            aliases = {3: 0}
+        else:
+            kernel = first_inside_kernel
         return pl.pallas_call(
-            inside_kernel,
-            grid=(1,),
-            in_specs=[spec, spec, spec, pl.BlockSpec(memory_space=pl.ANY)],
+            kernel,
+            grid=(pairs,),
+            in_specs=in_specs,
             out_specs=spec,
             out_shape=jax.ShapeDtypeStruct((token_count, model_width), jnp.float32),
-            input_output_aliases={3: 0},
+            input_output_aliases=aliases,
             cost_estimate=pl.CostEstimate(flops=8 * BLK * BLK * model_width, transcendentals=0,
                                           bytes_accessed=6 * BLK * model_width + 4 * BLK * model_width),
-        )(q, k, v, earlier)
+        )(*operands)
 
     local = states[0]
     for block in range(1, blocks):
         local = local + states[block]
     count = lax.axis_size("inner")
-    inside = jnp.zeros((token_count, model_width), jnp.float32)
+    inside = None
     total, steps, block = local, 1, 0
     while steps < count:
         if block < blocks:

time: 73.5 us -> 76.4 us (1.039); the launches traced: 73 us -> 74.9 us
  Pallas kernels: 34.9 us -> 38.6 us
  local copies, waits for them, and re-layouts: 5.54 us -> 3.7 us
    pallas_call x2, Pallas kernels: 13.2 us -> 16.8 us  [inside_block(): pl.pallas_call(kernel, grid=(pairs,), in_specs=in_specs, out_specs=spec,...]
    broadcast_in_dim x1 -> x0, local copies, waits for them, and re-layouts: 1.84 us -> none  [shards(): inside = jnp.zeros((token_count, model_width), jnp.float32)]
  transfers between devices with their start and end apart: 5 -> 5, of which waited for: 4 -> 3; matrix products, arithmetic and copies ran while one was open for 6% -> 3% of each run, Pallas kernels for 18% -> 22%
where the time goes in v7:
time: 76.4 us; the launch traced here: 74.9 us
  Pallas kernels  38.6 us (51%)
  waiting for transfers between devices  22.5 us (29%)
  starting transfers between devices  7.97 us (10%)
  local copies, waits for them, and re-layouts  3.7 us (5%)
  other arithmetic  1.98 us (3%)
    ppermute x5, waiting for transfers between devices, from_behind(): lax.ppermute(value, axis, [(source, source + steps) for source in range(i...  22.5 us
    pallas_call x2, Pallas kernels, inside_block(): pl.pallas_call(kernel, grid=(pairs,), in_specs=in_specs, out_specs=spec,...  16.8 us
    pallas_call x1, Pallas kernels, shards(): pl.pallas_call(embed_kernel, grid=(blocks,), in_specs=[pl.BlockSpec((bloc...  14.9 us
    ppermute x5, starting transfers between devices, from_behind(): lax.ppermute(value, axis, [(source, source + steps) for source in range(i...  7.97 us
    pallas_call x1, Pallas kernels, shards(): pl.pallas_call(out_kernel, grid=(blocks,), in_specs=[rows_spec, state_spe...  6.88 us
  transfers between devices with their start and end apart: 5, of which 3 were waited for; matrix products, arithmetic and copies ran while one was open for 3% of the time, Pallas kernels for 22%

profile of v7, /device:TPU:30, one launch (start us, length us, event | category | flops | bytes accessed | tf_op | source)
XLA Modules:
  0.0 74.9 jit_solution(12091535444899036530)
XLA Ops:
  0.0 0.7 slice.10
  0.7 1.9 %collective-permute-start = (bf16[16,128]{1,0:T(8,128)(2,1)S(1)}, bf16[16,128]{1,0:T(8,128)(2,1)S(1)}, u32[]{:S(2)}, u32[]{:S(2)}) collective-permute-start(bf16[16,128]{1,0:T(8,128)(2,1)S(1)} %slice.10), channel_id=1, source_target_pairs={{0,1},{1,2},{2,3},{3,4},{4,5},{5,6},{6,7},{7,8},{8,9},{9,10},{10,1... | collective-permute-start | bytes 12296 | tf_op jit(solution)/shard_map/ppermute | solution.py:18
  2.6 1.3 %reshape.12.gain_ref = f32[1,768]{1,0:T(1,128)} reshape(f32[768]{0:T(1024)} %param.9) | data formatting | bytes 6144 | tf_op jit(solution)/shard_map/reshape | solution.py:158
  3.9 1.7 %collective-permute-done.prev_ref = bf16[16,128]{1,0:T(8,128)(2,1)S(1)} collective-permute-done((bf16[16,128]{1,0:T(8,128)(2,1)S(1)}, bf16[16,128]{1,0:T(8,128)(2,1)S(1)}, u32[]{:S(2)}, u32[]{:S(2)}) %collective-permute-start) | collective-permute-done | bytes 4128 | tf_op jit(solution)/shard_map/ppermute | solution.py:18
  5.6 0.0 copy-start.2
  5.6 0.6 copy-done.2
  6.2 14.9 %shard_map.73 = (bf16[1024,768]{1,0:T(8,128)(2,1)}, bf16[1024,768]{1,0:T(8,128)(2,1)}, bf16[1024,768]{1,0:T(8,128)(2,1)}, bf16[1024,768]{1,0:T(8,128)(2,1)}, f32[2,6,64,128]{3,2,1,0:T(8,128)}) custom-call(bf16[8192,128]{1,0:T(8,128)(2,1)} %ticks_ref.1, bf16[16,128]{1,0:T(8,128)(2,1)} %copy-done.2, bf16[2048,768]{1,0:T(8,128)(2,1)} %conv_ref.1, ...), custom_call_target="tpu_custom_call" | custom-call | tf_op jit(solution)/shard_map/pallas_call | solution.py:142
  21.1 1.0 %bitcast_add_fusion = f32[6,64,128]{2,1,0:T(8,128)S(1)} fusion(f32[2,6,64,128]{3,2,1,0:T(8,128)} %get-tuple-element.23), kind=kLoop, calls=%fused_computation.2 | loop fusion | flops 49152 | bytes 589824 | tf_op jit(solution)/shard_map/add | solution.py:183
  22.1 1.9 %collective-permute-start.1 = (f32[6,64,128]{2,1,0:T(8,128)S(1)}, f32[6,64,128]{2,1,0:T(8,128)S(1)}, u32[]{:S(2)}, u32[]{:S(2)}) collective-permute-start(f32[6,64,128]{2,1,0:T(8,128)S(1)} %bitcast_add_fusion), channel_id=1, source_target_pairs={{0,1},{1,2},{2,3},{3,4},{4,5},{5,6},{6,7},{7,8},{8,9},{9,10},{10,1... | collective-permute-start | bytes 589832 | tf_op jit(solution)/shard_map/ppermute | solution.py:18
  24.1 8.4 %shard_map.74.earlier_ref = f32[1024,768]{1,0:T(8,128)} custom-call(bf16[1024,768]{1,0:T(8,128)(2,1)} %get-tuple-element.32.q_ref, bf16[1024,768]{1,0:T(8,128)(2,1)} %get-tuple-element.33.k_ref, bf16[1024,768]{1,0:T(8,128)(2,1)} %get-tuple-element.34.v_ref), custom_call_target="tpu_custom_call" | custom-call | flops 1610612736 | bytes 3932160 | tf_op jit(solution)/shard_map/pallas_call | solution.py:170
  32.5 0.0 collective-permute-done.1
  32.5 0.0 copy-start.1
  32.5 1.4 %collective-permute-start.2 = (f32[6,64,128]{2,1,0:T(8,128)S(1)}, f32[6,64,128]{2,1,0:T(8,128)S(1)}, u32[]{:S(2)}, u32[]{:S(2)}) collective-permute-start(f32[6,64,128]{2,1,0:T(8,128)S(1)} %add.22), channel_id=1, source_target_pairs={{0,2},{1,3},{2,4},{3,5},{4,6},{5,7},{6,8},{7,9},{8,10},{9,11},{10,... | collective-permute-start | bytes 589832 | tf_op jit(solution)/shard_map/ppermute | solution.py:18
  34.0 8.4 %shard_map.75.inside_ref = f32[1024,768]{1,0:T(8,128)} custom-call(bf16[1024,768]{1,0:T(8,128)(2,1)} %get-tuple-element.32.q_ref, bf16[1024,768]{1,0:T(8,128)(2,1)} %get-tuple-element.33.k_ref, bf16[1024,768]{1,0:T(8,128)(2,1)} %get-tuple-element.34.v_ref, f32[1024,768]{1,0:T(8,128)} %shard_map.74.earlier_ref), custom_call_target="tpu_custom_call", output_to_operand_aliasing={{}: (3, {})} | custom-call | flops 1610612736 | bytes 3932160 | tf_op jit(solution)/shard_map/pallas_call | solution.py:170
  42.4 0.0 copy-start.3
  42.4 0.0 copy-start
  42.4 0.0 collective-permute-done.2
  42.4 1.4 %collective-permute-start.3 = (f32[6,64,128]{2,1,0:T(8,128)S(1)}, f32[6,64,128]{2,1,0:T(8,128)S(1)}, u32[]{:S(2)}, u32[]{:S(2)}) collective-permute-start(f32[6,64,128]{2,1,0:T(8,128)S(1)} %add.23), channel_id=1, source_target_pairs={{0,4},{1,5},{2,6},{3,7},{4,8},{5,9},{6,10},{7,11},{8,12},{9,13},{1... | collective-permute-start | bytes 589832 | tf_op jit(solution)/shard_map/ppermute | solution.py:18
  43.9 9.6 %collective-permute-done.3 = f32[6,64,128]{2,1,0:T(8,128)S(1)} collective-permute-done((f32[6,64,128]{2,1,0:T(8,128)S(1)}, f32[6,64,128]{2,1,0:T(8,128)S(1)}, u32[]{:S(2)}, u32[]{:S(2)}) %collective-permute-start.3) | collective-permute-done | bytes 196640 | tf_op jit(solution)/shard_map/ppermute | solution.py:18
  53.5 1.3 %collective-permute-start.4 = (f32[6,64,128]{2,1,0:T(8,128)S(1)}, f32[6,64,128]{2,1,0:T(8,128)S(1)}, u32[]{:S(2)}, u32[]{:S(2)}) collective-permute-start(f32[6,64,128]{2,1,0:T(8,128)S(1)} %add.24), channel_id=1, source_target_pairs={{0,8},{1,9},{2,10},{3,11},{4,12},{5,13},{6,14},{7,15},{16,24},{17,... | collective-permute-start | bytes 589832 | tf_op jit(solution)/shard_map/ppermute | solution.py:18
  54.8 0.0 copy-done.1
  54.8 0.3 copy.11
  55.1 0.2 reshape.14
  55.3 0.0 copy-done.3
  55.3 0.6 reshape.15.hgain_ref
  55.9 11.2 %collective-permute-done.4 = f32[6,64,128]{2,1,0:T(8,128)S(1)} collective-permute-done((f32[6,64,128]{2,1,0:T(8,128)S(1)}, f32[6,64,128]{2,1,0:T(8,128)S(1)}, u32[]{:S(2)}, u32[]{:S(2)}) %collective-permute-start.4) | collective-permute-done | bytes 196640 | tf_op jit(solution)/shard_map/ppermute | solution.py:18
  67.1 0.0 copy-done
  67.1 0.1 fusion
  67.2 0.8 %pad_maximum_fusion.state_ref = f32[2,6,64,128]{3,2,1,0:T(8,128)} fusion(f32[1,6,64,128]{3,2,1,0:T(8,128)S(1)} %get-tuple-element.39, f32[1,6,64,128]{3,2,1,0:T(8,128)S(1)} %bitcast.19), kind=kLoop, calls=%fused_computation | loop fusion | flops 98304 | bytes 786432 | tf_op jit(solution)/shard_map/stack | solution.py:206
  68.0 6.9 %shard_map.76 = bf16[1024,768]{1,0:T(8,128)(2,1)} custom-call(bf16[1024,768]{1,0:T(8,128)(2,1)} %get-tuple-element.32.q_ref, f32[2,6,64,128]{3,2,1,0:T(8,128)} %pad_maximum_fusion.state_ref, f32[1024,768]{1,0:T(8,128)} %shard_map.75.inside_ref, bf16[1024,768]{1,0:T(8,128)(2,1)} %get-tuple-element.38.emb_ref, f32[1,768]{1,0:T(1,128)} %reshape.15.hgain_ref, ...), custom_call_target="tpu_custom_call" | custom-call | tf_op jit(solution)/shard_map/pallas_call | solution.py:208
  (3 shorter events, 0.1 us)
Async XLA Ops:
  0.7 4.9 %collective-permute-start = (bf16[16,128]{1,0:T(8,128)(2,1)S(1)}, bf16[16,128]{1,0:T(8,128)(2,1)S(1)}, u32[]{:S(2)}, u32[]{:S(2)}) collective-permute-start(bf16[16,128]{1,0:T(8,128)(2,1)S(1)} %slice.10), channel_id=1, source_target_pairs={{0,1},{1,2},{2,3},{3,4},{4,5},{5,6},{6,7},{7,8},{8,9},{9,10},{10,1... | collective-permute-start | bytes 12296 | tf_op jit(solution)/shard_map/ppermute | solution.py:18
  5.6 0.6 copy-start.2
  22.1 10.3 %collective-permute-start.1 = (f32[6,64,128]{2,1,0:T(8,128)S(1)}, f32[6,64,128]{2,1,0:T(8,128)S(1)}, u32[]{:S(2)}, u32[]{:S(2)}) collective-permute-start(f32[6,64,128]{2,1,0:T(8,128)S(1)} %bitcast_add_fusion), channel_id=1, source_target_pairs={{0,1},{1,2},{2,3},{3,4},{4,5},{5,6},{6,7},{7,8},{8,9},{9,10},{10,1... | collective-permute-start | bytes 589832 | tf_op jit(solution)/shard_map/ppermute | solution.py:18
  32.5 22.3 %copy-start.1 = (f32[12,64,64]{2,1,0:T(8,128)S(1)}, f32[12,64,64]{2,1,0:T(8,128)}, u32[]{:S(2)}) copy-start(f32[12,64,64]{2,1,0:T(8,128)} %param.13) | copy-start | bytes 589828
  32.5 9.9 %collective-permute-start.2 = (f32[6,64,128]{2,1,0:T(8,128)S(1)}, f32[6,64,128]{2,1,0:T(8,128)S(1)}, u32[]{:S(2)}, u32[]{:S(2)}) collective-permute-start(f32[6,64,128]{2,1,0:T(8,128)S(1)} %add.22), channel_id=1, source_target_pairs={{0,2},{1,3},{2,4},{3,5},{4,6},{5,7},{6,8},{7,9},{8,10},{9,11},{10,... | collective-permute-start | bytes 589832 | tf_op jit(solution)/shard_map/ppermute | solution.py:18
  42.4 13.0 %copy-start.3 = (f32[768]{0:T(1024)S(1)}, f32[768]{0:T(1024)}, u32[]{:S(2)}) copy-start(f32[768]{0:T(1024)} %param.11) | copy-start | bytes 9220
  42.4 24.8 %copy-start = (f32[2,6,64,128]{3,2,1,0:T(8,128)S(1)}, f32[2,6,64,128]{3,2,1,0:T(8,128)}, u32[]{:S(2)}) copy-start(f32[2,6,64,128]{3,2,1,0:T(8,128)} %get-tuple-element.23) | copy-start | bytes 1179652
  42.4 11.0 %collective-permute-start.3 = (f32[6,64,128]{2,1,0:T(8,128)S(1)}, f32[6,64,128]{2,1,0:T(8,128)S(1)}, u32[]{:S(2)}, u32[]{:S(2)}) collective-permute-start(f32[6,64,128]{2,1,0:T(8,128)S(1)} %add.23), channel_id=1, source_target_pairs={{0,4},{1,5},{2,6},{3,7},{4,8},{5,9},{6,10},{7,11},{8,12},{9,13},{1... | collective-permute-start | bytes 589832 | tf_op jit(solution)/shard_map/ppermute | solution.py:18
  53.5 13.7 %collective-permute-start.4 = (f32[6,64,128]{2,1,0:T(8,128)S(1)}, f32[6,64,128]{2,1,0:T(8,128)S(1)}, u32[]{:S(2)}, u32[]{:S(2)}) collective-permute-start(f32[6,64,128]{2,1,0:T(8,128)S(1)} %add.24), channel_id=1, source_target_pairs={{0,8},{1,9},{2,10},{3,11},{4,12},{5,13},{6,14},{7,15},{16,24},{17,... | collective-permute-start | bytes 589832 | tf_op jit(solution)/shard_map/ppermute | solution.py:18

commit v8 on v7

--- a/solution.py
+++ b/solution.py
@@ -158,7 +158,7 @@
     )(ticks, prev, conv_weight, norm_gain.reshape(1, model_width), qkv_weight)
 
     def inside_block(block, earlier, q, k, v):
-        spec = pl.BlockSpec((BLK, PAIR), lambda p, block=block: (block, p))
+        spec = pl.BlockSpec((BLK, 3 * PAIR), lambda p, block=block: (block, p))
         in_specs, operands, aliases = [spec, spec, spec], [q, k, v], {}
         kernel = inside_kernel
         if earlier is not None:
@@ -169,7 +169,7 @@
             kernel = first_inside_kernel
         return pl.pallas_call(
             kernel,
-            grid=(pairs,),
+            grid=(pairs // 3,),
             in_specs=in_specs,
             out_specs=spec,
             out_shape=jax.ShapeDtypeStruct((token_count, model_width), jnp.float32),

time: 76.4 us -> 71.6 us (0.937); the launches traced: 74.9 us -> 71.1 us
  Pallas kernels: 38.6 us -> 34.9 us
    pallas_call x2, Pallas kernels: 16.8 us -> 13.1 us  [inside_block(): pl.pallas_call(kernel, grid=(pairs // 3,), in_specs=in_specs, out_specs=s...]
  transfers between devices with their start and end apart: 5 -> 5, of which waited for: 3 -> 4; matrix products, arithmetic and copies ran while one was open for 3% -> 3% of each run, Pallas kernels for 22% -> 18%
where the time goes in v8:
time: 71.6 us; the launch traced here: 71.1 us
  Pallas kernels  34.9 us (49%)
  waiting for transfers between devices  22.7 us (32%)
  starting transfers between devices  7.84 us (11%)
  local copies, waits for them, and re-layouts  3.7 us (5%)
  other arithmetic  1.98 us (3%)
    ppermute x5, waiting for transfers between devices, from_behind(): lax.ppermute(value, axis, [(source, source + steps) for source in range(i...  22.7 us
    pallas_call x1, Pallas kernels, shards(): pl.pallas_call(embed_kernel, grid=(blocks,), in_specs=[pl.BlockSpec((bloc...  14.9 us
    pallas_call x2, Pallas kernels, inside_block(): pl.pallas_call(kernel, grid=(pairs // 3,), in_specs=in_specs, out_specs=s...  13.1 us
    ppermute x5, starting transfers between devices, from_behind(): lax.ppermute(value, axis, [(source, source + steps) for source in range(i...  7.84 us
    pallas_call x1, Pallas kernels, shards(): pl.pallas_call(out_kernel, grid=(blocks,), in_specs=[rows_spec, state_spe...  6.88 us
  transfers between devices with their start and end apart: 5, of which 4 were waited for; matrix products, arithmetic and copies ran while one was open for 3% of the time, Pallas kernels for 18%

profile of v8, /device:TPU:30, one launch (start us, length us, event | category | flops | bytes accessed | tf_op | source)
XLA Modules:
  0.0 71.1 jit_solution(13888360257553529650)
XLA Ops:
  0.0 0.7 slice.10
  0.7 1.9 %collective-permute-start = (bf16[16,128]{1,0:T(8,128)(2,1)S(1)}, bf16[16,128]{1,0:T(8,128)(2,1)S(1)}, u32[]{:S(2)}, u32[]{:S(2)}) collective-permute-start(bf16[16,128]{1,0:T(8,128)(2,1)S(1)} %slice.10), channel_id=1, source_target_pairs={{0,1},{1,2},{2,3},{3,4},{4,5},{5,6},{6,7},{7,8},{8,9},{9,10},{10,1... | collective-permute-start | bytes 12296 | tf_op jit(solution)/shard_map/ppermute | solution.py:18
  2.6 1.3 %reshape.12.gain_ref = f32[1,768]{1,0:T(1,128)} reshape(f32[768]{0:T(1024)} %param.9) | data formatting | bytes 6144 | tf_op jit(solution)/shard_map/reshape | solution.py:158
  3.9 1.7 %collective-permute-done.prev_ref = bf16[16,128]{1,0:T(8,128)(2,1)S(1)} collective-permute-done((bf16[16,128]{1,0:T(8,128)(2,1)S(1)}, bf16[16,128]{1,0:T(8,128)(2,1)S(1)}, u32[]{:S(2)}, u32[]{:S(2)}) %collective-permute-start) | collective-permute-done | bytes 4128 | tf_op jit(solution)/shard_map/ppermute | solution.py:18
  5.6 0.0 copy-start.2
  5.6 0.6 copy-done.2
  6.2 14.9 %shard_map.73 = (bf16[1024,768]{1,0:T(8,128)(2,1)}, bf16[1024,768]{1,0:T(8,128)(2,1)}, bf16[1024,768]{1,0:T(8,128)(2,1)}, bf16[1024,768]{1,0:T(8,128)(2,1)}, f32[2,6,64,128]{3,2,1,0:T(8,128)}) custom-call(bf16[8192,128]{1,0:T(8,128)(2,1)} %ticks_ref.1, bf16[16,128]{1,0:T(8,128)(2,1)} %copy-done.2, bf16[2048,768]{1,0:T(8,128)(2,1)} %conv_ref.1, ...), custom_call_target="tpu_custom_call" | custom-call | tf_op jit(solution)/shard_map/pallas_call | solution.py:142
  21.1 1.0 %bitcast_add_fusion = f32[6,64,128]{2,1,0:T(8,128)S(1)} fusion(f32[2,6,64,128]{3,2,1,0:T(8,128)} %get-tuple-element.23), kind=kLoop, calls=%fused_computation.2 | loop fusion | flops 49152 | bytes 589824 | tf_op jit(solution)/shard_map/add | solution.py:183
  22.1 1.9 %collective-permute-start.1 = (f32[6,64,128]{2,1,0:T(8,128)S(1)}, f32[6,64,128]{2,1,0:T(8,128)S(1)}, u32[]{:S(2)}, u32[]{:S(2)}) collective-permute-start(f32[6,64,128]{2,1,0:T(8,128)S(1)} %bitcast_add_fusion), channel_id=1, source_target_pairs={{0,1},{1,2},{2,3},{3,4},{4,5},{5,6},{6,7},{7,8},{8,9},{9,10},{10,1... | collective-permute-start | bytes 589832 | tf_op jit(solution)/shard_map/ppermute | solution.py:18
  24.1 6.5 %shard_map.74.earlier_ref = f32[1024,768]{1,0:T(8,128)} custom-call(bf16[1024,768]{1,0:T(8,128)(2,1)} %get-tuple-element.32.q_ref, bf16[1024,768]{1,0:T(8,128)(2,1)} %get-tuple-element.33.k_ref, bf16[1024,768]{1,0:T(8,128)(2,1)} %get-tuple-element.34.v_ref), custom_call_target="tpu_custom_call" | custom-call | flops 1610612736 | bytes 3932160 | tf_op jit(solution)/shard_map/pallas_call | solution.py:170
  30.6 0.0 collective-permute-done.1
  30.6 0.0 copy-start.1
  30.6 1.4 %collective-permute-start.2 = (f32[6,64,128]{2,1,0:T(8,128)S(1)}, f32[6,64,128]{2,1,0:T(8,128)S(1)}, u32[]{:S(2)}, u32[]{:S(2)}) collective-permute-start(f32[6,64,128]{2,1,0:T(8,128)S(1)} %add.22), channel_id=1, source_target_pairs={{0,2},{1,3},{2,4},{3,5},{4,6},{5,7},{6,8},{7,9},{8,10},{9,11},{10,... | collective-permute-start | bytes 589832 | tf_op jit(solution)/shard_map/ppermute | solution.py:18
  32.1 6.6 %shard_map.75.inside_ref = f32[1024,768]{1,0:T(8,128)} custom-call(bf16[1024,768]{1,0:T(8,128)(2,1)} %get-tuple-element.32.q_ref, bf16[1024,768]{1,0:T(8,128)(2,1)} %get-tuple-element.33.k_ref, bf16[1024,768]{1,0:T(8,128)(2,1)} %get-tuple-element.34.v_ref, f32[1024,768]{1,0:T(8,128)} %shard_map.74.earlier_ref), custom_call_target="tpu_custom_call", output_to_operand_aliasing={{}: (3, {})} | custom-call | flops 1610612736 | bytes 3932160 | tf_op jit(solution)/shard_map/pallas_call | solution.py:170
  38.6 0.0 copy-start.3
  38.6 0.0 copy-start
  38.6 1.2 %collective-permute-done.2 = f32[6,64,128]{2,1,0:T(8,128)S(1)} collective-permute-done((f32[6,64,128]{2,1,0:T(8,128)S(1)}, f32[6,64,128]{2,1,0:T(8,128)S(1)}, u32[]{:S(2)}, u32[]{:S(2)}) %collective-permute-start.2) | collective-permute-done | bytes 196640 | tf_op jit(solution)/shard_map/ppermute | solution.py:18
  39.9 1.3 %collective-permute-start.3 = (f32[6,64,128]{2,1,0:T(8,128)S(1)}, f32[6,64,128]{2,1,0:T(8,128)S(1)}, u32[]{:S(2)}, u32[]{:S(2)}) collective-permute-start(f32[6,64,128]{2,1,0:T(8,128)S(1)} %add.23), channel_id=1, source_target_pairs={{0,4},{1,5},{2,6},{3,7},{4,8},{5,9},{6,10},{7,11},{8,12},{9,13},{1... | collective-permute-start | bytes 589832 | tf_op jit(solution)/shard_map/ppermute | solution.py:18
  41.2 8.5 %collective-permute-done.3 = f32[6,64,128]{2,1,0:T(8,128)S(1)} collective-permute-done((f32[6,64,128]{2,1,0:T(8,128)S(1)}, f32[6,64,128]{2,1,0:T(8,128)S(1)}, u32[]{:S(2)}, u32[]{:S(2)}) %collective-permute-start.3) | collective-permute-done | bytes 196640 | tf_op jit(solution)/shard_map/ppermute | solution.py:18
  49.7 1.3 %collective-permute-start.4 = (f32[6,64,128]{2,1,0:T(8,128)S(1)}, f32[6,64,128]{2,1,0:T(8,128)S(1)}, u32[]{:S(2)}, u32[]{:S(2)}) collective-permute-start(f32[6,64,128]{2,1,0:T(8,128)S(1)} %add.24), channel_id=1, source_target_pairs={{0,8},{1,9},{2,10},{3,11},{4,12},{5,13},{6,14},{7,15},{16,24},{17,... | collective-permute-start | bytes 589832 | tf_op jit(solution)/shard_map/ppermute | solution.py:18
  51.0 0.0 copy-done.1
  51.0 0.3 copy.11
  51.4 0.2 reshape.14
  51.6 0.0 copy-done.3
  51.6 0.6 reshape.15.hgain_ref
  52.2 11.2 %collective-permute-done.4 = f32[6,64,128]{2,1,0:T(8,128)S(1)} collective-permute-done((f32[6,64,128]{2,1,0:T(8,128)S(1)}, f32[6,64,128]{2,1,0:T(8,128)S(1)}, u32[]{:S(2)}, u32[]{:S(2)}) %collective-permute-start.4) | collective-permute-done | bytes 196640 | tf_op jit(solution)/shard_map/ppermute | solution.py:18
  63.4 0.0 copy-done
  63.4 0.1 fusion
  63.5 0.8 %pad_maximum_fusion.state_ref = f32[2,6,64,128]{3,2,1,0:T(8,128)} fusion(f32[1,6,64,128]{3,2,1,0:T(8,128)S(1)} %get-tuple-element.39, f32[1,6,64,128]{3,2,1,0:T(8,128)S(1)} %bitcast.19), kind=kLoop, calls=%fused_computation | loop fusion | flops 98304 | bytes 786432 | tf_op jit(solution)/shard_map/stack | solution.py:206
  64.3 6.9 %shard_map.76 = bf16[1024,768]{1,0:T(8,128)(2,1)} custom-call(bf16[1024,768]{1,0:T(8,128)(2,1)} %get-tuple-element.32.q_ref, f32[2,6,64,128]{3,2,1,0:T(8,128)} %pad_maximum_fusion.state_ref, f32[1024,768]{1,0:T(8,128)} %shard_map.75.inside_ref, bf16[1024,768]{1,0:T(8,128)(2,1)} %get-tuple-element.38.emb_ref, f32[1,768]{1,0:T(1,128)} %reshape.15.hgain_ref, ...), custom_call_target="tpu_custom_call" | custom-call | tf_op jit(solution)/shard_map/pallas_call | solution.py:208
  (3 shorter events, 0.1 us)
Async XLA Ops:
  0.7 4.9 %collective-permute-start = (bf16[16,128]{1,0:T(8,128)(2,1)S(1)}, bf16[16,128]{1,0:T(8,128)(2,1)S(1)}, u32[]{:S(2)}, u32[]{:S(2)}) collective-permute-start(bf16[16,128]{1,0:T(8,128)(2,1)S(1)} %slice.10), channel_id=1, source_target_pairs={{0,1},{1,2},{2,3},{3,4},{4,5},{5,6},{6,7},{7,8},{8,9},{9,10},{10,1... | collective-permute-start | bytes 12296 | tf_op jit(solution)/shard_map/ppermute | solution.py:18
  5.6 0.6 copy-start.2
  22.1 8.4 %collective-permute-start.1 = (f32[6,64,128]{2,1,0:T(8,128)S(1)}, f32[6,64,128]{2,1,0:T(8,128)S(1)}, u32[]{:S(2)}, u32[]{:S(2)}) collective-permute-start(f32[6,64,128]{2,1,0:T(8,128)S(1)} %bitcast_add_fusion), channel_id=1, source_target_pairs={{0,1},{1,2},{2,3},{3,4},{4,5},{5,6},{6,7},{7,8},{8,9},{9,10},{10,1... | collective-permute-start | bytes 589832 | tf_op jit(solution)/shard_map/ppermute | solution.py:18
  30.6 20.4 %copy-start.1 = (f32[12,64,64]{2,1,0:T(8,128)S(1)}, f32[12,64,64]{2,1,0:T(8,128)}, u32[]{:S(2)}) copy-start(f32[12,64,64]{2,1,0:T(8,128)} %param.13) | copy-start | bytes 589828
  30.6 9.2 %collective-permute-start.2 = (f32[6,64,128]{2,1,0:T(8,128)S(1)}, f32[6,64,128]{2,1,0:T(8,128)S(1)}, u32[]{:S(2)}, u32[]{:S(2)}) collective-permute-start(f32[6,64,128]{2,1,0:T(8,128)S(1)} %add.22), channel_id=1, source_target_pairs={{0,2},{1,3},{2,4},{3,5},{4,6},{5,7},{6,8},{7,9},{8,10},{9,11},{10,... | collective-permute-start | bytes 589832 | tf_op jit(solution)/shard_map/ppermute | solution.py:18
  38.6 13.0 %copy-start.3 = (f32[768]{0:T(1024)S(1)}, f32[768]{0:T(1024)}, u32[]{:S(2)}) copy-start(f32[768]{0:T(1024)} %param.11) | copy-start | bytes 9220
  38.6 24.8 %copy-start = (f32[2,6,64,128]{3,2,1,0:T(8,128)S(1)}, f32[2,6,64,128]{3,2,1,0:T(8,128)}, u32[]{:S(2)}) copy-start(f32[2,6,64,128]{3,2,1,0:T(8,128)} %get-tuple-element.23) | copy-start | bytes 1179652
  39.9 9.8 %collective-permute-start.3 = (f32[6,64,128]{2,1,0:T(8,128)S(1)}, f32[6,64,128]{2,1,0:T(8,128)S(1)}, u32[]{:S(2)}, u32[]{:S(2)}) collective-permute-start(f32[6,64,128]{2,1,0:T(8,128)S(1)} %add.23), channel_id=1, source_target_pairs={{0,4},{1,5},{2,6},{3,7},{4,8},{5,9},{6,10},{7,11},{8,12},{9,13},{1... | collective-permute-start | bytes 589832 | tf_op jit(solution)/shard_map/ppermute | solution.py:18
  49.7 13.7 %collective-permute-start.4 = (f32[6,64,128]{2,1,0:T(8,128)S(1)}, f32[6,64,128]{2,1,0:T(8,128)S(1)}, u32[]{:S(2)}, u32[]{:S(2)}) collective-permute-start(f32[6,64,128]{2,1,0:T(8,128)S(1)} %add.24), channel_id=1, source_target_pairs={{0,8},{1,9},{2,10},{3,11},{4,12},{5,13},{6,14},{7,15},{16,24},{17,... | collective-permute-start | bytes 589832 | tf_op jit(solution)/shard_map/ppermute | solution.py:18

commit v9 on v8

--- a/solution.py
+++ b/solution.py
@@ -157,8 +157,12 @@
         compiler_params=pltpu.CompilerParams(dimension_semantics=("arbitrary",)),
     )(ticks, prev, conv_weight, norm_gain.reshape(1, model_width), qkv_weight)
 
-    def inside_block(block, earlier, q, k, v):
-        spec = pl.BlockSpec((BLK, 3 * PAIR), lambda p, block=block: (block, p))
+    halves = 2
+    piece_width = model_width // halves
+
+    def inside_block(piece, earlier, q, k, v):
+        block, half = divmod(piece, halves)
+        spec = pl.BlockSpec((BLK, piece_width), lambda p, block=block, half=half: (block, half + p))
         in_specs, operands, aliases = [spec, spec, spec], [q, k, v], {}
         kernel = inside_kernel
         if earlier is not None:
@@ -169,13 +173,13 @@
             kernel = first_inside_kernel
         return pl.pallas_call(
             kernel,
-            grid=(pairs // 3,),
+            grid=(1,),
             in_specs=in_specs,
             out_specs=spec,
             out_shape=jax.ShapeDtypeStruct((token_count, model_width), jnp.float32),
             input_output_aliases=aliases,
-            cost_estimate=pl.CostEstimate(flops=8 * BLK * BLK * model_width, transcendentals=0,
-                                          bytes_accessed=6 * BLK * model_width + 4 * BLK * model_width),
+            cost_estimate=pl.CostEstimate(flops=8 * BLK * BLK * piece_width, transcendentals=0,
+                                          bytes_accessed=10 * BLK * piece_width),
         )(*operands)
 
     local = states[0]
@@ -185,16 +189,16 @@
     inside = None
     total, steps, block = local, 1, 0
     while steps < count:
-        if block < blocks:
+        if block < blocks * halves:
             total, q_in, k_in, v_in = lax.optimization_barrier((total, queries, keys, values))
         received = from_behind(total, "inner", steps)
-        if block < blocks:
+        if block < blocks * halves:
             inside = inside_block(block, inside, q_in, k_in, v_in)
             received, inside = lax.optimization_barrier((received, inside))
             block += 1
         total = total + received
         steps *= 2
-    while block < blocks:
+    while block < blocks * halves:
         inside = inside_block(block, inside, queries, keys, values)
         block += 1
     prefix = total - local

time: 71.6 us -> 67.8 us (0.947)
  waiting for transfers between devices: 22.7 us -> 14.4 us
  Pallas kernels: 34.9 us -> 39.2 us
    ppermute x5, waiting for transfers between devices: 22.7 us -> 14.4 us  [from_behind(): lax.ppermute(value, axis, [(source, source + steps) for source in range(i...]
    pallas_call x2 -> x4, Pallas kernels: 13.1 us -> 17.4 us  [inside_block(): pl.pallas_call(kernel, grid=(1,), in_specs=in_specs, out_specs=spec, out_...]
  transfers between devices with their start and end apart: 5 -> 5, of which waited for: 4 -> 5; matrix products, arithmetic and copies ran while one was open for 3% -> 4% of each run, Pallas kernels for 18% -> 26%
where the time goes in v9:
time: 67.8 us; the launch traced here: 67.4 us
  Pallas kernels  39.2 us (58%)
  waiting for transfers between devices  14.4 us (21%)
  starting transfers between devices  8.02 us (12%)
  local copies, waits for them, and re-layouts  3.69 us (5%)
  other arithmetic  1.97 us (3%)
    pallas_call x4, Pallas kernels, inside_block(): pl.pallas_call(kernel, grid=(1,), in_specs=in_specs, out_specs=spec, out_...  17.4 us
    pallas_call x1, Pallas kernels, shards(): pl.pallas_call(embed_kernel, grid=(blocks,), in_specs=[pl.BlockSpec((bloc...  14.9 us
    ppermute x5, waiting for transfers between devices, from_behind(): lax.ppermute(value, axis, [(source, source + steps) for source in range(i...  14.4 us
    ppermute x5, starting transfers between devices, from_behind(): lax.ppermute(value, axis, [(source, source + steps) for source in range(i...  8.02 us
    pallas_call x1, Pallas kernels, shards(): pl.pallas_call(out_kernel, grid=(blocks,), in_specs=[rows_spec, state_spe...  6.88 us
  transfers between devices with their start and end apart: 5, of which 5 were waited for; matrix products, arithmetic and copies ran while one was open for 4% of the time, Pallas kernels for 26%

profile of v9, /device:TPU:30, one launch (start us, length us, event | category | flops | bytes accessed | tf_op | source)
XLA Modules:
  0.0 67.4 jit_solution(10052306876994175747)
XLA Ops:
  0.0 0.7 %slice.10 = bf16[16,128]{1,0:T(8,128)(2,1)S(1)} slice(bf16[8192,128]{1,0:T(8,128)(2,1)} %ticks_ref.1), slice={[8176:8192], [0:128]} | slice | bytes 8192 | tf_op jit(solution)/shard_map/slice | solution.py:139
  0.7 1.9 %collective-permute-start = (bf16[16,128]{1,0:T(8,128)(2,1)S(1)}, bf16[16,128]{1,0:T(8,128)(2,1)S(1)}, u32[]{:S(2)}, u32[]{:S(2)}) collective-permute-start(bf16[16,128]{1,0:T(8,128)(2,1)S(1)} %slice.10), channel_id=1, source_target_pairs={{0,1},{1,2},{2,3},{3,4},{4,5},{5,6},{6,7},{7,8},{8,9},{9,10},{10,1... | collective-permute-start | bytes 12296 | tf_op jit(solution)/shard_map/ppermute | solution.py:18
  2.6 1.3 %reshape.12.gain_ref = f32[1,768]{1,0:T(1,128)} reshape(f32[768]{0:T(1024)} %param.9) | data formatting | bytes 6144 | tf_op jit(solution)/shard_map/reshape | solution.py:158
  3.9 1.7 %collective-permute-done.prev_ref = bf16[16,128]{1,0:T(8,128)(2,1)S(1)} collective-permute-done((bf16[16,128]{1,0:T(8,128)(2,1)S(1)}, bf16[16,128]{1,0:T(8,128)(2,1)S(1)}, u32[]{:S(2)}, u32[]{:S(2)}) %collective-permute-start) | collective-permute-done | bytes 4128 | tf_op jit(solution)/shard_map/ppermute | solution.py:18
  5.6 0.0 copy-start.2
  5.6 0.6 copy-done.2
  6.2 14.9 %shard_map.73 = (bf16[1024,768]{1,0:T(8,128)(2,1)}, bf16[1024,768]{1,0:T(8,128)(2,1)}, bf16[1024,768]{1,0:T(8,128)(2,1)}, bf16[1024,768]{1,0:T(8,128)(2,1)}, f32[2,6,64,128]{3,2,1,0:T(8,128)}) custom-call(bf16[8192,128]{1,0:T(8,128)(2,1)} %ticks_ref.1, bf16[16,128]{1,0:T(8,128)(2,1)} %copy-done.2, bf16[2048,768]{1,0:T(8,128)(2,1)} %conv_ref.1, ...), custom_call_target="tpu_custom_call" | custom-call | tf_op jit(solution)/shard_map/pallas_call | solution.py:142
  21.1 1.0 %bitcast_add_fusion = f32[6,64,128]{2,1,0:T(8,128)S(1)} fusion(f32[2,6,64,128]{3,2,1,0:T(8,128)} %get-tuple-element.35), kind=kLoop, calls=%fused_computation.2 | loop fusion | flops 49152 | bytes 589824 | tf_op jit(solution)/shard_map/add | solution.py:187
  22.1 1.9 %collective-permute-start.1 = (f32[6,64,128]{2,1,0:T(8,128)S(1)}, f32[6,64,128]{2,1,0:T(8,128)S(1)}, u32[]{:S(2)}, u32[]{:S(2)}) collective-permute-start(f32[6,64,128]{2,1,0:T(8,128)S(1)} %bitcast_add_fusion), channel_id=1, source_target_pairs={{0,1},{1,2},{2,3},{3,4},{4,5},{5,6},{6,7},{7,8},{8,9},{9,10},{10,1... | collective-permute-start | bytes 589832 | tf_op jit(solution)/shard_map/ppermute | solution.py:18
  24.1 4.4 %shard_map.74.earlier_ref = f32[1024,768]{1,0:T(8,128)} custom-call(bf16[1024,768]{1,0:T(8,128)(2,1)} %get-tuple-element.56.q_ref, bf16[1024,768]{1,0:T(8,128)(2,1)} %get-tuple-element.57.k_ref, bf16[1024,768]{1,0:T(8,128)(2,1)} %get-tuple-element.58.v_ref), custom_call_target="tpu_custom_call" | custom-call | flops 805306368 | bytes 1966080 | tf_op jit(solution)/shard_map/pallas_call | solution.py:174
  28.4 0.7 %collective-permute-done.1 = f32[6,64,128]{2,1,0:T(8,128)S(1)} collective-permute-done((f32[6,64,128]{2,1,0:T(8,128)S(1)}, f32[6,64,128]{2,1,0:T(8,128)S(1)}, u32[]{:S(2)}, u32[]{:S(2)}) %collective-permute-start.1) | collective-permute-done | bytes 196640 | tf_op jit(solution)/shard_map/ppermute | solution.py:18
  29.2 1.3 %collective-permute-start.2 = (f32[6,64,128]{2,1,0:T(8,128)S(1)}, f32[6,64,128]{2,1,0:T(8,128)S(1)}, u32[]{:S(2)}, u32[]{:S(2)}) collective-permute-start(f32[6,64,128]{2,1,0:T(8,128)S(1)} %add.22), channel_id=1, source_target_pairs={{0,2},{1,3},{2,4},{3,5},{4,6},{5,7},{6,8},{7,9},{8,10},{9,11},{10,... | collective-permute-start | bytes 589832 | tf_op jit(solution)/shard_map/ppermute | solution.py:18
  30.5 4.3 %shard_map.75.earlier_ref = f32[1024,768]{1,0:T(8,128)} custom-call(bf16[1024,768]{1,0:T(8,128)(2,1)} %get-tuple-element.56.q_ref, bf16[1024,768]{1,0:T(8,128)(2,1)} %get-tuple-element.57.k_ref, bf16[1024,768]{1,0:T(8,128)(2,1)} %get-tuple-element.58.v_ref, f32[1024,768]{1,0:T(8,128)} %shard_map.74.earlier_ref), custom_call_target="tpu_custom_call", output_to_operand_aliasing={{}: (3, {})} | custom-call | flops 805306368 | bytes 1966080 | tf_op jit(solution)/shard_map/pallas_call | solution.py:174
  34.8 2.8 %collective-permute-done.2 = f32[6,64,128]{2,1,0:T(8,128)S(1)} collective-permute-done((f32[6,64,128]{2,1,0:T(8,128)S(1)}, f32[6,64,128]{2,1,0:T(8,128)S(1)}, u32[]{:S(2)}, u32[]{:S(2)}) %collective-permute-start.2) | collective-permute-done | bytes 196640 | tf_op jit(solution)/shard_map/ppermute | solution.py:18
  37.6 0.0 copy-start.1
  37.6 0.0 copy-start.3
  37.6 1.4 %collective-permute-start.3 = (f32[6,64,128]{2,1,0:T(8,128)S(1)}, f32[6,64,128]{2,1,0:T(8,128)S(1)}, u32[]{:S(2)}, u32[]{:S(2)}) collective-permute-start(f32[6,64,128]{2,1,0:T(8,128)S(1)} %add.23), channel_id=1, source_target_pairs={{0,4},{1,5},{2,6},{3,7},{4,8},{5,9},{6,10},{7,11},{8,12},{9,13},{1... | collective-permute-start | bytes 589832 | tf_op jit(solution)/shard_map/ppermute | solution.py:18
  39.0 4.4 %shard_map.76.earlier_ref = f32[1024,768]{1,0:T(8,128)} custom-call(bf16[1024,768]{1,0:T(8,128)(2,1)} %get-tuple-element.56.q_ref, bf16[1024,768]{1,0:T(8,128)(2,1)} %get-tuple-element.57.k_ref, bf16[1024,768]{1,0:T(8,128)(2,1)} %get-tuple-element.58.v_ref, f32[1024,768]{1,0:T(8,128)} %shard_map.75.earlier_ref), custom_call_target="tpu_custom_call", output_to_operand_aliasing={{}: (3, {})} | custom-call | flops 805306368 | bytes 1966080 | tf_op jit(solution)/shard_map/pallas_call | solution.py:174
  43.4 3.2 %collective-permute-done.3 = f32[6,64,128]{2,1,0:T(8,128)S(1)} collective-permute-done((f32[6,64,128]{2,1,0:T(8,128)S(1)}, f32[6,64,128]{2,1,0:T(8,128)S(1)}, u32[]{:S(2)}, u32[]{:S(2)}) %collective-permute-start.3) | collective-permute-done | bytes 196640 | tf_op jit(solution)/shard_map/ppermute | solution.py:18
  46.6 1.5 %collective-permute-start.4 = (f32[6,64,128]{2,1,0:T(8,128)S(1)}, f32[6,64,128]{2,1,0:T(8,128)S(1)}, u32[]{:S(2)}, u32[]{:S(2)}) collective-permute-start(f32[6,64,128]{2,1,0:T(8,128)S(1)} %add.24), channel_id=1, source_target_pairs={{0,8},{1,9},{2,10},{3,11},{4,12},{5,13},{6,14},{7,15},{16,24},{17,... | collective-permute-start | bytes 589832 | tf_op jit(solution)/shard_map/ppermute | solution.py:18
  48.1 0.0 copy-done.1
  48.1 0.3 copy.13
  48.4 0.2 reshape.14
  48.6 0.0 copy-done.3
  48.6 0.6 reshape.15.hgain_ref
  49.2 0.0 copy-start
  49.2 4.4 %shard_map.77.inside_ref = f32[1024,768]{1,0:T(8,128)} custom-call(bf16[1024,768]{1,0:T(8,128)(2,1)} %get-tuple-element.56.q_ref, bf16[1024,768]{1,0:T(8,128)(2,1)} %get-tuple-element.57.k_ref, bf16[1024,768]{1,0:T(8,128)(2,1)} %get-tuple-element.58.v_ref, f32[1024,768]{1,0:T(8,128)} %shard_map.76.earlier_ref), custom_call_target="tpu_custom_call", output_to_operand_aliasing={{}: (3, {})} | custom-call | flops 805306368 | bytes 1966080 | tf_op jit(solution)/shard_map/pallas_call | solution.py:174
  53.6 6.1 %collective-permute-done.4 = f32[6,64,128]{2,1,0:T(8,128)S(1)} collective-permute-done((f32[6,64,128]{2,1,0:T(8,128)S(1)}, f32[6,64,128]{2,1,0:T(8,128)S(1)}, u32[]{:S(2)}, u32[]{:S(2)}) %collective-permute-start.4) | collective-permute-done | bytes 196640 | tf_op jit(solution)/shard_map/ppermute | solution.py:18
  59.7 0.0 copy-done
  59.7 0.1 fusion
  59.7 0.8 %pad_maximum_fusion.state_ref = f32[2,6,64,128]{3,2,1,0:T(8,128)} fusion(f32[1,6,64,128]{3,2,1,0:T(8,128)S(1)} %get-tuple-element.63, f32[1,6,64,128]{3,2,1,0:T(8,128)S(1)} %bitcast.19), kind=kLoop, calls=%fused_computation | loop fusion | flops 98304 | bytes 786432 | tf_op jit(solution)/shard_map/stack | solution.py:210
  60.5 6.9 %shard_map.78 = bf16[1024,768]{1,0:T(8,128)(2,1)} custom-call(bf16[1024,768]{1,0:T(8,128)(2,1)} %get-tuple-element.56.q_ref, f32[2,6,64,128]{3,2,1,0:T(8,128)} %pad_maximum_fusion.state_ref, f32[1024,768]{1,0:T(8,128)} %shard_map.77.inside_ref, bf16[1024,768]{1,0:T(8,128)(2,1)} %get-tuple-element.62.emb_ref, f32[1,768]{1,0:T(1,128)} %reshape.15.hgain_ref, ...), custom_call_target="tpu_custom_call" | custom-call | tf_op jit(solution)/shard_map/pallas_call | solution.py:212
  (3 shorter events, 0.1 us)
Async XLA Ops:
  0.7 4.9 %collective-permute-start = (bf16[16,128]{1,0:T(8,128)(2,1)S(1)}, bf16[16,128]{1,0:T(8,128)(2,1)S(1)}, u32[]{:S(2)}, u32[]{:S(2)}) collective-permute-start(bf16[16,128]{1,0:T(8,128)(2,1)S(1)} %slice.10), channel_id=1, source_target_pairs={{0,1},{1,2},{2,3},{3,4},{4,5},{5,6},{6,7},{7,8},{8,9},{9,10},{10,1... | collective-permute-start | bytes 12296 | tf_op jit(solution)/shard_map/ppermute | solution.py:18
  5.6 0.6 copy-start.2
  22.1 7.0 %collective-permute-start.1 = (f32[6,64,128]{2,1,0:T(8,128)S(1)}, f32[6,64,128]{2,1,0:T(8,128)S(1)}, u32[]{:S(2)}, u32[]{:S(2)}) collective-permute-start(f32[6,64,128]{2,1,0:T(8,128)S(1)} %bitcast_add_fusion), channel_id=1, source_target_pairs={{0,1},{1,2},{2,3},{3,4},{4,5},{5,6},{6,7},{7,8},{8,9},{9,10},{10,1... | collective-permute-start | bytes 589832 | tf_op jit(solution)/shard_map/ppermute | solution.py:18
  29.2 8.4 %collective-permute-start.2 = (f32[6,64,128]{2,1,0:T(8,128)S(1)}, f32[6,64,128]{2,1,0:T(8,128)S(1)}, u32[]{:S(2)}, u32[]{:S(2)}) collective-permute-start(f32[6,64,128]{2,1,0:T(8,128)S(1)} %add.22), channel_id=1, source_target_pairs={{0,2},{1,3},{2,4},{3,5},{4,6},{5,7},{6,8},{7,9},{8,10},{9,11},{10,... | collective-permute-start | bytes 589832 | tf_op jit(solution)/shard_map/ppermute | solution.py:18
  37.6 10.5 %copy-start.1 = (f32[12,64,64]{2,1,0:T(8,128)S(1)}, f32[12,64,64]{2,1,0:T(8,128)}, u32[]{:S(2)}) copy-start(f32[12,64,64]{2,1,0:T(8,128)} %param.13) | copy-start | bytes 589828
  37.6 11.0 %copy-start.3 = (f32[768]{0:T(1024)S(1)}, f32[768]{0:T(1024)}, u32[]{:S(2)}) copy-start(f32[768]{0:T(1024)} %param.11) | copy-start | bytes 9220
  37.6 8.9 %collective-permute-start.3 = (f32[6,64,128]{2,1,0:T(8,128)S(1)}, f32[6,64,128]{2,1,0:T(8,128)S(1)}, u32[]{:S(2)}, u32[]{:S(2)}) collective-permute-start(f32[6,64,128]{2,1,0:T(8,128)S(1)} %add.23), channel_id=1, source_target_pairs={{0,4},{1,5},{2,6},{3,7},{4,8},{5,9},{6,10},{7,11},{8,12},{9,13},{1... | collective-permute-start | bytes 589832 | tf_op jit(solution)/shard_map/ppermute | solution.py:18
  46.6 13.1 %collective-permute-start.4 = (f32[6,64,128]{2,1,0:T(8,128)S(1)}, f32[6,64,128]{2,1,0:T(8,128)S(1)}, u32[]{:S(2)}, u32[]{:S(2)}) collective-permute-start(f32[6,64,128]{2,1,0:T(8,128)S(1)} %add.24), channel_id=1, source_target_pairs={{0,8},{1,9},{2,10},{3,11},{4,12},{5,13},{6,14},{7,15},{16,24},{17,... | collective-permute-start | bytes 589832 | tf_op jit(solution)/shard_map/ppermute | solution.py:18
  49.2 10.5 %copy-start = (f32[2,6,64,128]{3,2,1,0:T(8,128)S(1)}, f32[2,6,64,128]{3,2,1,0:T(8,128)}, u32[]{:S(2)}) copy-start(f32[2,6,64,128]{3,2,1,0:T(8,128)} %get-tuple-element.35) | copy-start | bytes 1179652

commit v10 on v9

--- a/solution.py
+++ b/solution.py
@@ -76,25 +76,28 @@
 
 
 def first_inside_kernel(q_ref, k_ref, v_ref, inside_ref):
-    queries, keys, values = q_ref[...], k_ref[...], v_ref[...]
-    tokens = queries.shape[0]
+    tokens = q_ref.shape[0]
+    part = tokens // 2
     lane = lax.broadcasted_iota(jnp.int32, (1, PAIR), 1)
     first = lane < PAIR // 2
-    causal = (lax.broadcasted_iota(jnp.int32, (tokens, tokens), 0)
-              >= lax.broadcasted_iota(jnp.int32, (tokens, tokens), 1))
     zero = jnp.zeros((), jnp.bfloat16)
-    for pair in range(queries.shape[1] // PAIR):
+    for pair in range(q_ref.shape[1] // PAIR):
         cols = slice(pair * PAIR, (pair + 1) * PAIR)
-        q_pair, k_pair, v_pair = queries[:, cols], keys[:, cols], values[:, cols]
-        inside = None
-        for use in (first, ~first):
-            q_one = jnp.where(use, q_pair, zero)
-            scores = lax.dot_general(q_one, k_pair, (((1,), (1,)), ((), ())),
-                                     preferred_element_type=jnp.float32)
-            scores = jnp.where(causal, scores, 0.0).astype(jnp.bfloat16)
-            term = jnp.dot(scores, jnp.where(use, v_pair, zero), preferred_element_type=jnp.float32)
-            inside = term if inside is None else inside + term
-        inside_ref[:, cols] = inside
+        for rows_at in (0, part):
+            seen = rows_at + part
+            q_rows = q_ref[rows_at : rows_at + part, cols]
+            k_seen, v_seen = k_ref[0:seen, cols], v_ref[0:seen, cols]
+            causal = (lax.broadcasted_iota(jnp.int32, (part, seen), 0) + rows_at
+                      >= lax.broadcasted_iota(jnp.int32, (part, seen), 1))
+            inside = None
+            for use in (first, ~first):
+                q_one = jnp.where(use, q_rows, zero)
+                scores = lax.dot_general(q_one, k_seen, (((1,), (1,)), ((), ())),
+                                         preferred_element_type=jnp.float32)
+                scores = jnp.where(causal, scores, 0.0).astype(jnp.bfloat16)
+                term = jnp.dot(scores, jnp.where(use, v_seen, zero), preferred_element_type=jnp.float32)
+                inside = term if inside is None else inside + term
+            inside_ref[rows_at : rows_at + part, cols] = inside
 
 
 def out_kernel(q_ref, state_ref, inside_ref, emb_ref, hgain_ref, out_w_ref, out_ref, att_ref):

time: 67.8 us -> 68.2 us (level)
  waiting for transfers between devices: 14.4 us -> 16.1 us
  Pallas kernels: 39.2 us -> 37.9 us
    ppermute x5, waiting for transfers between devices: 14.4 us -> 16.1 us  [from_behind(): lax.ppermute(value, axis, [(source, source + steps) for source in range(i...]
    pallas_call x4, Pallas kernels: 17.4 us -> 16.1 us  [inside_block(): pl.pallas_call(kernel, grid=(1,), in_specs=in_specs, out_specs=spec, out_...]
  transfers between devices with their start and end apart: 5 -> 5, of which waited for: 5 -> 5; matrix products, arithmetic and copies ran while one was open for 4% -> 4% of each run, Pallas kernels for 26% -> 24%
where the time goes in v10:
time: 68.2 us; the launch traced here: 67.8 us
  Pallas kernels  37.9 us (56%)
  waiting for transfers between devices  16.1 us (24%)
  starting transfers between devices  8.02 us (12%)
  local copies, waits for them, and re-layouts  3.69 us (5%)
  other arithmetic  1.97 us (3%)
    ppermute x5, waiting for transfers between devices, from_behind(): lax.ppermute(value, axis, [(source, source + steps) for source in range(i...  16.1 us
    pallas_call x4, Pallas kernels, inside_block(): pl.pallas_call(kernel, grid=(1,), in_specs=in_specs, out_specs=spec, out_...  16.1 us
    pallas_call x1, Pallas kernels, shards(): pl.pallas_call(embed_kernel, grid=(blocks,), in_specs=[pl.BlockSpec((bloc...  14.9 us
    ppermute x5, starting transfers between devices, from_behind(): lax.ppermute(value, axis, [(source, source + steps) for source in range(i...  8.02 us
    pallas_call x1, Pallas kernels, shards(): pl.pallas_call(out_kernel, grid=(blocks,), in_specs=[rows_spec, state_spe...  6.88 us
  transfers between devices with their start and end apart: 5, of which 5 were waited for; matrix products, arithmetic and copies ran while one was open for 4% of the time, Pallas kernels for 24%

profile of v10, /device:TPU:30, one launch (start us, length us, event | category | flops | bytes accessed | tf_op | source)
XLA Modules:
  0.0 67.8 jit_solution(14621540742941234352)
XLA Ops:
  0.0 0.7 %slice.10 = bf16[16,128]{1,0:T(8,128)(2,1)S(1)} slice(bf16[8192,128]{1,0:T(8,128)(2,1)} %ticks_ref.1), slice={[8176:8192], [0:128]} | slice | bytes 8192 | tf_op jit(solution)/shard_map/slice | solution.py:142
  0.7 1.9 %collective-permute-start = (bf16[16,128]{1,0:T(8,128)(2,1)S(1)}, bf16[16,128]{1,0:T(8,128)(2,1)S(1)}, u32[]{:S(2)}, u32[]{:S(2)}) collective-permute-start(bf16[16,128]{1,0:T(8,128)(2,1)S(1)} %slice.10), channel_id=1, source_target_pairs={{0,1},{1,2},{2,3},{3,4},{4,5},{5,6},{6,7},{7,8},{8,9},{9,10},{10,1... | collective-permute-start | bytes 12296 | tf_op jit(solution)/shard_map/ppermute | solution.py:18
  2.6 1.3 %reshape.12.gain_ref = f32[1,768]{1,0:T(1,128)} reshape(f32[768]{0:T(1024)} %param.9) | data formatting | bytes 6144 | tf_op jit(solution)/shard_map/reshape | solution.py:161
  3.9 1.7 %collective-permute-done.prev_ref = bf16[16,128]{1,0:T(8,128)(2,1)S(1)} collective-permute-done((bf16[16,128]{1,0:T(8,128)(2,1)S(1)}, bf16[16,128]{1,0:T(8,128)(2,1)S(1)}, u32[]{:S(2)}, u32[]{:S(2)}) %collective-permute-start) | collective-permute-done | bytes 4128 | tf_op jit(solution)/shard_map/ppermute | solution.py:18
  5.6 0.0 copy-start.2
  5.6 0.6 copy-done.2
  6.2 14.9 %shard_map.73 = (bf16[1024,768]{1,0:T(8,128)(2,1)}, bf16[1024,768]{1,0:T(8,128)(2,1)}, bf16[1024,768]{1,0:T(8,128)(2,1)}, bf16[1024,768]{1,0:T(8,128)(2,1)}, f32[2,6,64,128]{3,2,1,0:T(8,128)}) custom-call(bf16[8192,128]{1,0:T(8,128)(2,1)} %ticks_ref.1, bf16[16,128]{1,0:T(8,128)(2,1)} %copy-done.2, bf16[2048,768]{1,0:T(8,128)(2,1)} %conv_ref.1, ...), custom_call_target="tpu_custom_call" | custom-call | tf_op jit(solution)/shard_map/pallas_call | solution.py:145
  21.1 1.0 %bitcast_add_fusion = f32[6,64,128]{2,1,0:T(8,128)S(1)} fusion(f32[2,6,64,128]{3,2,1,0:T(8,128)} %get-tuple-element.35), kind=kLoop, calls=%fused_computation.2 | loop fusion | flops 49152 | bytes 589824 | tf_op jit(solution)/shard_map/add | solution.py:190
  22.1 1.9 %collective-permute-start.1 = (f32[6,64,128]{2,1,0:T(8,128)S(1)}, f32[6,64,128]{2,1,0:T(8,128)S(1)}, u32[]{:S(2)}, u32[]{:S(2)}) collective-permute-start(f32[6,64,128]{2,1,0:T(8,128)S(1)} %bitcast_add_fusion), channel_id=1, source_target_pairs={{0,1},{1,2},{2,3},{3,4},{4,5},{5,6},{6,7},{7,8},{8,9},{9,10},{10,1... | collective-permute-start | bytes 589832 | tf_op jit(solution)/shard_map/ppermute | solution.py:18
  24.1 4.0 %shard_map.74.earlier_ref = f32[1024,768]{1,0:T(8,128)} custom-call(bf16[1024,768]{1,0:T(8,128)(2,1)} %get-tuple-element.56.q_ref, bf16[1024,768]{1,0:T(8,128)(2,1)} %get-tuple-element.57.k_ref, bf16[1024,768]{1,0:T(8,128)(2,1)} %get-tuple-element.58.v_ref), custom_call_target="tpu_custom_call" | custom-call | flops 805306368 | bytes 1966080 | tf_op jit(solution)/shard_map/pallas_call | solution.py:177
  28.1 1.0 %collective-permute-done.1 = f32[6,64,128]{2,1,0:T(8,128)S(1)} collective-permute-done((f32[6,64,128]{2,1,0:T(8,128)S(1)}, f32[6,64,128]{2,1,0:T(8,128)S(1)}, u32[]{:S(2)}, u32[]{:S(2)}) %collective-permute-start.1) | collective-permute-done | bytes 196640 | tf_op jit(solution)/shard_map/ppermute | solution.py:18
  29.2 1.3 %collective-permute-start.2 = (f32[6,64,128]{2,1,0:T(8,128)S(1)}, f32[6,64,128]{2,1,0:T(8,128)S(1)}, u32[]{:S(2)}, u32[]{:S(2)}) collective-permute-start(f32[6,64,128]{2,1,0:T(8,128)S(1)} %add.22), channel_id=1, source_target_pairs={{0,2},{1,3},{2,4},{3,5},{4,6},{5,7},{6,8},{7,9},{8,10},{9,11},{10,... | collective-permute-start | bytes 589832 | tf_op jit(solution)/shard_map/ppermute | solution.py:18
  30.5 4.0 %shard_map.75.earlier_ref = f32[1024,768]{1,0:T(8,128)} custom-call(bf16[1024,768]{1,0:T(8,128)(2,1)} %get-tuple-element.56.q_ref, bf16[1024,768]{1,0:T(8,128)(2,1)} %get-tuple-element.57.k_ref, bf16[1024,768]{1,0:T(8,128)(2,1)} %get-tuple-element.58.v_ref, f32[1024,768]{1,0:T(8,128)} %shard_map.74.earlier_ref), custom_call_target="tpu_custom_call", output_to_operand_aliasing={{}: (3, {})} | custom-call | flops 805306368 | bytes 1966080 | tf_op jit(solution)/shard_map/pallas_call | solution.py:177
  34.4 2.8 %collective-permute-done.2 = f32[6,64,128]{2,1,0:T(8,128)S(1)} collective-permute-done((f32[6,64,128]{2,1,0:T(8,128)S(1)}, f32[6,64,128]{2,1,0:T(8,128)S(1)}, u32[]{:S(2)}, u32[]{:S(2)}) %collective-permute-start.2) | collective-permute-done | bytes 196640 | tf_op jit(solution)/shard_map/ppermute | solution.py:18
  37.2 0.0 copy-start.1
  37.3 0.0 copy-start.3
  37.3 1.4 %collective-permute-start.3 = (f32[6,64,128]{2,1,0:T(8,128)S(1)}, f32[6,64,128]{2,1,0:T(8,128)S(1)}, u32[]{:S(2)}, u32[]{:S(2)}) collective-permute-start(f32[6,64,128]{2,1,0:T(8,128)S(1)} %add.23), channel_id=1, source_target_pairs={{0,4},{1,5},{2,6},{3,7},{4,8},{5,9},{6,10},{7,11},{8,12},{9,13},{1... | collective-permute-start | bytes 589832 | tf_op jit(solution)/shard_map/ppermute | solution.py:18
  38.7 4.0 %shard_map.76.earlier_ref = f32[1024,768]{1,0:T(8,128)} custom-call(bf16[1024,768]{1,0:T(8,128)(2,1)} %get-tuple-element.56.q_ref, bf16[1024,768]{1,0:T(8,128)(2,1)} %get-tuple-element.57.k_ref, bf16[1024,768]{1,0:T(8,128)(2,1)} %get-tuple-element.58.v_ref, f32[1024,768]{1,0:T(8,128)} %shard_map.75.earlier_ref), custom_call_target="tpu_custom_call", output_to_operand_aliasing={{}: (3, {})} | custom-call | flops 805306368 | bytes 1966080 | tf_op jit(solution)/shard_map/pallas_call | solution.py:177
  42.7 3.9 %collective-permute-done.3 = f32[6,64,128]{2,1,0:T(8,128)S(1)} collective-permute-done((f32[6,64,128]{2,1,0:T(8,128)S(1)}, f32[6,64,128]{2,1,0:T(8,128)S(1)}, u32[]{:S(2)}, u32[]{:S(2)}) %collective-permute-start.3) | collective-permute-done | bytes 196640 | tf_op jit(solution)/shard_map/ppermute | solution.py:18
  46.6 1.5 %collective-permute-start.4 = (f32[6,64,128]{2,1,0:T(8,128)S(1)}, f32[6,64,128]{2,1,0:T(8,128)S(1)}, u32[]{:S(2)}, u32[]{:S(2)}) collective-permute-start(f32[6,64,128]{2,1,0:T(8,128)S(1)} %add.24), channel_id=1, source_target_pairs={{0,8},{1,9},{2,10},{3,11},{4,12},{5,13},{6,14},{7,15},{16,24},{17,... | collective-permute-start | bytes 589832 | tf_op jit(solution)/shard_map/ppermute | solution.py:18
  48.1 0.0 copy-done.1
  48.1 0.3 copy.13
  48.4 0.2 reshape.14
  48.7 0.0 copy-done.3
  48.7 0.6 reshape.15.hgain_ref
  49.3 0.0 copy-start
  49.3 4.1 %shard_map.77.inside_ref = f32[1024,768]{1,0:T(8,128)} custom-call(bf16[1024,768]{1,0:T(8,128)(2,1)} %get-tuple-element.56.q_ref, bf16[1024,768]{1,0:T(8,128)(2,1)} %get-tuple-element.57.k_ref, bf16[1024,768]{1,0:T(8,128)(2,1)} %get-tuple-element.58.v_ref, f32[1024,768]{1,0:T(8,128)} %shard_map.76.earlier_ref), custom_call_target="tpu_custom_call", output_to_operand_aliasing={{}: (3, {})} | custom-call | flops 805306368 | bytes 1966080 | tf_op jit(solution)/shard_map/pallas_call | solution.py:177
  53.3 6.7 %collective-permute-done.4 = f32[6,64,128]{2,1,0:T(8,128)S(1)} collective-permute-done((f32[6,64,128]{2,1,0:T(8,128)S(1)}, f32[6,64,128]{2,1,0:T(8,128)S(1)}, u32[]{:S(2)}, u32[]{:S(2)}) %collective-permute-start.4) | collective-permute-done | bytes 196640 | tf_op jit(solution)/shard_map/ppermute | solution.py:18
  60.0 0.0 copy-done
  60.0 0.1 fusion
  60.1 0.8 %pad_maximum_fusion.state_ref = f32[2,6,64,128]{3,2,1,0:T(8,128)} fusion(f32[1,6,64,128]{3,2,1,0:T(8,128)S(1)} %get-tuple-element.63, f32[1,6,64,128]{3,2,1,0:T(8,128)S(1)} %bitcast.19), kind=kLoop, calls=%fused_computation | loop fusion | flops 98304 | bytes 786432 | tf_op jit(solution)/shard_map/stack | solution.py:213
  60.9 6.9 %shard_map.78 = bf16[1024,768]{1,0:T(8,128)(2,1)} custom-call(bf16[1024,768]{1,0:T(8,128)(2,1)} %get-tuple-element.56.q_ref, f32[2,6,64,128]{3,2,1,0:T(8,128)} %pad_maximum_fusion.state_ref, f32[1024,768]{1,0:T(8,128)} %shard_map.77.inside_ref, bf16[1024,768]{1,0:T(8,128)(2,1)} %get-tuple-element.62.emb_ref, f32[1,768]{1,0:T(1,128)} %reshape.15.hgain_ref, ...), custom_call_target="tpu_custom_call" | custom-call | tf_op jit(solution)/shard_map/pallas_call | solution.py:215
  (3 shorter events, 0.1 us)
Async XLA Ops:
  0.7 4.9 %collective-permute-start = (bf16[16,128]{1,0:T(8,128)(2,1)S(1)}, bf16[16,128]{1,0:T(8,128)(2,1)S(1)}, u32[]{:S(2)}, u32[]{:S(2)}) collective-permute-start(bf16[16,128]{1,0:T(8,128)(2,1)S(1)} %slice.10), channel_id=1, source_target_pairs={{0,1},{1,2},{2,3},{3,4},{4,5},{5,6},{6,7},{7,8},{8,9},{9,10},{10,1... | collective-permute-start | bytes 12296 | tf_op jit(solution)/shard_map/ppermute | solution.py:18
  5.6 0.6 copy-start.2
  22.1 7.0 %collective-permute-start.1 = (f32[6,64,128]{2,1,0:T(8,128)S(1)}, f32[6,64,128]{2,1,0:T(8,128)S(1)}, u32[]{:S(2)}, u32[]{:S(2)}) collective-permute-start(f32[6,64,128]{2,1,0:T(8,128)S(1)} %bitcast_add_fusion), channel_id=1, source_target_pairs={{0,1},{1,2},{2,3},{3,4},{4,5},{5,6},{6,7},{7,8},{8,9},{9,10},{10,1... | collective-permute-start | bytes 589832 | tf_op jit(solution)/shard_map/ppermute | solution.py:18
  29.2 8.1 %collective-permute-start.2 = (f32[6,64,128]{2,1,0:T(8,128)S(1)}, f32[6,64,128]{2,1,0:T(8,128)S(1)}, u32[]{:S(2)}, u32[]{:S(2)}) collective-permute-start(f32[6,64,128]{2,1,0:T(8,128)S(1)} %add.22), channel_id=1, source_target_pairs={{0,2},{1,3},{2,4},{3,5},{4,6},{5,7},{6,8},{7,9},{8,10},{9,11},{10,... | collective-permute-start | bytes 589832 | tf_op jit(solution)/shard_map/ppermute | solution.py:18
  37.2 10.9 %copy-start.1 = (f32[12,64,64]{2,1,0:T(8,128)S(1)}, f32[12,64,64]{2,1,0:T(8,128)}, u32[]{:S(2)}) copy-start(f32[12,64,64]{2,1,0:T(8,128)} %param.13) | copy-start | bytes 589828
  37.3 11.4 %copy-start.3 = (f32[768]{0:T(1024)S(1)}, f32[768]{0:T(1024)}, u32[]{:S(2)}) copy-start(f32[768]{0:T(1024)} %param.11) | copy-start | bytes 9220
  37.3 9.3 %collective-permute-start.3 = (f32[6,64,128]{2,1,0:T(8,128)S(1)}, f32[6,64,128]{2,1,0:T(8,128)S(1)}, u32[]{:S(2)}, u32[]{:S(2)}) collective-permute-start(f32[6,64,128]{2,1,0:T(8,128)S(1)} %add.23), channel_id=1, source_target_pairs={{0,4},{1,5},{2,6},{3,7},{4,8},{5,9},{6,10},{7,11},{8,12},{9,13},{1... | collective-permute-start | bytes 589832 | tf_op jit(solution)/shard_map/ppermute | solution.py:18
  46.6 13.4 %collective-permute-start.4 = (f32[6,64,128]{2,1,0:T(8,128)S(1)}, f32[6,64,128]{2,1,0:T(8,128)S(1)}, u32[]{:S(2)}, u32[]{:S(2)}) collective-permute-start(f32[6,64,128]{2,1,0:T(8,128)S(1)} %add.24), channel_id=1, source_target_pairs={{0,8},{1,9},{2,10},{3,11},{4,12},{5,13},{6,14},{7,15},{16,24},{17,... | collective-permute-start | bytes 589832 | tf_op jit(solution)/shard_map/ppermute | solution.py:18
  49.3 10.8 %copy-start = (f32[2,6,64,128]{3,2,1,0:T(8,128)S(1)}, f32[2,6,64,128]{3,2,1,0:T(8,128)}, u32[]{:S(2)}) copy-start(f32[2,6,64,128]{3,2,1,0:T(8,128)} %get-tuple-element.35) | copy-start | bytes 1179652

commit v11 on v10

--- a/solution.py
+++ b/solution.py
@@ -29,7 +29,7 @@
 
 
 def embed_kernel(ticks_ref, prev_ref, conv_ref, gain_ref, qkv_w_ref,
-                 emb_ref, q_ref, k_ref, v_ref, state_ref, wide_ref):
+                 emb_ref, q_ref, k_ref, v_ref, total_ref, first_ref, wide_ref):
     b = pl.program_id(0)
     block_ticks = ticks_ref.shape[0]
     tokens = block_ticks // STRIDE
@@ -67,7 +67,9 @@
         kv = lax.dot_general(keys[:, cols], values[:, cols], (((0,), (0,)), ((), ())),
                              preferred_element_type=jnp.float32)
         half = PAIR // 2
-        state_ref[0, pair] = jnp.where(first, kv[:half], kv[half:])
+        packed = jnp.where(first, kv[:half], kv[half:])
+        total_ref[pair] = jnp.where(b > 0, total_ref[pair], 0.0) + packed
+        first_ref[pair] = jnp.where(b > 0, first_ref[pair], packed)
 
 
 def inside_kernel(q_ref, k_ref, v_ref, earlier_ref, inside_ref):
@@ -100,14 +102,17 @@
             inside_ref[rows_at : rows_at + part, cols] = inside
 
 
-def out_kernel(q_ref, state_ref, inside_ref, emb_ref, hgain_ref, out_w_ref, out_ref, att_ref):
+def out_kernel(q_ref, start_ref, total_ref, local_ref, first_ref, inside_ref, emb_ref, hgain_ref, out_w_ref,
+               out_ref, att_ref):
+    b = pl.program_id(0)
     model_width = out_ref.shape[1]
     lane = lax.broadcasted_iota(jnp.int32, (1, PAIR), 1)
     first = lane < PAIR // 2
     head_size = PAIR // 2
     for pair in range(model_width // PAIR):
         cols = slice(pair * PAIR, (pair + 1) * PAIR)
-        packed = state_ref[0, pair]
+        packed = (start_ref[pair] + (total_ref[pair] - local_ref[pair])
+                  + jnp.where(b > 0, first_ref[pair], 0.0))
         diag = jnp.concatenate([jnp.where(first, packed, 0.0), jnp.where(first, 0.0, packed)], axis=0)
         high = diag.astype(jnp.bfloat16)
         low = (diag - high.astype(jnp.float32)).astype(jnp.bfloat16)
@@ -141,8 +146,8 @@
 
     prev = from_behind(ticks[tick_count - 2 * STRIDE :], "inner", 1)
     rows_spec = pl.BlockSpec((BLK, model_width), lambda b: (b, 0))
-    state_spec = pl.BlockSpec((1, pairs, head_size, PAIR), lambda b: (b, 0, 0, 0))
-    emb, queries, keys, values, states = pl.pallas_call(
+    state_spec = full((pairs, head_size, PAIR))
+    emb, queries, keys, values, local, first_state = pl.pallas_call(
         embed_kernel,
         grid=(blocks,),
         in_specs=[
@@ -152,10 +157,10 @@
             full((1, model_width)),
             full(qkv_weight.shape),
         ],
-        out_specs=[rows_spec, rows_spec, rows_spec, rows_spec, state_spec],
+        out_specs=[rows_spec, rows_spec, rows_spec, rows_spec, state_spec, state_spec],
         out_shape=[jax.ShapeDtypeStruct((token_count, model_width), jnp.bfloat16)] * 4 + [
-            jax.ShapeDtypeStruct((blocks, pairs, head_size, PAIR), jnp.float32),
-        ],
+            jax.ShapeDtypeStruct((pairs, head_size, PAIR), jnp.float32),
+        ] * 2,
         scratch_shapes=[pltpu.VMEM((block_ticks + STRIDE, feat), jnp.float32)],
         compiler_params=pltpu.CompilerParams(dimension_semantics=("arbitrary",)),
     )(ticks, prev, conv_weight, norm_gain.reshape(1, model_width), qkv_weight)
@@ -185,9 +190,6 @@
                                           bytes_accessed=10 * BLK * piece_width),
         )(*operands)
 
-    local = states[0]
-    for block in range(1, blocks):
-        local = local + states[block]
     count = lax.axis_size("inner")
     inside = None
     total, steps, block = local, 1, 0
@@ -204,19 +206,17 @@
     while block < blocks * halves:
         inside = inside_block(block, inside, queries, keys, values)
         block += 1
-    prefix = total - local
     packed_in = state_in.reshape(pairs, 2, head_size, head_size).transpose(0, 2, 1, 3)
-    carried = packed_in.reshape(pairs, head_size, PAIR) + prefix
-    before = [carried]
-    for block in range(1, blocks):
-        before.append(before[-1] + states[block - 1])
-    before = jnp.stack(before)
+    packed_in = packed_in.reshape(pairs, head_size, PAIR)
 
     return pl.pallas_call(
         out_kernel,
         grid=(blocks,),
         in_specs=[
             rows_spec,
+            state_spec,
+            state_spec,
+            state_spec,
             state_spec,
             rows_spec,
             rows_spec,
@@ -227,7 +227,7 @@
         out_shape=jax.ShapeDtypeStruct((token_count, model_width), jnp.bfloat16),
         scratch_shapes=[pltpu.VMEM((BLK, model_width), jnp.bfloat16)],
         compiler_params=pltpu.CompilerParams(dimension_semantics=("arbitrary",)),
-    )(queries, before, inside, emb, head_gain.reshape(1, model_width), out_weight)
+    )(queries, packed_in, total, local, first_state, inside, emb, head_gain.reshape(1, model_width), out_weight)
 
 
 def solution(mesh):

time: 68.2 us -> 67.9 us (level)
  other arithmetic: 1.97 us -> 0.75 us
  local copies, waits for them, and re-layouts: 3.69 us -> 4.38 us
    add x1 -> x0, other arithmetic: 1.04 us -> none  [shards(): local = local + states[block]]
    another operation x2 -> x0, other arithmetic: 0.86 us -> none  [shards(): before = jnp.stack(before)]
    add x3 -> x4, other arithmetic: 0.07 us -> 0.75 us  [shards(): total = total + received]
  transfers between devices with their start and end apart: 5 -> 5, of which waited for: 5 -> 5; matrix products, arithmetic and copies ran while one was open for 4% -> 5% of each run, Pallas kernels for 24% -> 24%
where the time goes in v11:
time: 67.9 us; the launch traced here: 67.5 us
  Pallas kernels  38.2 us (56%)
  waiting for transfers between devices  16 us (24%)
  starting transfers between devices  8.15 us (12%)
  local copies, waits for them, and re-layouts  4.38 us (6%)
  other arithmetic  0.75 us (1%)
    pallas_call x4, Pallas kernels, inside_block(): pl.pallas_call(kernel, grid=(1,), in_specs=in_specs, out_specs=spec, out_...  16 us
    ppermute x5, waiting for transfers between devices, from_behind(): lax.ppermute(value, axis, [(source, source + steps) for source in range(i...  16 us
    pallas_call x1, Pallas kernels, shards(): pl.pallas_call(embed_kernel, grid=(blocks,), in_specs=[pl.BlockSpec((bloc...  14.7 us
    ppermute x5, starting transfers between devices, from_behind(): lax.ppermute(value, axis, [(source, source + steps) for source in range(i...  8.15 us
    pallas_call x1, Pallas kernels, shards(): pl.pallas_call(out_kernel, grid=(blocks,), in_specs=[rows_spec, state_spe...  7.41 us
  transfers between devices with their start and end apart: 5, of which 5 were waited for; matrix products, arithmetic and copies ran while one was open for 5% of the time, Pallas kernels for 24%

profile of v11, /device:TPU:30, one launch (start us, length us, event | category | flops | bytes accessed | tf_op | source)
XLA Modules:
  0.0 67.5 jit_solution(4592672466000201471)
XLA Ops:
  0.0 0.7 %slice.3 = bf16[16,128]{1,0:T(8,128)(2,1)S(1)} slice(bf16[8192,128]{1,0:T(8,128)(2,1)} %ticks_ref.1), slice={[8176:8192], [0:128]} | slice | bytes 8192 | tf_op jit(solution)/shard_map/slice | solution.py:147
  0.7 1.9 %collective-permute-start = (bf16[16,128]{1,0:T(8,128)(2,1)S(1)}, bf16[16,128]{1,0:T(8,128)(2,1)S(1)}, u32[]{:S(2)}, u32[]{:S(2)}) collective-permute-start(bf16[16,128]{1,0:T(8,128)(2,1)S(1)} %slice.3), channel_id=1, source_target_pairs={{0,1},{1,2},{2,3},{3,4},{4,5},{5,6},{6,7},{7,8},{8,9},{9,10},{10,1... | collective-permute-start | bytes 12296 | tf_op jit(solution)/shard_map/ppermute | solution.py:18
  2.6 1.3 %reshape.12.gain_ref = f32[1,768]{1,0:T(1,128)} reshape(f32[768]{0:T(1024)} %param.9) | data formatting | bytes 6144 | tf_op jit(solution)/shard_map/reshape | solution.py:166
  3.9 1.7 %collective-permute-done.prev_ref = bf16[16,128]{1,0:T(8,128)(2,1)S(1)} collective-permute-done((bf16[16,128]{1,0:T(8,128)(2,1)S(1)}, bf16[16,128]{1,0:T(8,128)(2,1)S(1)}, u32[]{:S(2)}, u32[]{:S(2)}) %collective-permute-start) | collective-permute-done | bytes 4128 | tf_op jit(solution)/shard_map/ppermute | solution.py:18
  5.6 0.0 copy-start.2
  5.6 0.6 copy-done.2
  6.2 14.7 %shard_map.73 = (bf16[1024,768]{1,0:T(8,128)(2,1)}, bf16[1024,768]{1,0:T(8,128)(2,1)}, bf16[1024,768]{1,0:T(8,128)(2,1)}, bf16[1024,768]{1,0:T(8,128)(2,1)}, f32...) custom-call(bf16[8192,128]{1,0:T(8,128)(2,1)} %ticks_ref.1, bf16[16,128]{1,0:T(8,128)(2,1)} %copy-done.2, ...), custom_call_target="tpu_custom_call" | custom-call | tf_op jit(solution)/shard_map/pallas_call | solution.py:150
  20.9 0.0 copy-start
  21.0 2.1 %collective-permute-start.1 = (f32[6,64,128]{2,1,0:T(8,128)}, f32[6,64,128]{2,1,0:T(8,128)S(1)}, u32[]{:S(2)}, u32[]{:S(2)}) collective-permute-start(f32[6,64,128]{2,1,0:T(8,128)} %get-tuple-element.39.local_ref), channel_id=1, source_target_pairs={{0,1},{1,2},{2,3},{3,4},{4,5},{5,6},{6,7},{7,8},{8,9},{9,10},{10,1... | collective-permute-start | bytes 589832 | tf_op jit(solution)/shard_map/ppermute | solution.py:18
  23.0 4.0 %shard_map.74.earlier_ref = f32[1024,768]{1,0:T(8,128)} custom-call(bf16[1024,768]{1,0:T(8,128)(2,1)} %get-tuple-element.57.q_ref, bf16[1024,768]{1,0:T(8,128)(2,1)} %get-tuple-element.58.k_ref, bf16[1024,768]{1,0:T(8,128)(2,1)} %get-tuple-element.59.v_ref), custom_call_target="tpu_custom_call" | custom-call | flops 805306368 | bytes 1966080 | tf_op jit(solution)/shard_map/pallas_call | solution.py:182
  27.0 1.3 %collective-permute-done.1 = f32[6,64,128]{2,1,0:T(8,128)S(1)} collective-permute-done((f32[6,64,128]{2,1,0:T(8,128)}, f32[6,64,128]{2,1,0:T(8,128)S(1)}, u32[]{:S(2)}, u32[]{:S(2)}) %collective-permute-start.1) | collective-permute-done | bytes 196640 | tf_op jit(solution)/shard_map/ppermute | solution.py:18
  28.3 0.0 copy-done
  28.3 1.3 %collective-permute-start.2 = (f32[6,64,128]{2,1,0:T(8,128)S(1)}, f32[6,64,128]{2,1,0:T(8,128)S(1)}, u32[]{:S(2)}, u32[]{:S(2)}) collective-permute-start(f32[6,64,128]{2,1,0:T(8,128)S(1)} %add.12), channel_id=1, source_target_pairs={{0,2},{1,3},{2,4},{3,5},{4,6},{5,7},{6,8},{7,9},{8,10},{9,11},{10,... | collective-permute-start | bytes 589832 | tf_op jit(solution)/shard_map/ppermute | solution.py:18
  29.6 4.0 %shard_map.75.earlier_ref = f32[1024,768]{1,0:T(8,128)} custom-call(bf16[1024,768]{1,0:T(8,128)(2,1)} %get-tuple-element.57.q_ref, bf16[1024,768]{1,0:T(8,128)(2,1)} %get-tuple-element.58.k_ref, bf16[1024,768]{1,0:T(8,128)(2,1)} %get-tuple-element.59.v_ref, f32[1024,768]{1,0:T(8,128)} %shard_map.74.earlier_ref), custom_call_target="tpu_custom_call", output_to_operand_aliasing={{}: (3, {})} | custom-call | flops 805306368 | bytes 1966080 | tf_op jit(solution)/shard_map/pallas_call | solution.py:182
  33.6 2.6 %collective-permute-done.2 = f32[6,64,128]{2,1,0:T(8,128)S(1)} collective-permute-done((f32[6,64,128]{2,1,0:T(8,128)S(1)}, f32[6,64,128]{2,1,0:T(8,128)S(1)}, u32[]{:S(2)}, u32[]{:S(2)}) %collective-permute-start.2) | collective-permute-done | bytes 196640 | tf_op jit(solution)/shard_map/ppermute | solution.py:18
  36.2 0.0 copy-start.1
  36.2 0.0 copy-start.3
  36.3 1.4 %collective-permute-start.3 = (f32[6,64,128]{2,1,0:T(8,128)S(1)}, f32[6,64,128]{2,1,0:T(8,128)S(1)}, u32[]{:S(2)}, u32[]{:S(2)}) collective-permute-start(f32[6,64,128]{2,1,0:T(8,128)S(1)} %add.13), channel_id=1, source_target_pairs={{0,4},{1,5},{2,6},{3,7},{4,8},{5,9},{6,10},{7,11},{8,12},{9,13},{1... | collective-permute-start | bytes 589832 | tf_op jit(solution)/shard_map/ppermute | solution.py:18
  37.7 4.0 %shard_map.76.earlier_ref = f32[1024,768]{1,0:T(8,128)} custom-call(bf16[1024,768]{1,0:T(8,128)(2,1)} %get-tuple-element.57.q_ref, bf16[1024,768]{1,0:T(8,128)(2,1)} %get-tuple-element.58.k_ref, bf16[1024,768]{1,0:T(8,128)(2,1)} %get-tuple-element.59.v_ref, f32[1024,768]{1,0:T(8,128)} %shard_map.75.earlier_ref), custom_call_target="tpu_custom_call", output_to_operand_aliasing={{}: (3, {})} | custom-call | flops 805306368 | bytes 1966080 | tf_op jit(solution)/shard_map/pallas_call | solution.py:182
  41.7 4.3 %collective-permute-done.3 = f32[6,64,128]{2,1,0:T(8,128)S(1)} collective-permute-done((f32[6,64,128]{2,1,0:T(8,128)S(1)}, f32[6,64,128]{2,1,0:T(8,128)S(1)}, u32[]{:S(2)}, u32[]{:S(2)}) %collective-permute-start.3) | collective-permute-done | bytes 196640 | tf_op jit(solution)/shard_map/ppermute | solution.py:18
  46.0 1.5 %collective-permute-start.4 = (f32[6,64,128]{2,1,0:T(8,128)S(1)}, f32[6,64,128]{2,1,0:T(8,128)S(1)}, u32[]{:S(2)}, u32[]{:S(2)}) collective-permute-start(f32[6,64,128]{2,1,0:T(8,128)S(1)} %add.14), channel_id=1, source_target_pairs={{0,8},{1,9},{2,10},{3,11},{4,12},{5,13},{6,14},{7,15},{16,24},{17,... | collective-permute-start | bytes 589832 | tf_op jit(solution)/shard_map/ppermute | solution.py:18
  47.5 0.0 copy-done.1
  47.5 0.3 copy.13
  47.8 0.9 %reshape.14.start_ref = f32[6,64,128]{2,1,0:T(8,128)} reshape(f32[6,64,2,64]{3,2,1,0:T(2,128)S(1)} %bitcast.4) | data formatting | bytes 393216 | tf_op jit(solution)/shard_map/reshape | solution.py:210
  48.7 0.0 copy-done.3
  48.8 0.6 reshape.15.hgain_ref
  49.3 4.0 %shard_map.77.inside_ref = f32[1024,768]{1,0:T(8,128)} custom-call(bf16[1024,768]{1,0:T(8,128)(2,1)} %get-tuple-element.57.q_ref, bf16[1024,768]{1,0:T(8,128)(2,1)} %get-tuple-element.58.k_ref, bf16[1024,768]{1,0:T(8,128)(2,1)} %get-tuple-element.59.v_ref, f32[1024,768]{1,0:T(8,128)} %shard_map.76.earlier_ref), custom_call_target="tpu_custom_call", output_to_operand_aliasing={{}: (3, {})} | custom-call | flops 805306368 | bytes 1966080 | tf_op jit(solution)/shard_map/pallas_call | solution.py:182
  53.4 6.1 %collective-permute-done.4 = f32[6,64,128]{2,1,0:T(8,128)S(1)} collective-permute-done((f32[6,64,128]{2,1,0:T(8,128)S(1)}, f32[6,64,128]{2,1,0:T(8,128)S(1)}, u32[]{:S(2)}, u32[]{:S(2)}) %collective-permute-start.4) | collective-permute-done | bytes 196640 | tf_op jit(solution)/shard_map/ppermute | solution.py:18
  59.4 0.7 %add.15.total_ref = f32[6,64,128]{2,1,0:T(8,128)} add(f32[6,64,128]{2,1,0:T(8,128)S(1)} %add.14, f32[6,64,128]{2,1,0:T(8,128)S(1)} %collective-permute-done.4) | non-fusion elementwise | flops 49152 | bytes 589824 | tf_op jit(solution)/shard_map/add | solution.py:204
  60.1 7.4 %shard_map.78 = bf16[1024,768]{1,0:T(8,128)(2,1)} custom-call(bf16[1024,768]{1,0:T(8,128)(2,1)} %get-tuple-element.57.q_ref, f32[6,64,128]{2,1,0:T(8,128)} %reshape.14.start_ref, f32[6,64,128]{2,1,0:T(8,128)} %add.15.total_ref, f32[6,64,128]{2,1,0:T(8,128)} %get-tuple-element.39.local_ref, f32[6,64,128]{2,1,0:T(8,128)} %get-tuple-element.62.first_ref, ...), custom_call_target="tpu_custom_call" | custom-call | tf_op jit(solution)/shard_map/pallas_call | solution.py:212
  (3 shorter events, 0.1 us)
Async XLA Ops:
  0.7 4.9 %collective-permute-start = (bf16[16,128]{1,0:T(8,128)(2,1)S(1)}, bf16[16,128]{1,0:T(8,128)(2,1)S(1)}, u32[]{:S(2)}, u32[]{:S(2)}) collective-permute-start(bf16[16,128]{1,0:T(8,128)(2,1)S(1)} %slice.3), channel_id=1, source_target_pairs={{0,1},{1,2},{2,3},{3,4},{4,5},{5,6},{6,7},{7,8},{8,9},{9,10},{10,1... | collective-permute-start | bytes 12296 | tf_op jit(solution)/shard_map/ppermute | solution.py:18
  5.6 0.6 copy-start.2
  20.9 7.3 %copy-start = (f32[6,64,128]{2,1,0:T(8,128)S(1)}, f32[6,64,128]{2,1,0:T(8,128)}, u32[]{:S(2)}) copy-start(f32[6,64,128]{2,1,0:T(8,128)} %get-tuple-element.39.local_ref) | copy-start | bytes 589828
  21.0 7.3 %collective-permute-start.1 = (f32[6,64,128]{2,1,0:T(8,128)}, f32[6,64,128]{2,1,0:T(8,128)S(1)}, u32[]{:S(2)}, u32[]{:S(2)}) collective-permute-start(f32[6,64,128]{2,1,0:T(8,128)} %get-tuple-element.39.local_ref), channel_id=1, source_target_pairs={{0,1},{1,2},{2,3},{3,4},{4,5},{5,6},{6,7},{7,8},{8,9},{9,10},{10,1... | collective-permute-start | bytes 589832 | tf_op jit(solution)/shard_map/ppermute | solution.py:18
  28.3 7.9 %collective-permute-start.2 = (f32[6,64,128]{2,1,0:T(8,128)S(1)}, f32[6,64,128]{2,1,0:T(8,128)S(1)}, u32[]{:S(2)}, u32[]{:S(2)}) collective-permute-start(f32[6,64,128]{2,1,0:T(8,128)S(1)} %add.12), channel_id=1, source_target_pairs={{0,2},{1,3},{2,4},{3,5},{4,6},{5,7},{6,8},{7,9},{8,10},{9,11},{10,... | collective-permute-start | bytes 589832 | tf_op jit(solution)/shard_map/ppermute | solution.py:18
  36.2 11.3 %copy-start.1 = (f32[12,64,64]{2,1,0:T(8,128)S(1)}, f32[12,64,64]{2,1,0:T(8,128)}, u32[]{:S(2)}) copy-start(f32[12,64,64]{2,1,0:T(8,128)} %param.13) | copy-start | bytes 589828
  36.2 12.5 %copy-start.3 = (f32[768]{0:T(1024)S(1)}, f32[768]{0:T(1024)}, u32[]{:S(2)}) copy-start(f32[768]{0:T(1024)} %param.11) | copy-start | bytes 9220
  36.3 9.8 %collective-permute-start.3 = (f32[6,64,128]{2,1,0:T(8,128)S(1)}, f32[6,64,128]{2,1,0:T(8,128)S(1)}, u32[]{:S(2)}, u32[]{:S(2)}) collective-permute-start(f32[6,64,128]{2,1,0:T(8,128)S(1)} %add.13), channel_id=1, source_target_pairs={{0,4},{1,5},{2,6},{3,7},{4,8},{5,9},{6,10},{7,11},{8,12},{9,13},{1... | collective-permute-start | bytes 589832 | tf_op jit(solution)/shard_map/ppermute | solution.py:18
  46.0 13.4 %collective-permute-start.4 = (f32[6,64,128]{2,1,0:T(8,128)S(1)}, f32[6,64,128]{2,1,0:T(8,128)S(1)}, u32[]{:S(2)}, u32[]{:S(2)}) collective-permute-start(f32[6,64,128]{2,1,0:T(8,128)S(1)} %add.14), channel_id=1, source_target_pairs={{0,8},{1,9},{2,10},{3,11},{4,12},{5,13},{6,14},{7,15},{16,24},{17,... | collective-permute-start | bytes 589832 | tf_op jit(solution)/shard_map/ppermute | solution.py:18

commit v12 on v11

--- a/solution.py
+++ b/solution.py
@@ -50,7 +50,7 @@
     emb_ref[...] = emb
     embed_f = emb.astype(jnp.float32)
     mean_sq = jnp.mean(embed_f * embed_f, axis=-1, keepdims=True)
-    normed = (embed_f * lax.rsqrt(mean_sq + 1e-05) * gain_ref[...]).astype(jnp.bfloat16)
+    normed = (embed_f * lax.rsqrt(mean_sq + 1e-05) * gain_ref[...][None, :]).astype(jnp.bfloat16)
 
     def project(part):
         weight = qkv_w_ref[:, part * model_width : (part + 1) * model_width]
@@ -102,7 +102,7 @@
             inside_ref[rows_at : rows_at + part, cols] = inside
 
 
-def out_kernel(q_ref, start_ref, total_ref, local_ref, first_ref, inside_ref, emb_ref, hgain_ref, out_w_ref,
+def out_kernel(q_ref, start_ref, total_ref, received_ref, local_ref, first_ref, inside_ref, emb_ref, hgain_ref, out_w_ref,
                out_ref, att_ref):
     b = pl.program_id(0)
     model_width = out_ref.shape[1]
@@ -111,7 +111,7 @@
     head_size = PAIR // 2
     for pair in range(model_width // PAIR):
         cols = slice(pair * PAIR, (pair + 1) * PAIR)
-        packed = (start_ref[pair] + (total_ref[pair] - local_ref[pair])
+        packed = (start_ref[pair] + (total_ref[pair] + received_ref[pair] - local_ref[pair])
                   + jnp.where(b > 0, first_ref[pair], 0.0))
         diag = jnp.concatenate([jnp.where(first, packed, 0.0), jnp.where(first, 0.0, packed)], axis=0)
         high = diag.astype(jnp.bfloat16)
@@ -154,7 +154,7 @@
             pl.BlockSpec((block_ticks, feat), lambda b: (b, 0)),
             full((2 * STRIDE, feat)),
             full(conv_weight.shape),
-            full((1, model_width)),
+            full((model_width,)),
             full(qkv_weight.shape),
         ],
         out_specs=[rows_spec, rows_spec, rows_spec, rows_spec, state_spec, state_spec],
@@ -163,7 +163,7 @@
         ] * 2,
         scratch_shapes=[pltpu.VMEM((block_ticks + STRIDE, feat), jnp.float32)],
         compiler_params=pltpu.CompilerParams(dimension_semantics=("arbitrary",)),
-    )(ticks, prev, conv_weight, norm_gain.reshape(1, model_width), qkv_weight)
+    )(ticks, prev, conv_weight, norm_gain, qkv_weight)
 
     halves = 2
     piece_width = model_width // halves
@@ -193,6 +193,7 @@
     count = lax.axis_size("inner")
     inside = None
     total, steps, block = local, 1, 0
+    received = jnp.zeros_like(local)
     while steps < count:
         if block < blocks * halves:
             total, q_in, k_in, v_in = lax.optimization_barrier((total, queries, keys, values))
@@ -201,8 +202,10 @@
             inside = inside_block(block, inside, q_in, k_in, v_in)
             received, inside = lax.optimization_barrier((received, inside))
             block += 1
+        steps *= 2
+        if steps >= count:
+            break
         total = total + received
-        steps *= 2
     while block < blocks * halves:
         inside = inside_block(block, inside, queries, keys, values)
         block += 1
@@ -214,6 +217,7 @@
         grid=(blocks,),
         in_specs=[
             rows_spec,
+            state_spec,
             state_spec,
             state_spec,
             state_spec,
@@ -227,7 +231,7 @@
         out_shape=jax.ShapeDtypeStruct((token_count, model_width), jnp.bfloat16),
         scratch_shapes=[pltpu.VMEM((BLK, model_width), jnp.bfloat16)],
         compiler_params=pltpu.CompilerParams(dimension_semantics=("arbitrary",)),
-    )(queries, packed_in, total, local, first_state, inside, emb, head_gain.reshape(1, model_width), out_weight)
+    )(queries, packed_in, total, received, local, first_state, inside, emb, head_gain.reshape(1, model_width), out_weight)
 
 
 def solution(mesh):

time: 67.9 us -> 67.9 us (level)
  waiting for transfers between devices: 16 us -> 17.2 us
  other arithmetic: 0.75 us -> 0.07 us
    reshape x1 -> x0, local copies, waits for them, and re-layouts: 1.28 us -> none  [shards(): norm_gain.reshape(1, model_width)]
    ppermute x5, waiting for transfers between devices: 16 us -> 17.2 us  [from_behind(): lax.ppermute(value, axis, [(source, source + steps) for source in range(i...]
    add x4 -> x3, other arithmetic: 0.75 us -> 0.07 us  [shards(): total = total + received]
  transfers between devices with their start and end apart: 5 -> 5, of which waited for: 5 -> 5; matrix products, arithmetic and copies ran while one was open for 5% -> 3% of each run, Pallas kernels for 24% -> 24%
where the time goes in v12:
time: 67.9 us; the launch traced here: 67.5 us
  Pallas kernels  38.2 us (56%)
  waiting for transfers between devices  17.2 us (25%)
  starting transfers between devices  8.15 us (12%)
  local copies, waits for them, and re-layouts  3.76 us (6%)
    ppermute x5, waiting for transfers between devices, from_behind(): lax.ppermute(value, axis, [(source, source + steps) for source in range(i...  17.2 us
    pallas_call x4, Pallas kernels, inside_block(): pl.pallas_call(kernel, grid=(1,), in_specs=in_specs, out_specs=spec, out_...  16.1 us
    pallas_call x1, Pallas kernels, shards(): pl.pallas_call(embed_kernel, grid=(blocks,), in_specs=[pl.BlockSpec((bloc...  14.7 us
    ppermute x5, starting transfers between devices, from_behind(): lax.ppermute(value, axis, [(source, source + steps) for source in range(i...  8.15 us
    pallas_call x1, Pallas kernels, shards(): pl.pallas_call(out_kernel, grid=(blocks,), in_specs=[rows_spec, state_spe...  7.42 us
  transfers between devices with their start and end apart: 5, of which 5 were waited for; matrix products, arithmetic and copies ran while one was open for 3% of the time, Pallas kernels for 24%

profile of v12, /device:TPU:30, one launch (start us, length us, event | category | flops | bytes accessed | tf_op | source)
XLA Modules:
  0.0 67.5 jit_solution(8111958555383275122)
XLA Ops:
  0.0 0.7 %slice.3 = bf16[16,128]{1,0:T(8,128)(2,1)S(1)} slice(bf16[8192,128]{1,0:T(8,128)(2,1)} %ticks_ref.1), slice={[8176:8192], [0:128]} | slice | bytes 8192 | tf_op jit(solution)/shard_map/slice | solution.py:147
  0.7 1.9 %collective-permute-start = (bf16[16,128]{1,0:T(8,128)(2,1)S(1)}, bf16[16,128]{1,0:T(8,128)(2,1)S(1)}, u32[]{:S(2)}, u32[]{:S(2)}) collective-permute-start(bf16[16,128]{1,0:T(8,128)(2,1)S(1)} %slice.3), channel_id=1, source_target_pairs={{0,1},{1,2},{2,3},{3,4},{4,5},{5,6},{6,7},{7,8},{8,9},{9,10},{10,1... | collective-permute-start | bytes 12296 | tf_op jit(solution)/shard_map/ppermute | solution.py:18
  2.6 3.0 %collective-permute-done.prev_ref = bf16[16,128]{1,0:T(8,128)(2,1)S(1)} collective-permute-done((bf16[16,128]{1,0:T(8,128)(2,1)S(1)}, bf16[16,128]{1,0:T(8,128)(2,1)S(1)}, u32[]{:S(2)}, u32[]{:S(2)}) %collective-permute-start) | collective-permute-done | bytes 4128 | tf_op jit(solution)/shard_map/ppermute | solution.py:18
  5.6 0.0 copy-start.4
  5.6 0.6 copy-done.4
  6.2 14.7 %shard_map.73 = (bf16[1024,768]{1,0:T(8,128)(2,1)}, bf16[1024,768]{1,0:T(8,128)(2,1)}, bf16[1024,768]{1,0:T(8,128)(2,1)}, bf16[1024,768]{1,0:T(8,128)(2,1)}, f32...) custom-call(bf16[8192,128]{1,0:T(8,128)(2,1)} %ticks_ref.1, bf16[16,128]{1,0:T(8,128)(2,1)} %copy-done.4, ...), custom_call_target="tpu_custom_call" | custom-call | tf_op jit(solution)/shard_map/pallas_call | solution.py:150
  20.9 0.0 copy-start
  20.9 2.1 %collective-permute-start.1 = (f32[6,64,128]{2,1,0:T(8,128)}, f32[6,64,128]{2,1,0:T(8,128)S(1)}, u32[]{:S(2)}, u32[]{:S(2)}) collective-permute-start(f32[6,64,128]{2,1,0:T(8,128)} %get-tuple-element.39.local_ref), channel_id=1, source_target_pairs={{0,1},{1,2},{2,3},{3,4},{4,5},{5,6},{6,7},{7,8},{8,9},{9,10},{10,1... | collective-permute-start | bytes 589832 | tf_op jit(solution)/shard_map/ppermute | solution.py:18
  23.0 4.0 %shard_map.74.earlier_ref = f32[1024,768]{1,0:T(8,128)} custom-call(bf16[1024,768]{1,0:T(8,128)(2,1)} %get-tuple-element.57.q_ref, bf16[1024,768]{1,0:T(8,128)(2,1)} %get-tuple-element.58.k_ref, bf16[1024,768]{1,0:T(8,128)(2,1)} %get-tuple-element.59.v_ref), custom_call_target="tpu_custom_call" | custom-call | flops 805306368 | bytes 1966080 | tf_op jit(solution)/shard_map/pallas_call | solution.py:182
  27.0 1.3 %collective-permute-done.1 = f32[6,64,128]{2,1,0:T(8,128)S(1)} collective-permute-done((f32[6,64,128]{2,1,0:T(8,128)}, f32[6,64,128]{2,1,0:T(8,128)S(1)}, u32[]{:S(2)}, u32[]{:S(2)}) %collective-permute-start.1) | collective-permute-done | bytes 196640 | tf_op jit(solution)/shard_map/ppermute | solution.py:18
  28.3 0.0 copy-done
  28.3 1.3 %collective-permute-start.2 = (f32[6,64,128]{2,1,0:T(8,128)S(1)}, f32[6,64,128]{2,1,0:T(8,128)S(1)}, u32[]{:S(2)}, u32[]{:S(2)}) collective-permute-start(f32[6,64,128]{2,1,0:T(8,128)S(1)} %add.9), channel_id=1, source_target_pairs={{0,2},{1,3},{2,4},{3,5},{4,6},{5,7},{6,8},{7,9},{8,10},{9,11},{10,... | collective-permute-start | bytes 589832 | tf_op jit(solution)/shard_map/ppermute | solution.py:18
  29.6 4.0 %shard_map.75.earlier_ref = f32[1024,768]{1,0:T(8,128)} custom-call(bf16[1024,768]{1,0:T(8,128)(2,1)} %get-tuple-element.57.q_ref, bf16[1024,768]{1,0:T(8,128)(2,1)} %get-tuple-element.58.k_ref, bf16[1024,768]{1,0:T(8,128)(2,1)} %get-tuple-element.59.v_ref, f32[1024,768]{1,0:T(8,128)} %shard_map.74.earlier_ref), custom_call_target="tpu_custom_call", output_to_operand_aliasing={{}: (3, {})} | custom-call | flops 805306368 | bytes 1966080 | tf_op jit(solution)/shard_map/pallas_call | solution.py:182
  33.6 2.6 %collective-permute-done.2 = f32[6,64,128]{2,1,0:T(8,128)S(1)} collective-permute-done((f32[6,64,128]{2,1,0:T(8,128)S(1)}, f32[6,64,128]{2,1,0:T(8,128)S(1)}, u32[]{:S(2)}, u32[]{:S(2)}) %collective-permute-start.2) | collective-permute-done | bytes 196640 | tf_op jit(solution)/shard_map/ppermute | solution.py:18
  36.2 0.0 copy-start.2
  36.2 0.0 copy-start.5
  36.2 1.4 %collective-permute-start.3 = (f32[6,64,128]{2,1,0:T(8,128)S(1)}, f32[6,64,128]{2,1,0:T(8,128)S(1)}, u32[]{:S(2)}, u32[]{:S(2)}) collective-permute-start(f32[6,64,128]{2,1,0:T(8,128)S(1)} %add.10), channel_id=1, source_target_pairs={{0,4},{1,5},{2,6},{3,7},{4,8},{5,9},{6,10},{7,11},{8,12},{9,13},{1... | collective-permute-start | bytes 589832 | tf_op jit(solution)/shard_map/ppermute | solution.py:18
  37.7 4.1 %shard_map.76.earlier_ref = f32[1024,768]{1,0:T(8,128)} custom-call(bf16[1024,768]{1,0:T(8,128)(2,1)} %get-tuple-element.57.q_ref, bf16[1024,768]{1,0:T(8,128)(2,1)} %get-tuple-element.58.k_ref, bf16[1024,768]{1,0:T(8,128)(2,1)} %get-tuple-element.59.v_ref, f32[1024,768]{1,0:T(8,128)} %shard_map.75.earlier_ref), custom_call_target="tpu_custom_call", output_to_operand_aliasing={{}: (3, {})} | custom-call | flops 805306368 | bytes 1966080 | tf_op jit(solution)/shard_map/pallas_call | solution.py:182
  41.7 4.2 %collective-permute-done.3 = f32[6,64,128]{2,1,0:T(8,128)S(1)} collective-permute-done((f32[6,64,128]{2,1,0:T(8,128)S(1)}, f32[6,64,128]{2,1,0:T(8,128)S(1)}, u32[]{:S(2)}, u32[]{:S(2)}) %collective-permute-start.3) | collective-permute-done | bytes 196640 | tf_op jit(solution)/shard_map/ppermute | solution.py:18
  46.0 0.0 copy-start.1
  46.0 1.5 %collective-permute-start.4 = (f32[6,64,128]{2,1,0:T(8,128)S(1)}, f32[6,64,128]{2,1,0:T(8,128)S(1)}, u32[]{:S(2)}, u32[]{:S(2)}) collective-permute-start(f32[6,64,128]{2,1,0:T(8,128)S(1)} %add.11.total_ref), channel_id=1, source_target_pairs={{0,8},{1,9},{2,10},{3,11},{4,12},{5,13},{6,14},{7,15},{16,24},{17,... | collective-permute-start | bytes 589832 | tf_op jit(solution)/shard_map/ppermute | solution.py:18
  47.5 0.0 copy-done.2
  47.5 0.3 copy.13
  47.8 0.9 %reshape.10.start_ref = f32[6,64,128]{2,1,0:T(8,128)} reshape(f32[6,64,2,64]{3,2,1,0:T(2,128)S(1)} %bitcast.4) | data formatting | bytes 393216 | tf_op jit(solution)/shard_map/reshape | solution.py:213
  48.7 0.0 copy-done.5
  48.7 0.6 reshape.11.hgain_ref
  49.3 4.0 %shard_map.77.inside_ref = f32[1024,768]{1,0:T(8,128)} custom-call(bf16[1024,768]{1,0:T(8,128)(2,1)} %get-tuple-element.57.q_ref, bf16[1024,768]{1,0:T(8,128)(2,1)} %get-tuple-element.58.k_ref, bf16[1024,768]{1,0:T(8,128)(2,1)} %get-tuple-element.59.v_ref, f32[1024,768]{1,0:T(8,128)} %shard_map.76.earlier_ref), custom_call_target="tpu_custom_call", output_to_operand_aliasing={{}: (3, {})} | custom-call | flops 805306368 | bytes 1966080 | tf_op jit(solution)/shard_map/pallas_call | solution.py:182
  53.3 0.0 copy-done.1
  53.3 6.1 %collective-permute-done.4.received_ref = f32[6,64,128]{2,1,0:T(8,128)S(1)} collective-permute-done((f32[6,64,128]{2,1,0:T(8,128)S(1)}, f32[6,64,128]{2,1,0:T(8,128)S(1)}, u32[]{:S(2)}, u32[]{:S(2)}) %collective-permute-start.4) | collective-permute-done | bytes 196640 | tf_op jit(solution)/shard_map/ppermute | solution.py:18
  59.4 0.0 copy-start.3
  59.4 0.7 copy-done.3
  60.1 7.4 %shard_map.78 = bf16[1024,768]{1,0:T(8,128)(2,1)} custom-call(bf16[1024,768]{1,0:T(8,128)(2,1)} %get-tuple-element.57.q_ref, f32[6,64,128]{2,1,0:T(8,128)} %reshape.10.start_ref, f32[6,64,128]{2,1,0:T(8,128)} %copy-done.1, f32[6,64,128]{2,1,0:T(8,128)} %copy-done.3, f32[6,64,128]{2,1,0:T(8,128)} %get-tuple-element.39.local_ref, ...), custom_call_target="tpu_custom_call" | custom-call | tf_op jit(solution)/shard_map/pallas_call | solution.py:215
  (3 shorter events, 0.1 us)
Async XLA Ops:
  0.7 4.9 %collective-permute-start = (bf16[16,128]{1,0:T(8,128)(2,1)S(1)}, bf16[16,128]{1,0:T(8,128)(2,1)S(1)}, u32[]{:S(2)}, u32[]{:S(2)}) collective-permute-start(bf16[16,128]{1,0:T(8,128)(2,1)S(1)} %slice.3), channel_id=1, source_target_pairs={{0,1},{1,2},{2,3},{3,4},{4,5},{5,6},{6,7},{7,8},{8,9},{9,10},{10,1... | collective-permute-start | bytes 12296 | tf_op jit(solution)/shard_map/ppermute | solution.py:18
  5.6 0.6 copy-start.4
  20.9 7.3 %copy-start = (f32[6,64,128]{2,1,0:T(8,128)S(1)}, f32[6,64,128]{2,1,0:T(8,128)}, u32[]{:S(2)}) copy-start(f32[6,64,128]{2,1,0:T(8,128)} %get-tuple-element.39.local_ref) | copy-start | bytes 589828
  20.9 7.3 %collective-permute-start.1 = (f32[6,64,128]{2,1,0:T(8,128)}, f32[6,64,128]{2,1,0:T(8,128)S(1)}, u32[]{:S(2)}, u32[]{:S(2)}) collective-permute-start(f32[6,64,128]{2,1,0:T(8,128)} %get-tuple-element.39.local_ref), channel_id=1, source_target_pairs={{0,1},{1,2},{2,3},{3,4},{4,5},{5,6},{6,7},{7,8},{8,9},{9,10},{10,1... | collective-permute-start | bytes 589832 | tf_op jit(solution)/shard_map/ppermute | solution.py:18
  28.3 7.9 %collective-permute-start.2 = (f32[6,64,128]{2,1,0:T(8,128)S(1)}, f32[6,64,128]{2,1,0:T(8,128)S(1)}, u32[]{:S(2)}, u32[]{:S(2)}) collective-permute-start(f32[6,64,128]{2,1,0:T(8,128)S(1)} %add.9), channel_id=1, source_target_pairs={{0,2},{1,3},{2,4},{3,5},{4,6},{5,7},{6,8},{7,9},{8,10},{9,11},{10,... | collective-permute-start | bytes 589832 | tf_op jit(solution)/shard_map/ppermute | solution.py:18
  36.2 11.3 %copy-start.2 = (f32[12,64,64]{2,1,0:T(8,128)S(1)}, f32[12,64,64]{2,1,0:T(8,128)}, u32[]{:S(2)}) copy-start(f32[12,64,64]{2,1,0:T(8,128)} %param.13) | copy-start | bytes 589828
  36.2 12.5 %copy-start.5 = (f32[768]{0:T(1024)S(1)}, f32[768]{0:T(1024)}, u32[]{:S(2)}) copy-start(f32[768]{0:T(1024)} %param.11) | copy-start | bytes 9220
  36.2 9.7 %collective-permute-start.3 = (f32[6,64,128]{2,1,0:T(8,128)S(1)}, f32[6,64,128]{2,1,0:T(8,128)S(1)}, u32[]{:S(2)}, u32[]{:S(2)}) collective-permute-start(f32[6,64,128]{2,1,0:T(8,128)S(1)} %add.10), channel_id=1, source_target_pairs={{0,4},{1,5},{2,6},{3,7},{4,8},{5,9},{6,10},{7,11},{8,12},{9,13},{1... | collective-permute-start | bytes 589832 | tf_op jit(solution)/shard_map/ppermute | solution.py:18
  46.0 7.3 %copy-start.1 = (f32[6,64,128]{2,1,0:T(8,128)}, f32[6,64,128]{2,1,0:T(8,128)S(1)}, u32[]{:S(2)}) copy-start(f32[6,64,128]{2,1,0:T(8,128)S(1)} %add.11.total_ref) | copy-start | bytes 589828
  46.0 13.4 %collective-permute-start.4 = (f32[6,64,128]{2,1,0:T(8,128)S(1)}, f32[6,64,128]{2,1,0:T(8,128)S(1)}, u32[]{:S(2)}, u32[]{:S(2)}) collective-permute-start(f32[6,64,128]{2,1,0:T(8,128)S(1)} %add.11.total_ref), channel_id=1, source_target_pairs={{0,8},{1,9},{2,10},{3,11},{4,12},{5,13},{6,14},{7,15},{16,24},{17,... | collective-permute-start | bytes 589832 | tf_op jit(solution)/shard_map/ppermute | solution.py:18
  59.4 0.7 copy-start.3

commit v13 on v12

--- a/solution.py
+++ b/solution.py
@@ -28,15 +28,18 @@
     return total - value
 
 
-def embed_kernel(ticks_ref, prev_ref, conv_ref, gain_ref, qkv_w_ref,
-                 emb_ref, q_ref, k_ref, v_ref, total_ref, first_ref, wide_ref):
+def embed_kernel(ticks_ref, prev_ref, conv_ref, gain_ref, qkv_hbm,
+                 emb_ref, q_ref, k_ref, v_ref, total_ref, first_ref, wide_ref, qkv_w_ref, copy_sem):
     b = pl.program_id(0)
     block_ticks = ticks_ref.shape[0]
     tokens = block_ticks // STRIDE
     model_width = emb_ref.shape[1]
 
-    @pl.when(b == 0)
-    def _():
+    weight_copy = pltpu.make_async_copy(qkv_hbm, qkv_w_ref, copy_sem)
+
+    @pl.when(b == 0)
+    def _():
+        weight_copy.start()
         wide_ref[0:STRIDE, :] = prev_ref[STRIDE : 2 * STRIDE, :].astype(jnp.float32)
 
     @pl.when(b > 0)
@@ -51,6 +54,10 @@
     embed_f = emb.astype(jnp.float32)
     mean_sq = jnp.mean(embed_f * embed_f, axis=-1, keepdims=True)
     normed = (embed_f * lax.rsqrt(mean_sq + 1e-05) * gain_ref[...][None, :]).astype(jnp.bfloat16)
+
+    @pl.when(b == 0)
+    def _():
+        weight_copy.wait()
 
     def project(part):
         weight = qkv_w_ref[:, part * model_width : (part + 1) * model_width]
@@ -102,9 +109,15 @@
             inside_ref[rows_at : rows_at + part, cols] = inside
 
 
-def out_kernel(q_ref, start_ref, total_ref, received_ref, local_ref, first_ref, inside_ref, emb_ref, hgain_ref, out_w_ref,
-               out_ref, att_ref):
+def out_kernel(q_ref, start_ref, total_ref, received_ref, local_ref, first_ref, inside_ref, emb_ref, hgain_ref, out_hbm,
+               out_ref, att_ref, out_w_ref, copy_sem):
     b = pl.program_id(0)
+    weight_copy = pltpu.make_async_copy(out_hbm, out_w_ref, copy_sem)
+
+    @pl.when(b == 0)
+    def _():
+        weight_copy.start()
+
     model_width = out_ref.shape[1]
     lane = lax.broadcasted_iota(jnp.int32, (1, PAIR), 1)
     first = lane < PAIR // 2
@@ -126,6 +139,11 @@
         scale = jnp.where(first, lax.rsqrt(sum_first / head_size + 1e-06),
                           lax.rsqrt(sum_second / head_size + 1e-06))
         att_ref[:, cols] = (combined * scale * hgain_ref[:, cols]).astype(jnp.bfloat16)
+
+    @pl.when(b == 0)
+    def _():
+        weight_copy.wait()
+
     out = emb_ref[...].astype(jnp.float32) + jnp.dot(att_ref[...], out_w_ref[...],
                                                      preferred_element_type=jnp.float32)
     out_ref[...] = out.astype(jnp.bfloat16)
@@ -155,13 +173,15 @@
             full((2 * STRIDE, feat)),
             full(conv_weight.shape),
             full((model_width,)),
-            full(qkv_weight.shape),
+            pl.BlockSpec(memory_space=pl.ANY),
         ],
         out_specs=[rows_spec, rows_spec, rows_spec, rows_spec, state_spec, state_spec],
         out_shape=[jax.ShapeDtypeStruct((token_count, model_width), jnp.bfloat16)] * 4 + [
             jax.ShapeDtypeStruct((pairs, head_size, PAIR), jnp.float32),
         ] * 2,
-        scratch_shapes=[pltpu.VMEM((block_ticks + STRIDE, feat), jnp.float32)],
+        scratch_shapes=[pltpu.VMEM((block_ticks + STRIDE, feat), jnp.float32),
+                        pltpu.VMEM(qkv_weight.shape, qkv_weight.dtype),
+                        pltpu.SemaphoreType.DMA(())],
         compiler_params=pltpu.CompilerParams(dimension_semantics=("arbitrary",)),
     )(ticks, prev, conv_weight, norm_gain, qkv_weight)
 
@@ -225,11 +245,13 @@
             rows_spec,
             rows_spec,
             full((1, model_width)),
-            full(out_weight.shape),
+            pl.BlockSpec(memory_space=pl.ANY),
         ],
         out_specs=rows_spec,
         out_shape=jax.ShapeDtypeStruct((token_count, model_width), jnp.bfloat16),
-        scratch_shapes=[pltpu.VMEM((BLK, model_width), jnp.bfloat16)],
+        scratch_shapes=[pltpu.VMEM((BLK, model_width), jnp.bfloat16),
+                        pltpu.VMEM(out_weight.shape, out_weight.dtype),
+                        pltpu.SemaphoreType.DMA(())],
         compiler_params=pltpu.CompilerParams(dimension_semantics=("arbitrary",)),
     )(queries, packed_in, total, received, local, first_state, inside, emb, head_gain.reshape(1, model_width), out_weight)
 

time: 67.9 us -> 67.6 us (level)
    pallas_call x1, Pallas kernels: 14.7 us -> 14 us  [shards(): pl.pallas_call(embed_kernel, grid=(blocks,), in_specs=[pl.BlockSpec((bloc...]
where the time goes in v13:
time: 67.6 us; the launch traced here: 67.2 us
  Pallas kernels  37.7 us (56%)
  waiting for transfers between devices  17.3 us (26%)
  starting transfers between devices  8.15 us (12%)
  local copies, waits for them, and re-layouts  3.76 us (6%)
    ppermute x5, waiting for transfers between devices, from_behind(): lax.ppermute(value, axis, [(source, source + steps) for source in range(i...  17.3 us
    pallas_call x4, Pallas kernels, inside_block(): pl.pallas_call(kernel, grid=(1,), in_specs=in_specs, out_specs=spec, out_...  16 us
    pallas_call x1, Pallas kernels, shards(): pl.pallas_call(embed_kernel, grid=(blocks,), in_specs=[pl.BlockSpec((bloc...  14 us
    ppermute x5, starting transfers between devices, from_behind(): lax.ppermute(value, axis, [(source, source + steps) for source in range(i...  8.15 us
    pallas_call x1, Pallas kernels, shards(): pl.pallas_call(out_kernel, grid=(blocks,), in_specs=[rows_spec, state_spe...  7.72 us
  transfers between devices with their start and end apart: 5, of which 5 were waited for; matrix products, arithmetic and copies ran while one was open for 3% of the time, Pallas kernels for 24%

profile of v13, /device:TPU:30, one launch (start us, length us, event | category | flops | bytes accessed | tf_op | source)
XLA Modules:
  0.0 67.2 jit_solution(15561940391704431156)
XLA Ops:
  0.0 0.7 %slice.3 = bf16[16,128]{1,0:T(8,128)(2,1)S(1)} slice(bf16[8192,128]{1,0:T(8,128)(2,1)} %ticks_ref.1), slice={[8176:8192], [0:128]} | slice | bytes 8192 | tf_op jit(solution)/shard_map/slice | solution.py:165
  0.7 1.9 %collective-permute-start = (bf16[16,128]{1,0:T(8,128)(2,1)S(1)}, bf16[16,128]{1,0:T(8,128)(2,1)S(1)}, u32[]{:S(2)}, u32[]{:S(2)}) collective-permute-start(bf16[16,128]{1,0:T(8,128)(2,1)S(1)} %slice.3), channel_id=1, source_target_pairs={{0,1},{1,2},{2,3},{3,4},{4,5},{5,6},{6,7},{7,8},{8,9},{9,10},{10,1... | collective-permute-start | bytes 12296 | tf_op jit(solution)/shard_map/ppermute | solution.py:18
  2.6 3.0 %collective-permute-done.prev_ref = bf16[16,128]{1,0:T(8,128)(2,1)S(1)} collective-permute-done((bf16[16,128]{1,0:T(8,128)(2,1)S(1)}, bf16[16,128]{1,0:T(8,128)(2,1)S(1)}, u32[]{:S(2)}, u32[]{:S(2)}) %collective-permute-start) | collective-permute-done | bytes 4128 | tf_op jit(solution)/shard_map/ppermute | solution.py:18
  5.6 0.0 copy-start.4
  5.6 0.6 copy-done.4
  6.2 14.0 %shard_map.73 = (bf16[1024,768]{1,0:T(8,128)(2,1)}, bf16[1024,768]{1,0:T(8,128)(2,1)}, bf16[1024,768]{1,0:T(8,128)(2,1)}, bf16[1024,768]{1,0:T(8,128)(2,1)}, f32...) custom-call(bf16[8192,128]{1,0:T(8,128)(2,1)} %ticks_ref.1, bf16[16,128]{1,0:T(8,128)(2,1)} %copy-done.4, ...), custom_call_target="tpu_custom_call" | custom-call | tf_op jit(solution)/shard_map/pallas_call | solution.py:168
  20.2 0.0 copy-start
  20.2 2.1 %collective-permute-start.1 = (f32[6,64,128]{2,1,0:T(8,128)}, f32[6,64,128]{2,1,0:T(8,128)S(1)}, u32[]{:S(2)}, u32[]{:S(2)}) collective-permute-start(f32[6,64,128]{2,1,0:T(8,128)} %get-tuple-element.39.local_ref), channel_id=1, source_target_pairs={{0,1},{1,2},{2,3},{3,4},{4,5},{5,6},{6,7},{7,8},{8,9},{9,10},{10,1... | collective-permute-start | bytes 589832 | tf_op jit(solution)/shard_map/ppermute | solution.py:18
  22.2 4.0 %shard_map.74.earlier_ref = f32[1024,768]{1,0:T(8,128)} custom-call(bf16[1024,768]{1,0:T(8,128)(2,1)} %get-tuple-element.57.q_ref, bf16[1024,768]{1,0:T(8,128)(2,1)} %get-tuple-element.58.k_ref, bf16[1024,768]{1,0:T(8,128)(2,1)} %get-tuple-element.59.v_ref), custom_call_target="tpu_custom_call" | custom-call | flops 805306368 | bytes 1966080 | tf_op jit(solution)/shard_map/pallas_call | solution.py:202
  26.2 1.3 %collective-permute-done.1 = f32[6,64,128]{2,1,0:T(8,128)S(1)} collective-permute-done((f32[6,64,128]{2,1,0:T(8,128)}, f32[6,64,128]{2,1,0:T(8,128)S(1)}, u32[]{:S(2)}, u32[]{:S(2)}) %collective-permute-start.1) | collective-permute-done | bytes 196640 | tf_op jit(solution)/shard_map/ppermute | solution.py:18
  27.5 0.0 copy-done
  27.5 1.3 %collective-permute-start.2 = (f32[6,64,128]{2,1,0:T(8,128)S(1)}, f32[6,64,128]{2,1,0:T(8,128)S(1)}, u32[]{:S(2)}, u32[]{:S(2)}) collective-permute-start(f32[6,64,128]{2,1,0:T(8,128)S(1)} %add.9), channel_id=1, source_target_pairs={{0,2},{1,3},{2,4},{3,5},{4,6},{5,7},{6,8},{7,9},{8,10},{9,11},{10,... | collective-permute-start | bytes 589832 | tf_op jit(solution)/shard_map/ppermute | solution.py:18
  28.8 4.0 %shard_map.75.earlier_ref = f32[1024,768]{1,0:T(8,128)} custom-call(bf16[1024,768]{1,0:T(8,128)(2,1)} %get-tuple-element.57.q_ref, bf16[1024,768]{1,0:T(8,128)(2,1)} %get-tuple-element.58.k_ref, bf16[1024,768]{1,0:T(8,128)(2,1)} %get-tuple-element.59.v_ref, f32[1024,768]{1,0:T(8,128)} %shard_map.74.earlier_ref), custom_call_target="tpu_custom_call", output_to_operand_aliasing={{}: (3, {})} | custom-call | flops 805306368 | bytes 1966080 | tf_op jit(solution)/shard_map/pallas_call | solution.py:202
  32.8 2.6 %collective-permute-done.2 = f32[6,64,128]{2,1,0:T(8,128)S(1)} collective-permute-done((f32[6,64,128]{2,1,0:T(8,128)S(1)}, f32[6,64,128]{2,1,0:T(8,128)S(1)}, u32[]{:S(2)}, u32[]{:S(2)}) %collective-permute-start.2) | collective-permute-done | bytes 196640 | tf_op jit(solution)/shard_map/ppermute | solution.py:18
  35.4 0.0 copy-start.2
  35.5 0.0 copy-start.5
  35.5 1.4 %collective-permute-start.3 = (f32[6,64,128]{2,1,0:T(8,128)S(1)}, f32[6,64,128]{2,1,0:T(8,128)S(1)}, u32[]{:S(2)}, u32[]{:S(2)}) collective-permute-start(f32[6,64,128]{2,1,0:T(8,128)S(1)} %add.10), channel_id=1, source_target_pairs={{0,4},{1,5},{2,6},{3,7},{4,8},{5,9},{6,10},{7,11},{8,12},{9,13},{1... | collective-permute-start | bytes 589832 | tf_op jit(solution)/shard_map/ppermute | solution.py:18
  36.9 4.0 %shard_map.76.earlier_ref = f32[1024,768]{1,0:T(8,128)} custom-call(bf16[1024,768]{1,0:T(8,128)(2,1)} %get-tuple-element.57.q_ref, bf16[1024,768]{1,0:T(8,128)(2,1)} %get-tuple-element.58.k_ref, bf16[1024,768]{1,0:T(8,128)(2,1)} %get-tuple-element.59.v_ref, f32[1024,768]{1,0:T(8,128)} %shard_map.75.earlier_ref), custom_call_target="tpu_custom_call", output_to_operand_aliasing={{}: (3, {})} | custom-call | flops 805306368 | bytes 1966080 | tf_op jit(solution)/shard_map/pallas_call | solution.py:202
  40.9 4.3 %collective-permute-done.3 = f32[6,64,128]{2,1,0:T(8,128)S(1)} collective-permute-done((f32[6,64,128]{2,1,0:T(8,128)S(1)}, f32[6,64,128]{2,1,0:T(8,128)S(1)}, u32[]{:S(2)}, u32[]{:S(2)}) %collective-permute-start.3) | collective-permute-done | bytes 196640 | tf_op jit(solution)/shard_map/ppermute | solution.py:18
  45.2 0.0 copy-start.1
  45.3 1.5 %collective-permute-start.4 = (f32[6,64,128]{2,1,0:T(8,128)S(1)}, f32[6,64,128]{2,1,0:T(8,128)S(1)}, u32[]{:S(2)}, u32[]{:S(2)}) collective-permute-start(f32[6,64,128]{2,1,0:T(8,128)S(1)} %add.11.total_ref), channel_id=1, source_target_pairs={{0,8},{1,9},{2,10},{3,11},{4,12},{5,13},{6,14},{7,15},{16,24},{17,... | collective-permute-start | bytes 589832 | tf_op jit(solution)/shard_map/ppermute | solution.py:18
  46.7 0.0 copy-done.2
  46.7 0.3 copy.13
  47.1 0.9 %reshape.10.start_ref = f32[6,64,128]{2,1,0:T(8,128)} reshape(f32[6,64,2,64]{3,2,1,0:T(2,128)S(1)} %bitcast.4) | data formatting | bytes 393216 | tf_op jit(solution)/shard_map/reshape | solution.py:233
  48.0 0.0 copy-done.5
  48.0 0.6 reshape.11.hgain_ref
  48.6 4.0 %shard_map.77.inside_ref = f32[1024,768]{1,0:T(8,128)} custom-call(bf16[1024,768]{1,0:T(8,128)(2,1)} %get-tuple-element.57.q_ref, bf16[1024,768]{1,0:T(8,128)(2,1)} %get-tuple-element.58.k_ref, bf16[1024,768]{1,0:T(8,128)(2,1)} %get-tuple-element.59.v_ref, f32[1024,768]{1,0:T(8,128)} %shard_map.76.earlier_ref), custom_call_target="tpu_custom_call", output_to_operand_aliasing={{}: (3, {})} | custom-call | flops 805306368 | bytes 1966080 | tf_op jit(solution)/shard_map/pallas_call | solution.py:202
  52.5 0.0 copy-done.1
  52.5 6.1 %collective-permute-done.4.received_ref = f32[6,64,128]{2,1,0:T(8,128)S(1)} collective-permute-done((f32[6,64,128]{2,1,0:T(8,128)S(1)}, f32[6,64,128]{2,1,0:T(8,128)S(1)}, u32[]{:S(2)}, u32[]{:S(2)}) %collective-permute-start.4) | collective-permute-done | bytes 196640 | tf_op jit(solution)/shard_map/ppermute | solution.py:18
  58.7 0.0 copy-start.3
  58.7 0.7 copy-done.3
  59.3 7.7 %shard_map.78 = bf16[1024,768]{1,0:T(8,128)(2,1)} custom-call(bf16[1024,768]{1,0:T(8,128)(2,1)} %get-tuple-element.57.q_ref, f32[6,64,128]{2,1,0:T(8,128)} %reshape.10.start_ref, f32[6,64,128]{2,1,0:T(8,128)} %copy-done.1, f32[6,64,128]{2,1,0:T(8,128)} %copy-done.3, f32[6,64,128]{2,1,0:T(8,128)} %get-tuple-element.39.local_ref, ...), custom_call_target="tpu_custom_call" | custom-call | tf_op jit(solution)/shard_map/pallas_call | solution.py:235
  (3 shorter events, 0.1 us)
Async XLA Ops:
  0.7 4.9 %collective-permute-start = (bf16[16,128]{1,0:T(8,128)(2,1)S(1)}, bf16[16,128]{1,0:T(8,128)(2,1)S(1)}, u32[]{:S(2)}, u32[]{:S(2)}) collective-permute-start(bf16[16,128]{1,0:T(8,128)(2,1)S(1)} %slice.3), channel_id=1, source_target_pairs={{0,1},{1,2},{2,3},{3,4},{4,5},{5,6},{6,7},{7,8},{8,9},{9,10},{10,1... | collective-permute-start | bytes 12296 | tf_op jit(solution)/shard_map/ppermute | solution.py:18
  5.6 0.6 copy-start.4
  20.2 7.3 %copy-start = (f32[6,64,128]{2,1,0:T(8,128)S(1)}, f32[6,64,128]{2,1,0:T(8,128)}, u32[]{:S(2)}) copy-start(f32[6,64,128]{2,1,0:T(8,128)} %get-tuple-element.39.local_ref) | copy-start | bytes 589828
  20.2 7.3 %collective-permute-start.1 = (f32[6,64,128]{2,1,0:T(8,128)}, f32[6,64,128]{2,1,0:T(8,128)S(1)}, u32[]{:S(2)}, u32[]{:S(2)}) collective-permute-start(f32[6,64,128]{2,1,0:T(8,128)} %get-tuple-element.39.local_ref), channel_id=1, source_target_pairs={{0,1},{1,2},{2,3},{3,4},{4,5},{5,6},{6,7},{7,8},{8,9},{9,10},{10,1... | collective-permute-start | bytes 589832 | tf_op jit(solution)/shard_map/ppermute | solution.py:18
  27.5 7.9 %collective-permute-start.2 = (f32[6,64,128]{2,1,0:T(8,128)S(1)}, f32[6,64,128]{2,1,0:T(8,128)S(1)}, u32[]{:S(2)}, u32[]{:S(2)}) collective-permute-start(f32[6,64,128]{2,1,0:T(8,128)S(1)} %add.9), channel_id=1, source_target_pairs={{0,2},{1,3},{2,4},{3,5},{4,6},{5,7},{6,8},{7,9},{8,10},{9,11},{10,... | collective-permute-start | bytes 589832 | tf_op jit(solution)/shard_map/ppermute | solution.py:18
  35.4 11.3 %copy-start.2 = (f32[12,64,64]{2,1,0:T(8,128)S(1)}, f32[12,64,64]{2,1,0:T(8,128)}, u32[]{:S(2)}) copy-start(f32[12,64,64]{2,1,0:T(8,128)} %param.13) | copy-start | bytes 589828
  35.5 12.5 %copy-start.5 = (f32[768]{0:T(1024)S(1)}, f32[768]{0:T(1024)}, u32[]{:S(2)}) copy-start(f32[768]{0:T(1024)} %param.11) | copy-start | bytes 9220
  35.5 9.8 %collective-permute-start.3 = (f32[6,64,128]{2,1,0:T(8,128)S(1)}, f32[6,64,128]{2,1,0:T(8,128)S(1)}, u32[]{:S(2)}, u32[]{:S(2)}) collective-permute-start(f32[6,64,128]{2,1,0:T(8,128)S(1)} %add.10), channel_id=1, source_target_pairs={{0,4},{1,5},{2,6},{3,7},{4,8},{5,9},{6,10},{7,11},{8,12},{9,13},{1... | collective-permute-start | bytes 589832 | tf_op jit(solution)/shard_map/ppermute | solution.py:18
  45.2 7.3 %copy-start.1 = (f32[6,64,128]{2,1,0:T(8,128)}, f32[6,64,128]{2,1,0:T(8,128)S(1)}, u32[]{:S(2)}) copy-start(f32[6,64,128]{2,1,0:T(8,128)S(1)} %add.11.total_ref) | copy-start | bytes 589828
  45.3 13.4 %collective-permute-start.4 = (f32[6,64,128]{2,1,0:T(8,128)S(1)}, f32[6,64,128]{2,1,0:T(8,128)S(1)}, u32[]{:S(2)}, u32[]{:S(2)}) collective-permute-start(f32[6,64,128]{2,1,0:T(8,128)S(1)} %add.11.total_ref), channel_id=1, source_target_pairs={{0,8},{1,9},{2,10},{3,11},{4,12},{5,13},{6,14},{7,15},{16,24},{17,... | collective-permute-start | bytes 589832 | tf_op jit(solution)/shard_map/ppermute | solution.py:18
  58.7 0.7 copy-start.3

commit v14 on v12

--- a/solution.py
+++ b/solution.py
@@ -28,15 +28,25 @@
     return total - value
 
 
-def embed_kernel(ticks_ref, prev_ref, conv_ref, gain_ref, qkv_w_ref,
-                 emb_ref, q_ref, k_ref, v_ref, total_ref, first_ref, wide_ref):
+def embed_kernel(ticks_ref, prev_ref, conv_hbm, gain_ref, qkv_hbm,
+                 emb_ref, q_ref, k_ref, v_ref, total_ref, first_ref, wide_ref, qkv_w_ref, copy_sem,
+                 conv_ref, conv_sems):
     b = pl.program_id(0)
     block_ticks = ticks_ref.shape[0]
     tokens = block_ticks // STRIDE
     model_width = emb_ref.shape[1]
 
-    @pl.when(b == 0)
-    def _():
+    weight_copy = pltpu.make_async_copy(qkv_hbm, qkv_w_ref, copy_sem)
+    width = conv_hbm.shape[0] // 2
+    conv_copies = [pltpu.make_async_copy(conv_hbm.at[pl.ds(part * width, width)],
+                                         conv_ref.at[pl.ds(part * width, width)], conv_sems.at[part])
+                   for part in range(2)]
+
+    @pl.when(b == 0)
+    def _():
+        for copy in conv_copies:
+            copy.start()
+        weight_copy.start()
         wide_ref[0:STRIDE, :] = prev_ref[STRIDE : 2 * STRIDE, :].astype(jnp.float32)
 
     @pl.when(b > 0)
@@ -46,11 +56,27 @@
     wide_ref[STRIDE:, :] = ticks_ref[...].astype(jnp.float32)
     pieces = [wide_ref[pl.ds(j, tokens, stride=STRIDE), :] for j in range(2 * STRIDE)]
     lhs = jnp.concatenate(pieces, axis=1).astype(jnp.bfloat16)
-    emb = jnp.dot(lhs, conv_ref[...], preferred_element_type=jnp.float32).astype(jnp.bfloat16)
+
+    @pl.when(b == 0)
+    def _():
+        conv_copies[0].wait()
+
+    emb_f = jnp.dot(lhs[:, :width], conv_ref[:width, :], preferred_element_type=jnp.float32)
+
+    @pl.when(b == 0)
+    def _():
+        conv_copies[1].wait()
+
+    emb_f = emb_f + jnp.dot(lhs[:, width:], conv_ref[width:, :], preferred_element_type=jnp.float32)
+    emb = emb_f.astype(jnp.bfloat16)
     emb_ref[...] = emb
     embed_f = emb.astype(jnp.float32)
     mean_sq = jnp.mean(embed_f * embed_f, axis=-1, keepdims=True)
     normed = (embed_f * lax.rsqrt(mean_sq + 1e-05) * gain_ref[...][None, :]).astype(jnp.bfloat16)
+
+    @pl.when(b == 0)
+    def _():
+        weight_copy.wait()
 
     def project(part):
         weight = qkv_w_ref[:, part * model_width : (part + 1) * model_width]
@@ -153,15 +179,19 @@
         in_specs=[
             pl.BlockSpec((block_ticks, feat), lambda b: (b, 0)),
             full((2 * STRIDE, feat)),
-            full(conv_weight.shape),
+            pl.BlockSpec(memory_space=pl.ANY),
             full((model_width,)),
-            full(qkv_weight.shape),
+            pl.BlockSpec(memory_space=pl.ANY),
         ],
         out_specs=[rows_spec, rows_spec, rows_spec, rows_spec, state_spec, state_spec],
         out_shape=[jax.ShapeDtypeStruct((token_count, model_width), jnp.bfloat16)] * 4 + [
             jax.ShapeDtypeStruct((pairs, head_size, PAIR), jnp.float32),
         ] * 2,
-        scratch_shapes=[pltpu.VMEM((block_ticks + STRIDE, feat), jnp.float32)],
+        scratch_shapes=[pltpu.VMEM((block_ticks + STRIDE, feat), jnp.float32),
+                        pltpu.VMEM(qkv_weight.shape, qkv_weight.dtype),
+                        pltpu.SemaphoreType.DMA(()),
+                        pltpu.VMEM(conv_weight.shape, conv_weight.dtype),
+                        pltpu.SemaphoreType.DMA((2,))],
         compiler_params=pltpu.CompilerParams(dimension_semantics=("arbitrary",)),
     )(ticks, prev, conv_weight, norm_gain, qkv_weight)
 

time: 67.9 us -> 69.3 us (1.021)
  Pallas kernels: 38.2 us -> 39.6 us
    pallas_call x1, Pallas kernels: 14.7 us -> 16.2 us  [shards(): pl.pallas_call(embed_kernel, grid=(blocks,), in_specs=[pl.BlockSpec((bloc...]
  transfers between devices with their start and end apart: 5 -> 5, of which waited for: 5 -> 5; matrix products, arithmetic and copies ran while one was open for 3% -> 3% of each run, Pallas kernels for 24% -> 23%
where the time goes in v14:
time: 69.3 us; the launch traced here: 68.9 us
  Pallas kernels  39.6 us (57%)
  waiting for transfers between devices  17.2 us (25%)
  starting transfers between devices  8.15 us (12%)
  local copies, waits for them, and re-layouts  3.76 us (5%)
    ppermute x5, waiting for transfers between devices, from_behind(): lax.ppermute(value, axis, [(source, source + steps) for source in range(i...  17.2 us
    pallas_call x1, Pallas kernels, shards(): pl.pallas_call(embed_kernel, grid=(blocks,), in_specs=[pl.BlockSpec((bloc...  16.2 us
    pallas_call x4, Pallas kernels, inside_block(): pl.pallas_call(kernel, grid=(1,), in_specs=in_specs, out_specs=spec, out_...  16 us
    ppermute x5, starting transfers between devices, from_behind(): lax.ppermute(value, axis, [(source, source + steps) for source in range(i...  8.15 us
    pallas_call x1, Pallas kernels, shards(): pl.pallas_call(out_kernel, grid=(blocks,), in_specs=[rows_spec, state_spe...  7.41 us
  transfers between devices with their start and end apart: 5, of which 5 were waited for; matrix products, arithmetic and copies ran while one was open for 3% of the time, Pallas kernels for 23%

profile of v14, /device:TPU:30, one launch (start us, length us, event | category | flops | bytes accessed | tf_op | source)
XLA Modules:
  0.0 68.9 jit_solution(17056184384226962617)
XLA Ops:
  0.0 0.7 slice.3
  0.7 1.9 %collective-permute-start = (bf16[16,128]{1,0:T(8,128)(2,1)S(1)}, bf16[16,128]{1,0:T(8,128)(2,1)S(1)}, u32[]{:S(2)}, u32[]{:S(2)}) collective-permute-start(bf16[16,128]{1,0:T(8,128)(2,1)S(1)} %slice.3), channel_id=1, source_target_pairs={{0,1},{1,2},{2,3},{3,4},{4,5},{5,6},{6,7},{7,8},{8,9},{9,10},{10,1... | collective-permute-start | bytes 12296 | tf_op jit(solution)/shard_map/ppermute | solution.py:18
  2.6 3.0 %collective-permute-done.prev_ref = bf16[16,128]{1,0:T(8,128)(2,1)S(1)} collective-permute-done((bf16[16,128]{1,0:T(8,128)(2,1)S(1)}, bf16[16,128]{1,0:T(8,128)(2,1)S(1)}, u32[]{:S(2)}, u32[]{:S(2)}) %collective-permute-start) | collective-permute-done | bytes 4128 | tf_op jit(solution)/shard_map/ppermute | solution.py:18
  5.6 0.0 copy-start.4
  5.6 0.6 copy-done.4
  6.2 16.2 %shard_map.73 = (bf16[1024,768]{1,0:T(8,128)(2,1)}, bf16[1024,768]{1,0:T(8,128)(2,1)}, bf16[1024,768]{1,0:T(8,128)(2,1)}, bf16[1024,768]{1,0:T(8,128)(2,1)}, f32...) custom-call(bf16[8192,128]{1,0:T(8,128)(2,1)} %ticks_ref.1, bf16[16,128]{1,0:T(8,128)(2,1)} %copy-done.4, ...), custom_call_target="tpu_custom_call" | custom-call | tf_op jit(solution)/shard_map/pallas_call | solution.py:176
  22.3 0.0 copy-start
  22.4 2.1 %collective-permute-start.1 = (f32[6,64,128]{2,1,0:T(8,128)}, f32[6,64,128]{2,1,0:T(8,128)S(1)}, u32[]{:S(2)}, u32[]{:S(2)}) collective-permute-start(f32[6,64,128]{2,1,0:T(8,128)} %get-tuple-element.39.local_ref), channel_id=1, source_target_pairs={{0,1},{1,2},{2,3},{3,4},{4,5},{5,6},{6,7},{7,8},{8,9},{9,10},{10,1... | collective-permute-start | bytes 589832 | tf_op jit(solution)/shard_map/ppermute | solution.py:18
  24.4 4.0 %shard_map.74.earlier_ref = f32[1024,768]{1,0:T(8,128)} custom-call(bf16[1024,768]{1,0:T(8,128)(2,1)} %get-tuple-element.57.q_ref, bf16[1024,768]{1,0:T(8,128)(2,1)} %get-tuple-element.58.k_ref, bf16[1024,768]{1,0:T(8,128)(2,1)} %get-tuple-element.59.v_ref), custom_call_target="tpu_custom_call" | custom-call | flops 805306368 | bytes 1966080 | tf_op jit(solution)/shard_map/pallas_call | solution.py:212
  28.4 1.3 %collective-permute-done.1 = f32[6,64,128]{2,1,0:T(8,128)S(1)} collective-permute-done((f32[6,64,128]{2,1,0:T(8,128)}, f32[6,64,128]{2,1,0:T(8,128)S(1)}, u32[]{:S(2)}, u32[]{:S(2)}) %collective-permute-start.1) | collective-permute-done | bytes 196640 | tf_op jit(solution)/shard_map/ppermute | solution.py:18
  29.7 0.0 copy-done
  29.7 1.3 %collective-permute-start.2 = (f32[6,64,128]{2,1,0:T(8,128)S(1)}, f32[6,64,128]{2,1,0:T(8,128)S(1)}, u32[]{:S(2)}, u32[]{:S(2)}) collective-permute-start(f32[6,64,128]{2,1,0:T(8,128)S(1)} %add.9), channel_id=1, source_target_pairs={{0,2},{1,3},{2,4},{3,5},{4,6},{5,7},{6,8},{7,9},{8,10},{9,11},{10,... | collective-permute-start | bytes 589832 | tf_op jit(solution)/shard_map/ppermute | solution.py:18
  31.0 4.0 %shard_map.75.earlier_ref = f32[1024,768]{1,0:T(8,128)} custom-call(bf16[1024,768]{1,0:T(8,128)(2,1)} %get-tuple-element.57.q_ref, bf16[1024,768]{1,0:T(8,128)(2,1)} %get-tuple-element.58.k_ref, bf16[1024,768]{1,0:T(8,128)(2,1)} %get-tuple-element.59.v_ref, f32[1024,768]{1,0:T(8,128)} %shard_map.74.earlier_ref), custom_call_target="tpu_custom_call", output_to_operand_aliasing={{}: (3, {})} | custom-call | flops 805306368 | bytes 1966080 | tf_op jit(solution)/shard_map/pallas_call | solution.py:212
  35.0 2.6 %collective-permute-done.2 = f32[6,64,128]{2,1,0:T(8,128)S(1)} collective-permute-done((f32[6,64,128]{2,1,0:T(8,128)S(1)}, f32[6,64,128]{2,1,0:T(8,128)S(1)}, u32[]{:S(2)}, u32[]{:S(2)}) %collective-permute-start.2) | collective-permute-done | bytes 196640 | tf_op jit(solution)/shard_map/ppermute | solution.py:18
  37.6 0.0 copy-start.2
  37.6 0.0 copy-start.5
  37.7 1.4 %collective-permute-start.3 = (f32[6,64,128]{2,1,0:T(8,128)S(1)}, f32[6,64,128]{2,1,0:T(8,128)S(1)}, u32[]{:S(2)}, u32[]{:S(2)}) collective-permute-start(f32[6,64,128]{2,1,0:T(8,128)S(1)} %add.10), channel_id=1, source_target_pairs={{0,4},{1,5},{2,6},{3,7},{4,8},{5,9},{6,10},{7,11},{8,12},{9,13},{1... | collective-permute-start | bytes 589832 | tf_op jit(solution)/shard_map/ppermute | solution.py:18
  39.1 4.1 %shard_map.76.earlier_ref = f32[1024,768]{1,0:T(8,128)} custom-call(bf16[1024,768]{1,0:T(8,128)(2,1)} %get-tuple-element.57.q_ref, bf16[1024,768]{1,0:T(8,128)(2,1)} %get-tuple-element.58.k_ref, bf16[1024,768]{1,0:T(8,128)(2,1)} %get-tuple-element.59.v_ref, f32[1024,768]{1,0:T(8,128)} %shard_map.75.earlier_ref), custom_call_target="tpu_custom_call", output_to_operand_aliasing={{}: (3, {})} | custom-call | flops 805306368 | bytes 1966080 | tf_op jit(solution)/shard_map/pallas_call | solution.py:212
  43.2 4.2 %collective-permute-done.3 = f32[6,64,128]{2,1,0:T(8,128)S(1)} collective-permute-done((f32[6,64,128]{2,1,0:T(8,128)S(1)}, f32[6,64,128]{2,1,0:T(8,128)S(1)}, u32[]{:S(2)}, u32[]{:S(2)}) %collective-permute-start.3) | collective-permute-done | bytes 196640 | tf_op jit(solution)/shard_map/ppermute | solution.py:18
  47.4 0.0 copy-start.1
  47.4 1.5 %collective-permute-start.4 = (f32[6,64,128]{2,1,0:T(8,128)S(1)}, f32[6,64,128]{2,1,0:T(8,128)S(1)}, u32[]{:S(2)}, u32[]{:S(2)}) collective-permute-start(f32[6,64,128]{2,1,0:T(8,128)S(1)} %add.11.total_ref), channel_id=1, source_target_pairs={{0,8},{1,9},{2,10},{3,11},{4,12},{5,13},{6,14},{7,15},{16,24},{17,... | collective-permute-start | bytes 589832 | tf_op jit(solution)/shard_map/ppermute | solution.py:18
  48.9 0.0 copy-done.2
  48.9 0.3 copy.13
  49.2 0.9 %reshape.10.start_ref = f32[6,64,128]{2,1,0:T(8,128)} reshape(f32[6,64,2,64]{3,2,1,0:T(2,128)S(1)} %bitcast.4) | data formatting | bytes 393216 | tf_op jit(solution)/shard_map/reshape | solution.py:243
  50.1 0.0 copy-done.5
  50.1 0.6 reshape.11.hgain_ref
  50.7 4.0 %shard_map.77.inside_ref = f32[1024,768]{1,0:T(8,128)} custom-call(bf16[1024,768]{1,0:T(8,128)(2,1)} %get-tuple-element.57.q_ref, bf16[1024,768]{1,0:T(8,128)(2,1)} %get-tuple-element.58.k_ref, bf16[1024,768]{1,0:T(8,128)(2,1)} %get-tuple-element.59.v_ref, f32[1024,768]{1,0:T(8,128)} %shard_map.76.earlier_ref), custom_call_target="tpu_custom_call", output_to_operand_aliasing={{}: (3, {})} | custom-call | flops 805306368 | bytes 1966080 | tf_op jit(solution)/shard_map/pallas_call | solution.py:212
  54.7 0.0 copy-done.1
  54.7 6.1 %collective-permute-done.4.received_ref = f32[6,64,128]{2,1,0:T(8,128)S(1)} collective-permute-done((f32[6,64,128]{2,1,0:T(8,128)S(1)}, f32[6,64,128]{2,1,0:T(8,128)S(1)}, u32[]{:S(2)}, u32[]{:S(2)}) %collective-permute-start.4) | collective-permute-done | bytes 196640 | tf_op jit(solution)/shard_map/ppermute | solution.py:18
  60.8 0.0 copy-start.3
  60.8 0.7 copy-done.3
  61.5 7.4 %shard_map.78 = bf16[1024,768]{1,0:T(8,128)(2,1)} custom-call(bf16[1024,768]{1,0:T(8,128)(2,1)} %get-tuple-element.57.q_ref, f32[6,64,128]{2,1,0:T(8,128)} %reshape.10.start_ref, f32[6,64,128]{2,1,0:T(8,128)} %copy-done.1, f32[6,64,128]{2,1,0:T(8,128)} %copy-done.3, f32[6,64,128]{2,1,0:T(8,128)} %get-tuple-element.39.local_ref, ...), custom_call_target="tpu_custom_call" | custom-call | tf_op jit(solution)/shard_map/pallas_call | solution.py:245
  (3 shorter events, 0.1 us)
Async XLA Ops:
  0.7 4.9 %collective-permute-start = (bf16[16,128]{1,0:T(8,128)(2,1)S(1)}, bf16[16,128]{1,0:T(8,128)(2,1)S(1)}, u32[]{:S(2)}, u32[]{:S(2)}) collective-permute-start(bf16[16,128]{1,0:T(8,128)(2,1)S(1)} %slice.3), channel_id=1, source_target_pairs={{0,1},{1,2},{2,3},{3,4},{4,5},{5,6},{6,7},{7,8},{8,9},{9,10},{10,1... | collective-permute-start | bytes 12296 | tf_op jit(solution)/shard_map/ppermute | solution.py:18
  5.6 0.6 copy-start.4
  22.3 7.3 %copy-start = (f32[6,64,128]{2,1,0:T(8,128)S(1)}, f32[6,64,128]{2,1,0:T(8,128)}, u32[]{:S(2)}) copy-start(f32[6,64,128]{2,1,0:T(8,128)} %get-tuple-element.39.local_ref) | copy-start | bytes 589828
  22.4 7.3 %collective-permute-start.1 = (f32[6,64,128]{2,1,0:T(8,128)}, f32[6,64,128]{2,1,0:T(8,128)S(1)}, u32[]{:S(2)}, u32[]{:S(2)}) collective-permute-start(f32[6,64,128]{2,1,0:T(8,128)} %get-tuple-element.39.local_ref), channel_id=1, source_target_pairs={{0,1},{1,2},{2,3},{3,4},{4,5},{5,6},{6,7},{7,8},{8,9},{9,10},{10,1... | collective-permute-start | bytes 589832 | tf_op jit(solution)/shard_map/ppermute | solution.py:18
  29.7 7.9 %collective-permute-start.2 = (f32[6,64,128]{2,1,0:T(8,128)S(1)}, f32[6,64,128]{2,1,0:T(8,128)S(1)}, u32[]{:S(2)}, u32[]{:S(2)}) collective-permute-start(f32[6,64,128]{2,1,0:T(8,128)S(1)} %add.9), channel_id=1, source_target_pairs={{0,2},{1,3},{2,4},{3,5},{4,6},{5,7},{6,8},{7,9},{8,10},{9,11},{10,... | collective-permute-start | bytes 589832 | tf_op jit(solution)/shard_map/ppermute | solution.py:18
  37.6 11.3 %copy-start.2 = (f32[12,64,64]{2,1,0:T(8,128)S(1)}, f32[12,64,64]{2,1,0:T(8,128)}, u32[]{:S(2)}) copy-start(f32[12,64,64]{2,1,0:T(8,128)} %param.13) | copy-start | bytes 589828
  37.6 12.5 %copy-start.5 = (f32[768]{0:T(1024)S(1)}, f32[768]{0:T(1024)}, u32[]{:S(2)}) copy-start(f32[768]{0:T(1024)} %param.11) | copy-start | bytes 9220
  37.7 9.7 %collective-permute-start.3 = (f32[6,64,128]{2,1,0:T(8,128)S(1)}, f32[6,64,128]{2,1,0:T(8,128)S(1)}, u32[]{:S(2)}, u32[]{:S(2)}) collective-permute-start(f32[6,64,128]{2,1,0:T(8,128)S(1)} %add.10), channel_id=1, source_target_pairs={{0,4},{1,5},{2,6},{3,7},{4,8},{5,9},{6,10},{7,11},{8,12},{9,13},{1... | collective-permute-start | bytes 589832 | tf_op jit(solution)/shard_map/ppermute | solution.py:18
  47.4 7.3 %copy-start.1 = (f32[6,64,128]{2,1,0:T(8,128)}, f32[6,64,128]{2,1,0:T(8,128)S(1)}, u32[]{:S(2)}) copy-start(f32[6,64,128]{2,1,0:T(8,128)S(1)} %add.11.total_ref) | copy-start | bytes 589828
  47.4 13.4 %collective-permute-start.4 = (f32[6,64,128]{2,1,0:T(8,128)S(1)}, f32[6,64,128]{2,1,0:T(8,128)S(1)}, u32[]{:S(2)}, u32[]{:S(2)}) collective-permute-start(f32[6,64,128]{2,1,0:T(8,128)S(1)} %add.11.total_ref), channel_id=1, source_target_pairs={{0,8},{1,9},{2,10},{3,11},{4,12},{5,13},{6,14},{7,15},{16,24},{17,... | collective-permute-start | bytes 589832 | tf_op jit(solution)/shard_map/ppermute | solution.py:18
  60.8 0.7 copy-start.3

commit v15 on v12

--- a/solution.py
+++ b/solution.py
@@ -28,15 +28,18 @@
     return total - value
 
 
-def embed_kernel(ticks_ref, prev_ref, conv_ref, gain_ref, qkv_w_ref,
-                 emb_ref, q_ref, k_ref, v_ref, total_ref, first_ref, wide_ref):
+def embed_kernel(ticks_ref, prev_ref, conv_ref, gain_ref, qkv_hbm,
+                 emb_ref, q_ref, k_ref, v_ref, total_ref, first_ref, wide_ref, qkv_w_ref, copy_sem):
     b = pl.program_id(0)
     block_ticks = ticks_ref.shape[0]
     tokens = block_ticks // STRIDE
     model_width = emb_ref.shape[1]
 
+    weight_copy = pltpu.make_async_copy(qkv_hbm, qkv_w_ref, copy_sem)
+
     @pl.when(b == 0)
     def _():
+        weight_copy.start()
         wide_ref[0:STRIDE, :] = prev_ref[STRIDE : 2 * STRIDE, :].astype(jnp.float32)
 
     @pl.when(b > 0)
@@ -51,6 +54,10 @@
     embed_f = emb.astype(jnp.float32)
     mean_sq = jnp.mean(embed_f * embed_f, axis=-1, keepdims=True)
     normed = (embed_f * lax.rsqrt(mean_sq + 1e-05) * gain_ref[...][None, :]).astype(jnp.bfloat16)
+
+    @pl.when(b == 0)
+    def _():
+        weight_copy.wait()
 
     def project(part):
         weight = qkv_w_ref[:, part * model_width : (part + 1) * model_width]
@@ -155,13 +162,15 @@
             full((2 * STRIDE, feat)),
             full(conv_weight.shape),
             full((model_width,)),
-            full(qkv_weight.shape),
+            pl.BlockSpec(memory_space=pl.ANY),
         ],
         out_specs=[rows_spec, rows_spec, rows_spec, rows_spec, state_spec, state_spec],
         out_shape=[jax.ShapeDtypeStruct((token_count, model_width), jnp.bfloat16)] * 4 + [
             jax.ShapeDtypeStruct((pairs, head_size, PAIR), jnp.float32),
         ] * 2,
-        scratch_shapes=[pltpu.VMEM((block_ticks + STRIDE, feat), jnp.float32)],
+        scratch_shapes=[pltpu.VMEM((block_ticks + STRIDE, feat), jnp.float32),
+                        pltpu.VMEM(qkv_weight.shape, qkv_weight.dtype),
+                        pltpu.SemaphoreType.DMA(())],
         compiler_params=pltpu.CompilerParams(dimension_semantics=("arbitrary",)),
     )(ticks, prev, conv_weight, norm_gain, qkv_weight)
 

time: 67.9 us -> 67.1 us (0.988)
  Pallas kernels: 38.2 us -> 37.4 us
    pallas_call x1, Pallas kernels: 14.7 us -> 14 us  [shards(): pl.pallas_call(embed_kernel, grid=(blocks,), in_specs=[pl.BlockSpec((bloc...]
where the time goes in v15:
time: 67.1 us; the launch traced here: 66.7 us
  Pallas kernels  37.4 us (56%)
  waiting for transfers between devices  17.3 us (26%)
  starting transfers between devices  8.15 us (12%)
  local copies, waits for them, and re-layouts  3.76 us (6%)
    ppermute x5, waiting for transfers between devices, from_behind(): lax.ppermute(value, axis, [(source, source + steps) for source in range(i...  17.3 us
    pallas_call x4, Pallas kernels, inside_block(): pl.pallas_call(kernel, grid=(1,), in_specs=in_specs, out_specs=spec, out_...  16 us
    pallas_call x1, Pallas kernels, shards(): pl.pallas_call(embed_kernel, grid=(blocks,), in_specs=[pl.BlockSpec((bloc...  14 us
    ppermute x5, starting transfers between devices, from_behind(): lax.ppermute(value, axis, [(source, source + steps) for source in range(i...  8.15 us
    pallas_call x1, Pallas kernels, shards(): pl.pallas_call(out_kernel, grid=(blocks,), in_specs=[rows_spec, state_spe...  7.41 us
  transfers between devices with their start and end apart: 5, of which 5 were waited for; matrix products, arithmetic and copies ran while one was open for 3% of the time, Pallas kernels for 24%

profile of v15, /device:TPU:30, one launch (start us, length us, event | category | flops | bytes accessed | tf_op | source)
XLA Modules:
  0.0 66.7 jit_solution(3827356512595237117)
XLA Ops:
  0.0 0.7 %slice.3 = bf16[16,128]{1,0:T(8,128)(2,1)S(1)} slice(bf16[8192,128]{1,0:T(8,128)(2,1)} %ticks_ref.1), slice={[8176:8192], [0:128]} | slice | bytes 8192 | tf_op jit(solution)/shard_map/slice | solution.py:154
  0.7 1.9 %collective-permute-start = (bf16[16,128]{1,0:T(8,128)(2,1)S(1)}, bf16[16,128]{1,0:T(8,128)(2,1)S(1)}, u32[]{:S(2)}, u32[]{:S(2)}) collective-permute-start(bf16[16,128]{1,0:T(8,128)(2,1)S(1)} %slice.3), channel_id=1, source_target_pairs={{0,1},{1,2},{2,3},{3,4},{4,5},{5,6},{6,7},{7,8},{8,9},{9,10},{10,1... | collective-permute-start | bytes 12296 | tf_op jit(solution)/shard_map/ppermute | solution.py:18
  2.6 3.0 %collective-permute-done.prev_ref = bf16[16,128]{1,0:T(8,128)(2,1)S(1)} collective-permute-done((bf16[16,128]{1,0:T(8,128)(2,1)S(1)}, bf16[16,128]{1,0:T(8,128)(2,1)S(1)}, u32[]{:S(2)}, u32[]{:S(2)}) %collective-permute-start) | collective-permute-done | bytes 4128 | tf_op jit(solution)/shard_map/ppermute | solution.py:18
  5.6 0.0 copy-start.4
  5.6 0.6 copy-done.4
  6.2 14.0 %shard_map.73 = (bf16[1024,768]{1,0:T(8,128)(2,1)}, bf16[1024,768]{1,0:T(8,128)(2,1)}, bf16[1024,768]{1,0:T(8,128)(2,1)}, bf16[1024,768]{1,0:T(8,128)(2,1)}, f32...) custom-call(bf16[8192,128]{1,0:T(8,128)(2,1)} %ticks_ref.1, bf16[16,128]{1,0:T(8,128)(2,1)} %copy-done.4, ...), custom_call_target="tpu_custom_call" | custom-call | tf_op jit(solution)/shard_map/pallas_call | solution.py:157
  20.2 0.0 copy-start
  20.2 2.1 %collective-permute-start.1 = (f32[6,64,128]{2,1,0:T(8,128)}, f32[6,64,128]{2,1,0:T(8,128)S(1)}, u32[]{:S(2)}, u32[]{:S(2)}) collective-permute-start(f32[6,64,128]{2,1,0:T(8,128)} %get-tuple-element.39.local_ref), channel_id=1, source_target_pairs={{0,1},{1,2},{2,3},{3,4},{4,5},{5,6},{6,7},{7,8},{8,9},{9,10},{10,1... | collective-permute-start | bytes 589832 | tf_op jit(solution)/shard_map/ppermute | solution.py:18
  22.2 4.0 %shard_map.74.earlier_ref = f32[1024,768]{1,0:T(8,128)} custom-call(bf16[1024,768]{1,0:T(8,128)(2,1)} %get-tuple-element.57.q_ref, bf16[1024,768]{1,0:T(8,128)(2,1)} %get-tuple-element.58.k_ref, bf16[1024,768]{1,0:T(8,128)(2,1)} %get-tuple-element.59.v_ref), custom_call_target="tpu_custom_call" | custom-call | flops 805306368 | bytes 1966080 | tf_op jit(solution)/shard_map/pallas_call | solution.py:191
  26.2 1.3 %collective-permute-done.1 = f32[6,64,128]{2,1,0:T(8,128)S(1)} collective-permute-done((f32[6,64,128]{2,1,0:T(8,128)}, f32[6,64,128]{2,1,0:T(8,128)S(1)}, u32[]{:S(2)}, u32[]{:S(2)}) %collective-permute-start.1) | collective-permute-done | bytes 196640 | tf_op jit(solution)/shard_map/ppermute | solution.py:18
  27.5 0.0 copy-done
  27.5 1.3 %collective-permute-start.2 = (f32[6,64,128]{2,1,0:T(8,128)S(1)}, f32[6,64,128]{2,1,0:T(8,128)S(1)}, u32[]{:S(2)}, u32[]{:S(2)}) collective-permute-start(f32[6,64,128]{2,1,0:T(8,128)S(1)} %add.9), channel_id=1, source_target_pairs={{0,2},{1,3},{2,4},{3,5},{4,6},{5,7},{6,8},{7,9},{8,10},{9,11},{10,... | collective-permute-start | bytes 589832 | tf_op jit(solution)/shard_map/ppermute | solution.py:18
  28.8 4.0 %shard_map.75.earlier_ref = f32[1024,768]{1,0:T(8,128)} custom-call(bf16[1024,768]{1,0:T(8,128)(2,1)} %get-tuple-element.57.q_ref, bf16[1024,768]{1,0:T(8,128)(2,1)} %get-tuple-element.58.k_ref, bf16[1024,768]{1,0:T(8,128)(2,1)} %get-tuple-element.59.v_ref, f32[1024,768]{1,0:T(8,128)} %shard_map.74.earlier_ref), custom_call_target="tpu_custom_call", output_to_operand_aliasing={{}: (3, {})} | custom-call | flops 805306368 | bytes 1966080 | tf_op jit(solution)/shard_map/pallas_call | solution.py:191
  32.8 2.6 %collective-permute-done.2 = f32[6,64,128]{2,1,0:T(8,128)S(1)} collective-permute-done((f32[6,64,128]{2,1,0:T(8,128)S(1)}, f32[6,64,128]{2,1,0:T(8,128)S(1)}, u32[]{:S(2)}, u32[]{:S(2)}) %collective-permute-start.2) | collective-permute-done | bytes 196640 | tf_op jit(solution)/shard_map/ppermute | solution.py:18
  35.4 0.0 copy-start.2
  35.5 0.0 copy-start.5
  35.5 1.4 %collective-permute-start.3 = (f32[6,64,128]{2,1,0:T(8,128)S(1)}, f32[6,64,128]{2,1,0:T(8,128)S(1)}, u32[]{:S(2)}, u32[]{:S(2)}) collective-permute-start(f32[6,64,128]{2,1,0:T(8,128)S(1)} %add.10), channel_id=1, source_target_pairs={{0,4},{1,5},{2,6},{3,7},{4,8},{5,9},{6,10},{7,11},{8,12},{9,13},{1... | collective-permute-start | bytes 589832 | tf_op jit(solution)/shard_map/ppermute | solution.py:18
  36.9 4.0 %shard_map.76.earlier_ref = f32[1024,768]{1,0:T(8,128)} custom-call(bf16[1024,768]{1,0:T(8,128)(2,1)} %get-tuple-element.57.q_ref, bf16[1024,768]{1,0:T(8,128)(2,1)} %get-tuple-element.58.k_ref, bf16[1024,768]{1,0:T(8,128)(2,1)} %get-tuple-element.59.v_ref, f32[1024,768]{1,0:T(8,128)} %shard_map.75.earlier_ref), custom_call_target="tpu_custom_call", output_to_operand_aliasing={{}: (3, {})} | custom-call | flops 805306368 | bytes 1966080 | tf_op jit(solution)/shard_map/pallas_call | solution.py:191
  40.9 4.3 %collective-permute-done.3 = f32[6,64,128]{2,1,0:T(8,128)S(1)} collective-permute-done((f32[6,64,128]{2,1,0:T(8,128)S(1)}, f32[6,64,128]{2,1,0:T(8,128)S(1)}, u32[]{:S(2)}, u32[]{:S(2)}) %collective-permute-start.3) | collective-permute-done | bytes 196640 | tf_op jit(solution)/shard_map/ppermute | solution.py:18
  45.2 0.0 copy-start.1
  45.3 1.5 %collective-permute-start.4 = (f32[6,64,128]{2,1,0:T(8,128)S(1)}, f32[6,64,128]{2,1,0:T(8,128)S(1)}, u32[]{:S(2)}, u32[]{:S(2)}) collective-permute-start(f32[6,64,128]{2,1,0:T(8,128)S(1)} %add.11.total_ref), channel_id=1, source_target_pairs={{0,8},{1,9},{2,10},{3,11},{4,12},{5,13},{6,14},{7,15},{16,24},{17,... | collective-permute-start | bytes 589832 | tf_op jit(solution)/shard_map/ppermute | solution.py:18
  46.7 0.0 copy-done.2
  46.7 0.3 copy.13
  47.1 0.9 %reshape.10.start_ref = f32[6,64,128]{2,1,0:T(8,128)} reshape(f32[6,64,2,64]{3,2,1,0:T(2,128)S(1)} %bitcast.4) | data formatting | bytes 393216 | tf_op jit(solution)/shard_map/reshape | solution.py:222
  48.0 0.0 copy-done.5
  48.0 0.6 reshape.11.hgain_ref
  48.6 4.0 %shard_map.77.inside_ref = f32[1024,768]{1,0:T(8,128)} custom-call(bf16[1024,768]{1,0:T(8,128)(2,1)} %get-tuple-element.57.q_ref, bf16[1024,768]{1,0:T(8,128)(2,1)} %get-tuple-element.58.k_ref, bf16[1024,768]{1,0:T(8,128)(2,1)} %get-tuple-element.59.v_ref, f32[1024,768]{1,0:T(8,128)} %shard_map.76.earlier_ref), custom_call_target="tpu_custom_call", output_to_operand_aliasing={{}: (3, {})} | custom-call | flops 805306368 | bytes 1966080 | tf_op jit(solution)/shard_map/pallas_call | solution.py:191
  52.5 0.0 copy-done.1
  52.5 6.1 %collective-permute-done.4.received_ref = f32[6,64,128]{2,1,0:T(8,128)S(1)} collective-permute-done((f32[6,64,128]{2,1,0:T(8,128)S(1)}, f32[6,64,128]{2,1,0:T(8,128)S(1)}, u32[]{:S(2)}, u32[]{:S(2)}) %collective-permute-start.4) | collective-permute-done | bytes 196640 | tf_op jit(solution)/shard_map/ppermute | solution.py:18
  58.7 0.0 copy-start.3
  58.7 0.7 %copy-done.3 = f32[6,64,128]{2,1,0:T(8,128)} copy-done((f32[6,64,128]{2,1,0:T(8,128)}, f32[6,64,128]{2,1,0:T(8,128)S(1)}, u32[]{:S(2)}) %copy-start.3) | copy-done | bytes 196632
  59.3 7.4 %shard_map.78 = bf16[1024,768]{1,0:T(8,128)(2,1)} custom-call(bf16[1024,768]{1,0:T(8,128)(2,1)} %get-tuple-element.57.q_ref, f32[6,64,128]{2,1,0:T(8,128)} %reshape.10.start_ref, f32[6,64,128]{2,1,0:T(8,128)} %copy-done.1, f32[6,64,128]{2,1,0:T(8,128)} %copy-done.3, f32[6,64,128]{2,1,0:T(8,128)} %get-tuple-element.39.local_ref, ...), custom_call_target="tpu_custom_call" | custom-call | tf_op jit(solution)/shard_map/pallas_call | solution.py:224
  (3 shorter events, 0.1 us)
Async XLA Ops:
  0.7 4.9 %collective-permute-start = (bf16[16,128]{1,0:T(8,128)(2,1)S(1)}, bf16[16,128]{1,0:T(8,128)(2,1)S(1)}, u32[]{:S(2)}, u32[]{:S(2)}) collective-permute-start(bf16[16,128]{1,0:T(8,128)(2,1)S(1)} %slice.3), channel_id=1, source_target_pairs={{0,1},{1,2},{2,3},{3,4},{4,5},{5,6},{6,7},{7,8},{8,9},{9,10},{10,1... | collective-permute-start | bytes 12296 | tf_op jit(solution)/shard_map/ppermute | solution.py:18
  5.6 0.6 copy-start.4
  20.2 7.3 %copy-start = (f32[6,64,128]{2,1,0:T(8,128)S(1)}, f32[6,64,128]{2,1,0:T(8,128)}, u32[]{:S(2)}) copy-start(f32[6,64,128]{2,1,0:T(8,128)} %get-tuple-element.39.local_ref) | copy-start | bytes 589828
  20.2 7.3 %collective-permute-start.1 = (f32[6,64,128]{2,1,0:T(8,128)}, f32[6,64,128]{2,1,0:T(8,128)S(1)}, u32[]{:S(2)}, u32[]{:S(2)}) collective-permute-start(f32[6,64,128]{2,1,0:T(8,128)} %get-tuple-element.39.local_ref), channel_id=1, source_target_pairs={{0,1},{1,2},{2,3},{3,4},{4,5},{5,6},{6,7},{7,8},{8,9},{9,10},{10,1... | collective-permute-start | bytes 589832 | tf_op jit(solution)/shard_map/ppermute | solution.py:18
  27.5 7.9 %collective-permute-start.2 = (f32[6,64,128]{2,1,0:T(8,128)S(1)}, f32[6,64,128]{2,1,0:T(8,128)S(1)}, u32[]{:S(2)}, u32[]{:S(2)}) collective-permute-start(f32[6,64,128]{2,1,0:T(8,128)S(1)} %add.9), channel_id=1, source_target_pairs={{0,2},{1,3},{2,4},{3,5},{4,6},{5,7},{6,8},{7,9},{8,10},{9,11},{10,... | collective-permute-start | bytes 589832 | tf_op jit(solution)/shard_map/ppermute | solution.py:18
  35.4 11.3 %copy-start.2 = (f32[12,64,64]{2,1,0:T(8,128)S(1)}, f32[12,64,64]{2,1,0:T(8,128)}, u32[]{:S(2)}) copy-start(f32[12,64,64]{2,1,0:T(8,128)} %param.13) | copy-start | bytes 589828
  35.5 12.5 %copy-start.5 = (f32[768]{0:T(1024)S(1)}, f32[768]{0:T(1024)}, u32[]{:S(2)}) copy-start(f32[768]{0:T(1024)} %param.11) | copy-start | bytes 9220
  35.5 9.8 %collective-permute-start.3 = (f32[6,64,128]{2,1,0:T(8,128)S(1)}, f32[6,64,128]{2,1,0:T(8,128)S(1)}, u32[]{:S(2)}, u32[]{:S(2)}) collective-permute-start(f32[6,64,128]{2,1,0:T(8,128)S(1)} %add.10), channel_id=1, source_target_pairs={{0,4},{1,5},{2,6},{3,7},{4,8},{5,9},{6,10},{7,11},{8,12},{9,13},{1... | collective-permute-start | bytes 589832 | tf_op jit(solution)/shard_map/ppermute | solution.py:18
  45.2 7.3 %copy-start.1 = (f32[6,64,128]{2,1,0:T(8,128)}, f32[6,64,128]{2,1,0:T(8,128)S(1)}, u32[]{:S(2)}) copy-start(f32[6,64,128]{2,1,0:T(8,128)S(1)} %add.11.total_ref) | copy-start | bytes 589828
  45.3 13.4 %collective-permute-start.4 = (f32[6,64,128]{2,1,0:T(8,128)S(1)}, f32[6,64,128]{2,1,0:T(8,128)S(1)}, u32[]{:S(2)}, u32[]{:S(2)}) collective-permute-start(f32[6,64,128]{2,1,0:T(8,128)S(1)} %add.11.total_ref), channel_id=1, source_target_pairs={{0,8},{1,9},{2,10},{3,11},{4,12},{5,13},{6,14},{7,15},{16,24},{17,... | collective-permute-start | bytes 589832 | tf_op jit(solution)/shard_map/ppermute | solution.py:18
  58.7 0.7 %copy-start.3 = (f32[6,64,128]{2,1,0:T(8,128)}, f32[6,64,128]{2,1,0:T(8,128)S(1)}, u32[]{:S(2)}) copy-start(f32[6,64,128]{2,1,0:T(8,128)S(1)} %collective-permute-done.4.received_ref) | copy-start | bytes 589828

commit v16 on v15

--- a/solution.py
+++ b/solution.py
@@ -109,17 +109,14 @@
             inside_ref[rows_at : rows_at + part, cols] = inside
 
 
-def out_kernel(q_ref, start_ref, total_ref, received_ref, local_ref, first_ref, inside_ref, emb_ref, hgain_ref, out_w_ref,
-               out_ref, att_ref):
-    b = pl.program_id(0)
+def out_kernel(q_ref, base_ref, total_ref, received_ref, inside_ref, emb_ref, hgain_ref, out_w_ref, out_ref, att_ref):
     model_width = out_ref.shape[1]
     lane = lax.broadcasted_iota(jnp.int32, (1, PAIR), 1)
     first = lane < PAIR // 2
     head_size = PAIR // 2
     for pair in range(model_width // PAIR):
         cols = slice(pair * PAIR, (pair + 1) * PAIR)
-        packed = (start_ref[pair] + (total_ref[pair] + received_ref[pair] - local_ref[pair])
-                  + jnp.where(b > 0, first_ref[pair], 0.0))
+        packed = base_ref[0, pair] + (total_ref[pair] + received_ref[pair])
         diag = jnp.concatenate([jnp.where(first, packed, 0.0), jnp.where(first, 0.0, packed)], axis=0)
         high = diag.astype(jnp.bfloat16)
         low = (diag - high.astype(jnp.float32)).astype(jnp.bfloat16)
@@ -220,15 +217,18 @@
         block += 1
     packed_in = state_in.reshape(pairs, 2, head_size, head_size).transpose(0, 2, 1, 3)
     packed_in = packed_in.reshape(pairs, head_size, PAIR)
+    base = [packed_in - local]
+    for block in range(1, blocks):
+        base.append(base[-1] + first_state)
+    base = jnp.stack(base)
+    base_spec = pl.BlockSpec((1, pairs, head_size, PAIR), lambda b: (b, 0, 0, 0))
 
     return pl.pallas_call(
         out_kernel,
         grid=(blocks,),
         in_specs=[
             rows_spec,
-            state_spec,
-            state_spec,
-            state_spec,
+            base_spec,
             state_spec,
             state_spec,
             rows_spec,
@@ -240,7 +240,7 @@
         out_shape=jax.ShapeDtypeStruct((token_count, model_width), jnp.bfloat16),
         scratch_shapes=[pltpu.VMEM((BLK, model_width), jnp.bfloat16)],
         compiler_params=pltpu.CompilerParams(dimension_semantics=("arbitrary",)),
-    )(queries, packed_in, total, received, local, first_state, inside, emb, head_gain.reshape(1, model_width), out_weight)
+    )(queries, base, total, received, inside, emb, head_gain.reshape(1, model_width), out_weight)
 
 
 def solution(mesh):

time: 67.1 us -> 66.1 us (0.985)
  waiting for transfers between devices: 17.3 us -> 16.4 us
  other arithmetic: 0.07 us -> 0.93 us
    another operation x0 -> x2, other arithmetic: none -> 0.86 us  [shards(): base = jnp.stack(base)]
    ppermute x5, waiting for transfers between devices: 17.3 us -> 16.4 us  [from_behind(): lax.ppermute(value, axis, [(source, source + steps) for source in range(i...]
    reshape x1, local copies, waits for them, and re-layouts: 0.91 us -> 0.24 us  [shards(): packed_in = packed_in.reshape(pairs, head_size, PAIR)]
where the time goes in v16:
time: 66.1 us; the launch traced here: 65.7 us
  Pallas kernels  37.1 us (56%)
  waiting for transfers between devices  16.4 us (25%)
  starting transfers between devices  8.02 us (12%)
  local copies, waits for them, and re-layouts  3.11 us (5%)
  other arithmetic  0.93 us (1%)
    ppermute x5, waiting for transfers between devices, from_behind(): lax.ppermute(value, axis, [(source, source + steps) for source in range(i...  16.4 us
    pallas_call x4, Pallas kernels, inside_block(): pl.pallas_call(kernel, grid=(1,), in_specs=in_specs, out_specs=spec, out_...  16.1 us
    pallas_call x1, Pallas kernels, shards(): pl.pallas_call(embed_kernel, grid=(blocks,), in_specs=[pl.BlockSpec((bloc...  14 us
    ppermute x5, starting transfers between devices, from_behind(): lax.ppermute(value, axis, [(source, source + steps) for source in range(i...  8.02 us
    pallas_call x1, Pallas kernels, shards(): pl.pallas_call(out_kernel, grid=(blocks,), in_specs=[rows_spec, base_spec...  7.01 us
  transfers between devices with their start and end apart: 5, of which 5 were waited for; matrix products, arithmetic and copies ran while one was open for 3% of the time, Pallas kernels for 24%

profile of v16, /device:TPU:30, one launch (start us, length us, event | category | flops | bytes accessed | tf_op | source)
XLA Modules:
  0.0 65.7 jit_solution(1129057174057797814)
XLA Ops:
  0.0 0.7 %slice.3 = bf16[16,128]{1,0:T(8,128)(2,1)S(1)} slice(bf16[8192,128]{1,0:T(8,128)(2,1)} %ticks_ref.1), slice={[8176:8192], [0:128]} | slice | bytes 8192 | tf_op jit(solution)/shard_map/slice | solution.py:151
  0.7 1.9 %collective-permute-start = (bf16[16,128]{1,0:T(8,128)(2,1)S(1)}, bf16[16,128]{1,0:T(8,128)(2,1)S(1)}, u32[]{:S(2)}, u32[]{:S(2)}) collective-permute-start(bf16[16,128]{1,0:T(8,128)(2,1)S(1)} %slice.3), channel_id=1, source_target_pairs={{0,1},{1,2},{2,3},{3,4},{4,5},{5,6},{6,7},{7,8},{8,9},{9,10},{10,1... | collective-permute-start | bytes 12296 | tf_op jit(solution)/shard_map/ppermute | solution.py:18
  2.6 3.0 %collective-permute-done.prev_ref = bf16[16,128]{1,0:T(8,128)(2,1)S(1)} collective-permute-done((bf16[16,128]{1,0:T(8,128)(2,1)S(1)}, bf16[16,128]{1,0:T(8,128)(2,1)S(1)}, u32[]{:S(2)}, u32[]{:S(2)}) %collective-permute-start) | collective-permute-done | bytes 4128 | tf_op jit(solution)/shard_map/ppermute | solution.py:18
  5.6 0.0 copy-start.5
  5.6 0.6 copy-done.5
  6.2 14.0 %shard_map.73 = (bf16[1024,768]{1,0:T(8,128)(2,1)}, bf16[1024,768]{1,0:T(8,128)(2,1)}, bf16[1024,768]{1,0:T(8,128)(2,1)}, bf16[1024,768]{1,0:T(8,128)(2,1)}, f32...) custom-call(bf16[8192,128]{1,0:T(8,128)(2,1)} %ticks_ref.1, bf16[16,128]{1,0:T(8,128)(2,1)} %copy-done.5, ...), custom_call_target="tpu_custom_call" | custom-call | tf_op jit(solution)/shard_map/pallas_call | solution.py:154
  20.2 0.0 copy-start
  20.2 0.0 copy-start.2
  20.2 0.0 copy-start.6
  20.3 2.1 %collective-permute-start.1 = (f32[6,64,128]{2,1,0:T(8,128)}, f32[6,64,128]{2,1,0:T(8,128)S(1)}, u32[]{:S(2)}, u32[]{:S(2)}) collective-permute-start(f32[6,64,128]{2,1,0:T(8,128)} %get-tuple-element.40), channel_id=1, source_target_pairs={{0,1},{1,2},{2,3},{3,4},{4,5},{5,6},{6,7},{7,8},{8,9},{9,10},{10,1... | collective-permute-start | bytes 589832 | tf_op jit(solution)/shard_map/ppermute | solution.py:18
  22.3 4.0 %shard_map.74.earlier_ref = f32[1024,768]{1,0:T(8,128)} custom-call(bf16[1024,768]{1,0:T(8,128)(2,1)} %get-tuple-element.58.q_ref, bf16[1024,768]{1,0:T(8,128)(2,1)} %get-tuple-element.59.k_ref, bf16[1024,768]{1,0:T(8,128)(2,1)} %get-tuple-element.60.v_ref), custom_call_target="tpu_custom_call" | custom-call | flops 805306368 | bytes 1966080 | tf_op jit(solution)/shard_map/pallas_call | solution.py:188
  26.3 1.2 %collective-permute-done.1 = f32[6,64,128]{2,1,0:T(8,128)S(1)} collective-permute-done((f32[6,64,128]{2,1,0:T(8,128)}, f32[6,64,128]{2,1,0:T(8,128)S(1)}, u32[]{:S(2)}, u32[]{:S(2)}) %collective-permute-start.1) | collective-permute-done | bytes 196640 | tf_op jit(solution)/shard_map/ppermute | solution.py:18
  27.6 0.0 copy-done
  27.6 1.3 %collective-permute-start.2 = (f32[6,64,128]{2,1,0:T(8,128)S(1)}, f32[6,64,128]{2,1,0:T(8,128)S(1)}, u32[]{:S(2)}, u32[]{:S(2)}) collective-permute-start(f32[6,64,128]{2,1,0:T(8,128)S(1)} %add.13), channel_id=1, source_target_pairs={{0,2},{1,3},{2,4},{3,5},{4,6},{5,7},{6,8},{7,9},{8,10},{9,11},{10,... | collective-permute-start | bytes 589832 | tf_op jit(solution)/shard_map/ppermute | solution.py:18
  28.9 0.0 copy-done.2
  28.9 0.3 copy.13
  29.2 0.2 reshape.10
  29.5 0.0 copy-done.6
  29.5 0.6 reshape.11.hgain_ref
  30.1 0.0 copy-start.3
  30.1 4.0 %shard_map.75.earlier_ref = f32[1024,768]{1,0:T(8,128)} custom-call(bf16[1024,768]{1,0:T(8,128)(2,1)} %get-tuple-element.58.q_ref, bf16[1024,768]{1,0:T(8,128)(2,1)} %get-tuple-element.59.k_ref, bf16[1024,768]{1,0:T(8,128)(2,1)} %get-tuple-element.60.v_ref, f32[1024,768]{1,0:T(8,128)} %shard_map.74.earlier_ref), custom_call_target="tpu_custom_call", output_to_operand_aliasing={{}: (3, {})} | custom-call | flops 805306368 | bytes 1966080 | tf_op jit(solution)/shard_map/pallas_call | solution.py:188
  34.1 1.4 %collective-permute-done.2 = f32[6,64,128]{2,1,0:T(8,128)S(1)} collective-permute-done((f32[6,64,128]{2,1,0:T(8,128)S(1)}, f32[6,64,128]{2,1,0:T(8,128)S(1)}, u32[]{:S(2)}, u32[]{:S(2)}) %collective-permute-start.2) | collective-permute-done | bytes 196640 | tf_op jit(solution)/shard_map/ppermute | solution.py:18
  35.5 1.3 %collective-permute-start.3 = (f32[6,64,128]{2,1,0:T(8,128)S(1)}, f32[6,64,128]{2,1,0:T(8,128)S(1)}, u32[]{:S(2)}, u32[]{:S(2)}) collective-permute-start(f32[6,64,128]{2,1,0:T(8,128)S(1)} %add.14), channel_id=1, source_target_pairs={{0,4},{1,5},{2,6},{3,7},{4,8},{5,9},{6,10},{7,11},{8,12},{9,13},{1... | collective-permute-start | bytes 589832 | tf_op jit(solution)/shard_map/ppermute | solution.py:18
  36.8 0.0 copy-done.3
  36.9 4.0 %shard_map.76.earlier_ref = f32[1024,768]{1,0:T(8,128)} custom-call(bf16[1024,768]{1,0:T(8,128)(2,1)} %get-tuple-element.58.q_ref, bf16[1024,768]{1,0:T(8,128)(2,1)} %get-tuple-element.59.k_ref, bf16[1024,768]{1,0:T(8,128)(2,1)} %get-tuple-element.60.v_ref, f32[1024,768]{1,0:T(8,128)} %shard_map.75.earlier_ref), custom_call_target="tpu_custom_call", output_to_operand_aliasing={{}: (3, {})} | custom-call | flops 805306368 | bytes 1966080 | tf_op jit(solution)/shard_map/pallas_call | solution.py:188
  40.9 4.3 %collective-permute-done.3 = f32[6,64,128]{2,1,0:T(8,128)S(1)} collective-permute-done((f32[6,64,128]{2,1,0:T(8,128)S(1)}, f32[6,64,128]{2,1,0:T(8,128)S(1)}, u32[]{:S(2)}, u32[]{:S(2)}) %collective-permute-start.3) | collective-permute-done | bytes 196640 | tf_op jit(solution)/shard_map/ppermute | solution.py:18
  45.2 0.0 copy-start.1
  45.2 1.5 %collective-permute-start.4 = (f32[6,64,128]{2,1,0:T(8,128)S(1)}, f32[6,64,128]{2,1,0:T(8,128)S(1)}, u32[]{:S(2)}, u32[]{:S(2)}) collective-permute-start(f32[6,64,128]{2,1,0:T(8,128)S(1)} %add.15.total_ref), channel_id=1, source_target_pairs={{0,8},{1,9},{2,10},{3,11},{4,12},{5,13},{6,14},{7,15},{16,24},{17,... | collective-permute-start | bytes 589832 | tf_op jit(solution)/shard_map/ppermute | solution.py:18
  46.7 0.8 %pad_maximum_fusion.base_ref = f32[2,6,64,128]{3,2,1,0:T(8,128)} fusion(f32[1,6,64,128]{3,2,1,0:T(8,128)S(1)} %get-tuple-element.66, f32[1,6,64,128]{3,2,1,0:T(8,128)S(1)} %get-tuple-element.65), kind=kLoop, calls=%fused_computation | loop fusion | flops 98304 | bytes 786432 | tf_op jit(solution)/shard_map/stack | solution.py:223
  47.5 4.0 %shard_map.77.inside_ref = f32[1024,768]{1,0:T(8,128)} custom-call(bf16[1024,768]{1,0:T(8,128)(2,1)} %get-tuple-element.58.q_ref, bf16[1024,768]{1,0:T(8,128)(2,1)} %get-tuple-element.59.k_ref, bf16[1024,768]{1,0:T(8,128)(2,1)} %get-tuple-element.60.v_ref, f32[1024,768]{1,0:T(8,128)} %shard_map.76.earlier_ref), custom_call_target="tpu_custom_call", output_to_operand_aliasing={{}: (3, {})} | custom-call | flops 805306368 | bytes 1966080 | tf_op jit(solution)/shard_map/pallas_call | solution.py:188
  51.5 0.0 copy-done.1
  51.5 6.5 %collective-permute-done.4.received_ref = f32[6,64,128]{2,1,0:T(8,128)S(1)} collective-permute-done((f32[6,64,128]{2,1,0:T(8,128)S(1)}, f32[6,64,128]{2,1,0:T(8,128)S(1)}, u32[]{:S(2)}, u32[]{:S(2)}) %collective-permute-start.4) | collective-permute-done | bytes 196640 | tf_op jit(solution)/shard_map/ppermute | solution.py:18
  58.1 0.0 copy-start.4
  58.1 0.7 %copy-done.4 = f32[6,64,128]{2,1,0:T(8,128)} copy-done((f32[6,64,128]{2,1,0:T(8,128)}, f32[6,64,128]{2,1,0:T(8,128)S(1)}, u32[]{:S(2)}) %copy-start.4) | copy-done | bytes 196632
  58.7 7.0 %shard_map.78 = bf16[1024,768]{1,0:T(8,128)(2,1)} custom-call(bf16[1024,768]{1,0:T(8,128)(2,1)} %get-tuple-element.58.q_ref, f32[2,6,64,128]{3,2,1,0:T(8,128)} %pad_maximum_fusion.base_ref, f32[6,64,128]{2,1,0:T(8,128)} %copy-done.1, f32[6,64,128]{2,1,0:T(8,128)} %copy-done.4, f32[1024,768]{1,0:T(8,128)} %shard_map.77.inside_ref, ...), custom_call_target="tpu_custom_call" | custom-call | tf_op jit(solution)/shard_map/pallas_call | solution.py:226
  (4 shorter events, 0.1 us)
Async XLA Ops:
  0.7 4.9 %collective-permute-start = (bf16[16,128]{1,0:T(8,128)(2,1)S(1)}, bf16[16,128]{1,0:T(8,128)(2,1)S(1)}, u32[]{:S(2)}, u32[]{:S(2)}) collective-permute-start(bf16[16,128]{1,0:T(8,128)(2,1)S(1)} %slice.3), channel_id=1, source_target_pairs={{0,1},{1,2},{2,3},{3,4},{4,5},{5,6},{6,7},{7,8},{8,9},{9,10},{10,1... | collective-permute-start | bytes 12296 | tf_op jit(solution)/shard_map/ppermute | solution.py:18
  5.6 0.6 copy-start.5
  20.2 7.4 %copy-start = (f32[6,64,128]{2,1,0:T(8,128)S(1)}, f32[6,64,128]{2,1,0:T(8,128)}, u32[]{:S(2)}) copy-start(f32[6,64,128]{2,1,0:T(8,128)} %get-tuple-element.40) | copy-start | bytes 589828
  20.2 8.7 %copy-start.2 = (f32[12,64,64]{2,1,0:T(8,128)S(1)}, f32[12,64,64]{2,1,0:T(8,128)}, u32[]{:S(2)}) copy-start(f32[12,64,64]{2,1,0:T(8,128)} %param.13) | copy-start | bytes 589828
  20.2 9.2 %copy-start.6 = (f32[768]{0:T(1024)S(1)}, f32[768]{0:T(1024)}, u32[]{:S(2)}) copy-start(f32[768]{0:T(1024)} %param.11) | copy-start | bytes 9220
  20.3 7.3 %collective-permute-start.1 = (f32[6,64,128]{2,1,0:T(8,128)}, f32[6,64,128]{2,1,0:T(8,128)S(1)}, u32[]{:S(2)}, u32[]{:S(2)}) collective-permute-start(f32[6,64,128]{2,1,0:T(8,128)} %get-tuple-element.40), channel_id=1, source_target_pairs={{0,1},{1,2},{2,3},{3,4},{4,5},{5,6},{6,7},{7,8},{8,9},{9,10},{10,1... | collective-permute-start | bytes 589832 | tf_op jit(solution)/shard_map/ppermute | solution.py:18
  27.6 7.9 %collective-permute-start.2 = (f32[6,64,128]{2,1,0:T(8,128)S(1)}, f32[6,64,128]{2,1,0:T(8,128)S(1)}, u32[]{:S(2)}, u32[]{:S(2)}) collective-permute-start(f32[6,64,128]{2,1,0:T(8,128)S(1)} %add.13), channel_id=1, source_target_pairs={{0,2},{1,3},{2,4},{3,5},{4,6},{5,7},{6,8},{7,9},{8,10},{9,11},{10,... | collective-permute-start | bytes 589832 | tf_op jit(solution)/shard_map/ppermute | solution.py:18
  30.1 6.7 %copy-start.3 = (f32[6,64,128]{2,1,0:T(8,128)S(1)}, f32[6,64,128]{2,1,0:T(8,128)}, u32[]{:S(2)}) copy-start(f32[6,64,128]{2,1,0:T(8,128)} %get-tuple-element.37) | copy-start | bytes 589828
  35.5 9.6 %collective-permute-start.3 = (f32[6,64,128]{2,1,0:T(8,128)S(1)}, f32[6,64,128]{2,1,0:T(8,128)S(1)}, u32[]{:S(2)}, u32[]{:S(2)}) collective-permute-start(f32[6,64,128]{2,1,0:T(8,128)S(1)} %add.14), channel_id=1, source_target_pairs={{0,4},{1,5},{2,6},{3,7},{4,8},{5,9},{6,10},{7,11},{8,12},{9,13},{1... | collective-permute-start | bytes 589832 | tf_op jit(solution)/shard_map/ppermute | solution.py:18
  45.2 6.4 %copy-start.1 = (f32[6,64,128]{2,1,0:T(8,128)}, f32[6,64,128]{2,1,0:T(8,128)S(1)}, u32[]{:S(2)}) copy-start(f32[6,64,128]{2,1,0:T(8,128)S(1)} %add.15.total_ref) | copy-start | bytes 589828
  45.2 12.9 %collective-permute-start.4 = (f32[6,64,128]{2,1,0:T(8,128)S(1)}, f32[6,64,128]{2,1,0:T(8,128)S(1)}, u32[]{:S(2)}, u32[]{:S(2)}) collective-permute-start(f32[6,64,128]{2,1,0:T(8,128)S(1)} %add.15.total_ref), channel_id=1, source_target_pairs={{0,8},{1,9},{2,10},{3,11},{4,12},{5,13},{6,14},{7,15},{16,24},{17,... | collective-permute-start | bytes 589832 | tf_op jit(solution)/shard_map/ppermute | solution.py:18
  58.1 0.7 %copy-start.4 = (f32[6,64,128]{2,1,0:T(8,128)}, f32[6,64,128]{2,1,0:T(8,128)S(1)}, u32[]{:S(2)}) copy-start(f32[6,64,128]{2,1,0:T(8,128)S(1)} %collective-permute-done.4.received_ref) | copy-start | bytes 589828

commit v17 on v16

--- a/solution.py
+++ b/solution.py
@@ -196,6 +196,13 @@
                                           bytes_accessed=10 * BLK * piece_width),
         )(*operands)
 
+    packed_in = state_in.reshape(pairs, 2, head_size, head_size).transpose(0, 2, 1, 3)
+    packed_in = packed_in.reshape(pairs, head_size, PAIR)
+    base = [packed_in - local]
+    for block in range(1, blocks):
+        base.append(base[-1] + first_state)
+    base = jnp.stack(base)
+    head_gain_row = head_gain.reshape(1, model_width)
     count = lax.axis_size("inner")
     inside = None
     total, steps, block = local, 1, 0
@@ -206,7 +213,11 @@
         received = from_behind(total, "inner", steps)
         if block < blocks * halves:
             inside = inside_block(block, inside, q_in, k_in, v_in)
-            received, inside = lax.optimization_barrier((received, inside))
+            if block == 1:
+                received, inside, base, head_gain_row = lax.optimization_barrier(
+                    (received, inside, base, head_gain_row))
+            else:
+                received, inside = lax.optimization_barrier((received, inside))
             block += 1
         steps *= 2
         if steps >= count:
@@ -215,12 +226,6 @@
     while block < blocks * halves:
         inside = inside_block(block, inside, queries, keys, values)
         block += 1
-    packed_in = state_in.reshape(pairs, 2, head_size, head_size).transpose(0, 2, 1, 3)
-    packed_in = packed_in.reshape(pairs, head_size, PAIR)
-    base = [packed_in - local]
-    for block in range(1, blocks):
-        base.append(base[-1] + first_state)
-    base = jnp.stack(base)
     base_spec = pl.BlockSpec((1, pairs, head_size, PAIR), lambda b: (b, 0, 0, 0))
 
     return pl.pallas_call(
@@ -240,7 +245,7 @@
         out_shape=jax.ShapeDtypeStruct((token_count, model_width), jnp.bfloat16),
         scratch_shapes=[pltpu.VMEM((BLK, model_width), jnp.bfloat16)],
         compiler_params=pltpu.CompilerParams(dimension_semantics=("arbitrary",)),
-    )(queries, base, total, received, inside, emb, head_gain.reshape(1, model_width), out_weight)
+    )(queries, base, total, received, inside, emb, head_gain_row, out_weight)
 
 
 def solution(mesh):

time: 66.1 us -> 66.5 us (level)
  local copies, waits for them, and re-layouts: 3.11 us -> 4.78 us
  waiting for transfers between devices: 16.4 us -> 15.2 us
    ppermute x5, waiting for transfers between devices: 16.4 us -> 15.2 us  [from_behind(): lax.ppermute(value, axis, [(source, source + steps) for source in range(i...]
    reshape x1, local copies, waits for them, and re-layouts: 0.31 us -> 1.3 us  [shards(): state_in.reshape(pairs, 2, head_size, head_size).transpose(0, 2, 1, 3)]
    reshape x1, local copies, waits for them, and re-layouts: 0.59 us -> 1.28 us  [shards(): head_gain_row = head_gain.reshape(1, model_width)]
  transfers between devices with their start and end apart: 5 -> 5, of which waited for: 5 -> 5; matrix products, arithmetic and copies ran while one was open for 3% -> 6% of each run, Pallas kernels for 24% -> 24%
where the time goes in v17:
time: 66.5 us; the launch traced here: 66 us
  Pallas kernels  37 us (56%)
  waiting for transfers between devices  15.2 us (23%)
  starting transfers between devices  8.02 us (12%)
  local copies, waits for them, and re-layouts  4.78 us (7%)
  other arithmetic  0.93 us (1%)
    pallas_call x4, Pallas kernels, inside_block(): pl.pallas_call(kernel, grid=(1,), in_specs=in_specs, out_specs=spec, out_...  16 us
    ppermute x5, waiting for transfers between devices, from_behind(): lax.ppermute(value, axis, [(source, source + steps) for source in range(i...  15.2 us
    pallas_call x1, Pallas kernels, shards(): pl.pallas_call(embed_kernel, grid=(blocks,), in_specs=[pl.BlockSpec((bloc...  14 us
    ppermute x5, starting transfers between devices, from_behind(): lax.ppermute(value, axis, [(source, source + steps) for source in range(i...  8.02 us
    pallas_call x1, Pallas kernels, shards(): pl.pallas_call(out_kernel, grid=(blocks,), in_specs=[rows_spec, base_spec...  7.01 us
  transfers between devices with their start and end apart: 5, of which 5 were waited for; matrix products, arithmetic and copies ran while one was open for 6% of the time, Pallas kernels for 24%

profile of v17, /device:TPU:30, one launch (start us, length us, event | category | flops | bytes accessed | tf_op | source)
XLA Modules:
  0.0 66.0 jit_solution(15791586769625633045)
XLA Ops:
  0.0 0.7 %slice.3 = bf16[16,128]{1,0:T(8,128)(2,1)S(1)} slice(bf16[8192,128]{1,0:T(8,128)(2,1)} %ticks_ref.1), slice={[8176:8192], [0:128]} | slice | bytes 8192 | tf_op jit(solution)/shard_map/slice | solution.py:151
  0.7 1.9 %collective-permute-start = (bf16[16,128]{1,0:T(8,128)(2,1)S(1)}, bf16[16,128]{1,0:T(8,128)(2,1)S(1)}, u32[]{:S(2)}, u32[]{:S(2)}) collective-permute-start(bf16[16,128]{1,0:T(8,128)(2,1)S(1)} %slice.3), channel_id=1, source_target_pairs={{0,1},{1,2},{2,3},{3,4},{4,5},{5,6},{6,7},{7,8},{8,9},{9,10},{10,1... | collective-permute-start | bytes 12296 | tf_op jit(solution)/shard_map/ppermute | solution.py:18
  2.6 1.3 %reshape.11.hgain_ref = f32[1,768]{1,0:T(1,128)} reshape(f32[768]{0:T(1024)} %param.11) | data formatting | bytes 6144 | tf_op jit(solution)/shard_map/reshape | solution.py:205
  3.9 1.3 %copy.13 = f32[6,2,64,64]{3,1,2,0:T(2,128)S(1)} copy(f32[6,2,64,64]{3,2,1,0:T(8,128)} %bitcast.9) | data formatting | bytes 393216 | tf_op jit(solution)/shard_map/reshape | solution.py:199
  5.2 0.2 reshape.10
  5.4 0.2 collective-permute-done.prev_ref
  5.6 0.0 copy-start.4
  5.6 0.6 copy-done.4
  6.2 14.0 %shard_map.73 = (bf16[1024,768]{1,0:T(8,128)(2,1)}, bf16[1024,768]{1,0:T(8,128)(2,1)}, bf16[1024,768]{1,0:T(8,128)(2,1)}, bf16[1024,768]{1,0:T(8,128)(2,1)}, f32...) custom-call(bf16[8192,128]{1,0:T(8,128)(2,1)} %ticks_ref.1, bf16[16,128]{1,0:T(8,128)(2,1)} %copy-done.4, ...), custom_call_target="tpu_custom_call" | custom-call | tf_op jit(solution)/shard_map/pallas_call | solution.py:154
  20.2 0.0 copy-start
  20.2 0.0 copy-start.2
  20.2 2.1 %collective-permute-start.1 = (f32[6,64,128]{2,1,0:T(8,128)}, f32[6,64,128]{2,1,0:T(8,128)S(1)}, u32[]{:S(2)}, u32[]{:S(2)}) collective-permute-start(f32[6,64,128]{2,1,0:T(8,128)} %get-tuple-element.41), channel_id=1, source_target_pairs={{0,1},{1,2},{2,3},{3,4},{4,5},{5,6},{6,7},{7,8},{8,9},{9,10},{10,1... | collective-permute-start | bytes 589832 | tf_op jit(solution)/shard_map/ppermute | solution.py:18
  22.2 4.0 %shard_map.74.earlier_ref = f32[1024,768]{1,0:T(8,128)} custom-call(bf16[1024,768]{1,0:T(8,128)(2,1)} %get-tuple-element.61.q_ref, bf16[1024,768]{1,0:T(8,128)(2,1)} %get-tuple-element.62.k_ref, bf16[1024,768]{1,0:T(8,128)(2,1)} %get-tuple-element.63.v_ref), custom_call_target="tpu_custom_call" | custom-call | flops 805306368 | bytes 1966080 | tf_op jit(solution)/shard_map/pallas_call | solution.py:188
  26.2 0.0 copy-done
  26.2 0.0 copy-done.2
  26.3 1.2 %collective-permute-done.1 = f32[6,64,128]{2,1,0:T(8,128)S(1)} collective-permute-done((f32[6,64,128]{2,1,0:T(8,128)}, f32[6,64,128]{2,1,0:T(8,128)S(1)}, u32[]{:S(2)}, u32[]{:S(2)}) %collective-permute-start.1) | collective-permute-done | bytes 196640 | tf_op jit(solution)/shard_map/ppermute | solution.py:18
  27.5 1.3 %collective-permute-start.2 = (f32[6,64,128]{2,1,0:T(8,128)S(1)}, f32[6,64,128]{2,1,0:T(8,128)S(1)}, u32[]{:S(2)}, u32[]{:S(2)}) collective-permute-start(f32[6,64,128]{2,1,0:T(8,128)S(1)} %add.12), channel_id=1, source_target_pairs={{0,2},{1,3},{2,4},{3,5},{4,6},{5,7},{6,8},{7,9},{8,10},{9,11},{10,... | collective-permute-start | bytes 589832 | tf_op jit(solution)/shard_map/ppermute | solution.py:18
  28.8 0.8 %pad_maximum_fusion.base_ref = f32[2,6,64,128]{3,2,1,0:T(8,128)} fusion(f32[1,6,64,128]{3,2,1,0:T(8,128)S(1)} %get-tuple-element.70, f32[1,6,64,128]{3,2,1,0:T(8,128)S(1)} %get-tuple-element.69), kind=kLoop, calls=%fused_computation | loop fusion | flops 98304 | bytes 786432 | tf_op jit(solution)/shard_map/stack | solution.py:204
  29.7 4.0 %shard_map.75.earlier_ref = f32[1024,768]{1,0:T(8,128)} custom-call(bf16[1024,768]{1,0:T(8,128)(2,1)} %get-tuple-element.61.q_ref, bf16[1024,768]{1,0:T(8,128)(2,1)} %get-tuple-element.62.k_ref, bf16[1024,768]{1,0:T(8,128)(2,1)} %get-tuple-element.63.v_ref, f32[1024,768]{1,0:T(8,128)} %shard_map.74.earlier_ref), custom_call_target="tpu_custom_call", output_to_operand_aliasing={{}: (3, {})} | custom-call | flops 805306368 | bytes 1966080 | tf_op jit(solution)/shard_map/pallas_call | solution.py:188
  33.6 1.8 %collective-permute-done.2 = f32[6,64,128]{2,1,0:T(8,128)S(1)} collective-permute-done((f32[6,64,128]{2,1,0:T(8,128)S(1)}, f32[6,64,128]{2,1,0:T(8,128)S(1)}, u32[]{:S(2)}, u32[]{:S(2)}) %collective-permute-start.2) | collective-permute-done | bytes 196640 | tf_op jit(solution)/shard_map/ppermute | solution.py:18
  35.4 1.3 %collective-permute-start.3 = (f32[6,64,128]{2,1,0:T(8,128)S(1)}, f32[6,64,128]{2,1,0:T(8,128)S(1)}, u32[]{:S(2)}, u32[]{:S(2)}) collective-permute-start(f32[6,64,128]{2,1,0:T(8,128)S(1)} %add.14), channel_id=1, source_target_pairs={{0,4},{1,5},{2,6},{3,7},{4,8},{5,9},{6,10},{7,11},{8,12},{9,13},{1... | collective-permute-start | bytes 589832 | tf_op jit(solution)/shard_map/ppermute | solution.py:18
  36.7 4.0 %shard_map.76.earlier_ref = f32[1024,768]{1,0:T(8,128)} custom-call(bf16[1024,768]{1,0:T(8,128)(2,1)} %get-tuple-element.61.q_ref, bf16[1024,768]{1,0:T(8,128)(2,1)} %get-tuple-element.62.k_ref, bf16[1024,768]{1,0:T(8,128)(2,1)} %get-tuple-element.63.v_ref, f32[1024,768]{1,0:T(8,128)} %shard_map.75.earlier_ref), custom_call_target="tpu_custom_call", output_to_operand_aliasing={{}: (3, {})} | custom-call | flops 805306368 | bytes 1966080 | tf_op jit(solution)/shard_map/pallas_call | solution.py:188
  40.8 4.2 %collective-permute-done.3 = f32[6,64,128]{2,1,0:T(8,128)S(1)} collective-permute-done((f32[6,64,128]{2,1,0:T(8,128)S(1)}, f32[6,64,128]{2,1,0:T(8,128)S(1)}, u32[]{:S(2)}, u32[]{:S(2)}) %collective-permute-start.3) | collective-permute-done | bytes 196640 | tf_op jit(solution)/shard_map/ppermute | solution.py:18
  45.1 0.0 copy-start.1
  45.1 1.5 %collective-permute-start.4 = (f32[6,64,128]{2,1,0:T(8,128)S(1)}, f32[6,64,128]{2,1,0:T(8,128)S(1)}, u32[]{:S(2)}, u32[]{:S(2)}) collective-permute-start(f32[6,64,128]{2,1,0:T(8,128)S(1)} %add.15.total_ref), channel_id=1, source_target_pairs={{0,8},{1,9},{2,10},{3,11},{4,12},{5,13},{6,14},{7,15},{16,24},{17,... | collective-permute-start | bytes 589832 | tf_op jit(solution)/shard_map/ppermute | solution.py:18
  46.6 4.0 %shard_map.77.inside_ref = f32[1024,768]{1,0:T(8,128)} custom-call(bf16[1024,768]{1,0:T(8,128)(2,1)} %get-tuple-element.61.q_ref, bf16[1024,768]{1,0:T(8,128)(2,1)} %get-tuple-element.62.k_ref, bf16[1024,768]{1,0:T(8,128)(2,1)} %get-tuple-element.63.v_ref, f32[1024,768]{1,0:T(8,128)} %shard_map.76.earlier_ref), custom_call_target="tpu_custom_call", output_to_operand_aliasing={{}: (3, {})} | custom-call | flops 805306368 | bytes 1966080 | tf_op jit(solution)/shard_map/pallas_call | solution.py:188
  50.6 0.0 copy-done.1
  50.6 7.8 %collective-permute-done.4.received_ref = f32[6,64,128]{2,1,0:T(8,128)S(1)} collective-permute-done((f32[6,64,128]{2,1,0:T(8,128)S(1)}, f32[6,64,128]{2,1,0:T(8,128)S(1)}, u32[]{:S(2)}, u32[]{:S(2)}) %collective-permute-start.4) | collective-permute-done | bytes 196640 | tf_op jit(solution)/shard_map/ppermute | solution.py:18
  58.4 0.0 copy-start.3
  58.4 0.7 %copy-done.3 = f32[6,64,128]{2,1,0:T(8,128)} copy-done((f32[6,64,128]{2,1,0:T(8,128)}, f32[6,64,128]{2,1,0:T(8,128)S(1)}, u32[]{:S(2)}) %copy-start.3) | copy-done | bytes 196632
  59.0 7.0 %shard_map.78 = bf16[1024,768]{1,0:T(8,128)(2,1)} custom-call(bf16[1024,768]{1,0:T(8,128)(2,1)} %get-tuple-element.61.q_ref, f32[2,6,64,128]{3,2,1,0:T(8,128)} %pad_maximum_fusion.base_ref, f32[6,64,128]{2,1,0:T(8,128)} %copy-done.1, f32[6,64,128]{2,1,0:T(8,128)} %copy-done.3, f32[1024,768]{1,0:T(8,128)} %shard_map.77.inside_ref, ...), custom_call_target="tpu_custom_call" | custom-call | tf_op jit(solution)/shard_map/pallas_call | solution.py:231
  (4 shorter events, 0.1 us)
Async XLA Ops:
  0.7 4.9 %collective-permute-start = (bf16[16,128]{1,0:T(8,128)(2,1)S(1)}, bf16[16,128]{1,0:T(8,128)(2,1)S(1)}, u32[]{:S(2)}, u32[]{:S(2)}) collective-permute-start(bf16[16,128]{1,0:T(8,128)(2,1)S(1)} %slice.3), channel_id=1, source_target_pairs={{0,1},{1,2},{2,3},{3,4},{4,5},{5,6},{6,7},{7,8},{8,9},{9,10},{10,1... | collective-permute-start | bytes 12296 | tf_op jit(solution)/shard_map/ppermute | solution.py:18
  5.6 0.6 copy-start.4
  20.2 6.1 %copy-start = (f32[6,64,128]{2,1,0:T(8,128)S(1)}, f32[6,64,128]{2,1,0:T(8,128)}, u32[]{:S(2)}) copy-start(f32[6,64,128]{2,1,0:T(8,128)} %get-tuple-element.41) | copy-start | bytes 589828
  20.2 6.1 %copy-start.2 = (f32[6,64,128]{2,1,0:T(8,128)S(1)}, f32[6,64,128]{2,1,0:T(8,128)}, u32[]{:S(2)}) copy-start(f32[6,64,128]{2,1,0:T(8,128)} %get-tuple-element.51) | copy-start | bytes 589828
  20.2 7.3 %collective-permute-start.1 = (f32[6,64,128]{2,1,0:T(8,128)}, f32[6,64,128]{2,1,0:T(8,128)S(1)}, u32[]{:S(2)}, u32[]{:S(2)}) collective-permute-start(f32[6,64,128]{2,1,0:T(8,128)} %get-tuple-element.41), channel_id=1, source_target_pairs={{0,1},{1,2},{2,3},{3,4},{4,5},{5,6},{6,7},{7,8},{8,9},{9,10},{10,1... | collective-permute-start | bytes 589832 | tf_op jit(solution)/shard_map/ppermute | solution.py:18
  27.5 7.9 %collective-permute-start.2 = (f32[6,64,128]{2,1,0:T(8,128)S(1)}, f32[6,64,128]{2,1,0:T(8,128)S(1)}, u32[]{:S(2)}, u32[]{:S(2)}) collective-permute-start(f32[6,64,128]{2,1,0:T(8,128)S(1)} %add.12), channel_id=1, source_target_pairs={{0,2},{1,3},{2,4},{3,5},{4,6},{5,7},{6,8},{7,9},{8,10},{9,11},{10,... | collective-permute-start | bytes 589832 | tf_op jit(solution)/shard_map/ppermute | solution.py:18
  35.4 9.6 %collective-permute-start.3 = (f32[6,64,128]{2,1,0:T(8,128)S(1)}, f32[6,64,128]{2,1,0:T(8,128)S(1)}, u32[]{:S(2)}, u32[]{:S(2)}) collective-permute-start(f32[6,64,128]{2,1,0:T(8,128)S(1)} %add.14), channel_id=1, source_target_pairs={{0,4},{1,5},{2,6},{3,7},{4,8},{5,9},{6,10},{7,11},{8,12},{9,13},{1... | collective-permute-start | bytes 589832 | tf_op jit(solution)/shard_map/ppermute | solution.py:18
  45.1 5.5 %copy-start.1 = (f32[6,64,128]{2,1,0:T(8,128)}, f32[6,64,128]{2,1,0:T(8,128)S(1)}, u32[]{:S(2)}) copy-start(f32[6,64,128]{2,1,0:T(8,128)S(1)} %add.15.total_ref) | copy-start | bytes 589828
  45.1 13.3 %collective-permute-start.4 = (f32[6,64,128]{2,1,0:T(8,128)S(1)}, f32[6,64,128]{2,1,0:T(8,128)S(1)}, u32[]{:S(2)}, u32[]{:S(2)}) collective-permute-start(f32[6,64,128]{2,1,0:T(8,128)S(1)} %add.15.total_ref), channel_id=1, source_target_pairs={{0,8},{1,9},{2,10},{3,11},{4,12},{5,13},{6,14},{7,15},{16,24},{17,... | collective-permute-start | bytes 589832 | tf_op jit(solution)/shard_map/ppermute | solution.py:18
  58.4 0.7 %copy-start.3 = (f32[6,64,128]{2,1,0:T(8,128)}, f32[6,64,128]{2,1,0:T(8,128)S(1)}, u32[]{:S(2)}) copy-start(f32[6,64,128]{2,1,0:T(8,128)S(1)} %collective-permute-done.4.received_ref) | copy-start | bytes 589828

commit v18 on v16

--- a/solution.py
+++ b/solution.py
@@ -28,17 +28,20 @@
     return total - value
 
 
-def embed_kernel(ticks_ref, prev_ref, conv_ref, gain_ref, qkv_hbm,
-                 emb_ref, q_ref, k_ref, v_ref, total_ref, first_ref, wide_ref, qkv_w_ref, copy_sem):
+def embed_kernel(ticks_ref, prev_ref, conv_hbm, gain_ref, qkv_hbm,
+                 emb_ref, q_ref, k_ref, v_ref, total_ref, first_ref, wide_ref, qkv_w_ref, copy_sem,
+                 conv_ref, conv_sem):
     b = pl.program_id(0)
     block_ticks = ticks_ref.shape[0]
     tokens = block_ticks // STRIDE
     model_width = emb_ref.shape[1]
 
     weight_copy = pltpu.make_async_copy(qkv_hbm, qkv_w_ref, copy_sem)
+    conv_copy = pltpu.make_async_copy(conv_hbm, conv_ref, conv_sem)
 
     @pl.when(b == 0)
     def _():
+        conv_copy.start()
         weight_copy.start()
         wide_ref[0:STRIDE, :] = prev_ref[STRIDE : 2 * STRIDE, :].astype(jnp.float32)
 
@@ -49,6 +52,11 @@
     wide_ref[STRIDE:, :] = ticks_ref[...].astype(jnp.float32)
     pieces = [wide_ref[pl.ds(j, tokens, stride=STRIDE), :] for j in range(2 * STRIDE)]
     lhs = jnp.concatenate(pieces, axis=1).astype(jnp.bfloat16)
+
+    @pl.when(b == 0)
+    def _():
+        conv_copy.wait()
+
     emb = jnp.dot(lhs, conv_ref[...], preferred_element_type=jnp.float32).astype(jnp.bfloat16)
     emb_ref[...] = emb
     embed_f = emb.astype(jnp.float32)
@@ -157,7 +165,7 @@
         in_specs=[
             pl.BlockSpec((block_ticks, feat), lambda b: (b, 0)),
             full((2 * STRIDE, feat)),
-            full(conv_weight.shape),
+            pl.BlockSpec(memory_space=pl.ANY),
             full((model_width,)),
             pl.BlockSpec(memory_space=pl.ANY),
         ],
@@ -167,6 +175,8 @@
         ] * 2,
         scratch_shapes=[pltpu.VMEM((block_ticks + STRIDE, feat), jnp.float32),
                         pltpu.VMEM(qkv_weight.shape, qkv_weight.dtype),
+                        pltpu.SemaphoreType.DMA(()),
+                        pltpu.VMEM(conv_weight.shape, conv_weight.dtype),
                         pltpu.SemaphoreType.DMA(())],
         compiler_params=pltpu.CompilerParams(dimension_semantics=("arbitrary",)),
     )(ticks, prev, conv_weight, norm_gain, qkv_weight)

time: 66.1 us -> 69.9 us (1.057)
  Pallas kernels: 37.1 us -> 40.9 us
    pallas_call x1, Pallas kernels: 14 us -> 17.8 us  [shards(): pl.pallas_call(embed_kernel, grid=(blocks,), in_specs=[pl.BlockSpec((bloc...]
  transfers between devices with their start and end apart: 5 -> 5, of which waited for: 5 -> 5; matrix products, arithmetic and copies ran while one was open for 3% -> 3% of each run, Pallas kernels for 24% -> 23%
where the time goes in v18:
time: 69.9 us; the launch traced here: 69.5 us
  Pallas kernels  40.9 us (59%)
  waiting for transfers between devices  16.4 us (23%)
  starting transfers between devices  8.02 us (11%)
  local copies, waits for them, and re-layouts  3.11 us (4%)
  other arithmetic  0.93 us (1%)
    pallas_call x1, Pallas kernels, shards(): pl.pallas_call(embed_kernel, grid=(blocks,), in_specs=[pl.BlockSpec((bloc...  17.8 us
    ppermute x5, waiting for transfers between devices, from_behind(): lax.ppermute(value, axis, [(source, source + steps) for source in range(i...  16.4 us
    pallas_call x4, Pallas kernels, inside_block(): pl.pallas_call(kernel, grid=(1,), in_specs=in_specs, out_specs=spec, out_...  16.1 us
    ppermute x5, starting transfers between devices, from_behind(): lax.ppermute(value, axis, [(source, source + steps) for source in range(i...  8.02 us
    pallas_call x1, Pallas kernels, shards(): pl.pallas_call(out_kernel, grid=(blocks,), in_specs=[rows_spec, base_spec...  7.02 us
  transfers between devices with their start and end apart: 5, of which 5 were waited for; matrix products, arithmetic and copies ran while one was open for 3% of the time, Pallas kernels for 23%

profile of v18, /device:TPU:30, one launch (start us, length us, event | category | flops | bytes accessed | tf_op | source)
XLA Modules:
  0.0 69.5 jit_solution(11128037302543047135)
XLA Ops:
  0.0 0.7 slice.3
  0.7 1.9 %collective-permute-start = (bf16[16,128]{1,0:T(8,128)(2,1)S(1)}, bf16[16,128]{1,0:T(8,128)(2,1)S(1)}, u32[]{:S(2)}, u32[]{:S(2)}) collective-permute-start(bf16[16,128]{1,0:T(8,128)(2,1)S(1)} %slice.3), channel_id=1, source_target_pairs={{0,1},{1,2},{2,3},{3,4},{4,5},{5,6},{6,7},{7,8},{8,9},{9,10},{10,1... | collective-permute-start | bytes 12296 | tf_op jit(solution)/shard_map/ppermute | solution.py:18
  2.6 3.0 %collective-permute-done.prev_ref = bf16[16,128]{1,0:T(8,128)(2,1)S(1)} collective-permute-done((bf16[16,128]{1,0:T(8,128)(2,1)S(1)}, bf16[16,128]{1,0:T(8,128)(2,1)S(1)}, u32[]{:S(2)}, u32[]{:S(2)}) %collective-permute-start) | collective-permute-done | bytes 4128 | tf_op jit(solution)/shard_map/ppermute | solution.py:18
  5.6 0.0 copy-start.5
  5.6 0.6 copy-done.5
  6.2 17.8 %shard_map.73 = (bf16[1024,768]{1,0:T(8,128)(2,1)}, bf16[1024,768]{1,0:T(8,128)(2,1)}, bf16[1024,768]{1,0:T(8,128)(2,1)}, bf16[1024,768]{1,0:T(8,128)(2,1)}, f32...) custom-call(bf16[8192,128]{1,0:T(8,128)(2,1)} %ticks_ref.1, bf16[16,128]{1,0:T(8,128)(2,1)} %copy-done.5, ...), custom_call_target="tpu_custom_call" | custom-call | tf_op jit(solution)/shard_map/pallas_call | solution.py:162
  24.0 0.0 copy-start
  24.0 0.0 copy-start.2
  24.0 0.0 copy-start.6
  24.0 2.1 %collective-permute-start.1 = (f32[6,64,128]{2,1,0:T(8,128)}, f32[6,64,128]{2,1,0:T(8,128)S(1)}, u32[]{:S(2)}, u32[]{:S(2)}) collective-permute-start(f32[6,64,128]{2,1,0:T(8,128)} %get-tuple-element.40), channel_id=1, source_target_pairs={{0,1},{1,2},{2,3},{3,4},{4,5},{5,6},{6,7},{7,8},{8,9},{9,10},{10,1... | collective-permute-start | bytes 589832 | tf_op jit(solution)/shard_map/ppermute | solution.py:18
  26.1 4.0 %shard_map.74.earlier_ref = f32[1024,768]{1,0:T(8,128)} custom-call(bf16[1024,768]{1,0:T(8,128)(2,1)} %get-tuple-element.58.q_ref, bf16[1024,768]{1,0:T(8,128)(2,1)} %get-tuple-element.59.k_ref, bf16[1024,768]{1,0:T(8,128)(2,1)} %get-tuple-element.60.v_ref), custom_call_target="tpu_custom_call" | custom-call | flops 805306368 | bytes 1966080 | tf_op jit(solution)/shard_map/pallas_call | solution.py:198
  30.1 1.3 %collective-permute-done.1 = f32[6,64,128]{2,1,0:T(8,128)S(1)} collective-permute-done((f32[6,64,128]{2,1,0:T(8,128)}, f32[6,64,128]{2,1,0:T(8,128)S(1)}, u32[]{:S(2)}, u32[]{:S(2)}) %collective-permute-start.1) | collective-permute-done | bytes 196640 | tf_op jit(solution)/shard_map/ppermute | solution.py:18
  31.3 0.0 copy-done
  31.4 1.3 %collective-permute-start.2 = (f32[6,64,128]{2,1,0:T(8,128)S(1)}, f32[6,64,128]{2,1,0:T(8,128)S(1)}, u32[]{:S(2)}, u32[]{:S(2)}) collective-permute-start(f32[6,64,128]{2,1,0:T(8,128)S(1)} %add.13), channel_id=1, source_target_pairs={{0,2},{1,3},{2,4},{3,5},{4,6},{5,7},{6,8},{7,9},{8,10},{9,11},{10,... | collective-permute-start | bytes 589832 | tf_op jit(solution)/shard_map/ppermute | solution.py:18
  32.7 0.0 copy-done.2
  32.7 0.3 copy.13
  33.0 0.2 reshape.10
  33.2 0.0 copy-done.6
  33.2 0.6 reshape.11.hgain_ref
  33.8 0.0 copy-start.3
  33.8 4.0 %shard_map.75.earlier_ref = f32[1024,768]{1,0:T(8,128)} custom-call(bf16[1024,768]{1,0:T(8,128)(2,1)} %get-tuple-element.58.q_ref, bf16[1024,768]{1,0:T(8,128)(2,1)} %get-tuple-element.59.k_ref, bf16[1024,768]{1,0:T(8,128)(2,1)} %get-tuple-element.60.v_ref, f32[1024,768]{1,0:T(8,128)} %shard_map.74.earlier_ref), custom_call_target="tpu_custom_call", output_to_operand_aliasing={{}: (3, {})} | custom-call | flops 805306368 | bytes 1966080 | tf_op jit(solution)/shard_map/pallas_call | solution.py:198
  37.9 1.4 %collective-permute-done.2 = f32[6,64,128]{2,1,0:T(8,128)S(1)} collective-permute-done((f32[6,64,128]{2,1,0:T(8,128)S(1)}, f32[6,64,128]{2,1,0:T(8,128)S(1)}, u32[]{:S(2)}, u32[]{:S(2)}) %collective-permute-start.2) | collective-permute-done | bytes 196640 | tf_op jit(solution)/shard_map/ppermute | solution.py:18
  39.3 1.3 %collective-permute-start.3 = (f32[6,64,128]{2,1,0:T(8,128)S(1)}, f32[6,64,128]{2,1,0:T(8,128)S(1)}, u32[]{:S(2)}, u32[]{:S(2)}) collective-permute-start(f32[6,64,128]{2,1,0:T(8,128)S(1)} %add.14), channel_id=1, source_target_pairs={{0,4},{1,5},{2,6},{3,7},{4,8},{5,9},{6,10},{7,11},{8,12},{9,13},{1... | collective-permute-start | bytes 589832 | tf_op jit(solution)/shard_map/ppermute | solution.py:18
  40.6 0.0 copy-done.3
  40.6 4.0 %shard_map.76.earlier_ref = f32[1024,768]{1,0:T(8,128)} custom-call(bf16[1024,768]{1,0:T(8,128)(2,1)} %get-tuple-element.58.q_ref, bf16[1024,768]{1,0:T(8,128)(2,1)} %get-tuple-element.59.k_ref, bf16[1024,768]{1,0:T(8,128)(2,1)} %get-tuple-element.60.v_ref, f32[1024,768]{1,0:T(8,128)} %shard_map.75.earlier_ref), custom_call_target="tpu_custom_call", output_to_operand_aliasing={{}: (3, {})} | custom-call | flops 805306368 | bytes 1966080 | tf_op jit(solution)/shard_map/pallas_call | solution.py:198
  44.6 4.3 %collective-permute-done.3 = f32[6,64,128]{2,1,0:T(8,128)S(1)} collective-permute-done((f32[6,64,128]{2,1,0:T(8,128)S(1)}, f32[6,64,128]{2,1,0:T(8,128)S(1)}, u32[]{:S(2)}, u32[]{:S(2)}) %collective-permute-start.3) | collective-permute-done | bytes 196640 | tf_op jit(solution)/shard_map/ppermute | solution.py:18
  48.9 0.0 copy-start.1
  48.9 1.5 %collective-permute-start.4 = (f32[6,64,128]{2,1,0:T(8,128)S(1)}, f32[6,64,128]{2,1,0:T(8,128)S(1)}, u32[]{:S(2)}, u32[]{:S(2)}) collective-permute-start(f32[6,64,128]{2,1,0:T(8,128)S(1)} %add.15.total_ref), channel_id=1, source_target_pairs={{0,8},{1,9},{2,10},{3,11},{4,12},{5,13},{6,14},{7,15},{16,24},{17,... | collective-permute-start | bytes 589832 | tf_op jit(solution)/shard_map/ppermute | solution.py:18
  50.4 0.8 %pad_maximum_fusion.base_ref = f32[2,6,64,128]{3,2,1,0:T(8,128)} fusion(f32[1,6,64,128]{3,2,1,0:T(8,128)S(1)} %get-tuple-element.66, f32[1,6,64,128]{3,2,1,0:T(8,128)S(1)} %get-tuple-element.65), kind=kLoop, calls=%fused_computation | loop fusion | flops 98304 | bytes 786432 | tf_op jit(solution)/shard_map/stack | solution.py:233
  51.2 4.0 %shard_map.77.inside_ref = f32[1024,768]{1,0:T(8,128)} custom-call(bf16[1024,768]{1,0:T(8,128)(2,1)} %get-tuple-element.58.q_ref, bf16[1024,768]{1,0:T(8,128)(2,1)} %get-tuple-element.59.k_ref, bf16[1024,768]{1,0:T(8,128)(2,1)} %get-tuple-element.60.v_ref, f32[1024,768]{1,0:T(8,128)} %shard_map.76.earlier_ref), custom_call_target="tpu_custom_call", output_to_operand_aliasing={{}: (3, {})} | custom-call | flops 805306368 | bytes 1966080 | tf_op jit(solution)/shard_map/pallas_call | solution.py:198
  55.3 0.0 copy-done.1
  55.3 6.5 %collective-permute-done.4.received_ref = f32[6,64,128]{2,1,0:T(8,128)S(1)} collective-permute-done((f32[6,64,128]{2,1,0:T(8,128)S(1)}, f32[6,64,128]{2,1,0:T(8,128)S(1)}, u32[]{:S(2)}, u32[]{:S(2)}) %collective-permute-start.4) | collective-permute-done | bytes 196640 | tf_op jit(solution)/shard_map/ppermute | solution.py:18
  61.8 0.0 copy-start.4
  61.8 0.7 copy-done.4
  62.5 7.0 %shard_map.78 = bf16[1024,768]{1,0:T(8,128)(2,1)} custom-call(bf16[1024,768]{1,0:T(8,128)(2,1)} %get-tuple-element.58.q_ref, f32[2,6,64,128]{3,2,1,0:T(8,128)} %pad_maximum_fusion.base_ref, f32[6,64,128]{2,1,0:T(8,128)} %copy-done.1, f32[6,64,128]{2,1,0:T(8,128)} %copy-done.4, f32[1024,768]{1,0:T(8,128)} %shard_map.77.inside_ref, ...), custom_call_target="tpu_custom_call" | custom-call | tf_op jit(solution)/shard_map/pallas_call | solution.py:236
  (4 shorter events, 0.1 us)
Async XLA Ops:
  0.7 4.9 %collective-permute-start = (bf16[16,128]{1,0:T(8,128)(2,1)S(1)}, bf16[16,128]{1,0:T(8,128)(2,1)S(1)}, u32[]{:S(2)}, u32[]{:S(2)}) collective-permute-start(bf16[16,128]{1,0:T(8,128)(2,1)S(1)} %slice.3), channel_id=1, source_target_pairs={{0,1},{1,2},{2,3},{3,4},{4,5},{5,6},{6,7},{7,8},{8,9},{9,10},{10,1... | collective-permute-start | bytes 12296 | tf_op jit(solution)/shard_map/ppermute | solution.py:18
  5.6 0.6 copy-start.5
  24.0 7.4 %copy-start = (f32[6,64,128]{2,1,0:T(8,128)S(1)}, f32[6,64,128]{2,1,0:T(8,128)}, u32[]{:S(2)}) copy-start(f32[6,64,128]{2,1,0:T(8,128)} %get-tuple-element.40) | copy-start | bytes 589828
  24.0 8.7 %copy-start.2 = (f32[12,64,64]{2,1,0:T(8,128)S(1)}, f32[12,64,64]{2,1,0:T(8,128)}, u32[]{:S(2)}) copy-start(f32[12,64,64]{2,1,0:T(8,128)} %param.13) | copy-start | bytes 589828
  24.0 9.2 %copy-start.6 = (f32[768]{0:T(1024)S(1)}, f32[768]{0:T(1024)}, u32[]{:S(2)}) copy-start(f32[768]{0:T(1024)} %param.11) | copy-start | bytes 9220
  24.0 7.3 %collective-permute-start.1 = (f32[6,64,128]{2,1,0:T(8,128)}, f32[6,64,128]{2,1,0:T(8,128)S(1)}, u32[]{:S(2)}, u32[]{:S(2)}) collective-permute-start(f32[6,64,128]{2,1,0:T(8,128)} %get-tuple-element.40), channel_id=1, source_target_pairs={{0,1},{1,2},{2,3},{3,4},{4,5},{5,6},{6,7},{7,8},{8,9},{9,10},{10,1... | collective-permute-start | bytes 589832 | tf_op jit(solution)/shard_map/ppermute | solution.py:18
  31.4 7.9 %collective-permute-start.2 = (f32[6,64,128]{2,1,0:T(8,128)S(1)}, f32[6,64,128]{2,1,0:T(8,128)S(1)}, u32[]{:S(2)}, u32[]{:S(2)}) collective-permute-start(f32[6,64,128]{2,1,0:T(8,128)S(1)} %add.13), channel_id=1, source_target_pairs={{0,2},{1,3},{2,4},{3,5},{4,6},{5,7},{6,8},{7,9},{8,10},{9,11},{10,... | collective-permute-start | bytes 589832 | tf_op jit(solution)/shard_map/ppermute | solution.py:18
  33.8 6.7 %copy-start.3 = (f32[6,64,128]{2,1,0:T(8,128)S(1)}, f32[6,64,128]{2,1,0:T(8,128)}, u32[]{:S(2)}) copy-start(f32[6,64,128]{2,1,0:T(8,128)} %get-tuple-element.37) | copy-start | bytes 589828
  39.3 9.6 %collective-permute-start.3 = (f32[6,64,128]{2,1,0:T(8,128)S(1)}, f32[6,64,128]{2,1,0:T(8,128)S(1)}, u32[]{:S(2)}, u32[]{:S(2)}) collective-permute-start(f32[6,64,128]{2,1,0:T(8,128)S(1)} %add.14), channel_id=1, source_target_pairs={{0,4},{1,5},{2,6},{3,7},{4,8},{5,9},{6,10},{7,11},{8,12},{9,13},{1... | collective-permute-start | bytes 589832 | tf_op jit(solution)/shard_map/ppermute | solution.py:18
  48.9 6.3 %copy-start.1 = (f32[6,64,128]{2,1,0:T(8,128)}, f32[6,64,128]{2,1,0:T(8,128)S(1)}, u32[]{:S(2)}) copy-start(f32[6,64,128]{2,1,0:T(8,128)S(1)} %add.15.total_ref) | copy-start | bytes 589828
  48.9 12.9 %collective-permute-start.4 = (f32[6,64,128]{2,1,0:T(8,128)S(1)}, f32[6,64,128]{2,1,0:T(8,128)S(1)}, u32[]{:S(2)}, u32[]{:S(2)}) collective-permute-start(f32[6,64,128]{2,1,0:T(8,128)S(1)} %add.15.total_ref), channel_id=1, source_target_pairs={{0,8},{1,9},{2,10},{3,11},{4,12},{5,13},{6,14},{7,15},{16,24},{17,... | collective-permute-start | bytes 589832 | tf_op jit(solution)/shard_map/ppermute | solution.py:18
  61.8 0.7 copy-start.4

commit v19 on v16

--- a/solution.py
+++ b/solution.py
@@ -221,24 +221,26 @@
     for block in range(1, blocks):
         base.append(base[-1] + first_state)
     base = jnp.stack(base)
-    base_spec = pl.BlockSpec((1, pairs, head_size, PAIR), lambda b: (b, 0, 0, 0))
+    out_rows = BLK // 2
+    base_spec = pl.BlockSpec((1, pairs, head_size, PAIR), lambda b: (b * out_rows // BLK, 0, 0, 0))
+    out_rows_spec = pl.BlockSpec((out_rows, model_width), lambda b: (b, 0))
 
     return pl.pallas_call(
         out_kernel,
-        grid=(blocks,),
+        grid=(token_count // out_rows,),
         in_specs=[
-            rows_spec,
+            out_rows_spec,
             base_spec,
             state_spec,
             state_spec,
-            rows_spec,
-            rows_spec,
+            out_rows_spec,
+            out_rows_spec,
             full((1, model_width)),
             full(out_weight.shape),
         ],
-        out_specs=rows_spec,
+        out_specs=out_rows_spec,
         out_shape=jax.ShapeDtypeStruct((token_count, model_width), jnp.bfloat16),
-        scratch_shapes=[pltpu.VMEM((BLK, model_width), jnp.bfloat16)],
+        scratch_shapes=[pltpu.VMEM((out_rows, model_width), jnp.bfloat16)],
         compiler_params=pltpu.CompilerParams(dimension_semantics=("arbitrary",)),
     )(queries, base, total, received, inside, emb, head_gain.reshape(1, model_width), out_weight)
 

time: 66.1 us -> 66.8 us (1.011)
  no operation moved by 1% of the time
where the time goes in v19:
time: 66.8 us; the launch traced here: 66.4 us
  Pallas kernels  37.7 us (56%)
  waiting for transfers between devices  16.6 us (25%)
  starting transfers between devices  7.84 us (12%)
  local copies, waits for them, and re-layouts  3.11 us (5%)
  other arithmetic  0.93 us (1%)
    ppermute x5, waiting for transfers between devices, from_behind(): lax.ppermute(value, axis, [(source, source + steps) for source in range(i...  16.6 us
    pallas_call x4, Pallas kernels, inside_block(): pl.pallas_call(kernel, grid=(1,), in_specs=in_specs, out_specs=spec, out_...  16.1 us
    pallas_call x1, Pallas kernels, shards(): pl.pallas_call(embed_kernel, grid=(blocks,), in_specs=[pl.BlockSpec((bloc...  14 us
    ppermute x5, starting transfers between devices, from_behind(): lax.ppermute(value, axis, [(source, source + steps) for source in range(i...  7.84 us
    pallas_call x1, Pallas kernels, shards(): pl.pallas_call(out_kernel, grid=(token_count // out_rows,), in_specs=[out...  7.62 us
  transfers between devices with their start and end apart: 5, of which 5 were waited for; matrix products, arithmetic and copies ran while one was open for 3% of the time, Pallas kernels for 24%

profile of v19, /device:TPU:30, one launch (start us, length us, event | category | flops | bytes accessed | tf_op | source)
XLA Modules:
  0.0 66.4 jit_solution(7823909628574297455)
XLA Ops:
  0.0 0.7 %slice.3 = bf16[16,128]{1,0:T(8,128)(2,1)S(1)} slice(bf16[8192,128]{1,0:T(8,128)(2,1)} %ticks_ref.1), slice={[8176:8192], [0:128]} | slice | bytes 8192 | tf_op jit(solution)/shard_map/slice | solution.py:151
  0.7 1.9 %collective-permute-start = (bf16[16,128]{1,0:T(8,128)(2,1)S(1)}, bf16[16,128]{1,0:T(8,128)(2,1)S(1)}, u32[]{:S(2)}, u32[]{:S(2)}) collective-permute-start(bf16[16,128]{1,0:T(8,128)(2,1)S(1)} %slice.3), channel_id=1, source_target_pairs={{0,1},{1,2},{2,3},{3,4},{4,5},{5,6},{6,7},{7,8},{8,9},{9,10},{10,1... | collective-permute-start | bytes 12296 | tf_op jit(solution)/shard_map/ppermute | solution.py:18
  2.6 3.0 %collective-permute-done.prev_ref = bf16[16,128]{1,0:T(8,128)(2,1)S(1)} collective-permute-done((bf16[16,128]{1,0:T(8,128)(2,1)S(1)}, bf16[16,128]{1,0:T(8,128)(2,1)S(1)}, u32[]{:S(2)}, u32[]{:S(2)}) %collective-permute-start) | collective-permute-done | bytes 4128 | tf_op jit(solution)/shard_map/ppermute | solution.py:18
  5.6 0.0 copy-start.5
  5.6 0.6 copy-done.5
  6.2 14.0 %shard_map.73 = (bf16[1024,768]{1,0:T(8,128)(2,1)}, bf16[1024,768]{1,0:T(8,128)(2,1)}, bf16[1024,768]{1,0:T(8,128)(2,1)}, bf16[1024,768]{1,0:T(8,128)(2,1)}, f32...) custom-call(bf16[8192,128]{1,0:T(8,128)(2,1)} %ticks_ref.1, bf16[16,128]{1,0:T(8,128)(2,1)} %copy-done.5, ...), custom_call_target="tpu_custom_call" | custom-call | tf_op jit(solution)/shard_map/pallas_call | solution.py:154
  20.2 0.0 copy-start
  20.2 0.0 copy-start.2
  20.2 0.0 copy-start.6
  20.2 2.1 %collective-permute-start.1 = (f32[6,64,128]{2,1,0:T(8,128)}, f32[6,64,128]{2,1,0:T(8,128)S(1)}, u32[]{:S(2)}, u32[]{:S(2)}) collective-permute-start(f32[6,64,128]{2,1,0:T(8,128)} %get-tuple-element.40), channel_id=1, source_target_pairs={{0,1},{1,2},{2,3},{3,4},{4,5},{5,6},{6,7},{7,8},{8,9},{9,10},{10,1... | collective-permute-start | bytes 589832 | tf_op jit(solution)/shard_map/ppermute | solution.py:18
  22.3 4.0 %shard_map.74.earlier_ref = f32[1024,768]{1,0:T(8,128)} custom-call(bf16[1024,768]{1,0:T(8,128)(2,1)} %get-tuple-element.58.q_ref, bf16[1024,768]{1,0:T(8,128)(2,1)} %get-tuple-element.59.k_ref, bf16[1024,768]{1,0:T(8,128)(2,1)} %get-tuple-element.60.v_ref), custom_call_target="tpu_custom_call" | custom-call | flops 805306368 | bytes 1966080 | tf_op jit(solution)/shard_map/pallas_call | solution.py:188
  26.3 1.3 %collective-permute-done.1 = f32[6,64,128]{2,1,0:T(8,128)S(1)} collective-permute-done((f32[6,64,128]{2,1,0:T(8,128)}, f32[6,64,128]{2,1,0:T(8,128)S(1)}, u32[]{:S(2)}, u32[]{:S(2)}) %collective-permute-start.1) | collective-permute-done | bytes 196640 | tf_op jit(solution)/shard_map/ppermute | solution.py:18
  27.6 0.0 copy-done
  27.6 1.3 %collective-permute-start.2 = (f32[6,64,128]{2,1,0:T(8,128)S(1)}, f32[6,64,128]{2,1,0:T(8,128)S(1)}, u32[]{:S(2)}, u32[]{:S(2)}) collective-permute-start(f32[6,64,128]{2,1,0:T(8,128)S(1)} %add.13), channel_id=1, source_target_pairs={{0,2},{1,3},{2,4},{3,5},{4,6},{5,7},{6,8},{7,9},{8,10},{9,11},{10,... | collective-permute-start | bytes 589832 | tf_op jit(solution)/shard_map/ppermute | solution.py:18
  28.9 0.0 copy-done.2
  28.9 0.3 copy.13
  29.2 0.2 reshape.10
  29.5 0.0 copy-done.6
  29.5 0.6 reshape.11.hgain_ref
  30.1 0.0 copy-start.3
  30.1 4.0 %shard_map.75.earlier_ref = f32[1024,768]{1,0:T(8,128)} custom-call(bf16[1024,768]{1,0:T(8,128)(2,1)} %get-tuple-element.58.q_ref, bf16[1024,768]{1,0:T(8,128)(2,1)} %get-tuple-element.59.k_ref, bf16[1024,768]{1,0:T(8,128)(2,1)} %get-tuple-element.60.v_ref, f32[1024,768]{1,0:T(8,128)} %shard_map.74.earlier_ref), custom_call_target="tpu_custom_call", output_to_operand_aliasing={{}: (3, {})} | custom-call | flops 805306368 | bytes 1966080 | tf_op jit(solution)/shard_map/pallas_call | solution.py:188
  34.1 1.4 %collective-permute-done.2 = f32[6,64,128]{2,1,0:T(8,128)S(1)} collective-permute-done((f32[6,64,128]{2,1,0:T(8,128)S(1)}, f32[6,64,128]{2,1,0:T(8,128)S(1)}, u32[]{:S(2)}, u32[]{:S(2)}) %collective-permute-start.2) | collective-permute-done | bytes 196640 | tf_op jit(solution)/shard_map/ppermute | solution.py:18
  35.5 1.3 %collective-permute-start.3 = (f32[6,64,128]{2,1,0:T(8,128)S(1)}, f32[6,64,128]{2,1,0:T(8,128)S(1)}, u32[]{:S(2)}, u32[]{:S(2)}) collective-permute-start(f32[6,64,128]{2,1,0:T(8,128)S(1)} %add.14), channel_id=1, source_target_pairs={{0,4},{1,5},{2,6},{3,7},{4,8},{5,9},{6,10},{7,11},{8,12},{9,13},{1... | collective-permute-start | bytes 589832 | tf_op jit(solution)/shard_map/ppermute | solution.py:18
  36.8 0.0 copy-done.3
  36.9 4.0 %shard_map.76.earlier_ref = f32[1024,768]{1,0:T(8,128)} custom-call(bf16[1024,768]{1,0:T(8,128)(2,1)} %get-tuple-element.58.q_ref, bf16[1024,768]{1,0:T(8,128)(2,1)} %get-tuple-element.59.k_ref, bf16[1024,768]{1,0:T(8,128)(2,1)} %get-tuple-element.60.v_ref, f32[1024,768]{1,0:T(8,128)} %shard_map.75.earlier_ref), custom_call_target="tpu_custom_call", output_to_operand_aliasing={{}: (3, {})} | custom-call | flops 805306368 | bytes 1966080 | tf_op jit(solution)/shard_map/pallas_call | solution.py:188
  40.9 4.3 %collective-permute-done.3 = f32[6,64,128]{2,1,0:T(8,128)S(1)} collective-permute-done((f32[6,64,128]{2,1,0:T(8,128)S(1)}, f32[6,64,128]{2,1,0:T(8,128)S(1)}, u32[]{:S(2)}, u32[]{:S(2)}) %collective-permute-start.3) | collective-permute-done | bytes 196640 | tf_op jit(solution)/shard_map/ppermute | solution.py:18
  45.2 0.0 copy-start.1
  45.2 1.3 %collective-permute-start.4 = (f32[6,64,128]{2,1,0:T(8,128)S(1)}, f32[6,64,128]{2,1,0:T(8,128)S(1)}, u32[]{:S(2)}, u32[]{:S(2)}) collective-permute-start(f32[6,64,128]{2,1,0:T(8,128)S(1)} %add.15.total_ref), channel_id=1, source_target_pairs={{0,8},{1,9},{2,10},{3,11},{4,12},{5,13},{6,14},{7,15},{16,24},{17,... | collective-permute-start | bytes 589832 | tf_op jit(solution)/shard_map/ppermute | solution.py:18
  46.5 0.8 %pad_maximum_fusion.base_ref = f32[2,6,64,128]{3,2,1,0:T(8,128)} fusion(f32[1,6,64,128]{3,2,1,0:T(8,128)S(1)} %get-tuple-element.66, f32[1,6,64,128]{3,2,1,0:T(8,128)S(1)} %get-tuple-element.65), kind=kLoop, calls=%fused_computation | loop fusion | flops 98304 | bytes 786432 | tf_op jit(solution)/shard_map/stack | solution.py:223
  47.3 4.0 %shard_map.77.inside_ref = f32[1024,768]{1,0:T(8,128)} custom-call(bf16[1024,768]{1,0:T(8,128)(2,1)} %get-tuple-element.58.q_ref, bf16[1024,768]{1,0:T(8,128)(2,1)} %get-tuple-element.59.k_ref, bf16[1024,768]{1,0:T(8,128)(2,1)} %get-tuple-element.60.v_ref, f32[1024,768]{1,0:T(8,128)} %shard_map.76.earlier_ref), custom_call_target="tpu_custom_call", output_to_operand_aliasing={{}: (3, {})} | custom-call | flops 805306368 | bytes 1966080 | tf_op jit(solution)/shard_map/pallas_call | solution.py:188
  51.3 0.0 copy-done.1
  51.3 6.7 %collective-permute-done.4.received_ref = f32[6,64,128]{2,1,0:T(8,128)S(1)} collective-permute-done((f32[6,64,128]{2,1,0:T(8,128)S(1)}, f32[6,64,128]{2,1,0:T(8,128)S(1)}, u32[]{:S(2)}, u32[]{:S(2)}) %collective-permute-start.4) | collective-permute-done | bytes 196640 | tf_op jit(solution)/shard_map/ppermute | solution.py:18
  58.1 0.0 copy-start.4
  58.1 0.7 %copy-done.4 = f32[6,64,128]{2,1,0:T(8,128)} copy-done((f32[6,64,128]{2,1,0:T(8,128)}, f32[6,64,128]{2,1,0:T(8,128)S(1)}, u32[]{:S(2)}) %copy-start.4) | copy-done | bytes 196632
  58.7 7.6 %shard_map.78 = bf16[1024,768]{1,0:T(8,128)(2,1)} custom-call(bf16[1024,768]{1,0:T(8,128)(2,1)} %get-tuple-element.58.q_ref, f32[2,6,64,128]{3,2,1,0:T(8,128)} %pad_maximum_fusion.base_ref, f32[6,64,128]{2,1,0:T(8,128)} %copy-done.1, f32[6,64,128]{2,1,0:T(8,128)} %copy-done.4, f32[1024,768]{1,0:T(8,128)} %shard_map.77.inside_ref, ...), custom_call_target="tpu_custom_call" | custom-call | tf_op jit(solution)/shard_map/pallas_call | solution.py:228
  (4 shorter events, 0.1 us)
Async XLA Ops:
  0.7 4.9 %collective-permute-start = (bf16[16,128]{1,0:T(8,128)(2,1)S(1)}, bf16[16,128]{1,0:T(8,128)(2,1)S(1)}, u32[]{:S(2)}, u32[]{:S(2)}) collective-permute-start(bf16[16,128]{1,0:T(8,128)(2,1)S(1)} %slice.3), channel_id=1, source_target_pairs={{0,1},{1,2},{2,3},{3,4},{4,5},{5,6},{6,7},{7,8},{8,9},{9,10},{10,1... | collective-permute-start | bytes 12296 | tf_op jit(solution)/shard_map/ppermute | solution.py:18
  5.6 0.6 copy-start.5
  20.2 7.4 %copy-start = (f32[6,64,128]{2,1,0:T(8,128)S(1)}, f32[6,64,128]{2,1,0:T(8,128)}, u32[]{:S(2)}) copy-start(f32[6,64,128]{2,1,0:T(8,128)} %get-tuple-element.40) | copy-start | bytes 589828
  20.2 8.7 %copy-start.2 = (f32[12,64,64]{2,1,0:T(8,128)S(1)}, f32[12,64,64]{2,1,0:T(8,128)}, u32[]{:S(2)}) copy-start(f32[12,64,64]{2,1,0:T(8,128)} %param.13) | copy-start | bytes 589828
  20.2 9.2 %copy-start.6 = (f32[768]{0:T(1024)S(1)}, f32[768]{0:T(1024)}, u32[]{:S(2)}) copy-start(f32[768]{0:T(1024)} %param.11) | copy-start | bytes 9220
  20.2 7.3 %collective-permute-start.1 = (f32[6,64,128]{2,1,0:T(8,128)}, f32[6,64,128]{2,1,0:T(8,128)S(1)}, u32[]{:S(2)}, u32[]{:S(2)}) collective-permute-start(f32[6,64,128]{2,1,0:T(8,128)} %get-tuple-element.40), channel_id=1, source_target_pairs={{0,1},{1,2},{2,3},{3,4},{4,5},{5,6},{6,7},{7,8},{8,9},{9,10},{10,1... | collective-permute-start | bytes 589832 | tf_op jit(solution)/shard_map/ppermute | solution.py:18
  27.6 7.9 %collective-permute-start.2 = (f32[6,64,128]{2,1,0:T(8,128)S(1)}, f32[6,64,128]{2,1,0:T(8,128)S(1)}, u32[]{:S(2)}, u32[]{:S(2)}) collective-permute-start(f32[6,64,128]{2,1,0:T(8,128)S(1)} %add.13), channel_id=1, source_target_pairs={{0,2},{1,3},{2,4},{3,5},{4,6},{5,7},{6,8},{7,9},{8,10},{9,11},{10,... | collective-permute-start | bytes 589832 | tf_op jit(solution)/shard_map/ppermute | solution.py:18
  30.1 6.8 %copy-start.3 = (f32[6,64,128]{2,1,0:T(8,128)S(1)}, f32[6,64,128]{2,1,0:T(8,128)}, u32[]{:S(2)}) copy-start(f32[6,64,128]{2,1,0:T(8,128)} %get-tuple-element.37) | copy-start | bytes 589828
  35.5 9.6 %collective-permute-start.3 = (f32[6,64,128]{2,1,0:T(8,128)S(1)}, f32[6,64,128]{2,1,0:T(8,128)S(1)}, u32[]{:S(2)}, u32[]{:S(2)}) collective-permute-start(f32[6,64,128]{2,1,0:T(8,128)S(1)} %add.14), channel_id=1, source_target_pairs={{0,4},{1,5},{2,6},{3,7},{4,8},{5,9},{6,10},{7,11},{8,12},{9,13},{1... | collective-permute-start | bytes 589832 | tf_op jit(solution)/shard_map/ppermute | solution.py:18
  45.2 6.2 %copy-start.1 = (f32[6,64,128]{2,1,0:T(8,128)}, f32[6,64,128]{2,1,0:T(8,128)S(1)}, u32[]{:S(2)}) copy-start(f32[6,64,128]{2,1,0:T(8,128)S(1)} %add.15.total_ref) | copy-start | bytes 589828
  45.2 12.9 %collective-permute-start.4 = (f32[6,64,128]{2,1,0:T(8,128)S(1)}, f32[6,64,128]{2,1,0:T(8,128)S(1)}, u32[]{:S(2)}, u32[]{:S(2)}) collective-permute-start(f32[6,64,128]{2,1,0:T(8,128)S(1)} %add.15.total_ref), channel_id=1, source_target_pairs={{0,8},{1,9},{2,10},{3,11},{4,12},{5,13},{6,14},{7,15},{16,24},{17,... | collective-permute-start | bytes 589832 | tf_op jit(solution)/shard_map/ppermute | solution.py:18
  58.1 0.7 %copy-start.4 = (f32[6,64,128]{2,1,0:T(8,128)}, f32[6,64,128]{2,1,0:T(8,128)S(1)}, u32[]{:S(2)}) copy-start(f32[6,64,128]{2,1,0:T(8,128)S(1)} %collective-permute-done.4.received_ref) | copy-start | bytes 589828

commit v20 on v16

--- a/solution.py
+++ b/solution.py
@@ -28,8 +28,8 @@
     return total - value
 
 
-def embed_kernel(ticks_ref, prev_ref, conv_ref, gain_ref, qkv_hbm,
-                 emb_ref, q_ref, k_ref, v_ref, total_ref, first_ref, wide_ref, qkv_w_ref, copy_sem):
+def embed_kernel(ticks_ref, prev_ref, conv_ref, gain_ref, qkv_hbm, start_ref,
+                 emb_ref, q_ref, k_ref, v_ref, total_ref, first_ref, base_ref, wide_ref, qkv_w_ref, copy_sem):
     b = pl.program_id(0)
     block_ticks = ticks_ref.shape[0]
     tokens = block_ticks // STRIDE
@@ -75,8 +75,13 @@
                              preferred_element_type=jnp.float32)
         half = PAIR // 2
         packed = jnp.where(first, kv[:half], kv[half:])
-        total_ref[pair] = jnp.where(b > 0, total_ref[pair], 0.0) + packed
-        first_ref[pair] = jnp.where(b > 0, first_ref[pair], packed)
+        total = jnp.where(b > 0, total_ref[pair], 0.0) + packed
+        first_block = jnp.where(b > 0, first_ref[pair], packed)
+        total_ref[pair] = total
+        first_ref[pair] = first_block
+        base = start_ref[pair] - total
+        base_ref[0, pair] = base
+        base_ref[1, pair] = base + first_block
 
 
 def inside_kernel(q_ref, k_ref, v_ref, earlier_ref, inside_ref):
@@ -151,7 +156,9 @@
     prev = from_behind(ticks[tick_count - 2 * STRIDE :], "inner", 1)
     rows_spec = pl.BlockSpec((BLK, model_width), lambda b: (b, 0))
     state_spec = full((pairs, head_size, PAIR))
-    emb, queries, keys, values, local, first_state = pl.pallas_call(
+    packed_in = state_in.reshape(pairs, 2, head_size, head_size).transpose(0, 2, 1, 3)
+    packed_in = packed_in.reshape(pairs, head_size, PAIR)
+    emb, queries, keys, values, local, first_state, base = pl.pallas_call(
         embed_kernel,
         grid=(blocks,),
         in_specs=[
@@ -160,16 +167,18 @@
             full(conv_weight.shape),
             full((model_width,)),
             pl.BlockSpec(memory_space=pl.ANY),
+            state_spec,
         ],
-        out_specs=[rows_spec, rows_spec, rows_spec, rows_spec, state_spec, state_spec],
+        out_specs=[rows_spec, rows_spec, rows_spec, rows_spec, state_spec, state_spec,
+                   full((blocks, pairs, head_size, PAIR))],
         out_shape=[jax.ShapeDtypeStruct((token_count, model_width), jnp.bfloat16)] * 4 + [
             jax.ShapeDtypeStruct((pairs, head_size, PAIR), jnp.float32),
-        ] * 2,
+        ] * 2 + [jax.ShapeDtypeStruct((blocks, pairs, head_size, PAIR), jnp.float32)],
         scratch_shapes=[pltpu.VMEM((block_ticks + STRIDE, feat), jnp.float32),
                         pltpu.VMEM(qkv_weight.shape, qkv_weight.dtype),
                         pltpu.SemaphoreType.DMA(())],
         compiler_params=pltpu.CompilerParams(dimension_semantics=("arbitrary",)),
-    )(ticks, prev, conv_weight, norm_gain, qkv_weight)
+    )(ticks, prev, conv_weight, norm_gain, qkv_weight, packed_in)
 
     halves = 2
     piece_width = model_width // halves
@@ -215,12 +224,6 @@
     while block < blocks * halves:
         inside = inside_block(block, inside, queries, keys, values)
         block += 1
-    packed_in = state_in.reshape(pairs, 2, head_size, head_size).transpose(0, 2, 1, 3)
-    packed_in = packed_in.reshape(pairs, head_size, PAIR)
-    base = [packed_in - local]
-    for block in range(1, blocks):
-        base.append(base[-1] + first_state)
-    base = jnp.stack(base)
     base_spec = pl.BlockSpec((1, pairs, head_size, PAIR), lambda b: (b, 0, 0, 0))
 
     return pl.pallas_call(

time: 66.1 us -> 67.4 us (1.020)
  local copies, waits for them, and re-layouts: 3.11 us -> 4.78 us
  other arithmetic: 0.93 us -> 0.07 us
  Pallas kernels: 37.1 us -> 37.8 us
    reshape x1, local copies, waits for them, and re-layouts: 0.31 us -> 1.3 us  [shards(): state_in.reshape(pairs, 2, head_size, head_size).transpose(0, 2, 1, 3)]
    another operation x2 -> x0, other arithmetic: 0.86 us -> none  [shards(): base = jnp.stack(base)]
    pallas_call x1, Pallas kernels: 14 us -> 14.7 us  [shards(): pl.pallas_call(embed_kernel, grid=(blocks,), in_specs=[pl.BlockSpec((bloc...]
    reshape x1, local copies, waits for them, and re-layouts: 0.24 us -> 0.92 us  [shards(): packed_in = packed_in.reshape(pairs, head_size, PAIR)]
  transfers between devices with their start and end apart: 5 -> 5, of which waited for: 5 -> 5; matrix products, arithmetic and copies ran while one was open for 3% -> 4% of each run, Pallas kernels for 24% -> 24%
where the time goes in v20:
time: 67.4 us; the launch traced here: 67 us
  Pallas kernels  37.8 us (56%)
  waiting for transfers between devices  16.2 us (24%)
  starting transfers between devices  8.02 us (12%)
  local copies, waits for them, and re-layouts  4.78 us (7%)
    ppermute x5, waiting for transfers between devices, from_behind(): lax.ppermute(value, axis, [(source, source + steps) for source in range(i...  16.2 us
    pallas_call x4, Pallas kernels, inside_block(): pl.pallas_call(kernel, grid=(1,), in_specs=in_specs, out_specs=spec, out_...  16.1 us
    pallas_call x1, Pallas kernels, shards(): pl.pallas_call(embed_kernel, grid=(blocks,), in_specs=[pl.BlockSpec((bloc...  14.7 us
    ppermute x5, starting transfers between devices, from_behind(): lax.ppermute(value, axis, [(source, source + steps) for source in range(i...  8.02 us
    pallas_call x1, Pallas kernels, shards(): pl.pallas_call(out_kernel, grid=(blocks,), in_specs=[rows_spec, base_spec...  7.01 us
  transfers between devices with their start and end apart: 5, of which 5 were waited for; matrix products, arithmetic and copies ran while one was open for 4% of the time, Pallas kernels for 24%

profile of v20, /device:TPU:30, one launch (start us, length us, event | category | flops | bytes accessed | tf_op | source)
XLA Modules:
  0.0 67.0 jit_solution(11418529551071911047)
XLA Ops:
  0.0 0.7 %slice.3 = bf16[16,128]{1,0:T(8,128)(2,1)S(1)} slice(bf16[8192,128]{1,0:T(8,128)(2,1)} %ticks_ref.1), slice={[8176:8192], [0:128]} | slice | bytes 8192 | tf_op jit(solution)/shard_map/slice | solution.py:156
  0.7 1.9 %collective-permute-start = (bf16[16,128]{1,0:T(8,128)(2,1)S(1)}, bf16[16,128]{1,0:T(8,128)(2,1)S(1)}, u32[]{:S(2)}, u32[]{:S(2)}) collective-permute-start(bf16[16,128]{1,0:T(8,128)(2,1)S(1)} %slice.3), channel_id=1, source_target_pairs={{0,1},{1,2},{2,3},{3,4},{4,5},{5,6},{6,7},{7,8},{8,9},{9,10},{10,1... | collective-permute-start | bytes 12296 | tf_op jit(solution)/shard_map/ppermute | solution.py:18
  2.6 1.3 %copy.13 = f32[6,2,64,64]{3,1,2,0:T(2,128)S(1)} copy(f32[6,2,64,64]{3,2,1,0:T(8,128)} %bitcast.5) | data formatting | bytes 393216 | tf_op jit(solution)/shard_map/reshape | solution.py:159
  3.9 0.9 %reshape.10.start_ref = f32[6,64,128]{2,1,0:T(8,128)} reshape(f32[6,64,2,64]{3,2,1,0:T(2,128)S(1)} %bitcast.4) | data formatting | bytes 393216 | tf_op jit(solution)/shard_map/reshape | solution.py:160
  4.8 0.8 %collective-permute-done.prev_ref = bf16[16,128]{1,0:T(8,128)(2,1)S(1)} collective-permute-done((bf16[16,128]{1,0:T(8,128)(2,1)S(1)}, bf16[16,128]{1,0:T(8,128)(2,1)S(1)}, u32[]{:S(2)}, u32[]{:S(2)}) %collective-permute-start) | collective-permute-done | bytes 4128 | tf_op jit(solution)/shard_map/ppermute | solution.py:18
  5.6 0.0 copy-start.3
  5.6 0.6 copy-done.3
  6.2 14.7 %shard_map.73 = (bf16[1024,768]{1,0:T(8,128)(2,1)}, bf16[1024,768]{1,0:T(8,128)(2,1)}, bf16[1024,768]{1,0:T(8,128)(2,1)}, bf16[1024,768]{1,0:T(8,128)(2,1)}, f32...) custom-call(bf16[8192,128]{1,0:T(8,128)(2,1)} %ticks_ref.1, bf16[16,128]{1,0:T(8,128)(2,1)} %copy-done.3, ...), custom_call_target="tpu_custom_call" | custom-call | tf_op jit(solution)/shard_map/pallas_call | solution.py:161
  20.9 0.0 copy-start.1
  20.9 2.1 %collective-permute-start.1 = (f32[6,64,128]{2,1,0:T(8,128)}, f32[6,64,128]{2,1,0:T(8,128)S(1)}, u32[]{:S(2)}, u32[]{:S(2)}) collective-permute-start(f32[6,64,128]{2,1,0:T(8,128)} %get-tuple-element.40), channel_id=1, source_target_pairs={{0,1},{1,2},{2,3},{3,4},{4,5},{5,6},{6,7},{7,8},{8,9},{9,10},{10,1... | collective-permute-start | bytes 589832 | tf_op jit(solution)/shard_map/ppermute | solution.py:18
  23.0 4.0 %shard_map.74.earlier_ref = f32[1024,768]{1,0:T(8,128)} custom-call(bf16[1024,768]{1,0:T(8,128)(2,1)} %get-tuple-element.58.q_ref, bf16[1024,768]{1,0:T(8,128)(2,1)} %get-tuple-element.59.k_ref, bf16[1024,768]{1,0:T(8,128)(2,1)} %get-tuple-element.60.v_ref), custom_call_target="tpu_custom_call" | custom-call | flops 805306368 | bytes 1966080 | tf_op jit(solution)/shard_map/pallas_call | solution.py:197
  27.0 1.2 %collective-permute-done.1 = f32[6,64,128]{2,1,0:T(8,128)S(1)} collective-permute-done((f32[6,64,128]{2,1,0:T(8,128)}, f32[6,64,128]{2,1,0:T(8,128)S(1)}, u32[]{:S(2)}, u32[]{:S(2)}) %collective-permute-start.1) | collective-permute-done | bytes 196640 | tf_op jit(solution)/shard_map/ppermute | solution.py:18
  28.3 0.0 copy-done.1
  28.3 1.3 %collective-permute-start.2 = (f32[6,64,128]{2,1,0:T(8,128)S(1)}, f32[6,64,128]{2,1,0:T(8,128)S(1)}, u32[]{:S(2)}, u32[]{:S(2)}) collective-permute-start(f32[6,64,128]{2,1,0:T(8,128)S(1)} %add.9), channel_id=1, source_target_pairs={{0,2},{1,3},{2,4},{3,5},{4,6},{5,7},{6,8},{7,9},{8,10},{9,11},{10,... | collective-permute-start | bytes 589832 | tf_op jit(solution)/shard_map/ppermute | solution.py:18
  29.6 4.0 %shard_map.75.earlier_ref = f32[1024,768]{1,0:T(8,128)} custom-call(bf16[1024,768]{1,0:T(8,128)(2,1)} %get-tuple-element.58.q_ref, bf16[1024,768]{1,0:T(8,128)(2,1)} %get-tuple-element.59.k_ref, bf16[1024,768]{1,0:T(8,128)(2,1)} %get-tuple-element.60.v_ref, f32[1024,768]{1,0:T(8,128)} %shard_map.74.earlier_ref), custom_call_target="tpu_custom_call", output_to_operand_aliasing={{}: (3, {})} | custom-call | flops 805306368 | bytes 1966080 | tf_op jit(solution)/shard_map/pallas_call | solution.py:197
  33.6 2.6 %collective-permute-done.2 = f32[6,64,128]{2,1,0:T(8,128)S(1)} collective-permute-done((f32[6,64,128]{2,1,0:T(8,128)S(1)}, f32[6,64,128]{2,1,0:T(8,128)S(1)}, u32[]{:S(2)}, u32[]{:S(2)}) %collective-permute-start.2) | collective-permute-done | bytes 196640 | tf_op jit(solution)/shard_map/ppermute | solution.py:18
  36.2 0.0 copy-start.4
  36.2 1.3 %collective-permute-start.3 = (f32[6,64,128]{2,1,0:T(8,128)S(1)}, f32[6,64,128]{2,1,0:T(8,128)S(1)}, u32[]{:S(2)}, u32[]{:S(2)}) collective-permute-start(f32[6,64,128]{2,1,0:T(8,128)S(1)} %add.10), channel_id=1, source_target_pairs={{0,4},{1,5},{2,6},{3,7},{4,8},{5,9},{6,10},{7,11},{8,12},{9,13},{1... | collective-permute-start | bytes 589832 | tf_op jit(solution)/shard_map/ppermute | solution.py:18
  37.5 4.0 %shard_map.76.earlier_ref = f32[1024,768]{1,0:T(8,128)} custom-call(bf16[1024,768]{1,0:T(8,128)(2,1)} %get-tuple-element.58.q_ref, bf16[1024,768]{1,0:T(8,128)(2,1)} %get-tuple-element.59.k_ref, bf16[1024,768]{1,0:T(8,128)(2,1)} %get-tuple-element.60.v_ref, f32[1024,768]{1,0:T(8,128)} %shard_map.75.earlier_ref), custom_call_target="tpu_custom_call", output_to_operand_aliasing={{}: (3, {})} | custom-call | flops 805306368 | bytes 1966080 | tf_op jit(solution)/shard_map/pallas_call | solution.py:197
  41.6 4.3 %collective-permute-done.3 = f32[6,64,128]{2,1,0:T(8,128)S(1)} collective-permute-done((f32[6,64,128]{2,1,0:T(8,128)S(1)}, f32[6,64,128]{2,1,0:T(8,128)S(1)}, u32[]{:S(2)}, u32[]{:S(2)}) %collective-permute-start.3) | collective-permute-done | bytes 196640 | tf_op jit(solution)/shard_map/ppermute | solution.py:18
  45.9 0.0 copy-start
  45.9 1.5 %collective-permute-start.4 = (f32[6,64,128]{2,1,0:T(8,128)S(1)}, f32[6,64,128]{2,1,0:T(8,128)S(1)}, u32[]{:S(2)}, u32[]{:S(2)}) collective-permute-start(f32[6,64,128]{2,1,0:T(8,128)S(1)} %add.11.total_ref), channel_id=1, source_target_pairs={{0,8},{1,9},{2,10},{3,11},{4,12},{5,13},{6,14},{7,15},{16,24},{17,... | collective-permute-start | bytes 589832 | tf_op jit(solution)/shard_map/ppermute | solution.py:18
  47.4 0.0 copy-done.4
  47.4 0.6 reshape.11.hgain_ref
  48.0 4.0 %shard_map.77.inside_ref = f32[1024,768]{1,0:T(8,128)} custom-call(bf16[1024,768]{1,0:T(8,128)(2,1)} %get-tuple-element.58.q_ref, bf16[1024,768]{1,0:T(8,128)(2,1)} %get-tuple-element.59.k_ref, bf16[1024,768]{1,0:T(8,128)(2,1)} %get-tuple-element.60.v_ref, f32[1024,768]{1,0:T(8,128)} %shard_map.76.earlier_ref), custom_call_target="tpu_custom_call", output_to_operand_aliasing={{}: (3, {})} | custom-call | flops 805306368 | bytes 1966080 | tf_op jit(solution)/shard_map/pallas_call | solution.py:197
  52.0 0.0 copy-done
  52.0 7.3 %collective-permute-done.4.received_ref = f32[6,64,128]{2,1,0:T(8,128)S(1)} collective-permute-done((f32[6,64,128]{2,1,0:T(8,128)S(1)}, f32[6,64,128]{2,1,0:T(8,128)S(1)}, u32[]{:S(2)}, u32[]{:S(2)}) %collective-permute-start.4) | collective-permute-done | bytes 196640 | tf_op jit(solution)/shard_map/ppermute | solution.py:18
  59.3 0.0 copy-start.2
  59.3 0.7 copy-done.2
  60.0 7.0 %shard_map.78 = bf16[1024,768]{1,0:T(8,128)(2,1)} custom-call(bf16[1024,768]{1,0:T(8,128)(2,1)} %get-tuple-element.58.q_ref, f32[2,6,64,128]{3,2,1,0:T(8,128)} %get-tuple-element.36.base_ref, f32[6,64,128]{2,1,0:T(8,128)} %copy-done, f32[6,64,128]{2,1,0:T(8,128)} %copy-done.2, f32[1024,768]{1,0:T(8,128)} %shard_map.77.inside_ref, ...), custom_call_target="tpu_custom_call" | custom-call | tf_op jit(solution)/shard_map/pallas_call | solution.py:229
  (3 shorter events, 0.1 us)
Async XLA Ops:
  0.7 4.9 %collective-permute-start = (bf16[16,128]{1,0:T(8,128)(2,1)S(1)}, bf16[16,128]{1,0:T(8,128)(2,1)S(1)}, u32[]{:S(2)}, u32[]{:S(2)}) collective-permute-start(bf16[16,128]{1,0:T(8,128)(2,1)S(1)} %slice.3), channel_id=1, source_target_pairs={{0,1},{1,2},{2,3},{3,4},{4,5},{5,6},{6,7},{7,8},{8,9},{9,10},{10,1... | collective-permute-start | bytes 12296 | tf_op jit(solution)/shard_map/ppermute | solution.py:18
  5.6 0.6 copy-start.3
  20.9 7.3 %copy-start.1 = (f32[6,64,128]{2,1,0:T(8,128)S(1)}, f32[6,64,128]{2,1,0:T(8,128)}, u32[]{:S(2)}) copy-start(f32[6,64,128]{2,1,0:T(8,128)} %get-tuple-element.40) | copy-start | bytes 589828
  20.9 7.3 %collective-permute-start.1 = (f32[6,64,128]{2,1,0:T(8,128)}, f32[6,64,128]{2,1,0:T(8,128)S(1)}, u32[]{:S(2)}, u32[]{:S(2)}) collective-permute-start(f32[6,64,128]{2,1,0:T(8,128)} %get-tuple-element.40), channel_id=1, source_target_pairs={{0,1},{1,2},{2,3},{3,4},{4,5},{5,6},{6,7},{7,8},{8,9},{9,10},{10,1... | collective-permute-start | bytes 589832 | tf_op jit(solution)/shard_map/ppermute | solution.py:18
  28.3 7.9 %collective-permute-start.2 = (f32[6,64,128]{2,1,0:T(8,128)S(1)}, f32[6,64,128]{2,1,0:T(8,128)S(1)}, u32[]{:S(2)}, u32[]{:S(2)}) collective-permute-start(f32[6,64,128]{2,1,0:T(8,128)S(1)} %add.9), channel_id=1, source_target_pairs={{0,2},{1,3},{2,4},{3,5},{4,6},{5,7},{6,8},{7,9},{8,10},{9,11},{10,... | collective-permute-start | bytes 589832 | tf_op jit(solution)/shard_map/ppermute | solution.py:18
  36.2 11.2 %copy-start.4 = (f32[768]{0:T(1024)S(1)}, f32[768]{0:T(1024)}, u32[]{:S(2)}) copy-start(f32[768]{0:T(1024)} %param.11) | copy-start | bytes 9220
  36.2 9.6 %collective-permute-start.3 = (f32[6,64,128]{2,1,0:T(8,128)S(1)}, f32[6,64,128]{2,1,0:T(8,128)S(1)}, u32[]{:S(2)}, u32[]{:S(2)}) collective-permute-start(f32[6,64,128]{2,1,0:T(8,128)S(1)} %add.10), channel_id=1, source_target_pairs={{0,4},{1,5},{2,6},{3,7},{4,8},{5,9},{6,10},{7,11},{8,12},{9,13},{1... | collective-permute-start | bytes 589832 | tf_op jit(solution)/shard_map/ppermute | solution.py:18
  45.9 6.1 %copy-start = (f32[6,64,128]{2,1,0:T(8,128)}, f32[6,64,128]{2,1,0:T(8,128)S(1)}, u32[]{:S(2)}) copy-start(f32[6,64,128]{2,1,0:T(8,128)S(1)} %add.11.total_ref) | copy-start | bytes 589828
  45.9 13.4 %collective-permute-start.4 = (f32[6,64,128]{2,1,0:T(8,128)S(1)}, f32[6,64,128]{2,1,0:T(8,128)S(1)}, u32[]{:S(2)}, u32[]{:S(2)}) collective-permute-start(f32[6,64,128]{2,1,0:T(8,128)S(1)} %add.11.total_ref), channel_id=1, source_target_pairs={{0,8},{1,9},{2,10},{3,11},{4,12},{5,13},{6,14},{7,15},{16,24},{17,... | collective-permute-start | bytes 589832 | tf_op jit(solution)/shard_map/ppermute | solution.py:18
  59.3 0.7 copy-start.2
